TPU v7x, 256 devices: a whole 4x4x8 slice. The times are simulated.
256 devices in a mesh: mem: 4 (over x), col: 64 (over y, z, core).
Axes of the slice: x: 4, y: 4, z: 8, core: 2. Of those that a mesh axis runs over, the one named last changes fastest.
Arguments:
- perturbations: bfloat16 [32, 256, 256, 128], P('mem', 'col'), may hold values from -4 to 4
- static_root: float32 [128, 128], replicated, may hold values from -0.5 to 1.5
- obs_jacobian: float32 [128, 128], replicated, may hold values from -0.5 to 0.5
- innovations: float32 [16384, 128], P('col'), may hold values from -6 to 6
- obs_weights: float32 [128], replicated, may hold values from 0.2 to 2
- length_scale: float32 [256, 256], P('col'), may hold values from 0.05 to 0.24
- obs_owner: int32 [16384, 1], P('col'), may hold values from 0 to 63; in each aligned block of 256 rows (0 to 255, 256 to 511, ...) at most 8 rows name the same one
- obs_cell: int32 [16384], P('col'), may hold values from 0 to 1023
- obs_count: int32 [64], P('col'), may hold values from 128 to 256, as said below
Outputs:
- increment: float32 [256, 256, 128], P('col', 'mem')
- control_static: float32 [256, 256, 128], P('col', 'mem')
- control_ensemble: float32 [32, 256, 256], P('mem', 'col')
Inputs may be any that keep to these rules, and one draw needn't show every extreme that they name: `obs_owner`: each holder's 256 rows name any one column block at most 8 times. `obs_count`: rows at or past a holder's count are padding and are ignored; at least one holder is full. `obs_cell`: the column within the owner's block, numbered y * 256 + x, where y is its grid row within the block (0 to 3).
All inputs are finite; a program needn't handle non-finite values.
Results may differ from a plain program's by a relative error of at most 0.004.
Values may be sent and summed in bfloat16 or wider, within the bound.
No kernel may reach another device: no remote copies, remote signals or barrier semaphores. Data moves between devices by JAX's collectives and lax.ppermute only.
A program may use at most 64 MiB of HBM per device.

v0:
```python
import jax
import jax.numpy as jnp
from jax import lax
from jax.sharding import PartitionSpec as P

NSWEEP = 4
ITERS = 2


def extended(block, sides, width):
    for axis, dim in sides:
        count = lax.axis_size(axis)
        forward = [(i, i + 1) for i in range(count - 1)]
        backward = [(target, source) for source, target in forward]
        low = lax.ppermute(
            lax.slice_in_dim(block, block.shape[dim] - width, None, axis=dim), axis, forward
        )
        high = lax.ppermute(lax.slice_in_dim(block, 0, width, axis=dim), axis, backward)
        block = jnp.concatenate([low, block, high], axis=dim)
    return block


def face_coefficients(length_scale):
    rimmed = extended(length_scale, (("col", 0),), 1)
    padded = jnp.pad(rimmed, ((0, 0), (1, 1)))
    return (
        jnp.sqrt(length_scale * padded[:-2, 1:-1]),
        jnp.sqrt(length_scale * padded[2:, 1:-1]),
        jnp.sqrt(length_scale * padded[1:-1, :-2]),
        jnp.sqrt(length_scale * padded[1:-1, 2:]),
    )


def sweeps(values, coeffs):
    face_up, face_down, face_left, face_right = coeffs
    for sweep_step in range(NSWEEP):
        rimmed = extended(values, (("col", 1),), 1)
        padded = jnp.pad(rimmed, ((0, 0), (0, 0), (1, 1)))
        centre = values
        values = (
            centre
            + face_up * (padded[:, :-2, 1:-1] - centre)
            + face_down * (padded[:, 2:, 1:-1] - centre)
            + face_left * (padded[:, 1:-1, :-2] - centre)
            + face_right * (padded[:, 1:-1, 2:] - centre)
        )
    return values


def local_inner(first, second):
    return jnp.sum(first[0] * second[0]) + jnp.sum(first[1] * second[1])


def shards(
    perturbations,
    static_root,
    obs_jacobian,
    innovations,
    obs_weights,
    length_scale,
    obs_owner,
    obs_cell,
    obs_count,
):
    members, rows_here, columns, features = perturbations.shape
    quarter = columns // lax.axis_size("mem")
    offset = lax.axis_index("mem") * quarter
    blocks = lax.axis_size("col")
    obs_dev, channels = innovations.shape
    capacity = max(2, 2 * obs_dev // blocks)
    total_slots = blocks * capacity
    coeffs = face_coefficients(length_scale)
    is_live = jnp.arange(obs_dev, dtype=jnp.int32) < obs_count[0]
    owner_ids = obs_owner[:, 0]
    onehot = (
        (owner_ids[:, None] == jnp.arange(blocks, dtype=jnp.int32)[None, :]) & is_live[:, None]
    ).astype(jnp.int32)
    slot_rank = jnp.sum((jnp.cumsum(onehot, axis=0) - onehot) * onehot, axis=1)
    slot_ids = jnp.where(is_live, owner_ids * capacity + slot_rank, total_slots)
    send_values = (
        jnp.zeros((total_slots, channels), jnp.float32).at[slot_ids].set(innovations, mode="drop")
    )
    send_cells = jnp.zeros((total_slots,), jnp.int32).at[slot_ids].set(obs_cell, mode="drop")
    send_marks = jnp.zeros((total_slots,), jnp.float32).at[slot_ids].set(1.0, mode="drop")
    got_values, got_cells, got_marks = (
        lax.all_to_all(
            send_values.reshape(blocks, capacity, channels),
            "col",
            split_axis=0,
            concat_axis=0,
            tiled=True,
        ),
        lax.all_to_all(
            send_cells.reshape(blocks, capacity), "col", split_axis=0, concat_axis=0, tiled=True
        ),
        lax.all_to_all(
            send_marks.reshape(blocks, capacity), "col", split_axis=0, concat_axis=0, tiled=True
        ),
    )
    got_values = got_values.reshape(total_slots, channels)
    got_cells = got_cells.reshape(total_slots)
    got_marks = got_marks.reshape(total_slots)
    obs_index = got_cells
    obs_gain = got_marks[:, None] * obs_weights[None, :]

    def spread_back(weighted):
        back = jnp.dot(weighted, obs_jacobian.T, precision=lax.Precision.HIGHEST)
        grid = jnp.zeros((rows_here * columns, features), jnp.float32).at[obs_index].add(back)
        return grid.reshape(rows_here, columns, features)

    def adjoint_map(gradient):
        own_gradient = lax.dynamic_slice_in_dim(gradient, offset, quarter, 1)
        rounded = gradient.astype(jnp.bfloat16)
        static = jnp.dot(
            own_gradient.reshape(rows_here * quarter, features),
            static_root.T,
            precision=lax.Precision.HIGHEST,
        ).reshape(rows_here, quarter, features)
        projected = jnp.einsum(
            "kyxf,yxf->kyx", perturbations, rounded, preferred_element_type=jnp.float32
        )
        return (static, sweeps(projected, coeffs))

    residual = adjoint_map(spread_back(obs_gain * got_values))
    direction = residual
    state = (jnp.zeros_like(residual[0]), jnp.zeros_like(residual[1]))
    increment = jnp.zeros((rows_here, quarter, features), jnp.float32)
    norm_now = lax.psum(local_inner(residual, residual), ("mem", "col"))
    for iteration in range(ITERS):
        smoothed = sweeps(direction[1], coeffs).astype(jnp.bfloat16)
        partial_sum = jnp.einsum(
            "kyxf,kyx->yxf", perturbations, smoothed, preferred_element_type=jnp.float32
        )
        forward_static = jnp.dot(
            direction[0].reshape(rows_here * quarter, features),
            static_root,
            precision=lax.Precision.HIGHEST,
        ).reshape(rows_here, quarter, features)
        own_slice = lax.dynamic_slice_in_dim(partial_sum, offset, quarter, 1) + forward_static
        partial_sum = lax.dynamic_update_slice_in_dim(partial_sum, own_slice, offset, 1)
        image_part = lax.psum(partial_sum, "mem")
        own_image = lax.dynamic_slice_in_dim(image_part, offset, quarter, 1)
        image_part, own_image = (image_part, own_image)
        gathered = image_part.reshape(rows_here * columns, features)[obs_index]
        model_obs = jnp.dot(gathered, obs_jacobian, precision=lax.Precision.HIGHEST)
        adj_static, adj_ensemble = adjoint_map(spread_back(obs_gain * model_obs))
        image = (direction[0] + adj_static, direction[1] + adj_ensemble)
        step = norm_now / lax.psum(local_inner(direction, image), ("mem", "col"))
        residual = (residual[0] - step * image[0], residual[1] - step * image[1])
        norm_next = lax.psum(local_inner(residual, residual), ("mem", "col"))
        state = (state[0] + step * direction[0], state[1] + step * direction[1])
        increment = increment + step * own_image
        ratio = norm_next / norm_now
        direction = (residual[0] + ratio * direction[0], residual[1] + ratio * direction[1])
        norm_now = norm_next
    return (increment, state[0], state[1])


def solution(mesh):
    placed = (
        P("mem", "col", None, None),
        P(),
        P(),
        P("col", None),
        P(),
        P("col", None),
        P("col", None),
        P("col"),
        P("col"),
    )
    return jax.shard_map(
        shards,
        mesh=mesh,
        in_specs=placed,
        out_specs=(P("col", "mem", None), P("col", "mem", None), P("mem", "col", None)),
        check_vma=False,
    )
```

profile of v0, /device:TPU:1, one launch (start us, length us, event | category | flops | bytes accessed | tf_op | source)
XLA Modules:
  0.0 627.2 jit_solution(7078985824332760388)
XLA Ops:
  13.3 13.1 %all-to-all-start = ((s32[64,1,8]{2,1,0:T(1,128)}), s32[64,1,8]{2,1,0:T(1,128)S(1)}, u32[]{:S(2)}, u32[]{:S(2)}) async-start(s32[64,1,8]{2,1,0:T(1,128)} %bitcast.6), calls=%async_computation | async-start | bytes 65536 | tf_op jit(solution)/shard_map/all_to_all | solution.py:93
  28.5 7.1 %all-to-all-done = s32[64,1,8]{2,1,0:T(1,128)S(1)} async-done(((s32[64,1,8]{2,1,0:T(1,128)}), s32[64,1,8]{2,1,0:T(1,128)S(1)}, u32[]{:S(2)}, u32[]{:S(2)}) %all-to-all-start) | async-done | bytes 2080 | tf_op jit(solution)/shard_map/all_to_all | solution.py:93
  35.7 4.7 all-to-all-start.1
  42.5 7.2 %all-to-all-done.1 = f32[64,1,8]{2,1,0:T(1,128)S(1)} async-done(((f32[64,1,8]{2,1,0:T(1,128)}), f32[64,1,8]{2,1,0:T(1,128)S(1)}, u32[]{:S(2)}, u32[]{:S(2)}) %all-to-all-start.1) | async-done | bytes 2080 | tf_op jit(solution)/shard_map/all_to_all | solution.py:96
  49.7 4.7 all-to-all-start.2
  55.3 3.5 collective-permute-start
  60.7 3.2 collective-permute-done.2
  68.7 3.3 scatter_custom_fusion.3
  93.0 3.7 collective-permute-done.7
  101.3 4.2 collective-permute-done.9
  110.3 3.8 collective-permute-done.11
  118.8 3.8 collective-permute-done.13
  142.7 54.6 %all-reduce.25.cloned.1.call-done = f32[4,256,128]{2,1,0:T(8,128)} async-done(((f32[4,256,128]{2,1,0:T(8,128)}), f32[4,256,128]{2,1,0:T(8,128)}) %all-reduce.25.cloned.1.call-update) | async-done | bytes 524304 | tf_op jit(solution)/shard_map/psum | solution.py:141
  200.1 3.3 scatter_custom_fusion.4
  207.1 5.8 collective-permute-start.18
  237.8 4.1 collective-permute-done.25
  245.4 80.9 %all-reduce.21 = (f32[]{:T(128)}, f32[]{:T(128)}) all-reduce(f32[]{:T(128)S(6)} %add.401, f32[]{:T(128)S(6)} %add.437), channel_id=1, replica_groups=mesh['mem'=4,'col'=64] {'mem','col'}, use_global_device_ids=true, to_apply=%region_9.10 | all-reduce | flops 2 | bytes 16 | tf_op jit(solution)/shard_map/psum | solution.py:128
  330.1 72.6 %psum.45 = f32[]{:T(128)} all-reduce(f32[]{:T(128)S(6)} %add.438), channel_id=1, replica_groups=mesh['mem'=4,'col'=64] {'mem','col'}, use_global_device_ids=true, to_apply=%region_17.18 | all-reduce | flops 1 | bytes 8 | tf_op jit(solution)/shard_map/psum | solution.py:150
  404.1 4.2 collective-permute-start.26
  440.1 49.0 %all-reduce.27.cloned.1.call-done = f32[4,256,128]{2,1,0:T(8,128)} async-done(((f32[4,256,128]{2,1,0:T(8,128)}), f32[4,256,128]{2,1,0:T(8,128)}) %all-reduce.27.cloned.1.call-update) | async-done | bytes 524304 | tf_op jit(solution)/shard_map/psum | solution.py:141
  491.9 3.3 scatter_custom_fusion.5
  498.9 5.8 collective-permute-start.34
  529.6 4.1 collective-permute-done.41
  535.9 80.8 %psum.47 = f32[]{:T(128)} all-reduce(f32[]{:T(128)S(6)} %add.476), channel_id=1, replica_groups=mesh['mem'=4,'col'=64] {'mem','col'}, use_global_device_ids=true, to_apply=%region_22.23 | all-reduce | flops 1 | bytes 8 | tf_op jit(solution)/shard_map/psum | solution.py:148
  (212 shorter events, 171.0 us)
Async XLA Ops:
  13.3 22.4 %all-to-all-start = ((s32[64,1,8]{2,1,0:T(1,128)}), s32[64,1,8]{2,1,0:T(1,128)S(1)}, u32[]{:S(2)}, u32[]{:S(2)}) async-start(s32[64,1,8]{2,1,0:T(1,128)} %bitcast.6), calls=%async_computation | async-start | bytes 65536 | tf_op jit(solution)/shard_map/all_to_all | solution.py:93
  35.7 14.1 %all-to-all-start.1 = ((f32[64,1,8]{2,1,0:T(1,128)}), f32[64,1,8]{2,1,0:T(1,128)S(1)}, u32[]{:S(2)}, u32[]{:S(2)}) async-start(f32[64,1,8]{2,1,0:T(1,128)} %bitcast.8), calls=%async_computation.1 | async-start | bytes 65536 | tf_op jit(solution)/shard_map/all_to_all | solution.py:96
  49.7 17.7 %all-to-all-start.2 = ((f32[64,8,128]{2,1,0:T(8,128)}), f32[64,8,128]{2,1,0:T(8,128)S(1)}, u32[]{:S(2)}, u32[]{:S(2)}) async-start(f32[64,8,128]{2,1,0:T(8,128)} %bitcast.9), calls=%async_computation.2 | async-start | bytes 524288 | tf_op jit(solution)/shard_map/all_to_all | solution.py:86
  54.4 142.8 %all-reduce.25.cloned.1.call-start = ((), (), s32[]{:S(2)}) async-start(), calls=%async_computation.3 | async-start | bytes 1048576 | tf_op jit(solution)/shard_map/psum | solution.py:141
  55.3 5.5 collective-permute-start
  58.8 5.2 collective-permute-start.2
  90.6 6.1 collective-permute-start.7
  98.9 6.6 %collective-permute-start.9 = (f32[8,1,256]{2,1,0:T(1,128)S(1)}, f32[8,1,256]{2,1,0:T(1,128)S(1)}, u32[]{:S(2)}, u32[]{:S(2)}) collective-permute-start(f32[8,1,256]{2,1,0:T(1,128)S(1)} %get-tuple-element.41), channel_id=1, source_target_pairs={{1,0},{2,1},{3,2},{4,3},{5,4},{6,5},{7,6},{8,7},{9,8},{10,9},{11,1... | collective-permute-start | bytes 24584 | tf_op jit(solution)/shard_map/ppermute | solution.py:18
  107.9 6.2 collective-permute-start.11
  116.3 6.2 collective-permute-start.13
  122.8 5.2 collective-permute-start.14
  124.7 6.2 collective-permute-start.15
  131.2 5.3 collective-permute-start.16
  133.1 6.2 collective-permute-start.17
  142.6 346.5 %all-reduce.27.cloned.1.call-start = ((), (), s32[]{:S(2)}) async-start(), calls=%async_computation.4 | async-start | bytes 1048576 | tf_op jit(solution)/shard_map/psum | solution.py:141
  207.1 7.8 %collective-permute-start.18 = (f32[8,1,256]{2,1,0:T(1,128)S(1)}, f32[8,1,256]{2,1,0:T(1,128)S(1)}, u32[]{:S(2)}, u32[]{:S(2)}) collective-permute-start(f32[8,1,256]{2,1,0:T(1,128)S(1)} %get-tuple-element.30), channel_id=1, source_target_pairs={{0,1},{1,2},{2,3},{3,4},{4,5},{5,6},{6,7},{7,8},{8,9},{9,10},{10,1... | collective-permute-start | bytes 24584 | tf_op jit(solution)/shard_map/ppermute | solution.py:15
  220.1 5.0 collective-permute-start.21
  232.6 5.2 collective-permute-start.24
  234.5 7.4 %collective-permute-start.25 = (f32[8,1,256]{2,1,0:T(1,128)S(1)}, f32[8,1,256]{2,1,0:T(1,128)S(1)}, u32[]{:S(2)}, u32[]{:S(2)}) collective-permute-start(f32[8,1,256]{2,1,0:T(1,128)S(1)} %get-tuple-element.25), channel_id=1, source_target_pairs={{1,0},{2,1},{3,2},{4,3},{5,4},{6,5},{7,6},{8,7},{9,8},{10,9},{11,1... | collective-permute-start | bytes 24584 | tf_op jit(solution)/shard_map/ppermute | solution.py:18
  404.1 6.4 %collective-permute-start.26 = (f32[8,1,256]{2,1,0:T(1,128)S(1)}, f32[8,1,256]{2,1,0:T(1,128)S(1)}, u32[]{:S(2)}, u32[]{:S(2)}) collective-permute-start(f32[8,1,256]{2,1,0:T(1,128)S(1)} %get-tuple-element.22), channel_id=1, source_target_pairs={{0,1},{1,2},{2,3},{3,4},{4,5},{5,6},{6,7},{7,8},{8,9},{9,10},{10,1... | collective-permute-start | bytes 24584 | tf_op jit(solution)/shard_map/ppermute | solution.py:15
  498.9 7.8 %collective-permute-start.34 = (f32[8,1,256]{2,1,0:T(1,128)S(1)}, f32[8,1,256]{2,1,0:T(1,128)S(1)}, u32[]{:S(2)}, u32[]{:S(2)}) collective-permute-start(f32[8,1,256]{2,1,0:T(1,128)S(1)} %get-tuple-element.14), channel_id=1, source_target_pairs={{0,1},{1,2},{2,3},{3,4},{4,5},{5,6},{6,7},{7,8},{8,9},{9,10},{10,1... | collective-permute-start | bytes 24584 | tf_op jit(solution)/shard_map/ppermute | solution.py:15
  511.9 5.0 collective-permute-start.37
  524.4 5.2 collective-permute-start.40
  526.3 7.4 %collective-permute-start.41 = (f32[8,1,256]{2,1,0:T(1,128)S(1)}, f32[8,1,256]{2,1,0:T(1,128)S(1)}, u32[]{:S(2)}, u32[]{:S(2)}) collective-permute-start(f32[8,1,256]{2,1,0:T(1,128)S(1)} %get-tuple-element.9), channel_id=1, source_target_pairs={{1,0},{2,1},{3,2},{4,3},{5,4},{6,5},{7,6},{8,7},{9,8},{10,9},{11,1... | collective-permute-start | bytes 24584 | tf_op jit(solution)/shard_map/ppermute | solution.py:18
  (31 other events, 349.7 us)
Sparse Core Ops, SparseCore 0:
  142.7 54.4 all-reduce.24
  440.2 48.8 all-reduce.26
where the time goes:
time: 629 us; the launch traced here: 627 us
  blocking collectives  234 us (37%)
  waiting for transfers between devices  183 us (29%)
  starting transfers between devices  124 us (20%)
  between operations  25.3 us (4%)
  other arithmetic  24.7 us (4%)
  local copies, waits for them, and re-layouts  18.9 us (3%)
  matrix products  17.4 us (3%)
    psum x2, waiting for transfers between devices, shards(): image_part = lax.psum(partial_sum, 'mem')  104 us
    psum x1, blocking collectives, shards(): norm_now = lax.psum(local_inner(residual, residual), ('mem', 'col'))  80.9 us
    psum x1, blocking collectives, shards(): step = norm_now / lax.psum(local_inner(direction, image), ('mem', 'col'))  80.8 us
    psum x1, blocking collectives, shards(): norm_next = lax.psum(local_inner(residual, residual), ('mem', 'col'))  72.6 us
    ppermute x21, waiting for transfers between devices, extended(): lax.ppermute(lax.slice_in_dim(block, 0, width, axis=dim), axis, backward)  65 us
    ppermute x21, starting transfers between devices, extended(): lax.ppermute(lax.slice_in_dim(block, block.shape[dim] - width, None, axis...  53 us
    ppermute x21, starting transfers between devices, extended(): lax.ppermute(lax.slice_in_dim(block, 0, width, axis=dim), axis, backward)  48 us
    all_to_all x1, starting transfers between devices, shards(): lax.all_to_all(send_cells.reshape(blocks, capacity), 'col', split_axis=0,...  13.1 us
  transfers between devices with their start and end apart: 47, of which 25 were waited for; matrix products, arithmetic and copies ran while one was open for 2% of the time, Pallas kernels for 0%

commit v1 on v0

v1 whole, which is shorter than its diff:
```python
import jax
import jax.numpy as jnp
from jax import lax
from jax.sharding import PartitionSpec as P

NSWEEP = 4
ITERS = 2


def neighbours(block, axis, dim):
    count = lax.axis_size(axis)
    forward = [(i, i + 1) for i in range(count - 1)]
    backward = [(target, source) for source, target in forward]
    low = lax.ppermute(block, axis, forward)
    high = lax.ppermute(block, axis, backward)
    return jnp.concatenate([low, block, high], axis=dim)


def face_coefficients(length_scale):
    rimmed = neighbours(length_scale, "col", 0)
    padded = jnp.pad(rimmed, ((1, 1), (1, 1)))
    centre = padded[1:-1, 1:-1]
    return (
        jnp.sqrt(centre * padded[:-2, 1:-1]),
        jnp.sqrt(centre * padded[2:, 1:-1]),
        jnp.sqrt(centre * padded[1:-1, :-2]),
        jnp.sqrt(centre * padded[1:-1, 2:]),
    )


def sweeps(values, coeffs):
    rows = values.shape[1]
    face_up, face_down, face_left, face_right = coeffs
    values = neighbours(values, "col", 1)
    for sweep_step in range(NSWEEP):
        padded = jnp.pad(values, ((0, 0), (1, 1), (1, 1)))
        centre = values
        values = (
            centre
            + face_up * (padded[:, :-2, 1:-1] - centre)
            + face_down * (padded[:, 2:, 1:-1] - centre)
            + face_left * (padded[:, 1:-1, :-2] - centre)
            + face_right * (padded[:, 1:-1, 2:] - centre)
        )
    return values[:, rows : 2 * rows]


def global_sum(values):
    for axis in ("col", "mem"):
        count = lax.axis_size(axis)
        stride = 1
        while stride < count:
            values = values + lax.ppermute(
                values, axis, [(i, i ^ stride) for i in range(count)]
            )
            stride *= 2
    return values


def mem_sum(values):
    parts = lax.axis_size("mem")
    pieces = values.reshape((parts, values.shape[0] // parts) + values.shape[1:])
    reduced = jnp.sum(lax.all_to_all(pieces, "mem", 0, 0, tiled=True), axis=0)
    spread = jnp.broadcast_to(reduced[None], pieces.shape)
    return lax.all_to_all(spread, "mem", 0, 0, tiled=True).reshape(values.shape)


def local_inner(first, second):
    return jnp.sum(first[0] * second[0]) + jnp.sum(first[1] * second[1])


def shards(
    perturbations,
    static_root,
    obs_jacobian,
    innovations,
    obs_weights,
    length_scale,
    obs_owner,
    obs_cell,
    obs_count,
):
    members, rows_here, columns, features = perturbations.shape
    parts = lax.axis_size("mem")
    quarter = columns // parts
    offset = lax.axis_index("mem") * quarter
    blocks = lax.axis_size("col")
    obs_dev, channels = innovations.shape
    capacity = max(2, 2 * obs_dev // blocks)
    total_slots = blocks * capacity
    coeffs = face_coefficients(length_scale)
    is_live = jnp.arange(obs_dev, dtype=jnp.int32) < obs_count[0]
    owner_ids = obs_owner[:, 0]
    onehot = (
        (owner_ids[:, None] == jnp.arange(blocks, dtype=jnp.int32)[None, :]) & is_live[:, None]
    ).astype(jnp.int32)
    slot_rank = jnp.sum((jnp.cumsum(onehot, axis=0) - onehot) * onehot, axis=1)
    slot_ids = jnp.where(is_live, owner_ids * capacity + slot_rank, total_slots)
    send_values = (
        jnp.zeros((total_slots, channels), jnp.float32).at[slot_ids].set(innovations, mode="drop")
    )
    send_cells = (
        jnp.zeros((total_slots,), jnp.float32)
        .at[slot_ids]
        .set(obs_cell.astype(jnp.float32), mode="drop")
    )
    send_marks = jnp.zeros((total_slots,), jnp.float32).at[slot_ids].set(1.0, mode="drop")
    side = jnp.zeros((blocks, 1, channels), jnp.float32)
    side = side.at[:, 0, :capacity].set(send_cells.reshape(blocks, capacity))
    side = side.at[:, 0, capacity : 2 * capacity].set(send_marks.reshape(blocks, capacity))
    packed = jnp.concatenate([send_values.reshape(blocks, capacity, channels), side], axis=1)
    got = lax.all_to_all(packed, "col", split_axis=0, concat_axis=0, tiled=True)
    got_values = got[:, :capacity, :].reshape(total_slots, channels)
    got_cells = got[:, capacity, :capacity].reshape(total_slots).astype(jnp.int32)
    got_marks = got[:, capacity, capacity : 2 * capacity].reshape(total_slots)
    obs_index = got_cells
    obs_gain = got_marks[:, None] * obs_weights[None, :]

    def spread_back(weighted):
        back = jnp.dot(weighted, obs_jacobian.T, precision=lax.Precision.HIGHEST)
        grid = jnp.zeros((rows_here * columns, features), jnp.float32).at[obs_index].add(back)
        return grid.reshape(rows_here, columns, features)

    def adjoint_map(gradient):
        own_gradient = lax.dynamic_slice_in_dim(gradient, offset, quarter, 1)
        rounded = gradient.astype(jnp.bfloat16)
        static = jnp.dot(
            own_gradient.reshape(rows_here * quarter, features),
            static_root.T,
            precision=lax.Precision.HIGHEST,
        ).reshape(rows_here, quarter, features)
        projected = jnp.einsum(
            "kyxf,yxf->kyx", perturbations, rounded, preferred_element_type=jnp.float32
        )
        return (static, sweeps(projected, coeffs))

    def forward_partial(direction):
        smoothed = sweeps(direction[1], coeffs).astype(jnp.bfloat16)
        partial_sum = jnp.einsum(
            "kyxf,kyx->yxf", perturbations, smoothed, preferred_element_type=jnp.float32
        )
        forward_static = jnp.dot(
            direction[0].reshape(rows_here * quarter, features),
            static_root,
            precision=lax.Precision.HIGHEST,
        ).reshape(rows_here, quarter, features)
        own_slice = lax.dynamic_slice_in_dim(partial_sum, offset, quarter, 1) + forward_static
        return lax.dynamic_update_slice_in_dim(partial_sum, own_slice, offset, 1)

    def hessian(direction, partial_sum):
        gathered = mem_sum(partial_sum.reshape(rows_here * columns, features)[obs_index])
        model_obs = jnp.dot(gathered, obs_jacobian, precision=lax.Precision.HIGHEST)
        adj_static, adj_ensemble = adjoint_map(spread_back(obs_gain * model_obs))
        return (direction[0] + adj_static, direction[1] + adj_ensemble)

    residual = adjoint_map(spread_back(obs_gain * got_values))
    direction = residual

    partial0 = forward_partial(direction)
    image = hessian(direction, partial0)
    sums = global_sum(
        jnp.stack(
            [
                local_inner(residual, residual),
                local_inner(direction, image),
                local_inner(image, image),
            ]
        )
    )
    norm_now, curve, image_norm = sums[0], sums[1], sums[2]
    step0 = norm_now / curve
    state = (step0 * direction[0], step0 * direction[1])
    residual = (residual[0] - step0 * image[0], residual[1] - step0 * image[1])
    norm_next = norm_now - 2.0 * step0 * curve + step0 * step0 * image_norm
    ratio = norm_next / norm_now
    direction = (residual[0] + ratio * direction[0], residual[1] + ratio * direction[1])
    norm_now = norm_next

    partial1 = forward_partial(direction)
    image = hessian(direction, partial1)
    step1 = norm_now / global_sum(local_inner(direction, image))
    state = (state[0] + step1 * direction[0], state[1] + step1 * direction[1])

    total = step0 * partial0 + step1 * partial1
    pieces = jnp.moveaxis(total.reshape(rows_here, parts, quarter, features), 1, 0)
    increment = jnp.sum(lax.all_to_all(pieces, "mem", 0, 0, tiled=True), axis=0)
    return (increment, state[0], state[1])


def solution(mesh):
    placed = (
        P("mem", "col", None, None),
        P(),
        P(),
        P("col", None),
        P(),
        P("col", None),
        P("col", None),
        P("col"),
        P("col"),
    )
    return jax.shard_map(
        shards,
        mesh=mesh,
        in_specs=placed,
        out_specs=(P("col", "mem", None), P("col", "mem", None), P("mem", "col", None)),
        check_vma=False,
    )
```

time: 629 us -> 290 us (0.46)
  the two profiles are of different devices: /device:TPU:1 before, /device:TPU:24 now
where the time goes in v1:
time: 290 us; the launch traced here: 285 us
  waiting for transfers between devices  85.6 us (30%)
  starting transfers between devices  73.1 us (25%)
  blocking collectives  39.7 us (14%)
  other arithmetic  30.5 us (11%)
  matrix products  21.4 us (7%)
  local copies, waits for them, and re-layouts  17.7 us (6%)
  between operations  17.2 us (6%)
    ppermute x16, waiting for transfers between devices, global_sum(): lax.ppermute(values, axis, [(i, i ^ stride) for i in range(count)])  50.3 us
    ppermute x16, starting transfers between devices, global_sum(): lax.ppermute(values, axis, [(i, i ^ stride) for i in range(count)])  27.6 us
    ppermute x6, waiting for transfers between devices, neighbours(): low = lax.ppermute(block, axis, forward)  24.5 us
    all_to_all x2, blocking collectives, mem_sum(): reduced = jnp.sum(lax.all_to_all(pieces, 'mem', 0, 0, tiled=True), axis=0)  21.6 us
    all_to_all x2, blocking collectives, mem_sum(): return lax.all_to_all(spread, 'mem', 0, 0, tiled=True).reshape(values.shape)  18.1 us
    ppermute x6, starting transfers between devices, neighbours(): high = lax.ppermute(block, axis, backward)  15.7 us
    ppermute x6, starting transfers between devices, neighbours(): low = lax.ppermute(block, axis, forward)  14.2 us
    all_to_all x1, starting transfers between devices, shards(): got = lax.all_to_all(packed, 'col', split_axis=0, concat_axis=0, tiled=True)  12.1 us
  transfers between devices with their start and end apart: 30, of which 24 were waited for; matrix products, arithmetic and copies ran while one was open for 2% of the time, Pallas kernels for 0%

profile of v1, /device:TPU:24, one launch (start us, length us, event | category | flops | bytes accessed | tf_op | source)
XLA Modules:
  0.0 285.2 jit_solution(6494666434687448216)
XLA Ops:
  15.0 12.1 %all-to-all-start = ((f32[64,9,128]{2,1,0:T(8,128)}), f32[64,9,128]{2,1,0:T(8,128)S(1)}, u32[]{:S(2)}, u32[]{:S(2)}) async-start(f32[64,9,128]{2,1,0:T(8,128)} %pad_maximum_fusion), calls=%async_computation | async-start | bytes 1048576 | tf_op jit(solution)/shard_map/all_to_all | solution.py:112
  29.2 5.6 %collective-permute-start.3 = (f32[4,256]{1,0:T(4,128)S(1)}, f32[4,256]{1,0:T(4,128)S(1)}, u32[]{:S(2)}, u32[]{:S(2)}) collective-permute-start(f32[4,256]{1,0:T(4,128)S(1)} %copy-done.15), channel_id=1, source_target_pairs={{1,0},{2,1},{3,2},{4,3},{5,4},{6,5},{7,6},{8,7},{9,8},{10,9},{11,1... | collective-permute-start | bytes 12296 | tf_op jit(solution)/shard_map/ppermute | solution.py:15
  34.8 4.9 %collective-permute-done.2 = f32[4,256]{1,0:T(4,128)S(1)} collective-permute-done((f32[4,256]{1,0:T(4,128)S(1)}, f32[4,256]{1,0:T(4,128)S(1)}, u32[]{:S(2)}, u32[]{:S(2)}) %collective-permute-start.2) | collective-permute-done | bytes 4128 | tf_op jit(solution)/shard_map/ppermute | solution.py:14
  39.9 4.0 %all-to-all-done = f32[64,9,128]{2,1,0:T(8,128)S(1)} async-done(((f32[64,9,128]{2,1,0:T(8,128)}), f32[64,9,128]{2,1,0:T(8,128)S(1)}, u32[]{:S(2)}, u32[]{:S(2)}) %all-to-all-start) | async-done | bytes 294944 | tf_op jit(solution)/shard_map/all_to_all | solution.py:112
  44.8 3.3 %scatter_custom_fusion.3 = f32[1024,128]{1,0:T(8,128)S(1)} fusion(s32[512]{0:T(512)S(1)} %bitcast.153, f32[512,128]{1,0:T(8,128)S(1)} %fusion.16, f32[]{:T(128)} %constant.77.clone.1), kind=kCustom, calls=%fused_computation.42 | custom fusion | flops 65536 | bytes 524292 | tf_op jit(solution)/shard_map/scatter-add | solution.py:121
  65.1 4.3 %collective-permute-done.4 = f32[8,4,256]{2,1,0:T(4,128)S(1)} collective-permute-done((f32[8,4,256]{2,1,0:T(4,128)S(1)}, f32[8,4,256]{2,1,0:T(4,128)S(1)}, u32[]{:S(2)}, u32[]{:S(2)}) %collective-permute-start.4) | collective-permute-done | bytes 32800 | tf_op jit(solution)/shard_map/ppermute | solution.py:14
  73.3 10.8 %all_to_all.30 = f32[4,128,128]{2,1,0:T(8,128)S(1)} all-to-all(f32[4,128,128]{2,1,0:T(8,128)S(1)} %bitcast.133), channel_id=1, replica_groups=mesh['mem'=4,'col'=64] {'mem'}, dimensions={0} | all-to-all | bytes 524288 | tf_op jit(solution)/shard_map/all_to_all | solution.py:63
  84.2 9.1 %all_to_all.31 = f32[4,128,128]{2,1,0:T(8,128)S(1)} all-to-all(f32[4,128,128]{2,1,0:T(8,128)S(1)} %broadcast_in_dim.15), channel_id=1, replica_groups=mesh['mem'=4,'col'=64] {'mem'}, dimensions={0} | all-to-all | bytes 524288 | tf_op jit(solution)/shard_map/all_to_all | solution.py:65
  95.4 3.6 %scatter_custom_fusion.4 = f32[1024,128]{1,0:T(8,128)S(1)} fusion(s32[512]{0:T(512)} %bitcast.154, f32[512,128]{1,0:T(8,128)} %fusion.282, f32[]{:T(128)} %constant.77.clone.1), kind=kCustom, calls=%fused_computation.40 | custom fusion | flops 65536 | bytes 524800 | tf_op jit(solution)/shard_map/scatter-add | solution.py:121
  108.6 4.2 %collective-permute-done.6 = f32[8,4,256]{2,1,0:T(4,128)S(1)} collective-permute-done((f32[8,4,256]{2,1,0:T(4,128)}, f32[8,4,256]{2,1,0:T(4,128)S(1)}, u32[]{:S(2)}, u32[]{:S(2)}) %collective-permute-start.6) | collective-permute-done | bytes 32800 | tf_op jit(solution)/shard_map/ppermute | solution.py:14
  120.2 3.6 %collective-permute-done.9 = f32[3]{0:T(128)S(1)} collective-permute-done((f32[3]{0:T(128)S(1)}, f32[3]{0:T(128)S(1)}, u32[]{:S(2)}, u32[]{:S(2)}) %collective-permute-start.9) | collective-permute-done | bytes 44 | tf_op jit(solution)/shard_map/ppermute | solution.py:53
  123.9 4.5 %collective-permute-done.10 = f32[3]{0:T(128)S(1)} collective-permute-done((f32[3]{0:T(128)S(1)}, f32[3]{0:T(128)S(1)}, u32[]{:S(2)}, u32[]{:S(2)}) %collective-permute-start.10) | collective-permute-done | bytes 44 | tf_op jit(solution)/shard_map/ppermute | solution.py:53
  129.5 6.3 %collective-permute-done.11 = f32[3]{0:T(128)S(1)} collective-permute-done((f32[3]{0:T(128)S(1)}, f32[3]{0:T(128)S(1)}, u32[]{:S(2)}, u32[]{:S(2)}) %collective-permute-start.11) | collective-permute-done | bytes 44 | tf_op jit(solution)/shard_map/ppermute | solution.py:53
  140.2 4.3 %collective-permute-done.13 = f32[3]{0:T(128)S(1)} collective-permute-done((f32[3]{0:T(128)S(1)}, f32[3]{0:T(128)S(1)}, u32[]{:S(2)}, u32[]{:S(2)}) %collective-permute-start.13) | collective-permute-done | bytes 44 | tf_op jit(solution)/shard_map/ppermute | solution.py:53
  144.5 10.2 %collective-permute-start.14 = (f32[3]{0:T(128)S(1)}, f32[3]{0:T(128)S(1)}, u32[]{:S(2)}, u32[]{:S(2)}) collective-permute-start(f32[3]{0:T(128)S(1)} %add.487), channel_id=1, source_target_pairs={{0,64},{64,0},{128,192},{192,128},{1,65},{65,1},{129,193},{193,129... | collective-permute-start | bytes 44 | tf_op jit(solution)/shard_map/ppermute | solution.py:53
  158.5 4.3 %collective-permute-done.15 = f32[3]{0:T(128)S(1)} collective-permute-done((f32[3]{0:T(128)S(1)}, f32[3]{0:T(128)S(1)}, u32[]{:S(2)}, u32[]{:S(2)}) %collective-permute-start.15) | collective-permute-done | bytes 44 | tf_op jit(solution)/shard_map/ppermute | solution.py:53
  172.5 4.9 %collective-permute-done.16 = f32[8,4,256]{2,1,0:T(4,128)S(1)} collective-permute-done((f32[8,4,256]{2,1,0:T(4,128)S(1)}, f32[8,4,256]{2,1,0:T(4,128)S(1)}, u32[]{:S(2)}, u32[]{:S(2)}) %collective-permute-start.16) | collective-permute-done | bytes 32800 | tf_op jit(solution)/shard_map/ppermute | solution.py:14
  184.0 10.8 %all_to_all.32 = f32[4,128,128]{2,1,0:T(8,128)} all-to-all(f32[4,128,128]{2,1,0:T(8,128)} %bitcast.132), channel_id=1, replica_groups=mesh['mem'=4,'col'=64] {'mem'}, dimensions={0} | all-to-all | bytes 524288 | tf_op jit(solution)/shard_map/all_to_all | solution.py:63
  197.2 9.1 %all_to_all.33 = f32[4,128,128]{2,1,0:T(8,128)S(1)} all-to-all(f32[4,128,128]{2,1,0:T(8,128)S(1)} %broadcast_in_dim.16), channel_id=1, replica_groups=mesh['mem'=4,'col'=64] {'mem'}, dimensions={0} | all-to-all | bytes 524288 | tf_op jit(solution)/shard_map/all_to_all | solution.py:65
  209.4 4.3 %scatter_custom_fusion.5 = f32[1024,128]{1,0:T(8,128)} fusion(s32[512]{0:T(512)} %bitcast.155, f32[512,128]{1,0:T(8,128)} %fusion.283, f32[]{:T(128)} %constant.77.clone.1), kind=kCustom, calls=%fused_computation.38 | custom fusion | flops 65536 | bytes 524800 | tf_op jit(solution)/shard_map/scatter-add | solution.py:121
  244.8 6.1 %collective-permute-done.23 = f32[]{:T(128)} collective-permute-done((f32[]{:T(128)}, f32[]{:T(128)}, u32[]{:S(2)}, u32[]{:S(2)}) %collective-permute-start.23) | collective-permute-done | bytes 36 | tf_op jit(solution)/shard_map/ppermute | solution.py:53
  257.3 3.7 %collective-permute-done.25 = f32[]{:T(128)} collective-permute-done((f32[]{:T(128)}, f32[]{:T(128)}, u32[]{:S(2)}, u32[]{:S(2)}) %collective-permute-start.25) | collective-permute-done | bytes 36 | tf_op jit(solution)/shard_map/ppermute | solution.py:53
  272.8 3.5 %all-to-all-start.5 = ((f32[4,4,64,128]{3,2,1,0:T(8,128)}), f32[4,4,64,128]{3,2,1,0:T(8,128)S(1)}, u32[]{:S(2)}, u32[]{:S(2)}) async-start(f32[4,4,64,128]{3,2,1,0:T(8,128)} %bitcast.104), calls=%async_computation.5 | async-start | bytes 1048576 | tf_op jit(solution)/shard_map/all_to_all | solution.py:186
  277.6 6.7 %all-to-all-done.5 = f32[4,4,64,128]{3,2,1,0:T(8,128)S(1)} async-done(((f32[4,4,64,128]{3,2,1,0:T(8,128)}), f32[4,4,64,128]{3,2,1,0:T(8,128)S(1)}, u32[]{:S(2)}, u32[]{:S(2)}) %all-to-all-start.5) | async-done | bytes 524320 | tf_op jit(solution)/shard_map/all_to_all | solution.py:186
  (187 shorter events, 124.0 us)
Async XLA Ops:
  15.0 28.8 %all-to-all-start = ((f32[64,9,128]{2,1,0:T(8,128)}), f32[64,9,128]{2,1,0:T(8,128)S(1)}, u32[]{:S(2)}, u32[]{:S(2)}) async-start(f32[64,9,128]{2,1,0:T(8,128)} %pad_maximum_fusion), calls=%async_computation | async-start | bytes 1048576 | tf_op jit(solution)/shard_map/all_to_all | solution.py:112
  27.1 12.6 %collective-permute-start.2 = (f32[4,256]{1,0:T(4,128)S(1)}, f32[4,256]{1,0:T(4,128)S(1)}, u32[]{:S(2)}, u32[]{:S(2)}) collective-permute-start(f32[4,256]{1,0:T(4,128)S(1)} %copy-done.15), channel_id=1, source_target_pairs={{0,1},{1,2},{2,3},{3,4},{4,5},{5,6},{6,7},{7,8},{8,9},{9,10},{10,1... | collective-permute-start | bytes 12296 | tf_op jit(solution)/shard_map/ppermute | solution.py:14
  29.2 10.5 %collective-permute-start.3 = (f32[4,256]{1,0:T(4,128)S(1)}, f32[4,256]{1,0:T(4,128)S(1)}, u32[]{:S(2)}, u32[]{:S(2)}) collective-permute-start(f32[4,256]{1,0:T(4,128)S(1)} %copy-done.15), channel_id=1, source_target_pairs={{1,0},{2,1},{3,2},{4,3},{5,4},{6,5},{7,6},{8,7},{9,8},{10,9},{11,1... | collective-permute-start | bytes 12296 | tf_op jit(solution)/shard_map/ppermute | solution.py:15
  50.0 6.3 %collective-permute-start.1 = (f32[8,4,256]{2,1,0:T(4,128)S(1)}, f32[8,4,256]{2,1,0:T(4,128)S(1)}, u32[]{:S(2)}, u32[]{:S(2)}) collective-permute-start(f32[8,4,256]{2,1,0:T(4,128)S(1)} %bitcast.143), channel_id=1, source_target_pairs={{1,0},{2,1},{3,2},{4,3},{5,4},{6,5},{7,6},{8,7},{9,8},{10,9},{11,1... | collective-permute-start | bytes 98312 | tf_op jit(solution)/shard_map/ppermute | solution.py:15
  51.9 7.3 %collective-permute-start = (f32[8,4,256]{2,1,0:T(4,128)S(1)}, f32[8,4,256]{2,1,0:T(4,128)S(1)}, u32[]{:S(2)}, u32[]{:S(2)}) collective-permute-start(f32[8,4,256]{2,1,0:T(4,128)S(1)} %bitcast.144), channel_id=1, source_target_pairs={{0,1},{1,2},{2,3},{3,4},{4,5},{5,6},{6,7},{7,8},{8,9},{9,10},{10,1... | collective-permute-start | bytes 98312 | tf_op jit(solution)/shard_map/ppermute | solution.py:14
  59.9 5.2 %collective-permute-start.5 = (f32[8,4,256]{2,1,0:T(4,128)S(1)}, f32[8,4,256]{2,1,0:T(4,128)S(1)}, u32[]{:S(2)}, u32[]{:S(2)}) collective-permute-start(f32[8,4,256]{2,1,0:T(4,128)S(1)} %fusion.255), channel_id=1, source_target_pairs={{1,0},{2,1},{3,2},{4,3},{5,4},{6,5},{7,6},{8,7},{9,8},{10,9},{11,1... | collective-permute-start | bytes 98312 | tf_op jit(solution)/shard_map/ppermute | solution.py:15
  62.1 7.3 %collective-permute-start.4 = (f32[8,4,256]{2,1,0:T(4,128)S(1)}, f32[8,4,256]{2,1,0:T(4,128)S(1)}, u32[]{:S(2)}, u32[]{:S(2)}) collective-permute-start(f32[8,4,256]{2,1,0:T(4,128)S(1)} %fusion.255), channel_id=1, source_target_pairs={{0,1},{1,2},{2,3},{3,4},{4,5},{5,6},{6,7},{7,8},{8,9},{9,10},{10,1... | collective-permute-start | bytes 98312 | tf_op jit(solution)/shard_map/ppermute | solution.py:14
  103.2 5.4 %collective-permute-start.7 = (f32[8,4,256]{2,1,0:T(4,128)}, f32[8,4,256]{2,1,0:T(4,128)S(1)}, u32[]{:S(2)}, u32[]{:S(2)}) collective-permute-start(f32[8,4,256]{2,1,0:T(4,128)} %bitcast.30), channel_id=1, source_target_pairs={{1,0},{2,1},{3,2},{4,3},{5,4},{6,5},{7,6},{8,7},{9,8},{10,9},{11,1... | collective-permute-start | bytes 98312 | tf_op jit(solution)/shard_map/ppermute | solution.py:15
  105.3 7.6 %collective-permute-start.6 = (f32[8,4,256]{2,1,0:T(4,128)}, f32[8,4,256]{2,1,0:T(4,128)S(1)}, u32[]{:S(2)}, u32[]{:S(2)}) collective-permute-start(f32[8,4,256]{2,1,0:T(4,128)} %bitcast.30), channel_id=1, source_target_pairs={{0,1},{1,2},{2,3},{3,4},{4,5},{5,6},{6,7},{7,8},{8,9},{9,10},{10,1... | collective-permute-start | bytes 98312 | tf_op jit(solution)/shard_map/ppermute | solution.py:14
  123.8 4.5 %collective-permute-start.10 = (f32[3]{0:T(128)S(1)}, f32[3]{0:T(128)S(1)}, u32[]{:S(2)}, u32[]{:S(2)}) collective-permute-start(f32[3]{0:T(128)S(1)} %fusion.300), channel_id=1, source_target_pairs={{0,4},{1,5},{2,6},{3,7},{4,0},{5,1},{6,2},{7,3},{8,12},{9,13},{10,... | collective-permute-start | bytes 44 | tf_op jit(solution)/shard_map/ppermute | solution.py:53
  128.3 7.5 %collective-permute-start.11 = (f32[3]{0:T(128)S(1)}, f32[3]{0:T(128)S(1)}, u32[]{:S(2)}, u32[]{:S(2)}) collective-permute-start(f32[3]{0:T(128)S(1)} %add.484), channel_id=1, source_target_pairs={{0,8},{1,9},{2,10},{3,11},{4,12},{5,13},{6,14},{7,15},{8,0},{9,1},... | collective-permute-start | bytes 44 | tf_op jit(solution)/shard_map/ppermute | solution.py:53
  139.4 5.1 %collective-permute-start.13 = (f32[3]{0:T(128)S(1)}, f32[3]{0:T(128)S(1)}, u32[]{:S(2)}, u32[]{:S(2)}) collective-permute-start(f32[3]{0:T(128)S(1)} %add.486), channel_id=1, source_target_pairs={{0,32},{1,33},{2,34},{3,35},{4,36},{5,37},{6,38},{7,39},{8,40},{9,... | collective-permute-start | bytes 44 | tf_op jit(solution)/shard_map/ppermute | solution.py:53
  144.5 13.2 %collective-permute-start.14 = (f32[3]{0:T(128)S(1)}, f32[3]{0:T(128)S(1)}, u32[]{:S(2)}, u32[]{:S(2)}) collective-permute-start(f32[3]{0:T(128)S(1)} %add.487), channel_id=1, source_target_pairs={{0,64},{64,0},{128,192},{192,128},{1,65},{65,1},{129,193},{193,129... | collective-permute-start | bytes 44 | tf_op jit(solution)/shard_map/ppermute | solution.py:53
  157.7 5.1 %collective-permute-start.15 = (f32[3]{0:T(128)S(1)}, f32[3]{0:T(128)S(1)}, u32[]{:S(2)}, u32[]{:S(2)}) collective-permute-start(f32[3]{0:T(128)S(1)} %add.488), channel_id=1, source_target_pairs={{0,128},{64,192},{128,0},{192,64},{1,129},{65,193},{129,1},{193,65... | collective-permute-start | bytes 44 | tf_op jit(solution)/shard_map/ppermute | solution.py:53
  168.1 4.3 %collective-permute-start.17 = (f32[8,4,256]{2,1,0:T(4,128)S(1)}, f32[8,4,256]{2,1,0:T(4,128)S(1)}, u32[]{:S(2)}, u32[]{:S(2)}) collective-permute-start(f32[8,4,256]{2,1,0:T(4,128)S(1)} %bitcast.137), channel_id=1, source_target_pairs={{1,0},{2,1},{3,2},{4,3},{5,4},{6,5},{7,6},{8,7},{9,8},{10,9},{11,1... | collective-permute-start | bytes 98312 | tf_op jit(solution)/shard_map/ppermute | solution.py:15
  170.1 7.3 %collective-permute-start.16 = (f32[8,4,256]{2,1,0:T(4,128)S(1)}, f32[8,4,256]{2,1,0:T(4,128)S(1)}, u32[]{:S(2)}, u32[]{:S(2)}) collective-permute-start(f32[8,4,256]{2,1,0:T(4,128)S(1)} %bitcast.138), channel_id=1, source_target_pairs={{0,1},{1,2},{2,3},{3,4},{4,5},{5,6},{6,7},{7,8},{8,9},{9,10},{10,1... | collective-permute-start | bytes 98312 | tf_op jit(solution)/shard_map/ppermute | solution.py:14
  219.0 6.3 %collective-permute-start.19 = (f32[8,4,256]{2,1,0:T(4,128)}, f32[8,4,256]{2,1,0:T(4,128)S(1)}, u32[]{:S(2)}, u32[]{:S(2)}) collective-permute-start(f32[8,4,256]{2,1,0:T(4,128)} %bitcast.146), channel_id=1, source_target_pairs={{1,0},{2,1},{3,2},{4,3},{5,4},{6,5},{7,6},{8,7},{9,8},{10,9},{11,1... | collective-permute-start | bytes 98312 | tf_op jit(solution)/shard_map/ppermute | solution.py:15
  221.0 7.6 %collective-permute-start.18 = (f32[8,4,256]{2,1,0:T(4,128)}, f32[8,4,256]{2,1,0:T(4,128)S(1)}, u32[]{:S(2)}, u32[]{:S(2)}) collective-permute-start(f32[8,4,256]{2,1,0:T(4,128)} %bitcast.147), channel_id=1, source_target_pairs={{0,1},{1,2},{2,3},{3,4},{4,5},{5,6},{6,7},{7,8},{8,9},{9,10},{10,1... | collective-permute-start | bytes 98312 | tf_op jit(solution)/shard_map/ppermute | solution.py:14
  233.9 3.6 %collective-permute-start.21 = (f32[]{:T(128)}, f32[]{:T(128)}, u32[]{:S(2)}, u32[]{:S(2)}) collective-permute-start(f32[]{:T(128)} %add.529), channel_id=1, source_target_pairs={{0,2},{1,3},{2,0},{3,1},{4,6},{5,7},{6,4},{7,5},{8,10},{9,11},{10,... | collective-permute-start | bytes 20 | tf_op jit(solution)/shard_map/ppermute | solution.py:53
  238.2 4.5 %collective-permute-start.22 = (f32[]{:T(128)}, f32[]{:T(128)}, u32[]{:S(2)}, u32[]{:S(2)}) collective-permute-start(f32[]{:T(128)} %add.530), channel_id=1, source_target_pairs={{0,4},{1,5},{2,6},{3,7},{4,0},{5,1},{6,2},{7,3},{8,12},{9,13},{10,... | collective-permute-start | bytes 20 | tf_op jit(solution)/shard_map/ppermute | solution.py:53
  243.4 7.5 %collective-permute-start.23 = (f32[]{:T(128)}, f32[]{:T(128)}, u32[]{:S(2)}, u32[]{:S(2)}) collective-permute-start(f32[]{:T(128)} %add.531), channel_id=1, source_target_pairs={{0,8},{1,9},{2,10},{3,11},{4,12},{5,13},{6,14},{7,15},{8,0},{9,1},... | collective-permute-start | bytes 20 | tf_op jit(solution)/shard_map/ppermute | solution.py:53
  255.9 5.1 %collective-permute-start.25 = (f32[]{:T(128)}, f32[]{:T(128)}, u32[]{:S(2)}, u32[]{:S(2)}) collective-permute-start(f32[]{:T(128)} %add.533), channel_id=1, source_target_pairs={{0,32},{1,33},{2,34},{3,35},{4,36},{5,37},{6,38},{7,39},{8,40},{9,... | collective-permute-start | bytes 20 | tf_op jit(solution)/shard_map/ppermute | solution.py:53
  266.0 5.1 %collective-permute-start.27 = (f32[]{:T(128)}, f32[]{:T(128)}, u32[]{:S(2)}, u32[]{:S(2)}) collective-permute-start(f32[]{:T(128)} %add.535), channel_id=1, source_target_pairs={{0,128},{64,192},{128,0},{192,64},{1,129},{65,193},{129,1},{193,65... | collective-permute-start | bytes 20 | tf_op jit(solution)/shard_map/ppermute | solution.py:53
  272.8 11.5 %all-to-all-start.5 = ((f32[4,4,64,128]{3,2,1,0:T(8,128)}), f32[4,4,64,128]{3,2,1,0:T(8,128)S(1)}, u32[]{:S(2)}, u32[]{:S(2)}) async-start(f32[4,4,64,128]{3,2,1,0:T(8,128)} %bitcast.104), calls=%async_computation.5 | async-start | bytes 1048576 | tf_op jit(solution)/shard_map/all_to_all | solution.py:186
  (22 other events, 346.3 us)

commit v2 on v1

v2 whole, which is shorter than its diff:
```python
import jax
import jax.numpy as jnp
from jax import lax
from jax.sharding import PartitionSpec as P

NSWEEP = 4
ITERS = 2


def neighbours(block, axis, dim, reach):
    count = lax.axis_size(axis)
    below, above = [], []
    for shift in range(1, reach + 1):
        forward = [(i, i + shift) for i in range(count - shift)]
        backward = [(target, source) for source, target in forward]
        below.insert(0, lax.ppermute(block, axis, forward))
        above.append(lax.ppermute(block, axis, backward))
    return jnp.concatenate(below + [block] + above, axis=dim)


def face_coefficients(length_scale, reach):
    rimmed = neighbours(length_scale, "col", 0, reach)
    padded = jnp.pad(rimmed, ((1, 1), (1, 1)))
    centre = padded[1:-1, 1:-1]
    return (
        jnp.sqrt(centre * padded[:-2, 1:-1]),
        jnp.sqrt(centre * padded[2:, 1:-1]),
        jnp.sqrt(centre * padded[1:-1, :-2]),
        jnp.sqrt(centre * padded[1:-1, 2:]),
    )


def sweep_steps(values, coeffs, count):
    face_up, face_down, face_left, face_right = coeffs
    for sweep_step in range(count):
        padded = jnp.pad(values, ((0, 0), (1, 1), (1, 1)))
        centre = values
        values = (
            centre
            + face_up * (padded[:, :-2, 1:-1] - centre)
            + face_down * (padded[:, 2:, 1:-1] - centre)
            + face_left * (padded[:, 1:-1, :-2] - centre)
            + face_right * (padded[:, 1:-1, 2:] - centre)
        )
    return values


def sweeps(values, coeffs):
    rows = values.shape[1]
    done = sweep_steps(neighbours(values, "col", 1, 1), coeffs, NSWEEP)
    return done[:, rows : 2 * rows]


def global_sum(values):
    axes = ("mem", "col")
    count = lax.axis_size(axes)
    spread = jnp.broadcast_to(values[None], (count,) + values.shape)
    return jnp.sum(lax.all_to_all(spread, axes, 0, 0, tiled=True), axis=0)


def mem_sum(values):
    parts = lax.axis_size("mem")
    spread = jnp.broadcast_to(values[None], (parts,) + values.shape)
    return jnp.sum(lax.all_to_all(spread, "mem", 0, 0, tiled=True), axis=0)


def local_inner(first, second):
    return jnp.sum(first[0] * second[0]) + jnp.sum(first[1] * second[1])


def shards(
    perturbations,
    static_root,
    obs_jacobian,
    innovations,
    obs_weights,
    length_scale,
    obs_owner,
    obs_cell,
    obs_count,
):
    members, rows_here, columns, features = perturbations.shape
    parts = lax.axis_size("mem")
    quarter = columns // parts
    offset = lax.axis_index("mem") * quarter
    blocks = lax.axis_size("col")
    obs_dev, channels = innovations.shape
    capacity = max(2, 2 * obs_dev // blocks)
    total_slots = blocks * capacity
    coeffs_wide = face_coefficients(length_scale, 2)
    coeffs = tuple(face[rows_here : 4 * rows_here] for face in coeffs_wide)
    is_live = jnp.arange(obs_dev, dtype=jnp.int32) < obs_count[0]
    owner_ids = obs_owner[:, 0]
    onehot = (
        (owner_ids[:, None] == jnp.arange(blocks, dtype=jnp.int32)[None, :]) & is_live[:, None]
    ).astype(jnp.int32)
    slot_rank = jnp.sum((jnp.cumsum(onehot, axis=0) - onehot) * onehot, axis=1)
    slot_ids = jnp.where(is_live, owner_ids * capacity + slot_rank, total_slots)
    source = (
        jnp.full((total_slots,), obs_dev, jnp.int32)
        .at[slot_ids]
        .set(jnp.arange(obs_dev, dtype=jnp.int32), mode="drop")
    )
    filled = source < obs_dev
    source = jnp.minimum(source, obs_dev - 1)
    send_values = jnp.where(filled[:, None], innovations[source], 0.0)
    send_cells = jnp.where(filled, obs_cell[source], 0).astype(jnp.float32)
    send_marks = filled.astype(jnp.float32)
    side = jnp.zeros((blocks, 1, channels), jnp.float32)
    side = side.at[:, 0, :capacity].set(send_cells.reshape(blocks, capacity))
    side = side.at[:, 0, capacity : 2 * capacity].set(send_marks.reshape(blocks, capacity))
    packed = jnp.concatenate([send_values.reshape(blocks, capacity, channels), side], axis=1)
    got = lax.all_to_all(packed, "col", split_axis=0, concat_axis=0, tiled=True)
    got_values = got[:, :capacity, :].reshape(total_slots, channels)
    got_cells = got[:, capacity, :capacity].reshape(total_slots).astype(jnp.int32)
    got_marks = got[:, capacity, capacity : 2 * capacity].reshape(total_slots)
    obs_index = got_cells
    obs_gain = got_marks[:, None] * obs_weights[None, :]

    def spread_back(weighted):
        back = jnp.dot(weighted, obs_jacobian.T, precision=lax.Precision.HIGHEST)
        grid = jnp.zeros((rows_here * columns, features), jnp.float32).at[obs_index].add(back)
        return grid.reshape(rows_here, columns, features)

    def adjoint_parts(gradient):
        own_gradient = lax.dynamic_slice_in_dim(gradient, offset, quarter, 1)
        rounded = gradient.astype(jnp.bfloat16)
        static = jnp.dot(
            own_gradient.reshape(rows_here * quarter, features),
            static_root.T,
            precision=lax.Precision.HIGHEST,
        ).reshape(rows_here, quarter, features)
        projected = jnp.einsum(
            "kyxf,yxf->kyx", perturbations, rounded, preferred_element_type=jnp.float32
        )
        return static, projected

    def forward_partial(static_part, smoothed_field):
        smoothed = smoothed_field.astype(jnp.bfloat16)
        partial_sum = jnp.einsum(
            "kyxf,kyx->yxf", perturbations, smoothed, preferred_element_type=jnp.float32
        )
        forward_static = jnp.dot(
            static_part.reshape(rows_here * quarter, features),
            static_root,
            precision=lax.Precision.HIGHEST,
        ).reshape(rows_here, quarter, features)
        own_slice = lax.dynamic_slice_in_dim(partial_sum, offset, quarter, 1) + forward_static
        return lax.dynamic_update_slice_in_dim(partial_sum, own_slice, offset, 1)

    def observed_gradient(partial_sum):
        gathered = mem_sum(partial_sum.reshape(rows_here * columns, features)[obs_index])
        model_obs = jnp.dot(gathered, obs_jacobian, precision=lax.Precision.HIGHEST)
        return spread_back(obs_gain * model_obs)

    right_static, right_projected = adjoint_parts(spread_back(obs_gain * got_values))
    wide = sweep_steps(neighbours(right_projected, "col", 1, 2), coeffs_wide, NSWEEP)
    right_ensemble = wide[:, 2 * rows_here : 3 * rows_here]
    wide = sweep_steps(wide, coeffs_wide, NSWEEP)
    smoothed_right = wide[:, 2 * rows_here : 3 * rows_here]
    direction = (right_static, right_ensemble)

    partial0 = forward_partial(right_static, smoothed_right)
    adj_static, adj_projected = adjoint_parts(observed_gradient(partial0))
    image = (right_static + adj_static, right_ensemble + sweeps(adj_projected, coeffs))
    sums = global_sum(
        jnp.stack(
            [
                local_inner(direction, direction),
                local_inner(direction, image),
                local_inner(image, image),
            ]
        )
    )
    smoothed_image = sweeps(image[1], coeffs)
    norm_now, curve, image_norm = sums[0], sums[1], sums[2]
    step0 = norm_now / curve
    state = (step0 * direction[0], step0 * direction[1])
    residual = (direction[0] - step0 * image[0], direction[1] - step0 * image[1])
    norm_next = norm_now - 2.0 * step0 * curve + step0 * step0 * image_norm
    ratio = norm_next / norm_now
    direction = (residual[0] + ratio * direction[0], residual[1] + ratio * direction[1])
    smoothed_direction = (smoothed_right - step0 * smoothed_image) + ratio * smoothed_right
    norm_now = norm_next

    partial1 = forward_partial(direction[0], smoothed_direction)
    adj_static, adj_projected = adjoint_parts(observed_gradient(partial1))
    curve = (
        jnp.sum(direction[0] * (direction[0] + adj_static))
        + jnp.sum(direction[1] * direction[1])
        + jnp.sum(smoothed_direction * adj_projected)
    )
    step1 = norm_now / global_sum(curve)
    state = (state[0] + step1 * direction[0], state[1] + step1 * direction[1])

    total = step0 * partial0 + step1 * partial1
    pieces = jnp.moveaxis(total.reshape(rows_here, parts, quarter, features), 1, 0)
    increment = jnp.sum(lax.all_to_all(pieces, "mem", 0, 0, tiled=True), axis=0)
    return (increment, state[0], state[1])


def solution(mesh):
    placed = (
        P("mem", "col", None, None),
        P(),
        P(),
        P("col", None),
        P(),
        P("col", None),
        P("col", None),
        P("col"),
        P("col"),
    )
    return jax.shard_map(
        shards,
        mesh=mesh,
        in_specs=placed,
        out_specs=(P("col", "mem", None), P("col", "mem", None), P("mem", "col", None)),
        check_vma=False,
    )
```

time: 290 us -> 237 us (0.82)
  the two profiles are of different devices: /device:TPU:24 before, /device:TPU:1 now
where the time goes in v2:
time: 237 us; the launch traced here: 236 us
  starting transfers between devices  68.1 us (29%)
  waiting for transfers between devices  50.2 us (21%)
  other arithmetic  40.7 us (17%)
  local copies, waits for them, and re-layouts  23.9 us (10%)
  blocking collectives  20.5 us (9%)
  matrix products  20 us (8%)
  between operations  12.6 us (5%)
    all_to_all x2, waiting for transfers between devices, mem_sum(): return jnp.sum(lax.all_to_all(spread, 'mem', 0, 0, tiled=True), axis=0)  25.7 us
    ppermute x6, starting transfers between devices, neighbours(): below.insert(0, lax.ppermute(block, axis, forward))  21.3 us
    all_to_all x1, blocking collectives, global_sum(): return jnp.sum(lax.all_to_all(spread, axes, 0, 0, tiled=True), axis=0)  20.5 us
    all_to_all x1, starting transfers between devices, shards(): got = lax.all_to_all(packed, 'col', split_axis=0, concat_axis=0, tiled=True)  13.1 us
    scatter-add x3, other arithmetic, spread_back(): jnp.zeros((rows_here * columns, features), jnp.float32).at[obs_index]  11.4 us
    all_to_all x1, starting transfers between devices, global_sum(): return jnp.sum(lax.all_to_all(spread, axes, 0, 0, tiled=True), axis=0)  10.9 us
    ppermute x6, starting transfers between devices, neighbours(): above.append(lax.ppermute(block, axis, backward))  10.7 us
    all_to_all x2, starting transfers between devices, mem_sum(): return jnp.sum(lax.all_to_all(spread, 'mem', 0, 0, tiled=True), axis=0)  8.6 us
  transfers between devices with their start and end apart: 17, of which 8 were waited for; matrix products, arithmetic and copies ran while one was open for 5% of the time, Pallas kernels for 0%

profile of v2, /device:TPU:1, one launch (start us, length us, event | category | flops | bytes accessed | tf_op | source)
XLA Modules:
  0.0 236.0 jit_solution(3652509740393027814)
XLA Ops:
  6.1 3.6 %gather_fusion.1 = s32[512]{0:T(512)S(1)} fusion(s32[256]{0:T(256)} %param.20, s32[1024]{0:T(1024)S(1)} %pad_clamp_fusion.1), kind=kCustom, calls=%fused_computation.1 | custom fusion | bytes 6144 | tf_op jit(solution)/shard_map/gather | solution.py:107
  15.7 13.1 %all-to-all-start = ((f32[64,9,128]{2,1,0:T(8,128)}), f32[64,9,128]{2,1,0:T(8,128)S(1)}, u32[]{:S(2)}, u32[]{:S(2)}) async-start(f32[64,9,128]{2,1,0:T(8,128)} %pad_maximum_fusion), calls=%async_computation | async-start | bytes 1048576 | tf_op jit(solution)/shard_map/all_to_all | solution.py:113
  28.9 3.3 %collective-permute-start.4 = (f32[4,256]{1,0:T(4,128)S(1)}, f32[4,256]{1,0:T(4,128)S(1)}, u32[]{:S(2)}, u32[]{:S(2)}) collective-permute-start(f32[4,256]{1,0:T(4,128)S(1)} %copy-done.31), channel_id=1, source_target_pairs={{0,2},{1,3},{2,4},{3,5},{4,6},{5,7},{6,8},{7,9},{8,10},{9,11},{10,... | collective-permute-start | bytes 12296 | tf_op jit(solution)/shard_map/ppermute | solution.py:16
  32.1 3.7 %collective-permute-start.5 = (f32[4,256]{1,0:T(4,128)S(1)}, f32[4,256]{1,0:T(4,128)S(1)}, u32[]{:S(2)}, u32[]{:S(2)}) collective-permute-start(f32[4,256]{1,0:T(4,128)S(1)} %copy-done.31), channel_id=1, source_target_pairs={{0,1},{1,2},{2,3},{3,4},{4,5},{5,6},{6,7},{7,8},{8,9},{9,10},{10,1... | collective-permute-start | bytes 12296 | tf_op jit(solution)/shard_map/ppermute | solution.py:16
  39.0 3.6 %collective-permute-done.6 = f32[4,256]{1,0:T(4,128)S(1)} collective-permute-done((f32[4,256]{1,0:T(4,128)S(1)}, f32[4,256]{1,0:T(4,128)S(1)}, u32[]{:S(2)}, u32[]{:S(2)}) %collective-permute-start.6) | collective-permute-done | bytes 4128 | tf_op jit(solution)/shard_map/ppermute | solution.py:17
  42.9 3.6 %all-to-all-done = f32[64,9,128]{2,1,0:T(8,128)S(1)} async-done(((f32[64,9,128]{2,1,0:T(8,128)}), f32[64,9,128]{2,1,0:T(8,128)S(1)}, u32[]{:S(2)}, u32[]{:S(2)}) %all-to-all-start) | async-done | bytes 294944 | tf_op jit(solution)/shard_map/all_to_all | solution.py:113
  47.4 3.3 %scatter_custom_fusion.1 = f32[1024,128]{1,0:T(8,128)S(1)} fusion(s32[512]{0:T(512)S(1)} %bitcast.130, f32[512,128]{1,0:T(8,128)S(1)} %fusion.16, f32[]{:T(128)} %constant.76.clone.1), kind=kCustom, calls=%fused_computation.75 | custom fusion | flops 65536 | bytes 524292 | tf_op jit(solution)/shard_map/scatter-add | solution.py:122
  54.2 4.4 %collective-permute-start.1 = (f32[8,4,256]{2,1,0:T(4,128)S(1)}, f32[8,4,256]{2,1,0:T(4,128)S(1)}, u32[]{:S(2)}, u32[]{:S(2)}) collective-permute-start(f32[8,4,256]{2,1,0:T(4,128)S(1)} %bitcast.124), channel_id=1, source_target_pairs={{0,1},{1,2},{2,3},{3,4},{4,5},{5,6},{6,7},{7,8},{8,9},{9,10},{10,1... | collective-permute-start | bytes 98312 | tf_op jit(solution)/shard_map/ppermute | solution.py:16
  72.8 4.4 %all-to-all-start.1 = ((f32[4,512,128]{2,1,0:T(8,128)}), f32[4,512,128]{2,1,0:T(8,128)}, u32[]{:S(2)}, u32[]{:S(2)}) async-start(f32[4,512,128]{2,1,0:T(8,128)} %broadcast_in_dim.35), calls=%async_computation.1 | async-start | bytes 2097152 | tf_op jit(solution)/shard_map/all_to_all | solution.py:64
  79.0 12.8 %all-to-all-done.1 = f32[4,512,128]{2,1,0:T(8,128)} async-done(((f32[4,512,128]{2,1,0:T(8,128)}), f32[4,512,128]{2,1,0:T(8,128)}, u32[]{:S(2)}, u32[]{:S(2)}) %all-to-all-start.1) | async-done | bytes 1048608 | tf_op jit(solution)/shard_map/all_to_all | solution.py:64
  94.6 3.7 %scatter_custom_fusion.2 = f32[1024,128]{1,0:T(8,128)S(1)} fusion(s32[512]{0:T(512)} %bitcast.132, f32[512,128]{1,0:T(8,128)} %fusion.240, f32[]{:T(128)} %constant.76.clone.1), kind=kCustom, calls=%fused_computation.73 | custom fusion | flops 65536 | bytes 524800 | tf_op jit(solution)/shard_map/scatter-add | solution.py:122
  102.5 4.8 %collective-permute-start.8 = (f32[8,4,256]{2,1,0:T(4,128)}, f32[8,4,256]{2,1,0:T(4,128)S(1)}, u32[]{:S(2)}, u32[]{:S(2)}) collective-permute-start(f32[8,4,256]{2,1,0:T(4,128)} %bitcast.28), channel_id=1, source_target_pairs={{0,1},{1,2},{2,3},{3,4},{4,5},{5,6},{6,7},{7,8},{8,9},{9,10},{10,1... | collective-permute-start | bytes 98312 | tf_op jit(solution)/shard_map/ppermute | solution.py:16
  110.2 2.5 %collective-permute-done.9 = f32[8,4,256]{2,1,0:T(4,128)S(1)} collective-permute-done((f32[8,4,256]{2,1,0:T(4,128)}, f32[8,4,256]{2,1,0:T(4,128)S(1)}, u32[]{:S(2)}, u32[]{:S(2)}) %collective-permute-start.9) | collective-permute-done | bytes 32800 | tf_op jit(solution)/shard_map/ppermute | solution.py:17
  122.5 10.9 %all-to-all-start.2 = ((f32[256,1,3]{2,1,0:T(1,128)}), f32[256,1,3]{2,1,0:T(1,128)S(1)}, u32[]{:S(2)}, u32[]{:S(2)}) async-start(f32[256,1,3]{2,1,0:T(1,128)} %broadcast_in_dim.36), calls=%async_computation.2 | async-start | bytes 262144 | tf_op jit(solution)/shard_map/all_to_all | solution.py:58
  133.4 3.7 %collective-permute-start.10 = (f32[8,4,256]{2,1,0:T(4,128)S(1)}, f32[8,4,256]{2,1,0:T(4,128)S(1)}, u32[]{:S(2)}, u32[]{:S(2)}) collective-permute-start(f32[8,4,256]{2,1,0:T(4,128)S(1)} %get-tuple-element.34), channel_id=1, source_target_pairs={{0,1},{1,2},{2,3},{3,4},{4,5},{5,6},{6,7},{7,8},{8,9},{9,10},{10,1... | collective-permute-start | bytes 98312 | tf_op jit(solution)/shard_map/ppermute | solution.py:16
  139.2 7.0 %all-to-all-done.2 = f32[256,1,3]{2,1,0:T(1,128)S(1)} async-done(((f32[256,1,3]{2,1,0:T(1,128)}), f32[256,1,3]{2,1,0:T(1,128)S(1)}, u32[]{:S(2)}, u32[]{:S(2)}) %all-to-all-start.2) | async-done | bytes 3104 | tf_op jit(solution)/shard_map/all_to_all | solution.py:58
  155.7 2.7 %fusion.4 = f32[4,256,1,128]{3,2,1,0:T(1,128)S(1)} fusion(bf16[8,4,256,1]{0,3,2,1:T(2,128)(2,1)} %copy.40, bf16[8,4,256,128]{3,2,1,0:T(8,128)(2,1)S(1)} %copy-done), kind=kOutput, calls=%fused_computation.17 | convolution fusion | flops 2097152 | bytes 2637824 | tf_op jit(solution)/shard_map/kyxf,kyx->yxf/dot_general | solution.py:140
  162.5 4.2 %all-to-all-start.3 = ((f32[4,512,128]{2,1,0:T(8,128)}), f32[4,512,128]{2,1,0:T(8,128)}, u32[]{:S(2)}, u32[]{:S(2)}) async-start(f32[4,512,128]{2,1,0:T(8,128)} %broadcast_in_dim.37), calls=%async_computation.3 | async-start | bytes 2097152 | tf_op jit(solution)/shard_map/all_to_all | solution.py:64
  168.2 12.9 %all-to-all-done.3 = f32[4,512,128]{2,1,0:T(8,128)} async-done(((f32[4,512,128]{2,1,0:T(8,128)}), f32[4,512,128]{2,1,0:T(8,128)}, u32[]{:S(2)}, u32[]{:S(2)}) %all-to-all-start.3) | async-done | bytes 1048608 | tf_op jit(solution)/shard_map/all_to_all | solution.py:64
  185.5 4.4 %scatter_custom_fusion.3 = f32[1024,128]{1,0:T(8,128)} fusion(s32[512]{0:T(512)} %bitcast.133, f32[512,128]{1,0:T(8,128)} %fusion.241, f32[]{:T(128)} %constant.76.clone.1), kind=kCustom, calls=%fused_computation.71 | custom fusion | flops 65536 | bytes 524800 | tf_op jit(solution)/shard_map/scatter-add | solution.py:122
  191.0 2.4 %fusion.2 = f32[4,256,1,8]{3,2,1,0:T(1,128)} fusion(bf16[8,4,256,128]{3,2,1,0:T(8,128)(2,1)S(1)} %copy-done, bf16[4,256,128,1]{2,1,0,3:T(8,128)(2,1)S(1)} %convert_bitcast_fusion), kind=kOutput, calls=%fused_computation.15 | convolution fusion | flops 2097152 | bytes 2392064 | tf_op jit(solution)/shard_map/kyxf,yxf->kyx/dot_general | solution.py:133
  199.0 20.5 %all_to_all.32 = f32[256,1,1]{2,1,0:T(1,128)} all-to-all(f32[256,1,1]{2,1,0:T(1,128)S(1)} %broadcast_in_dim.38), channel_id=1, replica_groups=mesh['mem'=4,'col'=64] {'mem','col'}, dimensions={0} | all-to-all | bytes 2048 | tf_op jit(solution)/shard_map/all_to_all | solution.py:58
  222.9 3.5 %all-to-all-start.5 = ((f32[4,4,64,128]{3,2,1,0:T(8,128)}), f32[4,4,64,128]{3,2,1,0:T(8,128)S(1)}, u32[]{:S(2)}, u32[]{:S(2)}) async-start(f32[4,4,64,128]{3,2,1,0:T(8,128)} %bitcast.104), calls=%async_computation.5 | async-start | bytes 1048576 | tf_op jit(solution)/shard_map/all_to_all | solution.py:198
  228.5 6.8 %all-to-all-done.5 = f32[4,4,64,128]{3,2,1,0:T(8,128)S(1)} async-done(((f32[4,4,64,128]{3,2,1,0:T(8,128)}), f32[4,4,64,128]{3,2,1,0:T(8,128)S(1)}, u32[]{:S(2)}, u32[]{:S(2)}) %all-to-all-start.5) | async-done | bytes 524320 | tf_op jit(solution)/shard_map/all_to_all | solution.py:198
  (190 shorter events, 77.8 us)
Async XLA Ops:
  0.6 50.1 %copy-start = (bf16[8,4,256,128]{3,2,1,0:T(8,128)(2,1)S(1)}, bf16[8,4,256,128]{3,2,1,0:T(8,128)(2,1)}, u32[]{:S(2)}) copy-start(bf16[8,4,256,128]{3,2,1,0:T(8,128)(2,1)} %param.13) | copy-start | bytes 6291460
  15.7 30.7 %all-to-all-start = ((f32[64,9,128]{2,1,0:T(8,128)}), f32[64,9,128]{2,1,0:T(8,128)S(1)}, u32[]{:S(2)}, u32[]{:S(2)}) async-start(f32[64,9,128]{2,1,0:T(8,128)} %pad_maximum_fusion), calls=%async_computation | async-start | bytes 1048576 | tf_op jit(solution)/shard_map/all_to_all | solution.py:113
  28.9 10.2 %collective-permute-start.4 = (f32[4,256]{1,0:T(4,128)S(1)}, f32[4,256]{1,0:T(4,128)S(1)}, u32[]{:S(2)}, u32[]{:S(2)}) collective-permute-start(f32[4,256]{1,0:T(4,128)S(1)} %copy-done.31), channel_id=1, source_target_pairs={{0,2},{1,3},{2,4},{3,5},{4,6},{5,7},{6,8},{7,9},{8,10},{9,11},{10,... | collective-permute-start | bytes 12296 | tf_op jit(solution)/shard_map/ppermute | solution.py:16
  32.1 6.9 %collective-permute-start.5 = (f32[4,256]{1,0:T(4,128)S(1)}, f32[4,256]{1,0:T(4,128)S(1)}, u32[]{:S(2)}, u32[]{:S(2)}) collective-permute-start(f32[4,256]{1,0:T(4,128)S(1)} %copy-done.31), channel_id=1, source_target_pairs={{0,1},{1,2},{2,3},{3,4},{4,5},{5,6},{6,7},{7,8},{8,9},{9,10},{10,1... | collective-permute-start | bytes 12296 | tf_op jit(solution)/shard_map/ppermute | solution.py:16
  35.8 6.8 %collective-permute-start.6 = (f32[4,256]{1,0:T(4,128)S(1)}, f32[4,256]{1,0:T(4,128)S(1)}, u32[]{:S(2)}, u32[]{:S(2)}) collective-permute-start(f32[4,256]{1,0:T(4,128)S(1)} %copy-done.31), channel_id=1, source_target_pairs={{1,0},{2,1},{3,2},{4,3},{5,4},{6,5},{7,6},{8,7},{9,8},{10,9},{11,1... | collective-permute-start | bytes 12296 | tf_op jit(solution)/shard_map/ppermute | solution.py:17
  37.7 4.9 %collective-permute-start.7 = (f32[4,256]{1,0:T(4,128)S(1)}, f32[4,256]{1,0:T(4,128)S(1)}, u32[]{:S(2)}, u32[]{:S(2)}) collective-permute-start(f32[4,256]{1,0:T(4,128)S(1)} %copy-done.31), channel_id=1, source_target_pairs={{2,0},{3,1},{4,2},{5,3},{6,4},{7,5},{8,6},{9,7},{10,8},{11,9},{12,... | collective-permute-start | bytes 12296 | tf_op jit(solution)/shard_map/ppermute | solution.py:17
  52.6 12.5 %collective-permute-start = (f32[8,4,256]{2,1,0:T(4,128)S(1)}, f32[8,4,256]{2,1,0:T(4,128)S(1)}, u32[]{:S(2)}, u32[]{:S(2)}) collective-permute-start(f32[8,4,256]{2,1,0:T(4,128)S(1)} %bitcast.123), channel_id=1, source_target_pairs={{0,2},{1,3},{2,4},{3,5},{4,6},{5,7},{6,8},{7,9},{8,10},{9,11},{10,... | collective-permute-start | bytes 98312 | tf_op jit(solution)/shard_map/ppermute | solution.py:16
  54.2 10.9 %collective-permute-start.1 = (f32[8,4,256]{2,1,0:T(4,128)S(1)}, f32[8,4,256]{2,1,0:T(4,128)S(1)}, u32[]{:S(2)}, u32[]{:S(2)}) collective-permute-start(f32[8,4,256]{2,1,0:T(4,128)S(1)} %bitcast.124), channel_id=1, source_target_pairs={{0,1},{1,2},{2,3},{3,4},{4,5},{5,6},{6,7},{7,8},{8,9},{9,10},{10,1... | collective-permute-start | bytes 98312 | tf_op jit(solution)/shard_map/ppermute | solution.py:16
  58.6 6.6 %collective-permute-start.2 = (f32[8,4,256]{2,1,0:T(4,128)S(1)}, f32[8,4,256]{2,1,0:T(4,128)S(1)}, u32[]{:S(2)}, u32[]{:S(2)}) collective-permute-start(f32[8,4,256]{2,1,0:T(4,128)S(1)} %bitcast.125), channel_id=1, source_target_pairs={{1,0},{2,1},{3,2},{4,3},{5,4},{6,5},{7,6},{8,7},{9,8},{10,9},{11,1... | collective-permute-start | bytes 98312 | tf_op jit(solution)/shard_map/ppermute | solution.py:17
  60.5 5.6 %collective-permute-start.3 = (f32[8,4,256]{2,1,0:T(4,128)S(1)}, f32[8,4,256]{2,1,0:T(4,128)S(1)}, u32[]{:S(2)}, u32[]{:S(2)}) collective-permute-start(f32[8,4,256]{2,1,0:T(4,128)S(1)} %bitcast.126), channel_id=1, source_target_pairs={{2,0},{3,1},{4,2},{5,3},{6,4},{7,5},{8,6},{9,7},{10,8},{11,9},{12,... | collective-permute-start | bytes 98312 | tf_op jit(solution)/shard_map/ppermute | solution.py:17
  72.8 19.0 %all-to-all-start.1 = ((f32[4,512,128]{2,1,0:T(8,128)}), f32[4,512,128]{2,1,0:T(8,128)}, u32[]{:S(2)}, u32[]{:S(2)}) async-start(f32[4,512,128]{2,1,0:T(8,128)} %broadcast_in_dim.35), calls=%async_computation.1 | async-start | bytes 2097152 | tf_op jit(solution)/shard_map/all_to_all | solution.py:64
  102.5 7.7 %collective-permute-start.8 = (f32[8,4,256]{2,1,0:T(4,128)}, f32[8,4,256]{2,1,0:T(4,128)S(1)}, u32[]{:S(2)}, u32[]{:S(2)}) collective-permute-start(f32[8,4,256]{2,1,0:T(4,128)} %bitcast.28), channel_id=1, source_target_pairs={{0,1},{1,2},{2,3},{3,4},{4,5},{5,6},{6,7},{7,8},{8,9},{9,10},{10,1... | collective-permute-start | bytes 98312 | tf_op jit(solution)/shard_map/ppermute | solution.py:16
  107.3 5.4 %collective-permute-start.9 = (f32[8,4,256]{2,1,0:T(4,128)}, f32[8,4,256]{2,1,0:T(4,128)S(1)}, u32[]{:S(2)}, u32[]{:S(2)}) collective-permute-start(f32[8,4,256]{2,1,0:T(4,128)} %bitcast.28), channel_id=1, source_target_pairs={{1,0},{2,1},{3,2},{4,3},{5,4},{6,5},{7,6},{8,7},{9,8},{10,9},{11,1... | collective-permute-start | bytes 98312 | tf_op jit(solution)/shard_map/ppermute | solution.py:17
  113.5 40.4 %copy-start.8 = (f32[8,4,256]{2,1,0:T(4,128)S(1)}, f32[8,4,256]{2,1,0:T(4,128)}, u32[]{:S(2)}) copy-start(f32[8,4,256]{2,1,0:T(4,128)} %get-tuple-element.36) | copy-start | bytes 98308
  113.5 40.4 %copy-start.12 = (f32[4,256]{1,0:T(4,128)S(1)}, f32[4,256]{1,0:T(4,128)}, u32[]{:S(2)}) copy-start(f32[4,256]{1,0:T(4,128)} %copy-done.10) | copy-start | bytes 12292
  113.5 40.4 %copy-start.15 = (f32[4,256]{1,0:T(4,128)S(1)}, f32[4,256]{1,0:T(4,128)}, u32[]{:S(2)}) copy-start(f32[4,256]{1,0:T(4,128)} %copy-done.13) | copy-start | bytes 12292
  113.5 40.4 %copy-start.18 = (f32[4,256]{1,0:T(4,128)S(1)}, f32[4,256]{1,0:T(4,128)}, u32[]{:S(2)}) copy-start(f32[4,256]{1,0:T(4,128)} %copy-done.16) | copy-start | bytes 12292
  113.5 40.4 %copy-start.21 = (f32[4,256]{1,0:T(4,128)S(1)}, f32[4,256]{1,0:T(4,128)}, u32[]{:S(2)}) copy-start(f32[4,256]{1,0:T(4,128)} %copy-done.19) | copy-start | bytes 12292
  118.0 36.7 %copy-start.5 = (f32[8,4,256]{2,1,0:T(4,128)}, f32[8,4,256]{2,1,0:T(4,128)S(1)}, u32[]{:S(2)}) copy-start(f32[8,4,256]{2,1,0:T(4,128)S(1)} %get-tuple-element.34) | copy-start | bytes 98308
  122.5 23.7 %all-to-all-start.2 = ((f32[256,1,3]{2,1,0:T(1,128)}), f32[256,1,3]{2,1,0:T(1,128)S(1)}, u32[]{:S(2)}, u32[]{:S(2)}) async-start(f32[256,1,3]{2,1,0:T(1,128)} %broadcast_in_dim.36), calls=%async_computation.2 | async-start | bytes 262144 | tf_op jit(solution)/shard_map/all_to_all | solution.py:58
  133.4 17.6 %collective-permute-start.10 = (f32[8,4,256]{2,1,0:T(4,128)S(1)}, f32[8,4,256]{2,1,0:T(4,128)S(1)}, u32[]{:S(2)}, u32[]{:S(2)}) collective-permute-start(f32[8,4,256]{2,1,0:T(4,128)S(1)} %get-tuple-element.34), channel_id=1, source_target_pairs={{0,1},{1,2},{2,3},{3,4},{4,5},{5,6},{6,7},{7,8},{8,9},{9,10},{10,1... | collective-permute-start | bytes 98312 | tf_op jit(solution)/shard_map/ppermute | solution.py:16
  137.1 13.9 %collective-permute-start.11 = (f32[8,4,256]{2,1,0:T(4,128)S(1)}, f32[8,4,256]{2,1,0:T(4,128)S(1)}, u32[]{:S(2)}, u32[]{:S(2)}) collective-permute-start(f32[8,4,256]{2,1,0:T(4,128)S(1)} %get-tuple-element.34), channel_id=1, source_target_pairs={{1,0},{2,1},{3,2},{4,3},{5,4},{6,5},{7,6},{8,7},{9,8},{10,9},{11,1... | collective-permute-start | bytes 98312 | tf_op jit(solution)/shard_map/ppermute | solution.py:17
  162.5 18.7 %all-to-all-start.3 = ((f32[4,512,128]{2,1,0:T(8,128)}), f32[4,512,128]{2,1,0:T(8,128)}, u32[]{:S(2)}, u32[]{:S(2)}) async-start(f32[4,512,128]{2,1,0:T(8,128)} %broadcast_in_dim.37), calls=%async_computation.3 | async-start | bytes 2097152 | tf_op jit(solution)/shard_map/all_to_all | solution.py:64
  222.9 12.4 %all-to-all-start.5 = ((f32[4,4,64,128]{3,2,1,0:T(8,128)}), f32[4,4,64,128]{3,2,1,0:T(8,128)S(1)}, u32[]{:S(2)}, u32[]{:S(2)}) async-start(f32[4,4,64,128]{3,2,1,0:T(8,128)} %bitcast.104), calls=%async_computation.5 | async-start | bytes 1048576 | tf_op jit(solution)/shard_map/all_to_all | solution.py:198
  (26 other events, 402.6 us)

commit v3 on v2

--- a/solution.py
+++ b/solution.py
@@ -56,12 +56,6 @@
     count = lax.axis_size(axes)
     spread = jnp.broadcast_to(values[None], (count,) + values.shape)
     return jnp.sum(lax.all_to_all(spread, axes, 0, 0, tiled=True), axis=0)
-
-
-def mem_sum(values):
-    parts = lax.axis_size("mem")
-    spread = jnp.broadcast_to(values[None], (parts,) + values.shape)
-    return jnp.sum(lax.all_to_all(spread, "mem", 0, 0, tiled=True), axis=0)
 
 
 def local_inner(first, second):
@@ -149,9 +143,19 @@
         return lax.dynamic_update_slice_in_dim(partial_sum, own_slice, offset, 1)
 
     def observed_gradient(partial_sum):
-        gathered = mem_sum(partial_sum.reshape(rows_here * columns, features)[obs_index])
-        model_obs = jnp.dot(gathered, obs_jacobian, precision=lax.Precision.HIGHEST)
-        return spread_back(obs_gain * model_obs)
+        gathered = partial_sum.reshape(rows_here * columns, features)[obs_index]
+        pieces = jnp.moveaxis(partial_sum.reshape(rows_here, parts, quarter, features), 1, 0)
+        send = jnp.concatenate(
+            [
+                jnp.broadcast_to(gathered[None], (parts,) + gathered.shape),
+                pieces.reshape(parts, rows_here * quarter, features),
+            ],
+            axis=1,
+        )
+        got = jnp.sum(lax.all_to_all(send, "mem", 0, 0, tiled=True), axis=0)
+        own_image = got[total_slots:].reshape(rows_here, quarter, features)
+        model_obs = jnp.dot(got[:total_slots], obs_jacobian, precision=lax.Precision.HIGHEST)
+        return spread_back(obs_gain * model_obs), own_image
 
     right_static, right_projected = adjoint_parts(spread_back(obs_gain * got_values))
     wide = sweep_steps(neighbours(right_projected, "col", 1, 2), coeffs_wide, NSWEEP)
@@ -161,7 +165,8 @@
     direction = (right_static, right_ensemble)
 
     partial0 = forward_partial(right_static, smoothed_right)
-    adj_static, adj_projected = adjoint_parts(observed_gradient(partial0))
+    gradient, own_image0 = observed_gradient(partial0)
+    adj_static, adj_projected = adjoint_parts(gradient)
     image = (right_static + adj_static, right_ensemble + sweeps(adj_projected, coeffs))
     sums = global_sum(
         jnp.stack(
@@ -184,7 +189,8 @@
     norm_now = norm_next
 
     partial1 = forward_partial(direction[0], smoothed_direction)
-    adj_static, adj_projected = adjoint_parts(observed_gradient(partial1))
+    gradient, own_image1 = observed_gradient(partial1)
+    adj_static, adj_projected = adjoint_parts(gradient)
     curve = (
         jnp.sum(direction[0] * (direction[0] + adj_static))
         + jnp.sum(direction[1] * direction[1])
@@ -193,9 +199,7 @@
     step1 = norm_now / global_sum(curve)
     state = (state[0] + step1 * direction[0], state[1] + step1 * direction[1])
 
-    total = step0 * partial0 + step1 * partial1
-    pieces = jnp.moveaxis(total.reshape(rows_here, parts, quarter, features), 1, 0)
-    increment = jnp.sum(lax.all_to_all(pieces, "mem", 0, 0, tiled=True), axis=0)
+    increment = step0 * own_image0 + step1 * own_image1
     return (increment, state[0], state[1])
 
 

time: 237 us -> 228 us (0.962)
  other arithmetic: 40.7 us -> 34.8 us
  waiting for transfers between devices: 50.2 us -> 56.1 us
  starting transfers between devices: 68.1 us -> 65.2 us
  local copies, waits for them, and re-layouts: 23.9 us -> 21.4 us
    all_to_all x3 -> x2, waiting for transfers between devices: 32.5 us -> 38.7 us  [observed_gradient(): got = jnp.sum(lax.all_to_all(send, 'mem', 0, 0, tiled=True), axis=0)]
    add x13, other arithmetic: 6.6 us -> 2.09 us  [sweep_steps(): centre + face_up * (padded[:, :-2, 1:-1] - centre)]
    all_to_all x3 -> x2, starting transfers between devices: 12.1 us -> 8.93 us  [observed_gradient(): got = jnp.sum(lax.all_to_all(send, 'mem', 0, 0, tiled=True), axis=0)]
    concatenate x0 -> x2, other arithmetic: none -> 2.5 us  [observed_gradient(): jnp.concatenate([jnp.broadcast_to(gathered[None], (parts,) + gathered.sha...]
  transfers between devices with their start and end apart: 17 -> 16, of which waited for: 8 -> 7; matrix products, arithmetic and copies ran while one was open for 5% -> 3% of each run, Pallas kernels for 0% -> 0%
where the time goes in v3:
time: 228 us; the launch traced here: 227 us
  starting transfers between devices  65.2 us (29%)
  waiting for transfers between devices  56.1 us (25%)
  other arithmetic  34.8 us (15%)
  local copies, waits for them, and re-layouts  21.4 us (9%)
  blocking collectives  18.7 us (8%)
  matrix products  18.1 us (8%)
  between operations  12.4 us (5%)
    all_to_all x2, waiting for transfers between devices, observed_gradient(): got = jnp.sum(lax.all_to_all(send, 'mem', 0, 0, tiled=True), axis=0)  38.7 us
    ppermute x6, starting transfers between devices, neighbours(): below.insert(0, lax.ppermute(block, axis, forward))  20.4 us
    all_to_all x1, blocking collectives, global_sum(): return jnp.sum(lax.all_to_all(spread, axes, 0, 0, tiled=True), axis=0)  18.7 us
    all_to_all x1, starting transfers between devices, shards(): got = lax.all_to_all(packed, 'col', split_axis=0, concat_axis=0, tiled=True)  13.1 us
    all_to_all x1, starting transfers between devices, global_sum(): return jnp.sum(lax.all_to_all(spread, axes, 0, 0, tiled=True), axis=0)  12.1 us
    scatter-add x3, other arithmetic, spread_back(): jnp.zeros((rows_here * columns, features), jnp.float32).at[obs_index]  10.8 us
    ppermute x6, starting transfers between devices, neighbours(): above.append(lax.ppermute(block, axis, backward))  10.7 us
    all_to_all x2, starting transfers between devices, observed_gradient(): got = jnp.sum(lax.all_to_all(send, 'mem', 0, 0, tiled=True), axis=0)  8.93 us
  transfers between devices with their start and end apart: 16, of which 7 were waited for; matrix products, arithmetic and copies ran while one was open for 3% of the time, Pallas kernels for 0%

profile of v3, /device:TPU:1, one launch (start us, length us, event | category | flops | bytes accessed | tf_op | source)
XLA Modules:
  0.0 226.7 jit_solution(15044377363179891276)
XLA Ops:
  6.1 3.6 %gather_fusion.1 = s32[512]{0:T(512)S(1)} fusion(s32[256]{0:T(256)} %param.20, s32[1024]{0:T(1024)S(1)} %pad_clamp_fusion.1), kind=kCustom, calls=%fused_computation.1 | custom fusion | bytes 6144 | tf_op jit(solution)/shard_map/gather | solution.py:101
  15.7 13.1 %all-to-all-start = ((f32[64,9,128]{2,1,0:T(8,128)}), f32[64,9,128]{2,1,0:T(8,128)S(1)}, u32[]{:S(2)}, u32[]{:S(2)}) async-start(f32[64,9,128]{2,1,0:T(8,128)} %pad_maximum_fusion.2), calls=%async_computation | async-start | bytes 1048576 | tf_op jit(solution)/shard_map/all_to_all | solution.py:107
  28.9 3.3 %collective-permute-start.4 = (f32[4,256]{1,0:T(4,128)S(1)}, f32[4,256]{1,0:T(4,128)S(1)}, u32[]{:S(2)}, u32[]{:S(2)}) collective-permute-start(f32[4,256]{1,0:T(4,128)S(1)} %copy-done.15), channel_id=1, source_target_pairs={{0,2},{1,3},{2,4},{3,5},{4,6},{5,7},{6,8},{7,9},{8,10},{9,11},{10,... | collective-permute-start | bytes 12296 | tf_op jit(solution)/shard_map/ppermute | solution.py:16
  32.1 3.7 %collective-permute-start.5 = (f32[4,256]{1,0:T(4,128)S(1)}, f32[4,256]{1,0:T(4,128)S(1)}, u32[]{:S(2)}, u32[]{:S(2)}) collective-permute-start(f32[4,256]{1,0:T(4,128)S(1)} %copy-done.15), channel_id=1, source_target_pairs={{0,1},{1,2},{2,3},{3,4},{4,5},{5,6},{6,7},{7,8},{8,9},{9,10},{10,1... | collective-permute-start | bytes 12296 | tf_op jit(solution)/shard_map/ppermute | solution.py:16
  39.0 3.6 %collective-permute-done.6 = f32[4,256]{1,0:T(4,128)S(1)} collective-permute-done((f32[4,256]{1,0:T(4,128)S(1)}, f32[4,256]{1,0:T(4,128)S(1)}, u32[]{:S(2)}, u32[]{:S(2)}) %collective-permute-start.6) | collective-permute-done | bytes 4128 | tf_op jit(solution)/shard_map/ppermute | solution.py:17
  42.8 3.6 %all-to-all-done = f32[64,9,128]{2,1,0:T(8,128)S(1)} async-done(((f32[64,9,128]{2,1,0:T(8,128)}), f32[64,9,128]{2,1,0:T(8,128)S(1)}, u32[]{:S(2)}, u32[]{:S(2)}) %all-to-all-start) | async-done | bytes 294944 | tf_op jit(solution)/shard_map/all_to_all | solution.py:107
  47.3 3.3 %scatter_custom_fusion.1 = f32[1024,128]{1,0:T(8,128)S(1)} fusion(s32[512]{0:T(512)S(1)} %bitcast.140, f32[512,128]{1,0:T(8,128)S(1)} %fusion.16, f32[]{:T(128)} %constant.76.clone.1), kind=kCustom, calls=%fused_computation.77 | custom fusion | flops 65536 | bytes 524292 | tf_op jit(solution)/shard_map/scatter-add | solution.py:116
  52.6 2.5 %collective-permute-start = (f32[8,4,256]{2,1,0:T(4,128)S(1)}, f32[8,4,256]{2,1,0:T(4,128)S(1)}, u32[]{:S(2)}, u32[]{:S(2)}) collective-permute-start(f32[8,4,256]{2,1,0:T(4,128)S(1)} %bitcast.133), channel_id=1, source_target_pairs={{0,2},{1,3},{2,4},{3,5},{4,6},{5,7},{6,8},{7,9},{8,10},{9,11},{10,... | collective-permute-start | bytes 98312 | tf_op jit(solution)/shard_map/ppermute | solution.py:16
  55.1 3.3 %collective-permute-start.1 = (f32[8,4,256]{2,1,0:T(4,128)S(1)}, f32[8,4,256]{2,1,0:T(4,128)S(1)}, u32[]{:S(2)}, u32[]{:S(2)}) collective-permute-start(f32[8,4,256]{2,1,0:T(4,128)S(1)} %bitcast.134), channel_id=1, source_target_pairs={{0,1},{1,2},{2,3},{3,4},{4,5},{5,6},{6,7},{7,8},{8,9},{9,10},{10,1... | collective-permute-start | bytes 98312 | tf_op jit(solution)/shard_map/ppermute | solution.py:16
  74.3 4.5 %all-to-all-start.1 = ((f32[4,768,128]{2,1,0:T(8,128)}), f32[4,768,128]{2,1,0:T(8,128)}, u32[]{:S(2)}, u32[]{:S(2)}) async-start(f32[4,768,128]{2,1,0:T(8,128)} %pad_maximum_fusion), calls=%async_computation.1 | async-start | bytes 3145728 | tf_op jit(solution)/shard_map/all_to_all | solution.py:155
  78.8 20.2 %all-to-all-done.1 = f32[4,768,128]{2,1,0:T(8,128)} async-done(((f32[4,768,128]{2,1,0:T(8,128)}), f32[4,768,128]{2,1,0:T(8,128)}, u32[]{:S(2)}, u32[]{:S(2)}) %all-to-all-start.1) | async-done | bytes 1572896 | tf_op jit(solution)/shard_map/all_to_all | solution.py:155
  102.0 3.7 %scatter_custom_fusion.2 = f32[1024,128]{1,0:T(8,128)S(1)} fusion(s32[512]{0:T(512)} %bitcast.142, f32[512,128]{1,0:T(8,128)} %fusion.243, f32[]{:T(128)} %constant.76.clone.1), kind=kCustom, calls=%fused_computation.75 | custom fusion | flops 65536 | bytes 524800 | tf_op jit(solution)/shard_map/scatter-add | solution.py:116
  105.8 2.4 %fusion.6 = f32[4,256,1,8]{3,2,1,0:T(1,128)} fusion(bf16[8,4,256,128]{3,2,1,0:T(8,128)(2,1)S(1)} %copy-done, bf16[4,256,128,1]{2,1,0,3:T(8,128)(2,1)S(1)} %convert_bitcast_fusion.1), kind=kOutput, calls=%fused_computation.21 | convolution fusion | flops 2097152 | bytes 2392064 | tf_op jit(solution)/shard_map/kyxf,yxf->kyx/dot_general | solution.py:127
  109.4 4.1 %collective-permute-start.8 = (f32[8,4,256]{2,1,0:T(4,128)S(1)}, f32[8,4,256]{2,1,0:T(4,128)S(1)}, u32[]{:S(2)}, u32[]{:S(2)}) collective-permute-start(f32[8,4,256]{2,1,0:T(4,128)S(1)} %bitcast.129), channel_id=1, source_target_pairs={{0,1},{1,2},{2,3},{3,4},{4,5},{5,6},{6,7},{7,8},{8,9},{9,10},{10,1... | collective-permute-start | bytes 98312 | tf_op jit(solution)/shard_map/ppermute | solution.py:16
  116.3 2.3 %collective-permute-done.9 = f32[8,4,256]{2,1,0:T(4,128)S(1)} collective-permute-done((f32[8,4,256]{2,1,0:T(4,128)S(1)}, f32[8,4,256]{2,1,0:T(4,128)S(1)}, u32[]{:S(2)}, u32[]{:S(2)}) %collective-permute-start.9) | collective-permute-done | bytes 32800 | tf_op jit(solution)/shard_map/ppermute | solution.py:17
  125.4 12.1 %all-to-all-start.2 = ((f32[256,1,3]{2,1,0:T(1,128)}), f32[256,1,3]{2,1,0:T(1,128)S(1)}, u32[]{:S(2)}, u32[]{:S(2)}) async-start(f32[256,1,3]{2,1,0:T(1,128)} %broadcast_in_dim.36), calls=%async_computation.2 | async-start | bytes 262144 | tf_op jit(solution)/shard_map/all_to_all | solution.py:58
  137.5 3.7 %collective-permute-start.10 = (f32[8,4,256]{2,1,0:T(4,128)S(1)}, f32[8,4,256]{2,1,0:T(4,128)S(1)}, u32[]{:S(2)}, u32[]{:S(2)}) collective-permute-start(f32[8,4,256]{2,1,0:T(4,128)S(1)} %get-tuple-element.34), channel_id=1, source_target_pairs={{0,1},{1,2},{2,3},{3,4},{4,5},{5,6},{6,7},{7,8},{8,9},{9,10},{10,1... | collective-permute-start | bytes 98312 | tf_op jit(solution)/shard_map/ppermute | solution.py:16
  143.3 7.0 %all-to-all-done.2 = f32[256,1,3]{2,1,0:T(1,128)S(1)} async-done(((f32[256,1,3]{2,1,0:T(1,128)}), f32[256,1,3]{2,1,0:T(1,128)S(1)}, u32[]{:S(2)}, u32[]{:S(2)}) %all-to-all-start.2) | async-done | bytes 3104 | tf_op jit(solution)/shard_map/all_to_all | solution.py:58
  156.9 2.8 %fusion.4 = f32[4,256,1,128]{3,2,1,0:T(1,128)S(1)} fusion(bf16[8,4,256,1]{0,3,2,1:T(2,128)(2,1)} %copy.43, bf16[8,4,256,128]{3,2,1,0:T(8,128)(2,1)S(1)} %copy-done), kind=kOutput, calls=%fused_computation.19 | convolution fusion | flops 2097152 | bytes 2637824 | tf_op jit(solution)/shard_map/kyxf,kyx->yxf/dot_general | solution.py:134
  163.9 4.5 %all-to-all-start.3 = ((f32[4,768,128]{2,1,0:T(8,128)}), f32[4,768,128]{2,1,0:T(8,128)}, u32[]{:S(2)}, u32[]{:S(2)}) async-start(f32[4,768,128]{2,1,0:T(8,128)} %pad_maximum_fusion.1), calls=%async_computation.3 | async-start | bytes 3145728 | tf_op jit(solution)/shard_map/all_to_all | solution.py:155
  169.8 18.6 %all-to-all-done.3 = f32[4,768,128]{2,1,0:T(8,128)} async-done(((f32[4,768,128]{2,1,0:T(8,128)}), f32[4,768,128]{2,1,0:T(8,128)}, u32[]{:S(2)}, u32[]{:S(2)}) %all-to-all-start.3) | async-done | bytes 1572896 | tf_op jit(solution)/shard_map/all_to_all | solution.py:155
  191.8 3.7 %scatter_custom_fusion.3 = f32[1024,128]{1,0:T(8,128)S(1)} fusion(s32[512]{0:T(512)} %bitcast.143, f32[512,128]{1,0:T(8,128)} %fusion.244, f32[]{:T(128)} %constant.76.clone.1), kind=kCustom, calls=%fused_computation.73 | custom fusion | flops 65536 | bytes 524800 | tf_op jit(solution)/shard_map/scatter-add | solution.py:116
  195.6 2.4 %fusion.2 = f32[4,256,1,8]{3,2,1,0:T(1,128)} fusion(bf16[8,4,256,128]{3,2,1,0:T(8,128)(2,1)S(1)} %copy-done, bf16[4,256,128,1]{2,1,0,3:T(8,128)(2,1)S(1)} %convert_bitcast_fusion), kind=kOutput, calls=%fused_computation.17 | convolution fusion | flops 2097152 | bytes 2392064 | tf_op jit(solution)/shard_map/kyxf,yxf->kyx/dot_general | solution.py:127
  202.7 18.7 %all_to_all.27 = f32[256,1,1]{2,1,0:T(1,128)S(1)} all-to-all(f32[256,1,1]{2,1,0:T(1,128)S(1)} %broadcast_in_dim.38), channel_id=1, replica_groups=mesh['mem'=4,'col'=64] {'mem','col'}, dimensions={0} | all-to-all | bytes 2048 | tf_op jit(solution)/shard_map/all_to_all | solution.py:58
  (158 shorter events, 63.7 us)
Async XLA Ops:
  0.6 50.1 %copy-start = (bf16[8,4,256,128]{3,2,1,0:T(8,128)(2,1)S(1)}, bf16[8,4,256,128]{3,2,1,0:T(8,128)(2,1)}, u32[]{:S(2)}) copy-start(bf16[8,4,256,128]{3,2,1,0:T(8,128)(2,1)} %param.13) | copy-start | bytes 6291460
  10.5 18.4 %copy-start.15 = (f32[4,256]{1,0:T(4,128)S(1)}, f32[4,256]{1,0:T(4,128)}, u32[]{:S(2)}) copy-start(f32[4,256]{1,0:T(4,128)} %param.18) | copy-start | bytes 12292
  11.5 35.4 %copy-start.3 = (f32[128,128]{1,0:T(8,128)S(1)}, f32[128,128]{1,0:T(8,128)}, u32[]{:S(2)}) copy-start(f32[128,128]{1,0:T(8,128)} %param.15) | copy-start | bytes 196612
  11.5 35.4 %copy-start.12 = (f32[128]{0:T(128)S(1)}, f32[128]{0:T(128)}, u32[]{:S(2)}) copy-start(f32[128]{0:T(128)} %param.17) | copy-start | bytes 1540
  15.7 30.7 %all-to-all-start = ((f32[64,9,128]{2,1,0:T(8,128)}), f32[64,9,128]{2,1,0:T(8,128)S(1)}, u32[]{:S(2)}, u32[]{:S(2)}) async-start(f32[64,9,128]{2,1,0:T(8,128)} %pad_maximum_fusion.2), calls=%async_computation | async-start | bytes 1048576 | tf_op jit(solution)/shard_map/all_to_all | solution.py:107
  28.9 10.2 %collective-permute-start.4 = (f32[4,256]{1,0:T(4,128)S(1)}, f32[4,256]{1,0:T(4,128)S(1)}, u32[]{:S(2)}, u32[]{:S(2)}) collective-permute-start(f32[4,256]{1,0:T(4,128)S(1)} %copy-done.15), channel_id=1, source_target_pairs={{0,2},{1,3},{2,4},{3,5},{4,6},{5,7},{6,8},{7,9},{8,10},{9,11},{10,... | collective-permute-start | bytes 12296 | tf_op jit(solution)/shard_map/ppermute | solution.py:16
  32.1 6.9 %collective-permute-start.5 = (f32[4,256]{1,0:T(4,128)S(1)}, f32[4,256]{1,0:T(4,128)S(1)}, u32[]{:S(2)}, u32[]{:S(2)}) collective-permute-start(f32[4,256]{1,0:T(4,128)S(1)} %copy-done.15), channel_id=1, source_target_pairs={{0,1},{1,2},{2,3},{3,4},{4,5},{5,6},{6,7},{7,8},{8,9},{9,10},{10,1... | collective-permute-start | bytes 12296 | tf_op jit(solution)/shard_map/ppermute | solution.py:16
  35.8 6.8 %collective-permute-start.6 = (f32[4,256]{1,0:T(4,128)S(1)}, f32[4,256]{1,0:T(4,128)S(1)}, u32[]{:S(2)}, u32[]{:S(2)}) collective-permute-start(f32[4,256]{1,0:T(4,128)S(1)} %copy-done.15), channel_id=1, source_target_pairs={{1,0},{2,1},{3,2},{4,3},{5,4},{6,5},{7,6},{8,7},{9,8},{10,9},{11,1... | collective-permute-start | bytes 12296 | tf_op jit(solution)/shard_map/ppermute | solution.py:17
  37.7 4.9 %collective-permute-start.7 = (f32[4,256]{1,0:T(4,128)S(1)}, f32[4,256]{1,0:T(4,128)S(1)}, u32[]{:S(2)}, u32[]{:S(2)}) collective-permute-start(f32[4,256]{1,0:T(4,128)S(1)} %copy-done.15), channel_id=1, source_target_pairs={{2,0},{3,1},{4,2},{5,3},{6,4},{7,5},{8,6},{9,7},{10,8},{11,9},{12,... | collective-permute-start | bytes 12296 | tf_op jit(solution)/shard_map/ppermute | solution.py:17
  52.6 12.3 %collective-permute-start = (f32[8,4,256]{2,1,0:T(4,128)S(1)}, f32[8,4,256]{2,1,0:T(4,128)S(1)}, u32[]{:S(2)}, u32[]{:S(2)}) collective-permute-start(f32[8,4,256]{2,1,0:T(4,128)S(1)} %bitcast.133), channel_id=1, source_target_pairs={{0,2},{1,3},{2,4},{3,5},{4,6},{5,7},{6,8},{7,9},{8,10},{9,11},{10,... | collective-permute-start | bytes 98312 | tf_op jit(solution)/shard_map/ppermute | solution.py:16
  55.1 9.8 %collective-permute-start.1 = (f32[8,4,256]{2,1,0:T(4,128)S(1)}, f32[8,4,256]{2,1,0:T(4,128)S(1)}, u32[]{:S(2)}, u32[]{:S(2)}) collective-permute-start(f32[8,4,256]{2,1,0:T(4,128)S(1)} %bitcast.134), channel_id=1, source_target_pairs={{0,1},{1,2},{2,3},{3,4},{4,5},{5,6},{6,7},{7,8},{8,9},{9,10},{10,1... | collective-permute-start | bytes 98312 | tf_op jit(solution)/shard_map/ppermute | solution.py:16
  58.4 6.6 %collective-permute-start.2 = (f32[8,4,256]{2,1,0:T(4,128)S(1)}, f32[8,4,256]{2,1,0:T(4,128)S(1)}, u32[]{:S(2)}, u32[]{:S(2)}) collective-permute-start(f32[8,4,256]{2,1,0:T(4,128)S(1)} %bitcast.135), channel_id=1, source_target_pairs={{1,0},{2,1},{3,2},{4,3},{5,4},{6,5},{7,6},{8,7},{9,8},{10,9},{11,1... | collective-permute-start | bytes 98312 | tf_op jit(solution)/shard_map/ppermute | solution.py:17
  60.4 5.4 %collective-permute-start.3 = (f32[8,4,256]{2,1,0:T(4,128)S(1)}, f32[8,4,256]{2,1,0:T(4,128)S(1)}, u32[]{:S(2)}, u32[]{:S(2)}) collective-permute-start(f32[8,4,256]{2,1,0:T(4,128)S(1)} %bitcast.136), channel_id=1, source_target_pairs={{2,0},{3,1},{4,2},{5,3},{6,4},{7,5},{8,6},{9,7},{10,8},{11,9},{12,... | collective-permute-start | bytes 98312 | tf_op jit(solution)/shard_map/ppermute | solution.py:17
  74.3 26.2 %copy-start.8 = (f32[512]{0:T(512)S(1)}, f32[512]{0:T(512)}, u32[]{:S(2)}) copy-start(f32[512]{0:T(512)} %copy-done.7) | copy-start | bytes 6148
  74.3 26.2 %copy-start.13 = (f32[128]{0:T(128)S(1)}, f32[128]{0:T(128)}, u32[]{:S(2)}) copy-start(f32[128]{0:T(128)} %param.17) | copy-start | bytes 1540
  74.3 24.7 %all-to-all-start.1 = ((f32[4,768,128]{2,1,0:T(8,128)}), f32[4,768,128]{2,1,0:T(8,128)}, u32[]{:S(2)}, u32[]{:S(2)}) async-start(f32[4,768,128]{2,1,0:T(8,128)} %pad_maximum_fusion), calls=%async_computation.1 | async-start | bytes 3145728 | tf_op jit(solution)/shard_map/all_to_all | solution.py:155
  109.4 7.0 %collective-permute-start.8 = (f32[8,4,256]{2,1,0:T(4,128)S(1)}, f32[8,4,256]{2,1,0:T(4,128)S(1)}, u32[]{:S(2)}, u32[]{:S(2)}) collective-permute-start(f32[8,4,256]{2,1,0:T(4,128)S(1)} %bitcast.129), channel_id=1, source_target_pairs={{0,1},{1,2},{2,3},{3,4},{4,5},{5,6},{6,7},{7,8},{8,9},{9,10},{10,1... | collective-permute-start | bytes 98312 | tf_op jit(solution)/shard_map/ppermute | solution.py:16
  113.4 5.2 %collective-permute-start.9 = (f32[8,4,256]{2,1,0:T(4,128)S(1)}, f32[8,4,256]{2,1,0:T(4,128)S(1)}, u32[]{:S(2)}, u32[]{:S(2)}) collective-permute-start(f32[8,4,256]{2,1,0:T(4,128)S(1)} %bitcast.130), channel_id=1, source_target_pairs={{1,0},{2,1},{3,2},{4,3},{5,4},{6,5},{7,6},{8,7},{9,8},{10,9},{11,1... | collective-permute-start | bytes 98312 | tf_op jit(solution)/shard_map/ppermute | solution.py:17
  125.4 24.9 %all-to-all-start.2 = ((f32[256,1,3]{2,1,0:T(1,128)}), f32[256,1,3]{2,1,0:T(1,128)S(1)}, u32[]{:S(2)}, u32[]{:S(2)}) async-start(f32[256,1,3]{2,1,0:T(1,128)} %broadcast_in_dim.36), calls=%async_computation.2 | async-start | bytes 262144 | tf_op jit(solution)/shard_map/all_to_all | solution.py:58
  137.5 17.6 %collective-permute-start.10 = (f32[8,4,256]{2,1,0:T(4,128)S(1)}, f32[8,4,256]{2,1,0:T(4,128)S(1)}, u32[]{:S(2)}, u32[]{:S(2)}) collective-permute-start(f32[8,4,256]{2,1,0:T(4,128)S(1)} %get-tuple-element.34), channel_id=1, source_target_pairs={{0,1},{1,2},{2,3},{3,4},{4,5},{5,6},{6,7},{7,8},{8,9},{9,10},{10,1... | collective-permute-start | bytes 98312 | tf_op jit(solution)/shard_map/ppermute | solution.py:16
  141.1 13.9 %collective-permute-start.11 = (f32[8,4,256]{2,1,0:T(4,128)S(1)}, f32[8,4,256]{2,1,0:T(4,128)S(1)}, u32[]{:S(2)}, u32[]{:S(2)}) collective-permute-start(f32[8,4,256]{2,1,0:T(4,128)S(1)} %get-tuple-element.34), channel_id=1, source_target_pairs={{1,0},{2,1},{3,2},{4,3},{5,4},{6,5},{7,6},{8,7},{9,8},{10,9},{11,1... | collective-permute-start | bytes 98312 | tf_op jit(solution)/shard_map/ppermute | solution.py:17
  163.9 26.1 %copy-start.9 = (f32[512]{0:T(512)S(1)}, f32[512]{0:T(512)}, u32[]{:S(2)}) copy-start(f32[512]{0:T(512)} %copy-done.7) | copy-start | bytes 6148
  163.9 26.1 %copy-start.14 = (f32[128]{0:T(128)S(1)}, f32[128]{0:T(128)}, u32[]{:S(2)}) copy-start(f32[128]{0:T(128)} %param.17) | copy-start | bytes 1540
  163.9 24.5 %all-to-all-start.3 = ((f32[4,768,128]{2,1,0:T(8,128)}), f32[4,768,128]{2,1,0:T(8,128)}, u32[]{:S(2)}, u32[]{:S(2)}) async-start(f32[4,768,128]{2,1,0:T(8,128)} %pad_maximum_fusion.1), calls=%async_computation.3 | async-start | bytes 3145728 | tf_op jit(solution)/shard_map/all_to_all | solution.py:155
  (9 other events, 43.7 us)

commit v4 on v2

--- a/solution.py
+++ b/solution.py
@@ -56,12 +56,6 @@
     count = lax.axis_size(axes)
     spread = jnp.broadcast_to(values[None], (count,) + values.shape)
     return jnp.sum(lax.all_to_all(spread, axes, 0, 0, tiled=True), axis=0)
-
-
-def mem_sum(values):
-    parts = lax.axis_size("mem")
-    spread = jnp.broadcast_to(values[None], (parts,) + values.shape)
-    return jnp.sum(lax.all_to_all(spread, "mem", 0, 0, tiled=True), axis=0)
 
 
 def local_inner(first, second):
@@ -148,10 +142,29 @@
         own_slice = lax.dynamic_slice_in_dim(partial_sum, offset, quarter, 1) + forward_static
         return lax.dynamic_update_slice_in_dim(partial_sum, own_slice, offset, 1)
 
-    def observed_gradient(partial_sum):
-        gathered = mem_sum(partial_sum.reshape(rows_here * columns, features)[obs_index])
+    cell_x = obs_index % columns
+    in_quarter = (cell_x >= offset) & (cell_x < offset + quarter)
+    quarter_index = jnp.where(in_quarter, (obs_index // columns) * quarter + cell_x - offset, 0)
+    quarter_gain = jnp.where(in_quarter[:, None], obs_gain, 0.0)
+
+    def observed_adjoint(partial_sum):
+        pieces = jnp.moveaxis(partial_sum.reshape(rows_here, parts, quarter, features), 1, 0)
+        own_image = jnp.sum(lax.all_to_all(pieces, "mem", 0, 0, tiled=True), axis=0)
+        gathered = own_image.reshape(rows_here * quarter, features)[quarter_index]
         model_obs = jnp.dot(gathered, obs_jacobian, precision=lax.Precision.HIGHEST)
-        return spread_back(obs_gain * model_obs)
+        back = jnp.dot(quarter_gain * model_obs, obs_jacobian.T, precision=lax.Precision.HIGHEST)
+        own_gradient = jnp.zeros((rows_here * quarter, features), jnp.float32).at[quarter_index].add(back)
+        static = jnp.dot(own_gradient, static_root.T, precision=lax.Precision.HIGHEST).reshape(
+            rows_here, quarter, features
+        )
+        rounded = own_gradient.reshape(rows_here, quarter, features).astype(jnp.bfloat16)
+        spread = jnp.broadcast_to(rounded[None], (parts,) + rounded.shape)
+        quarters = lax.all_to_all(spread, "mem", 0, 0, tiled=True)
+        rounded = jnp.moveaxis(quarters, 0, 1).reshape(rows_here, columns, features)
+        projected = jnp.einsum(
+            "kyxf,yxf->kyx", perturbations, rounded, preferred_element_type=jnp.float32
+        )
+        return own_image, static, projected
 
     right_static, right_projected = adjoint_parts(spread_back(obs_gain * got_values))
     wide = sweep_steps(neighbours(right_projected, "col", 1, 2), coeffs_wide, NSWEEP)
@@ -161,7 +174,7 @@
     direction = (right_static, right_ensemble)
 
     partial0 = forward_partial(right_static, smoothed_right)
-    adj_static, adj_projected = adjoint_parts(observed_gradient(partial0))
+    own_image0, adj_static, adj_projected = observed_adjoint(partial0)
     image = (right_static + adj_static, right_ensemble + sweeps(adj_projected, coeffs))
     sums = global_sum(
         jnp.stack(
@@ -184,7 +197,7 @@
     norm_now = norm_next
 
     partial1 = forward_partial(direction[0], smoothed_direction)
-    adj_static, adj_projected = adjoint_parts(observed_gradient(partial1))
+    own_image1, adj_static, adj_projected = observed_adjoint(partial1)
     curve = (
         jnp.sum(direction[0] * (direction[0] + adj_static))
         + jnp.sum(direction[1] * direction[1])
@@ -193,9 +206,7 @@
     step1 = norm_now / global_sum(curve)
     state = (state[0] + step1 * direction[0], state[1] + step1 * direction[1])
 
-    total = step0 * partial0 + step1 * partial1
-    pieces = jnp.moveaxis(total.reshape(rows_here, parts, quarter, features), 1, 0)
-    increment = jnp.sum(lax.all_to_all(pieces, "mem", 0, 0, tiled=True), axis=0)
+    increment = step0 * own_image0 + step1 * own_image1
     return (increment, state[0], state[1])
 
 

time: 237 us -> 205 us (0.86)
  waiting for transfers between devices: 50.2 us -> 33.8 us
  other arithmetic: 40.7 us -> 24.5 us
  blocking collectives: 20.5 us -> 33 us
  local copies, waits for them, and re-layouts: 23.9 us -> 17.6 us
  matrix products: 20 us -> 14.9 us
    all_to_all x3, waiting for transfers between devices: 32.5 us -> 16.6 us  [the longest x1 8.54 us: observed_adjoint(): own_image = jnp.sum(lax.all_to_all(pieces, 'mem', 0, 0, tiled=True), axis=0)]
    all_to_all x0 -> x1, blocking collectives: none -> 10.9 us  [observed_adjoint(): own_image = jnp.sum(lax.all_to_all(pieces, 'mem', 0, 0, tiled=True), axis=0)]
    scatter-add x3 -> x1, other arithmetic: 11.4 us -> 3.44 us  [spread_back(): jnp.zeros((rows_here * columns, features), jnp.float32).at[obs_index]]
    scatter-add x0 -> x2, other arithmetic: none -> 7.64 us  [observed_adjoint(): jnp.zeros((rows_here * quarter, features), jnp.float32).at[quarter_index]]
    dot_general x2 -> x8, matrix products: 1.67 us -> 7.14 us  [the longest x2 3.15 us: observed_adjoint(): jnp.einsum('kyxf,yxf->kyx', perturbations, rounded, preferred_element_typ...]
    ppermute x6, starting transfers between devices: 10.7 us -> 15.5 us  [neighbours(): above.append(lax.ppermute(block, axis, backward))]
    add x13, other arithmetic: 6.6 us -> 2.1 us  [sweep_steps(): centre + face_up * (padded[:, :-2, 1:-1] - centre)]
    dot_general x3 -> x1, matrix products: 6.37 us -> 2.38 us  [adjoint_parts(): jnp.einsum('kyxf,yxf->kyx', perturbations, rounded, preferred_element_typ...]
  transfers between devices with their start and end apart: 17 -> 17, of which waited for: 8 -> 8; matrix products, arithmetic and copies ran while one was open for 5% -> 2% of each run, Pallas kernels for 0% -> 0%
where the time goes in v4:
time: 205 us; the launch traced here: 204 us
  starting transfers between devices  67.4 us (33%)
  waiting for transfers between devices  33.8 us (16%)
  blocking collectives  33 us (16%)
  other arithmetic  24.5 us (12%)
  local copies, waits for them, and re-layouts  17.6 us (9%)
  matrix products  14.9 us (7%)
  between operations  12.8 us (6%)
    all_to_all x1, blocking collectives, global_sum(): return jnp.sum(lax.all_to_all(spread, axes, 0, 0, tiled=True), axis=0)  22.1 us
    ppermute x6, starting transfers between devices, neighbours(): below.insert(0, lax.ppermute(block, axis, forward))  18.1 us
    ppermute x6, starting transfers between devices, neighbours(): above.append(lax.ppermute(block, axis, backward))  15.5 us
    all_to_all x1, starting transfers between devices, shards(): got = lax.all_to_all(packed, 'col', split_axis=0, concat_axis=0, tiled=True)  13.1 us
    all_to_all x1, blocking collectives, observed_adjoint(): own_image = jnp.sum(lax.all_to_all(pieces, 'mem', 0, 0, tiled=True), axis=0)  10.9 us
    all_to_all x1, starting transfers between devices, global_sum(): return jnp.sum(lax.all_to_all(spread, axes, 0, 0, tiled=True), axis=0)  9.81 us
    all_to_all x1, waiting for transfers between devices, observed_adjoint(): own_image = jnp.sum(lax.all_to_all(pieces, 'mem', 0, 0, tiled=True), axis=0)  8.54 us
    all_to_all x2, waiting for transfers between devices, observed_adjoint(): quarters = lax.all_to_all(spread, 'mem', 0, 0, tiled=True)  8.1 us
  transfers between devices with their start and end apart: 17, of which 8 were waited for; matrix products, arithmetic and copies ran while one was open for 2% of the time, Pallas kernels for 0%

profile of v4, /device:TPU:1, one launch (start us, length us, event | category | flops | bytes accessed | tf_op | source)
XLA Modules:
  0.0 204.0 jit_solution(6035903969124713292)
XLA Ops:
  6.1 3.6 %gather_fusion.1 = s32[512]{0:T(512)S(1)} fusion(s32[256]{0:T(256)} %param.20, s32[1024]{0:T(1024)S(1)} %pad_clamp_fusion.1), kind=kCustom, calls=%fused_computation.1 | custom fusion | bytes 6144 | tf_op jit(solution)/shard_map/gather | solution.py:101
  15.7 13.1 %all-to-all-start = ((f32[64,9,128]{2,1,0:T(8,128)}), f32[64,9,128]{2,1,0:T(8,128)S(1)}, u32[]{:S(2)}, u32[]{:S(2)}) async-start(f32[64,9,128]{2,1,0:T(8,128)} %pad_maximum_fusion), calls=%async_computation | async-start | bytes 1048576 | tf_op jit(solution)/shard_map/all_to_all | solution.py:107
  28.9 3.3 %collective-permute-start.4 = (f32[4,256]{1,0:T(4,128)S(1)}, f32[4,256]{1,0:T(4,128)S(1)}, u32[]{:S(2)}, u32[]{:S(2)}) collective-permute-start(f32[4,256]{1,0:T(4,128)S(1)} %copy-done.10), channel_id=1, source_target_pairs={{0,2},{1,3},{2,4},{3,5},{4,6},{5,7},{6,8},{7,9},{8,10},{9,11},{10,... | collective-permute-start | bytes 12296 | tf_op jit(solution)/shard_map/ppermute | solution.py:16
  32.1 3.7 %collective-permute-start.5 = (f32[4,256]{1,0:T(4,128)S(1)}, f32[4,256]{1,0:T(4,128)S(1)}, u32[]{:S(2)}, u32[]{:S(2)}) collective-permute-start(f32[4,256]{1,0:T(4,128)S(1)} %copy-done.10), channel_id=1, source_target_pairs={{0,1},{1,2},{2,3},{3,4},{4,5},{5,6},{6,7},{7,8},{8,9},{9,10},{10,1... | collective-permute-start | bytes 12296 | tf_op jit(solution)/shard_map/ppermute | solution.py:16
  39.1 3.6 %collective-permute-done.6 = f32[4,256]{1,0:T(4,128)S(1)} collective-permute-done((f32[4,256]{1,0:T(4,128)S(1)}, f32[4,256]{1,0:T(4,128)S(1)}, u32[]{:S(2)}, u32[]{:S(2)}) %collective-permute-start.6) | collective-permute-done | bytes 4128 | tf_op jit(solution)/shard_map/ppermute | solution.py:17
  42.8 3.6 %all-to-all-done = f32[64,9,128]{2,1,0:T(8,128)S(1)} async-done(((f32[64,9,128]{2,1,0:T(8,128)}), f32[64,9,128]{2,1,0:T(8,128)S(1)}, u32[]{:S(2)}, u32[]{:S(2)}) %all-to-all-start) | async-done | bytes 294944 | tf_op jit(solution)/shard_map/all_to_all | solution.py:107
  48.1 3.4 %scatter_custom_fusion.1 = f32[1024,128]{1,0:T(8,128)S(1)} fusion(s32[512]{0:T(512)S(1)} %bitcast.151, f32[512,128]{1,0:T(8,128)} %fusion.16, f32[]{:T(128)} %constant.99.clone.1), kind=kCustom, calls=%fused_computation.68 | custom fusion | flops 65536 | bytes 524800 | tf_op jit(solution)/shard_map/scatter-add | solution.py:116
  55.1 2.7 %collective-permute-start = (f32[8,4,256]{2,1,0:T(4,128)S(1)}, f32[8,4,256]{2,1,0:T(4,128)S(1)}, u32[]{:S(2)}, u32[]{:S(2)}) collective-permute-start(f32[8,4,256]{2,1,0:T(4,128)S(1)} %bitcast.140), channel_id=1, source_target_pairs={{0,2},{1,3},{2,4},{3,5},{4,6},{5,7},{6,8},{7,9},{8,10},{9,11},{10,... | collective-permute-start | bytes 98312 | tf_op jit(solution)/shard_map/ppermute | solution.py:16
  57.9 3.4 %collective-permute-start.1 = (f32[8,4,256]{2,1,0:T(4,128)S(1)}, f32[8,4,256]{2,1,0:T(4,128)S(1)}, u32[]{:S(2)}, u32[]{:S(2)}) collective-permute-start(f32[8,4,256]{2,1,0:T(4,128)S(1)} %bitcast.141), channel_id=1, source_target_pairs={{0,1},{1,2},{2,3},{3,4},{4,5},{5,6},{6,7},{7,8},{8,9},{9,10},{10,1... | collective-permute-start | bytes 98312 | tf_op jit(solution)/shard_map/ppermute | solution.py:16
  73.2 4.1 %all-to-all-start.1 = ((f32[4,4,64,128]{3,2,1,0:T(8,128)}), f32[4,4,64,128]{3,2,1,0:T(8,128)S(1)}, u32[]{:S(2)}, u32[]{:S(2)}) async-start(f32[4,4,64,128]{3,2,1,0:T(8,128)} %copy.44), calls=%async_computation.1 | async-start | bytes 1048576 | tf_op jit(solution)/shard_map/all_to_all | solution.py:152
  77.4 8.5 %all-to-all-done.1 = f32[4,4,64,128]{3,2,1,0:T(8,128)S(1)} async-done(((f32[4,4,64,128]{3,2,1,0:T(8,128)}), f32[4,4,64,128]{3,2,1,0:T(8,128)S(1)}, u32[]{:S(2)}, u32[]{:S(2)}) %all-to-all-start.1) | async-done | bytes 524320 | tf_op jit(solution)/shard_map/all_to_all | solution.py:152
  87.8 3.8 %scatter_custom_fusion.2 = f32[256,128]{1,0:T(8,128)S(1)} fusion(s32[512]{0:T(512)S(1)} %bitcast.148, f32[512,128]{1,0:T(8,128)S(1)} %fusion.236, f32[]{:T(128)} %constant.99.clone.1), kind=kCustom, calls=%fused_computation.277 | custom fusion | flops 65536 | bytes 131076 | tf_op jit(solution)/shard_map/scatter-add | solution.py:156
  92.4 3.4 %all-to-all-start.2 = ((bf16[4,4,64,128]{3,2,1,0:T(8,128)(2,1)}), bf16[4,4,64,128]{3,2,1,0:T(8,128)(2,1)S(1)}, u32[]{:S(2)}, u32[]{:S(2)}) async-start(bf16[4,4,64,128]{3,2,1,0:T(8,128)(2,1)} %broadcast_in_dim.49), calls=%async_computation.2 | async-start | bytes 524288 | tf_op jit(solution)/shard_map/all_to_all | solution.py:162
  95.9 5.4 %all-to-all-done.2 = bf16[4,4,64,128]{3,2,1,0:T(8,128)(2,1)S(1)} async-done(((bf16[4,4,64,128]{3,2,1,0:T(8,128)(2,1)}), bf16[4,4,64,128]{3,2,1,0:T(8,128)(2,1)S(1)}, u32[]{:S(2)}, u32[]{:S(2)}) %all-to-all-start.2) | async-done | bytes 262176 | tf_op jit(solution)/shard_map/all_to_all | solution.py:162
  103.2 4.8 %collective-permute-start.9 = (f32[8,4,256]{2,1,0:T(4,128)S(1)}, f32[8,4,256]{2,1,0:T(4,128)S(1)}, u32[]{:S(2)}, u32[]{:S(2)}) collective-permute-start(f32[8,4,256]{2,1,0:T(4,128)S(1)} %bitcast.135), channel_id=1, source_target_pairs={{1,0},{2,1},{3,2},{4,3},{5,4},{6,5},{7,6},{8,7},{9,8},{10,9},{11,1... | collective-permute-start | bytes 98312 | tf_op jit(solution)/shard_map/ppermute | solution.py:17
  108.0 2.9 %collective-permute-start.8 = (f32[8,4,256]{2,1,0:T(4,128)S(1)}, f32[8,4,256]{2,1,0:T(4,128)S(1)}, u32[]{:S(2)}, u32[]{:S(2)}) collective-permute-start(f32[8,4,256]{2,1,0:T(4,128)S(1)} %bitcast.136), channel_id=1, source_target_pairs={{0,1},{1,2},{2,3},{3,4},{4,5},{5,6},{6,7},{7,8},{8,9},{9,10},{10,1... | collective-permute-start | bytes 98312 | tf_op jit(solution)/shard_map/ppermute | solution.py:16
  118.5 9.8 %all-to-all-start.3 = ((f32[256,1,3]{2,1,0:T(1,128)}), f32[256,1,3]{2,1,0:T(1,128)S(1)}, u32[]{:S(2)}, u32[]{:S(2)}) async-start(f32[256,1,3]{2,1,0:T(1,128)} %broadcast_in_dim.50), calls=%async_computation.3 | async-start | bytes 262144 | tf_op jit(solution)/shard_map/all_to_all | solution.py:58
  128.3 4.1 %collective-permute-start.11 = (f32[8,4,256]{2,1,0:T(4,128)S(1)}, f32[8,4,256]{2,1,0:T(4,128)S(1)}, u32[]{:S(2)}, u32[]{:S(2)}) collective-permute-start(f32[8,4,256]{2,1,0:T(4,128)S(1)} %get-tuple-element.35), channel_id=1, source_target_pairs={{1,0},{2,1},{3,2},{4,3},{5,4},{6,5},{7,6},{8,7},{9,8},{10,9},{11,1... | collective-permute-start | bytes 98312 | tf_op jit(solution)/shard_map/ppermute | solution.py:17
  134.6 6.6 %all-to-all-done.3 = f32[256,1,3]{2,1,0:T(1,128)S(1)} async-done(((f32[256,1,3]{2,1,0:T(1,128)}), f32[256,1,3]{2,1,0:T(1,128)S(1)}, u32[]{:S(2)}, u32[]{:S(2)}) %all-to-all-start.3) | async-done | bytes 3104 | tf_op jit(solution)/shard_map/all_to_all | solution.py:58
  149.5 10.9 %all_to_all.37 = f32[4,4,64,128]{3,2,1,0:T(8,128)S(1)} all-to-all(f32[4,4,64,128]{3,2,1,0:T(8,128)S(1)} %bitcast.122), channel_id=1, replica_groups=mesh['mem'=4,'col'=64] {'mem'}, dimensions={0} | all-to-all | bytes 1048576 | tf_op jit(solution)/shard_map/all_to_all | solution.py:152
  162.2 3.8 %scatter_custom_fusion.3 = f32[256,128]{1,0:T(8,128)S(1)} fusion(s32[512]{0:T(512)S(1)} %bitcast.149, f32[512,128]{1,0:T(8,128)S(1)} %fusion.237, f32[]{:T(128)} %constant.99.clone.1), kind=kCustom, calls=%fused_computation.275 | custom fusion | flops 65536 | bytes 131076 | tf_op jit(solution)/shard_map/scatter-add | solution.py:156
  166.8 3.4 %all-to-all-start.5 = ((bf16[4,4,64,128]{3,2,1,0:T(8,128)(2,1)}), bf16[4,4,64,128]{3,2,1,0:T(8,128)(2,1)S(1)}, u32[]{:S(2)}, u32[]{:S(2)}) async-start(bf16[4,4,64,128]{3,2,1,0:T(8,128)(2,1)} %broadcast_in_dim.51), calls=%async_computation.5 | async-start | bytes 524288 | tf_op jit(solution)/shard_map/all_to_all | solution.py:162
  173.1 2.7 %all-to-all-done.5 = bf16[4,4,64,128]{3,2,1,0:T(8,128)(2,1)S(1)} async-done(((bf16[4,4,64,128]{3,2,1,0:T(8,128)(2,1)}), bf16[4,4,64,128]{3,2,1,0:T(8,128)(2,1)S(1)}, u32[]{:S(2)}, u32[]{:S(2)}) %all-to-all-start.5) | async-done | bytes 262176 | tf_op jit(solution)/shard_map/all_to_all | solution.py:162
  179.0 22.1 %all_to_all.38 = f32[256,1,1]{2,1,0:T(1,128)S(1)} all-to-all(f32[256,1,1]{2,1,0:T(1,128)S(1)} %broadcast_in_dim.52), channel_id=1, replica_groups=mesh['mem'=4,'col'=64] {'mem','col'}, dimensions={0} | all-to-all | bytes 2048 | tf_op jit(solution)/shard_map/all_to_all | solution.py:58
  (153 shorter events, 54.3 us)
Async XLA Ops:
  0.6 50.9 %copy-start = (bf16[8,4,256,128]{3,2,1,0:T(8,128)(2,1)S(1)}, bf16[8,4,256,128]{3,2,1,0:T(8,128)(2,1)}, u32[]{:S(2)}) copy-start(bf16[8,4,256,128]{3,2,1,0:T(8,128)(2,1)} %param.13) | copy-start | bytes 6291460
  10.5 18.4 %copy-start.10 = (f32[4,256]{1,0:T(4,128)S(1)}, f32[4,256]{1,0:T(4,128)}, u32[]{:S(2)}) copy-start(f32[4,256]{1,0:T(4,128)} %param.18) | copy-start | bytes 12292
  11.5 35.4 %copy-start.2 = (f32[128,128]{1,0:T(8,128)S(1)}, f32[128,128]{1,0:T(8,128)}, u32[]{:S(2)}) copy-start(f32[128,128]{1,0:T(8,128)} %param.15) | copy-start | bytes 196612
  11.5 35.4 %copy-start.7 = (f32[128]{0:T(128)S(1)}, f32[128]{0:T(128)}, u32[]{:S(2)}) copy-start(f32[128]{0:T(128)} %param.17) | copy-start | bytes 1540
  15.7 30.7 %all-to-all-start = ((f32[64,9,128]{2,1,0:T(8,128)}), f32[64,9,128]{2,1,0:T(8,128)S(1)}, u32[]{:S(2)}, u32[]{:S(2)}) async-start(f32[64,9,128]{2,1,0:T(8,128)} %pad_maximum_fusion), calls=%async_computation | async-start | bytes 1048576 | tf_op jit(solution)/shard_map/all_to_all | solution.py:107
  28.9 10.2 %collective-permute-start.4 = (f32[4,256]{1,0:T(4,128)S(1)}, f32[4,256]{1,0:T(4,128)S(1)}, u32[]{:S(2)}, u32[]{:S(2)}) collective-permute-start(f32[4,256]{1,0:T(4,128)S(1)} %copy-done.10), channel_id=1, source_target_pairs={{0,2},{1,3},{2,4},{3,5},{4,6},{5,7},{6,8},{7,9},{8,10},{9,11},{10,... | collective-permute-start | bytes 12296 | tf_op jit(solution)/shard_map/ppermute | solution.py:16
  32.1 6.9 %collective-permute-start.5 = (f32[4,256]{1,0:T(4,128)S(1)}, f32[4,256]{1,0:T(4,128)S(1)}, u32[]{:S(2)}, u32[]{:S(2)}) collective-permute-start(f32[4,256]{1,0:T(4,128)S(1)} %copy-done.10), channel_id=1, source_target_pairs={{0,1},{1,2},{2,3},{3,4},{4,5},{5,6},{6,7},{7,8},{8,9},{9,10},{10,1... | collective-permute-start | bytes 12296 | tf_op jit(solution)/shard_map/ppermute | solution.py:16
  35.8 6.8 %collective-permute-start.6 = (f32[4,256]{1,0:T(4,128)S(1)}, f32[4,256]{1,0:T(4,128)S(1)}, u32[]{:S(2)}, u32[]{:S(2)}) collective-permute-start(f32[4,256]{1,0:T(4,128)S(1)} %copy-done.10), channel_id=1, source_target_pairs={{1,0},{2,1},{3,2},{4,3},{5,4},{6,5},{7,6},{8,7},{9,8},{10,9},{11,1... | collective-permute-start | bytes 12296 | tf_op jit(solution)/shard_map/ppermute | solution.py:17
  37.7 4.9 %collective-permute-start.7 = (f32[4,256]{1,0:T(4,128)S(1)}, f32[4,256]{1,0:T(4,128)S(1)}, u32[]{:S(2)}, u32[]{:S(2)}) collective-permute-start(f32[4,256]{1,0:T(4,128)S(1)} %copy-done.10), channel_id=1, source_target_pairs={{2,0},{3,1},{4,2},{5,3},{6,4},{7,5},{8,6},{9,7},{10,8},{11,9},{12,... | collective-permute-start | bytes 12296 | tf_op jit(solution)/shard_map/ppermute | solution.py:17
  51.6 13.1 %copy-start.3 = (f32[128,128]{1,0:T(8,128)S(1)}, f32[128,128]{1,0:T(8,128)}, u32[]{:S(2)}) copy-start(f32[128,128]{1,0:T(8,128)} %param.14) | copy-start | bytes 196612
  55.1 10.1 %collective-permute-start = (f32[8,4,256]{2,1,0:T(4,128)S(1)}, f32[8,4,256]{2,1,0:T(4,128)S(1)}, u32[]{:S(2)}, u32[]{:S(2)}) collective-permute-start(f32[8,4,256]{2,1,0:T(4,128)S(1)} %bitcast.140), channel_id=1, source_target_pairs={{0,2},{1,3},{2,4},{3,5},{4,6},{5,7},{6,8},{7,9},{8,10},{9,11},{10,... | collective-permute-start | bytes 98312 | tf_op jit(solution)/shard_map/ppermute | solution.py:16
  57.9 7.4 %collective-permute-start.1 = (f32[8,4,256]{2,1,0:T(4,128)S(1)}, f32[8,4,256]{2,1,0:T(4,128)S(1)}, u32[]{:S(2)}, u32[]{:S(2)}) collective-permute-start(f32[8,4,256]{2,1,0:T(4,128)S(1)} %bitcast.141), channel_id=1, source_target_pairs={{0,1},{1,2},{2,3},{3,4},{4,5},{5,6},{6,7},{7,8},{8,9},{9,10},{10,1... | collective-permute-start | bytes 98312 | tf_op jit(solution)/shard_map/ppermute | solution.py:16
  61.2 5.2 %collective-permute-start.2 = (f32[8,4,256]{2,1,0:T(4,128)S(1)}, f32[8,4,256]{2,1,0:T(4,128)S(1)}, u32[]{:S(2)}, u32[]{:S(2)}) collective-permute-start(f32[8,4,256]{2,1,0:T(4,128)S(1)} %bitcast.142), channel_id=1, source_target_pairs={{1,0},{2,1},{3,2},{4,3},{5,4},{6,5},{7,6},{8,7},{9,8},{10,9},{11,1... | collective-permute-start | bytes 98312 | tf_op jit(solution)/shard_map/ppermute | solution.py:17
  63.2 5.4 %collective-permute-start.3 = (f32[8,4,256]{2,1,0:T(4,128)S(1)}, f32[8,4,256]{2,1,0:T(4,128)S(1)}, u32[]{:S(2)}, u32[]{:S(2)}) collective-permute-start(f32[8,4,256]{2,1,0:T(4,128)S(1)} %bitcast.143), channel_id=1, source_target_pairs={{2,0},{3,1},{4,2},{5,3},{6,4},{7,5},{8,6},{9,7},{10,8},{11,9},{12,... | collective-permute-start | bytes 98312 | tf_op jit(solution)/shard_map/ppermute | solution.py:17
  73.2 13.9 %copy-start.8 = (f32[128]{0:T(128)S(1)}, f32[128]{0:T(128)}, u32[]{:S(2)}) copy-start(f32[128]{0:T(128)} %param.17) | copy-start | bytes 1540
  73.2 12.8 %all-to-all-start.1 = ((f32[4,4,64,128]{3,2,1,0:T(8,128)}), f32[4,4,64,128]{3,2,1,0:T(8,128)S(1)}, u32[]{:S(2)}, u32[]{:S(2)}) async-start(f32[4,4,64,128]{3,2,1,0:T(8,128)} %copy.44), calls=%async_computation.1 | async-start | bytes 1048576 | tf_op jit(solution)/shard_map/all_to_all | solution.py:152
  92.4 8.9 %all-to-all-start.2 = ((bf16[4,4,64,128]{3,2,1,0:T(8,128)(2,1)}), bf16[4,4,64,128]{3,2,1,0:T(8,128)(2,1)S(1)}, u32[]{:S(2)}, u32[]{:S(2)}) async-start(bf16[4,4,64,128]{3,2,1,0:T(8,128)(2,1)} %broadcast_in_dim.49), calls=%async_computation.2 | async-start | bytes 524288 | tf_op jit(solution)/shard_map/all_to_all | solution.py:162
  103.2 9.4 %collective-permute-start.9 = (f32[8,4,256]{2,1,0:T(4,128)S(1)}, f32[8,4,256]{2,1,0:T(4,128)S(1)}, u32[]{:S(2)}, u32[]{:S(2)}) collective-permute-start(f32[8,4,256]{2,1,0:T(4,128)S(1)} %bitcast.135), channel_id=1, source_target_pairs={{1,0},{2,1},{3,2},{4,3},{5,4},{6,5},{7,6},{8,7},{9,8},{10,9},{11,1... | collective-permute-start | bytes 98312 | tf_op jit(solution)/shard_map/ppermute | solution.py:17
  108.0 4.6 %collective-permute-start.8 = (f32[8,4,256]{2,1,0:T(4,128)S(1)}, f32[8,4,256]{2,1,0:T(4,128)S(1)}, u32[]{:S(2)}, u32[]{:S(2)}) collective-permute-start(f32[8,4,256]{2,1,0:T(4,128)S(1)} %bitcast.136), channel_id=1, source_target_pairs={{0,1},{1,2},{2,3},{3,4},{4,5},{5,6},{6,7},{7,8},{8,9},{9,10},{10,1... | collective-permute-start | bytes 98312 | tf_op jit(solution)/shard_map/ppermute | solution.py:16
  118.5 22.7 %all-to-all-start.3 = ((f32[256,1,3]{2,1,0:T(1,128)}), f32[256,1,3]{2,1,0:T(1,128)S(1)}, u32[]{:S(2)}, u32[]{:S(2)}) async-start(f32[256,1,3]{2,1,0:T(1,128)} %broadcast_in_dim.50), calls=%async_computation.3 | async-start | bytes 262144 | tf_op jit(solution)/shard_map/all_to_all | solution.py:58
  128.3 18.0 %collective-permute-start.11 = (f32[8,4,256]{2,1,0:T(4,128)S(1)}, f32[8,4,256]{2,1,0:T(4,128)S(1)}, u32[]{:S(2)}, u32[]{:S(2)}) collective-permute-start(f32[8,4,256]{2,1,0:T(4,128)S(1)} %get-tuple-element.35), channel_id=1, source_target_pairs={{1,0},{2,1},{3,2},{4,3},{5,4},{6,5},{7,6},{8,7},{9,8},{10,9},{11,1... | collective-permute-start | bytes 98312 | tf_op jit(solution)/shard_map/ppermute | solution.py:17
  132.4 13.9 %collective-permute-start.10 = (f32[8,4,256]{2,1,0:T(4,128)S(1)}, f32[8,4,256]{2,1,0:T(4,128)S(1)}, u32[]{:S(2)}, u32[]{:S(2)}) collective-permute-start(f32[8,4,256]{2,1,0:T(4,128)S(1)} %get-tuple-element.35), channel_id=1, source_target_pairs={{0,1},{1,2},{2,3},{3,4},{4,5},{5,6},{6,7},{7,8},{8,9},{9,10},{10,1... | collective-permute-start | bytes 98312 | tf_op jit(solution)/shard_map/ppermute | solution.py:16
  166.8 8.9 %all-to-all-start.5 = ((bf16[4,4,64,128]{3,2,1,0:T(8,128)(2,1)}), bf16[4,4,64,128]{3,2,1,0:T(8,128)(2,1)S(1)}, u32[]{:S(2)}, u32[]{:S(2)}) async-start(bf16[4,4,64,128]{3,2,1,0:T(8,128)(2,1)} %broadcast_in_dim.51), calls=%async_computation.5 | async-start | bytes 524288 | tf_op jit(solution)/shard_map/all_to_all | solution.py:162
  175.8 27.5 %copy-start.6 = (f32[256,128]{1,0:T(8,128)S(1)}, f32[256,128]{1,0:T(8,128)}, u32[]{:S(2)}) copy-start(f32[256,128]{1,0:T(8,128)} %get-tuple-element.64) | copy-start | bytes 393220
  (5 other events, 40.7 us)

commit v5 on v4

--- a/solution.py
+++ b/solution.py
@@ -100,9 +100,14 @@
     send_values = jnp.where(filled[:, None], innovations[source], 0.0)
     send_cells = jnp.where(filled, obs_cell[source], 0).astype(jnp.float32)
     send_marks = filled.astype(jnp.float32)
-    side = jnp.zeros((blocks, 1, channels), jnp.float32)
-    side = side.at[:, 0, :capacity].set(send_cells.reshape(blocks, capacity))
-    side = side.at[:, 0, capacity : 2 * capacity].set(send_marks.reshape(blocks, capacity))
+    side = jnp.concatenate(
+        [
+            send_cells.reshape(blocks, capacity),
+            send_marks.reshape(blocks, capacity),
+            jnp.zeros((blocks, channels - 2 * capacity), jnp.float32),
+        ],
+        axis=1,
+    )[:, None, :]
     packed = jnp.concatenate([send_values.reshape(blocks, capacity, channels), side], axis=1)
     got = lax.all_to_all(packed, "col", split_axis=0, concat_axis=0, tiled=True)
     got_values = got[:, :capacity, :].reshape(total_slots, channels)
@@ -147,11 +152,14 @@
     quarter_index = jnp.where(in_quarter, (obs_index // columns) * quarter + cell_x - offset, 0)
     quarter_gain = jnp.where(in_quarter[:, None], obs_gain, 0.0)
 
-    def observed_adjoint(partial_sum):
+    def observed(partial_sum):
         pieces = jnp.moveaxis(partial_sum.reshape(rows_here, parts, quarter, features), 1, 0)
         own_image = jnp.sum(lax.all_to_all(pieces, "mem", 0, 0, tiled=True), axis=0)
         gathered = own_image.reshape(rows_here * quarter, features)[quarter_index]
         model_obs = jnp.dot(gathered, obs_jacobian, precision=lax.Precision.HIGHEST)
+        return own_image, model_obs
+
+    def observed_adjoint(model_obs):
         back = jnp.dot(quarter_gain * model_obs, obs_jacobian.T, precision=lax.Precision.HIGHEST)
         own_gradient = jnp.zeros((rows_here * quarter, features), jnp.float32).at[quarter_index].add(back)
         static = jnp.dot(own_gradient, static_root.T, precision=lax.Precision.HIGHEST).reshape(
@@ -164,7 +172,7 @@
         projected = jnp.einsum(
             "kyxf,yxf->kyx", perturbations, rounded, preferred_element_type=jnp.float32
         )
-        return own_image, static, projected
+        return static, projected
 
     right_static, right_projected = adjoint_parts(spread_back(obs_gain * got_values))
     wide = sweep_steps(neighbours(right_projected, "col", 1, 2), coeffs_wide, NSWEEP)
@@ -174,7 +182,8 @@
     direction = (right_static, right_ensemble)
 
     partial0 = forward_partial(right_static, smoothed_right)
-    own_image0, adj_static, adj_projected = observed_adjoint(partial0)
+    own_image0, model_obs = observed(partial0)
+    adj_static, adj_projected = observed_adjoint(model_obs)
     image = (right_static + adj_static, right_ensemble + sweeps(adj_projected, coeffs))
     sums = global_sum(
         jnp.stack(
@@ -197,11 +206,11 @@
     norm_now = norm_next
 
     partial1 = forward_partial(direction[0], smoothed_direction)
-    own_image1, adj_static, adj_projected = observed_adjoint(partial1)
+    own_image1, model_obs = observed(partial1)
     curve = (
-        jnp.sum(direction[0] * (direction[0] + adj_static))
+        jnp.sum(direction[0] * direction[0])
         + jnp.sum(direction[1] * direction[1])
-        + jnp.sum(smoothed_direction * adj_projected)
+        + jnp.sum(quarter_gain * model_obs * model_obs)
     )
     step1 = norm_now / global_sum(curve)
     state = (state[0] + step1 * direction[0], state[1] + step1 * direction[1])

time: 205 us -> 188 us (0.917)
  blocking collectives: 33 us -> 19.5 us
  other arithmetic: 24.5 us -> 20 us
  matrix products: 14.9 us -> 11.3 us
  waiting for transfers between devices: 33.8 us -> 36.9 us
  starting transfers between devices: 67.4 us -> 70.1 us
    all_to_all x1 -> x0, blocking collectives: 10.9 us -> none  [observed_adjoint(): own_image = jnp.sum(lax.all_to_all(pieces, 'mem', 0, 0, tiled=True), axis=0)]
    all_to_all x1 -> x2, waiting for transfers between devices: 8.54 us -> 16.3 us  [observed(): own_image = jnp.sum(lax.all_to_all(pieces, 'mem', 0, 0, tiled=True), axis=0)]
    scatter-add x2 -> x1, other arithmetic: 7.64 us -> 4 us  [observed_adjoint(): jnp.zeros((rows_here * quarter, features), jnp.float32).at[quarter_index]]
    all_to_all x1 -> x2, starting transfers between devices: 4.14 us -> 7.74 us  [observed(): own_image = jnp.sum(lax.all_to_all(pieces, 'mem', 0, 0, tiled=True), axis=0)]
    all_to_all x2 -> x1, starting transfers between devices: 6.81 us -> 3.4 us  [observed_adjoint(): quarters = lax.all_to_all(spread, 'mem', 0, 0, tiled=True)]
    ppermute x6, waiting for transfers between devices: 6.89 us -> 3.62 us  [neighbours(): above.append(lax.ppermute(block, axis, backward))]
    all_to_all x1, blocking collectives: 22.1 us -> 19.5 us  [global_sum(): return jnp.sum(lax.all_to_all(spread, axes, 0, 0, tiled=True), axis=0)]
    all_to_all x1, starting transfers between devices: 9.81 us -> 12.3 us  [global_sum(): return jnp.sum(lax.all_to_all(spread, axes, 0, 0, tiled=True), axis=0)]
  transfers between devices with their start and end apart: 17 -> 17, of which waited for: 8 -> 7; matrix products, arithmetic and copies ran while one was open for 2% -> 2% of each run, Pallas kernels for 0% -> 0%
where the time goes in v5:
time: 188 us; the launch traced here: 187 us
  starting transfers between devices  70.1 us (37%)
  waiting for transfers between devices  36.9 us (20%)
  other arithmetic  20 us (11%)
  blocking collectives  19.5 us (10%)
  local copies, waits for them, and re-layouts  16.5 us (9%)
  between operations  12.8 us (7%)
  matrix products  11.3 us (6%)
    ppermute x6, starting transfers between devices, neighbours(): below.insert(0, lax.ppermute(block, axis, forward))  19.6 us
    all_to_all x1, blocking collectives, global_sum(): return jnp.sum(lax.all_to_all(spread, axes, 0, 0, tiled=True), axis=0)  19.5 us
    all_to_all x2, waiting for transfers between devices, observed(): own_image = jnp.sum(lax.all_to_all(pieces, 'mem', 0, 0, tiled=True), axis=0)  16.3 us
    ppermute x6, starting transfers between devices, neighbours(): above.append(lax.ppermute(block, axis, backward))  13.9 us
    all_to_all x1, starting transfers between devices, shards(): got = lax.all_to_all(packed, 'col', split_axis=0, concat_axis=0, tiled=True)  13.1 us
    all_to_all x1, starting transfers between devices, global_sum(): return jnp.sum(lax.all_to_all(spread, axes, 0, 0, tiled=True), axis=0)  12.3 us
    all_to_all x2, starting transfers between devices, observed(): own_image = jnp.sum(lax.all_to_all(pieces, 'mem', 0, 0, tiled=True), axis=0)  7.74 us
    all_to_all x1, waiting for transfers between devices, global_sum(): return jnp.sum(lax.all_to_all(spread, axes, 0, 0, tiled=True), axis=0)  6.65 us
  transfers between devices with their start and end apart: 17, of which 7 were waited for; matrix products, arithmetic and copies ran while one was open for 2% of the time, Pallas kernels for 0%

profile of v5, /device:TPU:1, one launch (start us, length us, event | category | flops | bytes accessed | tf_op | source)
XLA Modules:
  0.0 187.0 jit_solution(14127646638123105453)
XLA Ops:
  5.9 3.6 %gather_fusion.1 = s32[512]{0:T(512)S(1)} fusion(s32[256]{0:T(256)} %param.16, s32[1024]{0:T(1024)S(1)} %pad_clamp_fusion.1), kind=kCustom, calls=%fused_computation.1 | custom fusion | bytes 6144 | tf_op jit(solution)/shard_map/gather | solution.py:101
  12.0 13.1 %all-to-all-start = ((f32[64,9,128]{2,1,0:T(8,128)}), f32[64,9,128]{2,1,0:T(8,128)S(1)}, u32[]{:S(2)}, u32[]{:S(2)}) async-start(f32[64,9,128]{2,1,0:T(8,128)} %pad_maximum_fusion), calls=%async_computation | async-start | bytes 1048576 | tf_op jit(solution)/shard_map/all_to_all | solution.py:112
  25.2 2.4 %collective-permute-start.6 = (f32[4,256]{1,0:T(4,128)S(1)}, f32[4,256]{1,0:T(4,128)S(1)}, u32[]{:S(2)}, u32[]{:S(2)}) collective-permute-start(f32[4,256]{1,0:T(4,128)S(1)} %copy-done.10), channel_id=1, source_target_pairs={{1,0},{2,1},{3,2},{4,3},{5,4},{6,5},{7,6},{8,7},{9,8},{10,9},{11,1... | collective-permute-start | bytes 12296 | tf_op jit(solution)/shard_map/ppermute | solution.py:17
  27.5 3.2 %collective-permute-start.5 = (f32[4,256]{1,0:T(4,128)S(1)}, f32[4,256]{1,0:T(4,128)S(1)}, u32[]{:S(2)}, u32[]{:S(2)}) collective-permute-start(f32[4,256]{1,0:T(4,128)S(1)} %copy-done.10), channel_id=1, source_target_pairs={{0,1},{1,2},{2,3},{3,4},{4,5},{5,6},{6,7},{7,8},{8,9},{9,10},{10,1... | collective-permute-start | bytes 12296 | tf_op jit(solution)/shard_map/ppermute | solution.py:16
  30.7 3.3 %collective-permute-start.4 = (f32[4,256]{1,0:T(4,128)S(1)}, f32[4,256]{1,0:T(4,128)S(1)}, u32[]{:S(2)}, u32[]{:S(2)}) collective-permute-start(f32[4,256]{1,0:T(4,128)S(1)} %copy-done.10), channel_id=1, source_target_pairs={{0,2},{1,3},{2,4},{3,5},{4,6},{5,7},{6,8},{7,9},{8,10},{9,11},{10,... | collective-permute-start | bytes 12296 | tf_op jit(solution)/shard_map/ppermute | solution.py:16
  35.3 3.6 %collective-permute-done.6 = f32[4,256]{1,0:T(4,128)S(1)} collective-permute-done((f32[4,256]{1,0:T(4,128)S(1)}, f32[4,256]{1,0:T(4,128)S(1)}, u32[]{:S(2)}, u32[]{:S(2)}) %collective-permute-start.6) | collective-permute-done | bytes 4128 | tf_op jit(solution)/shard_map/ppermute | solution.py:17
  39.1 3.6 %all-to-all-done = f32[64,9,128]{2,1,0:T(8,128)S(1)} async-done(((f32[64,9,128]{2,1,0:T(8,128)}), f32[64,9,128]{2,1,0:T(8,128)S(1)}, u32[]{:S(2)}, u32[]{:S(2)}) %all-to-all-start) | async-done | bytes 294944 | tf_op jit(solution)/shard_map/all_to_all | solution.py:112
  44.2 3.5 %scatter_custom_fusion.1 = f32[1024,128]{1,0:T(8,128)S(1)} fusion(s32[512]{0:T(512)S(1)} %bitcast.131, f32[512,128]{1,0:T(8,128)S(1)} %fusion.11, f32[]{:T(128)} %constant.27.clone.1), kind=kCustom, calls=%fused_computation.62 | custom fusion | flops 65536 | bytes 524292 | tf_op jit(solution)/shard_map/scatter-add | solution.py:121
  47.8 2.4 %fusion.6 = f32[4,256,1,8]{3,2,1,0:T(1,128)} fusion(bf16[8,4,256,128]{3,2,1,0:T(8,128)(2,1)S(1)} %copy-done, bf16[4,256,128,1]{2,1,0,3:T(8,128)(2,1)S(1)} %convert_bitcast_fusion), kind=kOutput, calls=%fused_computation.13 | convolution fusion | flops 2097152 | bytes 2392064 | tf_op jit(solution)/shard_map/kyxf,yxf->kyx/dot_general | solution.py:132
  54.6 3.6 %collective-permute-start.1 = (f32[8,4,256]{2,1,0:T(4,128)S(1)}, f32[8,4,256]{2,1,0:T(4,128)S(1)}, u32[]{:S(2)}, u32[]{:S(2)}) collective-permute-start(f32[8,4,256]{2,1,0:T(4,128)S(1)} %bitcast.123), channel_id=1, source_target_pairs={{0,1},{1,2},{2,3},{3,4},{4,5},{5,6},{6,7},{7,8},{8,9},{9,10},{10,1... | collective-permute-start | bytes 98312 | tf_op jit(solution)/shard_map/ppermute | solution.py:16
  58.2 4.2 %collective-permute-start = (f32[8,4,256]{2,1,0:T(4,128)S(1)}, f32[8,4,256]{2,1,0:T(4,128)S(1)}, u32[]{:S(2)}, u32[]{:S(2)}) collective-permute-start(f32[8,4,256]{2,1,0:T(4,128)S(1)} %bitcast.124), channel_id=1, source_target_pairs={{0,2},{1,3},{2,4},{3,5},{4,6},{5,7},{6,8},{7,9},{8,10},{9,11},{10,... | collective-permute-start | bytes 98312 | tf_op jit(solution)/shard_map/ppermute | solution.py:16
  67.8 4.1 %all-to-all-start.1 = ((f32[4,4,64,128]{3,2,1,0:T(8,128)}), f32[4,4,64,128]{3,2,1,0:T(8,128)S(1)}, u32[]{:S(2)}, u32[]{:S(2)}) async-start(f32[4,4,64,128]{3,2,1,0:T(8,128)} %copy.34), calls=%async_computation.1 | async-start | bytes 1048576 | tf_op jit(solution)/shard_map/all_to_all | solution.py:157
  72.1 9.5 %all-to-all-done.1 = f32[4,4,64,128]{3,2,1,0:T(8,128)S(1)} async-done(((f32[4,4,64,128]{3,2,1,0:T(8,128)}), f32[4,4,64,128]{3,2,1,0:T(8,128)S(1)}, u32[]{:S(2)}, u32[]{:S(2)}) %all-to-all-start.1) | async-done | bytes 524320 | tf_op jit(solution)/shard_map/all_to_all | solution.py:157
  83.5 4.0 %scatter_custom_fusion.2 = f32[256,128]{1,0:T(8,128)S(1)} fusion(s32[512]{0:T(512)S(1)} %bitcast.129, f32[512,128]{1,0:T(8,128)S(1)} %fusion.229, f32[]{:T(128)} %constant.27.clone.1), kind=kCustom, calls=%fused_computation.270 | custom fusion | flops 65536 | bytes 131076 | tf_op jit(solution)/shard_map/scatter-add | solution.py:164
  88.3 3.4 %all-to-all-start.2 = ((bf16[4,4,64,128]{3,2,1,0:T(8,128)(2,1)}), bf16[4,4,64,128]{3,2,1,0:T(8,128)(2,1)S(1)}, u32[]{:S(2)}, u32[]{:S(2)}) async-start(bf16[4,4,64,128]{3,2,1,0:T(8,128)(2,1)} %broadcast_in_dim.56), calls=%async_computation.2 | async-start | bytes 524288 | tf_op jit(solution)/shard_map/all_to_all | solution.py:170
  91.7 6.5 %all-to-all-done.2 = bf16[4,4,64,128]{3,2,1,0:T(8,128)(2,1)S(1)} async-done(((bf16[4,4,64,128]{3,2,1,0:T(8,128)(2,1)}), bf16[4,4,64,128]{3,2,1,0:T(8,128)(2,1)S(1)}, u32[]{:S(2)}, u32[]{:S(2)}) %all-to-all-start.2) | async-done | bytes 262176 | tf_op jit(solution)/shard_map/all_to_all | solution.py:170
  100.1 3.0 %collective-permute-start.9 = (f32[8,4,256]{2,1,0:T(4,128)S(1)}, f32[8,4,256]{2,1,0:T(4,128)S(1)}, u32[]{:S(2)}, u32[]{:S(2)}) collective-permute-start(f32[8,4,256]{2,1,0:T(4,128)S(1)} %bitcast.116), channel_id=1, source_target_pairs={{1,0},{2,1},{3,2},{4,3},{5,4},{6,5},{7,6},{8,7},{9,8},{10,9},{11,1... | collective-permute-start | bytes 98312 | tf_op jit(solution)/shard_map/ppermute | solution.py:17
  103.1 3.2 %collective-permute-start.8 = (f32[8,4,256]{2,1,0:T(4,128)S(1)}, f32[8,4,256]{2,1,0:T(4,128)S(1)}, u32[]{:S(2)}, u32[]{:S(2)}) collective-permute-start(f32[8,4,256]{2,1,0:T(4,128)S(1)} %bitcast.117), channel_id=1, source_target_pairs={{0,1},{1,2},{2,3},{3,4},{4,5},{5,6},{6,7},{7,8},{8,9},{9,10},{10,1... | collective-permute-start | bytes 98312 | tf_op jit(solution)/shard_map/ppermute | solution.py:16
  113.2 12.3 %all-to-all-start.3 = ((f32[256,1,3]{2,1,0:T(1,128)}), f32[256,1,3]{2,1,0:T(1,128)S(1)}, u32[]{:S(2)}, u32[]{:S(2)}) async-start(f32[256,1,3]{2,1,0:T(1,128)} %broadcast_in_dim.57), calls=%async_computation.3 | async-start | bytes 262144 | tf_op jit(solution)/shard_map/all_to_all | solution.py:58
  125.5 4.1 %collective-permute-start.11 = (f32[8,4,256]{2,1,0:T(4,128)S(1)}, f32[8,4,256]{2,1,0:T(4,128)S(1)}, u32[]{:S(2)}, u32[]{:S(2)}) collective-permute-start(f32[8,4,256]{2,1,0:T(4,128)S(1)} %get-tuple-element.11), channel_id=1, source_target_pairs={{1,0},{2,1},{3,2},{4,3},{5,4},{6,5},{7,6},{8,7},{9,8},{10,9},{11,1... | collective-permute-start | bytes 98312 | tf_op jit(solution)/shard_map/ppermute | solution.py:17
  131.7 6.6 %all-to-all-done.3 = f32[256,1,3]{2,1,0:T(1,128)S(1)} async-done(((f32[256,1,3]{2,1,0:T(1,128)}), f32[256,1,3]{2,1,0:T(1,128)S(1)}, u32[]{:S(2)}, u32[]{:S(2)}) %all-to-all-start.3) | async-done | bytes 3104 | tf_op jit(solution)/shard_map/all_to_all | solution.py:58
  149.4 3.6 %all-to-all-start.4 = ((f32[4,4,64,128]{3,2,1,0:T(8,128)}), f32[4,4,64,128]{3,2,1,0:T(8,128)S(1)}, u32[]{:S(2)}, u32[]{:S(2)}) async-start(f32[4,4,64,128]{3,2,1,0:T(8,128)} %bitcast.96), calls=%async_computation.4 | async-start | bytes 1048576 | tf_op jit(solution)/shard_map/all_to_all | solution.py:157
  154.9 6.8 %all-to-all-done.4 = f32[4,4,64,128]{3,2,1,0:T(8,128)S(1)} async-done(((f32[4,4,64,128]{3,2,1,0:T(8,128)}), f32[4,4,64,128]{3,2,1,0:T(8,128)S(1)}, u32[]{:S(2)}, u32[]{:S(2)}) %all-to-all-start.4) | async-done | bytes 524320 | tf_op jit(solution)/shard_map/all_to_all | solution.py:157
  164.5 19.5 %all_to_all.32 = f32[256,1,1]{2,1,0:T(1,128)S(1)} all-to-all(f32[256,1,1]{2,1,0:T(1,128)S(1)} %broadcast_in_dim.58), channel_id=1, replica_groups=mesh['mem'=4,'col'=64] {'mem','col'}, dimensions={0} | all-to-all | bytes 2048 | tf_op jit(solution)/shard_map/all_to_all | solution.py:58
  (147 shorter events, 41.2 us)
Async XLA Ops:
  0.6 47.1 %copy-start = (bf16[8,4,256,128]{3,2,1,0:T(8,128)(2,1)S(1)}, bf16[8,4,256,128]{3,2,1,0:T(8,128)(2,1)}, u32[]{:S(2)}) copy-start(bf16[8,4,256,128]{3,2,1,0:T(8,128)(2,1)} %param.9) | copy-start | bytes 6291460
  9.8 15.4 %copy-start.10 = (f32[4,256]{1,0:T(4,128)S(1)}, f32[4,256]{1,0:T(4,128)}, u32[]{:S(2)}) copy-start(f32[4,256]{1,0:T(4,128)} %param.14) | copy-start | bytes 12292
  9.8 34.0 %copy-start.3 = (f32[128,128]{1,0:T(8,128)S(1)}, f32[128,128]{1,0:T(8,128)}, u32[]{:S(2)}) copy-start(f32[128,128]{1,0:T(8,128)} %param.11) | copy-start | bytes 196612
  9.8 34.0 %copy-start.13 = (f32[128]{0:T(128)S(1)}, f32[128]{0:T(128)}, u32[]{:S(2)}) copy-start(f32[128]{0:T(128)} %param.13) | copy-start | bytes 1540
  12.0 30.7 %all-to-all-start = ((f32[64,9,128]{2,1,0:T(8,128)}), f32[64,9,128]{2,1,0:T(8,128)S(1)}, u32[]{:S(2)}, u32[]{:S(2)}) async-start(f32[64,9,128]{2,1,0:T(8,128)} %pad_maximum_fusion), calls=%async_computation | async-start | bytes 1048576 | tf_op jit(solution)/shard_map/all_to_all | solution.py:112
  25.2 13.8 %collective-permute-start.6 = (f32[4,256]{1,0:T(4,128)S(1)}, f32[4,256]{1,0:T(4,128)S(1)}, u32[]{:S(2)}, u32[]{:S(2)}) collective-permute-start(f32[4,256]{1,0:T(4,128)S(1)} %copy-done.10), channel_id=1, source_target_pairs={{1,0},{2,1},{3,2},{4,3},{5,4},{6,5},{7,6},{8,7},{9,8},{10,9},{11,1... | collective-permute-start | bytes 12296 | tf_op jit(solution)/shard_map/ppermute | solution.py:17
  27.5 11.4 %collective-permute-start.5 = (f32[4,256]{1,0:T(4,128)S(1)}, f32[4,256]{1,0:T(4,128)S(1)}, u32[]{:S(2)}, u32[]{:S(2)}) collective-permute-start(f32[4,256]{1,0:T(4,128)S(1)} %copy-done.10), channel_id=1, source_target_pairs={{0,1},{1,2},{2,3},{3,4},{4,5},{5,6},{6,7},{7,8},{8,9},{9,10},{10,1... | collective-permute-start | bytes 12296 | tf_op jit(solution)/shard_map/ppermute | solution.py:16
  30.7 8.2 %collective-permute-start.4 = (f32[4,256]{1,0:T(4,128)S(1)}, f32[4,256]{1,0:T(4,128)S(1)}, u32[]{:S(2)}, u32[]{:S(2)}) collective-permute-start(f32[4,256]{1,0:T(4,128)S(1)} %copy-done.10), channel_id=1, source_target_pairs={{0,2},{1,3},{2,4},{3,5},{4,6},{5,7},{6,8},{7,9},{8,10},{9,11},{10,... | collective-permute-start | bytes 12296 | tf_op jit(solution)/shard_map/ppermute | solution.py:16
  34.0 4.9 %collective-permute-start.7 = (f32[4,256]{1,0:T(4,128)S(1)}, f32[4,256]{1,0:T(4,128)S(1)}, u32[]{:S(2)}, u32[]{:S(2)}) collective-permute-start(f32[4,256]{1,0:T(4,128)S(1)} %copy-done.10), channel_id=1, source_target_pairs={{2,0},{3,1},{4,2},{5,3},{6,4},{7,5},{8,6},{9,7},{10,8},{11,9},{12,... | collective-permute-start | bytes 12296 | tf_op jit(solution)/shard_map/ppermute | solution.py:17
  47.8 14.6 %copy-start.2 = (f32[128,128]{1,0:T(8,128)S(1)}, f32[128,128]{1,0:T(8,128)}, u32[]{:S(2)}) copy-start(f32[128,128]{1,0:T(8,128)} %param.10) | copy-start | bytes 196612
  51.3 11.6 %collective-permute-start.3 = (f32[8,4,256]{2,1,0:T(4,128)S(1)}, f32[8,4,256]{2,1,0:T(4,128)S(1)}, u32[]{:S(2)}, u32[]{:S(2)}) collective-permute-start(f32[8,4,256]{2,1,0:T(4,128)S(1)} %bitcast.121), channel_id=1, source_target_pairs={{2,0},{3,1},{4,2},{5,3},{6,4},{7,5},{8,6},{9,7},{10,8},{11,9},{12,... | collective-permute-start | bytes 98312 | tf_op jit(solution)/shard_map/ppermute | solution.py:17
  52.6 10.4 %collective-permute-start.2 = (f32[8,4,256]{2,1,0:T(4,128)S(1)}, f32[8,4,256]{2,1,0:T(4,128)S(1)}, u32[]{:S(2)}, u32[]{:S(2)}) collective-permute-start(f32[8,4,256]{2,1,0:T(4,128)S(1)} %bitcast.122), channel_id=1, source_target_pairs={{1,0},{2,1},{3,2},{4,3},{5,4},{6,5},{7,6},{8,7},{9,8},{10,9},{11,1... | collective-permute-start | bytes 98312 | tf_op jit(solution)/shard_map/ppermute | solution.py:17
  54.6 8.4 %collective-permute-start.1 = (f32[8,4,256]{2,1,0:T(4,128)S(1)}, f32[8,4,256]{2,1,0:T(4,128)S(1)}, u32[]{:S(2)}, u32[]{:S(2)}) collective-permute-start(f32[8,4,256]{2,1,0:T(4,128)S(1)} %bitcast.123), channel_id=1, source_target_pairs={{0,1},{1,2},{2,3},{3,4},{4,5},{5,6},{6,7},{7,8},{8,9},{9,10},{10,1... | collective-permute-start | bytes 98312 | tf_op jit(solution)/shard_map/ppermute | solution.py:16
  58.2 5.0 %collective-permute-start = (f32[8,4,256]{2,1,0:T(4,128)S(1)}, f32[8,4,256]{2,1,0:T(4,128)S(1)}, u32[]{:S(2)}, u32[]{:S(2)}) collective-permute-start(f32[8,4,256]{2,1,0:T(4,128)S(1)} %bitcast.124), channel_id=1, source_target_pairs={{0,2},{1,3},{2,4},{3,5},{4,6},{5,7},{6,8},{7,9},{8,10},{9,11},{10,... | collective-permute-start | bytes 98312 | tf_op jit(solution)/shard_map/ppermute | solution.py:16
  67.8 14.9 %copy-start.5 = (f32[512]{0:T(512)S(1)}, f32[512]{0:T(512)}, u32[]{:S(2)}) copy-start(f32[512]{0:T(512)} %copy-done.4) | copy-start | bytes 6148
  67.8 14.9 %copy-start.14 = (f32[128]{0:T(128)S(1)}, f32[128]{0:T(128)}, u32[]{:S(2)}) copy-start(f32[128]{0:T(128)} %param.13) | copy-start | bytes 1540
  67.8 13.8 %all-to-all-start.1 = ((f32[4,4,64,128]{3,2,1,0:T(8,128)}), f32[4,4,64,128]{3,2,1,0:T(8,128)S(1)}, u32[]{:S(2)}, u32[]{:S(2)}) async-start(f32[4,4,64,128]{3,2,1,0:T(8,128)} %copy.34), calls=%async_computation.1 | async-start | bytes 1048576 | tf_op jit(solution)/shard_map/all_to_all | solution.py:157
  88.3 9.9 %all-to-all-start.2 = ((bf16[4,4,64,128]{3,2,1,0:T(8,128)(2,1)}), bf16[4,4,64,128]{3,2,1,0:T(8,128)(2,1)S(1)}, u32[]{:S(2)}, u32[]{:S(2)}) async-start(bf16[4,4,64,128]{3,2,1,0:T(8,128)(2,1)} %broadcast_in_dim.56), calls=%async_computation.2 | async-start | bytes 524288 | tf_op jit(solution)/shard_map/all_to_all | solution.py:170
  100.1 7.1 %collective-permute-start.9 = (f32[8,4,256]{2,1,0:T(4,128)S(1)}, f32[8,4,256]{2,1,0:T(4,128)S(1)}, u32[]{:S(2)}, u32[]{:S(2)}) collective-permute-start(f32[8,4,256]{2,1,0:T(4,128)S(1)} %bitcast.116), channel_id=1, source_target_pairs={{1,0},{2,1},{3,2},{4,3},{5,4},{6,5},{7,6},{8,7},{9,8},{10,9},{11,1... | collective-permute-start | bytes 98312 | tf_op jit(solution)/shard_map/ppermute | solution.py:17
  103.1 4.2 %collective-permute-start.8 = (f32[8,4,256]{2,1,0:T(4,128)S(1)}, f32[8,4,256]{2,1,0:T(4,128)S(1)}, u32[]{:S(2)}, u32[]{:S(2)}) collective-permute-start(f32[8,4,256]{2,1,0:T(4,128)S(1)} %bitcast.117), channel_id=1, source_target_pairs={{0,1},{1,2},{2,3},{3,4},{4,5},{5,6},{6,7},{7,8},{8,9},{9,10},{10,1... | collective-permute-start | bytes 98312 | tf_op jit(solution)/shard_map/ppermute | solution.py:16
  113.2 25.2 %all-to-all-start.3 = ((f32[256,1,3]{2,1,0:T(1,128)}), f32[256,1,3]{2,1,0:T(1,128)S(1)}, u32[]{:S(2)}, u32[]{:S(2)}) async-start(f32[256,1,3]{2,1,0:T(1,128)} %broadcast_in_dim.57), calls=%async_computation.3 | async-start | bytes 262144 | tf_op jit(solution)/shard_map/all_to_all | solution.py:58
  125.5 18.6 %collective-permute-start.11 = (f32[8,4,256]{2,1,0:T(4,128)S(1)}, f32[8,4,256]{2,1,0:T(4,128)S(1)}, u32[]{:S(2)}, u32[]{:S(2)}) collective-permute-start(f32[8,4,256]{2,1,0:T(4,128)S(1)} %get-tuple-element.11), channel_id=1, source_target_pairs={{1,0},{2,1},{3,2},{4,3},{5,4},{6,5},{7,6},{8,7},{9,8},{10,9},{11,1... | collective-permute-start | bytes 98312 | tf_op jit(solution)/shard_map/ppermute | solution.py:17
  129.6 14.5 %collective-permute-start.10 = (f32[8,4,256]{2,1,0:T(4,128)S(1)}, f32[8,4,256]{2,1,0:T(4,128)S(1)}, u32[]{:S(2)}, u32[]{:S(2)}) collective-permute-start(f32[8,4,256]{2,1,0:T(4,128)S(1)} %get-tuple-element.11), channel_id=1, source_target_pairs={{0,1},{1,2},{2,3},{3,4},{4,5},{5,6},{6,7},{7,8},{8,9},{9,10},{10,1... | collective-permute-start | bytes 98312 | tf_op jit(solution)/shard_map/ppermute | solution.py:16
  149.4 12.3 %all-to-all-start.4 = ((f32[4,4,64,128]{3,2,1,0:T(8,128)}), f32[4,4,64,128]{3,2,1,0:T(8,128)S(1)}, u32[]{:S(2)}, u32[]{:S(2)}) async-start(f32[4,4,64,128]{3,2,1,0:T(8,128)} %bitcast.96), calls=%async_computation.4 | async-start | bytes 1048576 | tf_op jit(solution)/shard_map/all_to_all | solution.py:157
  (9 other events, 97.7 us)

commit v6 on v5

--- a/solution.py
+++ b/solution.py
@@ -195,6 +195,18 @@
         )
     )
     smoothed_image = sweeps(image[1], coeffs)
+    ensemble_parts = jnp.stack(
+        [
+            jnp.einsum(
+                "kyxf,kyx->yxf", perturbations, field, preferred_element_type=jnp.float32
+            )
+            for field in (smoothed_right, smoothed_image)
+        ]
+    )
+    pieces = jnp.moveaxis(
+        ensemble_parts.reshape(2, rows_here, parts, quarter, features), 2, 0
+    )
+    own_right, own_image = jnp.sum(lax.all_to_all(pieces, "mem", 0, 0, tiled=True), axis=0)
     norm_now, curve, image_norm = sums[0], sums[1], sums[2]
     step0 = norm_now / curve
     state = (step0 * direction[0], step0 * direction[1])
@@ -202,11 +214,16 @@
     norm_next = norm_now - 2.0 * step0 * curve + step0 * step0 * image_norm
     ratio = norm_next / norm_now
     direction = (residual[0] + ratio * direction[0], residual[1] + ratio * direction[1])
-    smoothed_direction = (smoothed_right - step0 * smoothed_image) + ratio * smoothed_right
     norm_now = norm_next
 
-    partial1 = forward_partial(direction[0], smoothed_direction)
-    own_image1, model_obs = observed(partial1)
+    forward_static = jnp.dot(
+        direction[0].reshape(rows_here * quarter, features),
+        static_root,
+        precision=lax.Precision.HIGHEST,
+    ).reshape(rows_here, quarter, features)
+    own_image1 = ((own_right - step0 * own_image) + ratio * own_right) + forward_static
+    gathered = own_image1.reshape(rows_here * quarter, features)[quarter_index]
+    model_obs = jnp.dot(gathered, obs_jacobian, precision=lax.Precision.HIGHEST)
     curve = (
         jnp.sum(direction[0] * direction[0])
         + jnp.sum(direction[1] * direction[1])

time: 188 us -> 191 us (1.016)
  matrix products: 11.3 us -> 16.6 us
  starting transfers between devices: 70.1 us -> 65.8 us
  other arithmetic: 20 us -> 23.2 us
  waiting for transfers between devices: 36.9 us -> 34.5 us
    all_to_all x2 -> x1, waiting for transfers between devices: 16.3 us -> 7.55 us  [observed(): own_image = jnp.sum(lax.all_to_all(pieces, 'mem', 0, 0, tiled=True), axis=0)]
    dot_general x0 -> x4, matrix products: none -> 7.56 us  [the longest x2 5.27 us: shards(): jnp.einsum('kyxf,kyx->yxf', perturbations, field, preferred_element_type=...]
    ppermute x6, waiting for transfers between devices: 3.62 us -> 8.85 us  [neighbours(): above.append(lax.ppermute(block, axis, backward))]
    all_to_all x1, waiting for transfers between devices: 6.47 us -> 1.93 us  [observed_adjoint(): quarters = lax.all_to_all(spread, 'mem', 0, 0, tiled=True)]
    all_to_all x2 -> x1, starting transfers between devices: 7.74 us -> 3.99 us  [observed(): own_image = jnp.sum(lax.all_to_all(pieces, 'mem', 0, 0, tiled=True), axis=0)]
    all_to_all x0 -> x1, waiting for transfers between devices: none -> 3.65 us  [shards(): lax.all_to_all(pieces, 'mem', 0, 0, tiled=True)]
    all_to_all x0 -> x1, starting transfers between devices: none -> 3.51 us  [shards(): lax.all_to_all(pieces, 'mem', 0, 0, tiled=True)]
    ppermute x6, starting transfers between devices: 13.9 us -> 10.8 us  [neighbours(): above.append(lax.ppermute(block, axis, backward))]
  transfers between devices with their start and end apart: 17 -> 17, of which waited for: 7 -> 9; matrix products, arithmetic and copies ran while one was open for 2% -> 9% of each run, Pallas kernels for 0% -> 0%
where the time goes in v6:
time: 191 us; the launch traced here: 190 us
  starting transfers between devices  65.8 us (34%)
  waiting for transfers between devices  34.5 us (18%)
  other arithmetic  23.2 us (12%)
  blocking collectives  19.5 us (10%)
  local copies, waits for them, and re-layouts  17.7 us (9%)
  matrix products  16.6 us (9%)
  between operations  12.4 us (6%)
    ppermute x6, starting transfers between devices, neighbours(): below.insert(0, lax.ppermute(block, axis, forward))  20.4 us
    all_to_all x1, blocking collectives, global_sum(): return jnp.sum(lax.all_to_all(spread, axes, 0, 0, tiled=True), axis=0)  19.5 us
    all_to_all x1, starting transfers between devices, shards(): got = lax.all_to_all(packed, 'col', split_axis=0, concat_axis=0, tiled=True)  13.1 us
    ppermute x6, starting transfers between devices, neighbours(): above.append(lax.ppermute(block, axis, backward))  10.8 us
    all_to_all x1, starting transfers between devices, global_sum(): return jnp.sum(lax.all_to_all(spread, axes, 0, 0, tiled=True), axis=0)  10.6 us
    all_to_all x1, waiting for transfers between devices, global_sum(): return jnp.sum(lax.all_to_all(spread, axes, 0, 0, tiled=True), axis=0)  8.9 us
    ppermute x6, waiting for transfers between devices, neighbours(): above.append(lax.ppermute(block, axis, backward))  8.85 us
    all_to_all x1, waiting for transfers between devices, observed(): own_image = jnp.sum(lax.all_to_all(pieces, 'mem', 0, 0, tiled=True), axis=0)  7.55 us
  transfers between devices with their start and end apart: 17, of which 9 were waited for; matrix products, arithmetic and copies ran while one was open for 9% of the time, Pallas kernels for 0%

profile of v6, /device:TPU:1, one launch (start us, length us, event | category | flops | bytes accessed | tf_op | source)
XLA Modules:
  0.0 189.7 jit_solution(14284301001352906240)
XLA Ops:
  5.9 3.6 %gather_fusion.1 = s32[512]{0:T(512)S(1)} fusion(s32[256]{0:T(256)} %param.16, s32[1024]{0:T(1024)S(1)} %pad_clamp_fusion.1), kind=kCustom, calls=%fused_computation.1 | custom fusion | bytes 6144 | tf_op jit(solution)/shard_map/gather | solution.py:101
  12.0 13.1 %all-to-all-start = ((f32[64,9,128]{2,1,0:T(8,128)}), f32[64,9,128]{2,1,0:T(8,128)S(1)}, u32[]{:S(2)}, u32[]{:S(2)}) async-start(f32[64,9,128]{2,1,0:T(8,128)} %pad_maximum_fusion), calls=%async_computation | async-start | bytes 1048576 | tf_op jit(solution)/shard_map/all_to_all | solution.py:112
  25.2 3.3 %collective-permute-start.4 = (f32[4,256]{1,0:T(4,128)S(1)}, f32[4,256]{1,0:T(4,128)S(1)}, u32[]{:S(2)}, u32[]{:S(2)}) collective-permute-start(f32[4,256]{1,0:T(4,128)S(1)} %copy-done.10), channel_id=1, source_target_pairs={{0,2},{1,3},{2,4},{3,5},{4,6},{5,7},{6,8},{7,9},{8,10},{9,11},{10,... | collective-permute-start | bytes 12296 | tf_op jit(solution)/shard_map/ppermute | solution.py:16
  28.4 3.7 %collective-permute-start.5 = (f32[4,256]{1,0:T(4,128)S(1)}, f32[4,256]{1,0:T(4,128)S(1)}, u32[]{:S(2)}, u32[]{:S(2)}) collective-permute-start(f32[4,256]{1,0:T(4,128)S(1)} %copy-done.10), channel_id=1, source_target_pairs={{0,1},{1,2},{2,3},{3,4},{4,5},{5,6},{6,7},{7,8},{8,9},{9,10},{10,1... | collective-permute-start | bytes 12296 | tf_op jit(solution)/shard_map/ppermute | solution.py:16
  35.3 3.6 %collective-permute-done.6 = f32[4,256]{1,0:T(4,128)S(1)} collective-permute-done((f32[4,256]{1,0:T(4,128)S(1)}, f32[4,256]{1,0:T(4,128)S(1)}, u32[]{:S(2)}, u32[]{:S(2)}) %collective-permute-start.6) | collective-permute-done | bytes 4128 | tf_op jit(solution)/shard_map/ppermute | solution.py:17
  39.1 3.6 %all-to-all-done = f32[64,9,128]{2,1,0:T(8,128)S(1)} async-done(((f32[64,9,128]{2,1,0:T(8,128)}), f32[64,9,128]{2,1,0:T(8,128)S(1)}, u32[]{:S(2)}, u32[]{:S(2)}) %all-to-all-start) | async-done | bytes 294944 | tf_op jit(solution)/shard_map/all_to_all | solution.py:112
  43.7 3.1 %scatter_custom_fusion.1 = f32[1024,128]{1,0:T(8,128)S(1)} fusion(s32[512]{0:T(512)S(1)} %bitcast.143, f32[512,128]{1,0:T(8,128)S(1)} %fusion.12, f32[]{:T(128)} %constant.27.clone.1), kind=kCustom, calls=%fused_computation.63 | custom fusion | flops 65536 | bytes 524292 | tf_op jit(solution)/shard_map/scatter-add | solution.py:121
  46.8 2.4 %fusion.8 = f32[4,256,1,8]{3,2,1,0:T(1,128)} fusion(bf16[8,4,256,128]{3,2,1,0:T(8,128)(2,1)S(1)} %copy-done, bf16[4,256,128,1]{2,1,0,3:T(8,128)(2,1)S(1)} %convert_bitcast_fusion), kind=kOutput, calls=%fused_computation.17 | convolution fusion | flops 2097152 | bytes 2392064 | tf_op jit(solution)/shard_map/kyxf,yxf->kyx/dot_general | solution.py:132
  50.3 2.6 %collective-permute-start = (f32[8,4,256]{2,1,0:T(4,128)S(1)}, f32[8,4,256]{2,1,0:T(4,128)S(1)}, u32[]{:S(2)}, u32[]{:S(2)}) collective-permute-start(f32[8,4,256]{2,1,0:T(4,128)S(1)} %bitcast.133), channel_id=1, source_target_pairs={{0,2},{1,3},{2,4},{3,5},{4,6},{5,7},{6,8},{7,9},{8,10},{9,11},{10,... | collective-permute-start | bytes 98312 | tf_op jit(solution)/shard_map/ppermute | solution.py:16
  53.0 3.3 %collective-permute-start.1 = (f32[8,4,256]{2,1,0:T(4,128)S(1)}, f32[8,4,256]{2,1,0:T(4,128)S(1)}, u32[]{:S(2)}, u32[]{:S(2)}) collective-permute-start(f32[8,4,256]{2,1,0:T(4,128)S(1)} %bitcast.134), channel_id=1, source_target_pairs={{0,1},{1,2},{2,3},{3,4},{4,5},{5,6},{6,7},{7,8},{8,9},{9,10},{10,1... | collective-permute-start | bytes 98312 | tf_op jit(solution)/shard_map/ppermute | solution.py:16
  61.5 2.4 %collective-permute-done.3 = f32[8,4,256]{2,1,0:T(4,128)S(1)} collective-permute-done((f32[8,4,256]{2,1,0:T(4,128)S(1)}, f32[8,4,256]{2,1,0:T(4,128)S(1)}, u32[]{:S(2)}, u32[]{:S(2)}) %collective-permute-start.3) | collective-permute-done | bytes 32800 | tf_op jit(solution)/shard_map/ppermute | solution.py:17
  68.5 4.0 %all-to-all-start.1 = ((f32[4,4,64,128]{3,2,1,0:T(8,128)}), f32[4,4,64,128]{3,2,1,0:T(8,128)S(1)}, u32[]{:S(2)}, u32[]{:S(2)}) async-start(f32[4,4,64,128]{3,2,1,0:T(8,128)} %copy.33), calls=%async_computation.1 | async-start | bytes 1048576 | tf_op jit(solution)/shard_map/all_to_all | solution.py:157
  73.8 7.6 %all-to-all-done.1 = f32[4,4,64,128]{3,2,1,0:T(8,128)S(1)} async-done(((f32[4,4,64,128]{3,2,1,0:T(8,128)}), f32[4,4,64,128]{3,2,1,0:T(8,128)S(1)}, u32[]{:S(2)}, u32[]{:S(2)}) %all-to-all-start.1) | async-done | bytes 524320 | tf_op jit(solution)/shard_map/all_to_all | solution.py:157
  83.2 3.7 %scatter_custom_fusion.2 = f32[256,128]{1,0:T(8,128)S(1)} fusion(s32[512]{0:T(512)S(1)} %bitcast.141, f32[512,128]{1,0:T(8,128)S(1)} %fusion.228, f32[]{:T(128)} %constant.27.clone.1), kind=kCustom, calls=%fused_computation.275 | custom fusion | flops 65536 | bytes 131076 | tf_op jit(solution)/shard_map/scatter-add | solution.py:164
  87.7 3.4 %all-to-all-start.2 = ((bf16[4,4,64,128]{3,2,1,0:T(8,128)(2,1)}), bf16[4,4,64,128]{3,2,1,0:T(8,128)(2,1)S(1)}, u32[]{:S(2)}, u32[]{:S(2)}) async-start(bf16[4,4,64,128]{3,2,1,0:T(8,128)(2,1)} %broadcast_in_dim.56), calls=%async_computation.2 | async-start | bytes 524288 | tf_op jit(solution)/shard_map/all_to_all | solution.py:170
  91.1 3.6 %fusion.2 = f32[4,256,1,128]{3,2,1,0:T(1,128)} fusion(bf16[8,4,256,1]{0,3,2,1:T(2,128)(2,1)} %copy.45, bf16[8,4,256,128]{3,2,1,0:T(8,128)(2,1)S(1)} %copy-done), kind=kOutput, calls=%fused_computation.11 | convolution fusion | flops 2097152 | bytes 2637824 | tf_op jit(solution)/shard_map/kyxf,kyx->yxf/dot_general | solution.py:200
  98.5 5.6 %collective-permute-start.8 = (f32[8,4,256]{2,1,0:T(4,128)S(1)}, f32[8,4,256]{2,1,0:T(4,128)S(1)}, u32[]{:S(2)}, u32[]{:S(2)}) collective-permute-start(f32[8,4,256]{2,1,0:T(4,128)S(1)} %bitcast.128), channel_id=1, source_target_pairs={{0,1},{1,2},{2,3},{3,4},{4,5},{5,6},{6,7},{7,8},{8,9},{9,10},{10,1... | collective-permute-start | bytes 98312 | tf_op jit(solution)/shard_map/ppermute | solution.py:16
  112.6 2.3 %collective-permute-start.11 = (f32[8,4,256]{2,1,0:T(4,128)S(1)}, f32[8,4,256]{2,1,0:T(4,128)S(1)}, u32[]{:S(2)}, u32[]{:S(2)}) collective-permute-start(f32[8,4,256]{2,1,0:T(4,128)S(1)} %get-tuple-element.11), channel_id=1, source_target_pairs={{1,0},{2,1},{3,2},{4,3},{5,4},{6,5},{7,6},{8,7},{9,8},{10,9},{11,1... | collective-permute-start | bytes 98312 | tf_op jit(solution)/shard_map/ppermute | solution.py:17
  119.5 10.6 %all-to-all-start.3 = ((f32[256,1,3]{2,1,0:T(1,128)}), f32[256,1,3]{2,1,0:T(1,128)S(1)}, u32[]{:S(2)}, u32[]{:S(2)}) async-start(f32[256,1,3]{2,1,0:T(1,128)} %broadcast_in_dim.57), calls=%async_computation.3 | async-start | bytes 262144 | tf_op jit(solution)/shard_map/all_to_all | solution.py:58
  134.1 8.9 %all-to-all-done.3 = f32[256,1,3]{2,1,0:T(1,128)S(1)} async-done(((f32[256,1,3]{2,1,0:T(1,128)}), f32[256,1,3]{2,1,0:T(1,128)S(1)}, u32[]{:S(2)}, u32[]{:S(2)}) %all-to-all-start.3) | async-done | bytes 3104 | tf_op jit(solution)/shard_map/all_to_all | solution.py:58
  143.7 3.5 %all-to-all-start.4 = ((f32[4,2,4,64,128]{4,3,2,1,0:T(8,128)}), f32[4,2,4,64,128]{4,3,2,1,0:T(8,128)S(1)}, u32[]{:S(2)}, u32[]{:S(2)}) async-start(f32[4,2,4,64,128]{4,3,2,1,0:T(8,128)} %copy.36), calls=%async_computation.4 | async-start | bytes 2097152 | tf_op jit(solution)/shard_map/all_to_all | solution.py:209
  154.4 2.3 %multiply_reduce_fusion = (f32[]{:T(128)}, f32[256,128]{1,0:T(8,128)}) fusion(f32[256,128]{1,0:T(8,128)S(1)} %fusion.226, f32[]{:T(128)S(6)} %div.26, f32[256,128]{1,0:T(8,128)} %get-tuple-element.12, f32[]{:T(128)S(6)} %div.25), kind=kLoop, calls=%fused_computation.261 | loop fusion | flops 196607 | bytes 393228 | tf_op jit(solution)/shard_map/reduce_sum | solution.py:228
  157.9 3.6 %all-to-all-done.4 = f32[4,2,4,64,128]{4,3,2,1,0:T(8,128)S(1)} async-done(((f32[4,2,4,64,128]{4,3,2,1,0:T(8,128)}), f32[4,2,4,64,128]{4,3,2,1,0:T(8,128)S(1)}, u32[]{:S(2)}, u32[]{:S(2)}) %all-to-all-start.4) | async-done | bytes 1048608 | tf_op jit(solution)/shard_map/all_to_all | solution.py:209
  166.4 19.5 %all_to_all.32 = f32[256,1,1]{2,1,0:T(1,128)S(1)} all-to-all(f32[256,1,1]{2,1,0:T(1,128)S(1)} %broadcast_in_dim.58), channel_id=1, replica_groups=mesh['mem'=4,'col'=64] {'mem','col'}, dimensions={0} | all-to-all | bytes 2048 | tf_op jit(solution)/shard_map/all_to_all | solution.py:58
  (144 shorter events, 54.2 us)
Async XLA Ops:
  0.6 46.1 %copy-start = (bf16[8,4,256,128]{3,2,1,0:T(8,128)(2,1)S(1)}, bf16[8,4,256,128]{3,2,1,0:T(8,128)(2,1)}, u32[]{:S(2)}) copy-start(bf16[8,4,256,128]{3,2,1,0:T(8,128)(2,1)} %param.9) | copy-start | bytes 6291460
  9.8 33.4 %copy-start.4 = (f32[128,128]{1,0:T(8,128)S(1)}, f32[128,128]{1,0:T(8,128)}, u32[]{:S(2)}) copy-start(f32[128,128]{1,0:T(8,128)} %param.11) | copy-start | bytes 196612
  9.8 33.4 %copy-start.11 = (f32[128]{0:T(128)S(1)}, f32[128]{0:T(128)}, u32[]{:S(2)}) copy-start(f32[128]{0:T(128)} %param.13) | copy-start | bytes 1540
  12.0 30.7 %all-to-all-start = ((f32[64,9,128]{2,1,0:T(8,128)}), f32[64,9,128]{2,1,0:T(8,128)S(1)}, u32[]{:S(2)}, u32[]{:S(2)}) async-start(f32[64,9,128]{2,1,0:T(8,128)} %pad_maximum_fusion), calls=%async_computation | async-start | bytes 1048576 | tf_op jit(solution)/shard_map/all_to_all | solution.py:112
  25.2 10.2 %collective-permute-start.4 = (f32[4,256]{1,0:T(4,128)S(1)}, f32[4,256]{1,0:T(4,128)S(1)}, u32[]{:S(2)}, u32[]{:S(2)}) collective-permute-start(f32[4,256]{1,0:T(4,128)S(1)} %copy-done.10), channel_id=1, source_target_pairs={{0,2},{1,3},{2,4},{3,5},{4,6},{5,7},{6,8},{7,9},{8,10},{9,11},{10,... | collective-permute-start | bytes 12296 | tf_op jit(solution)/shard_map/ppermute | solution.py:16
  28.4 6.9 %collective-permute-start.5 = (f32[4,256]{1,0:T(4,128)S(1)}, f32[4,256]{1,0:T(4,128)S(1)}, u32[]{:S(2)}, u32[]{:S(2)}) collective-permute-start(f32[4,256]{1,0:T(4,128)S(1)} %copy-done.10), channel_id=1, source_target_pairs={{0,1},{1,2},{2,3},{3,4},{4,5},{5,6},{6,7},{7,8},{8,9},{9,10},{10,1... | collective-permute-start | bytes 12296 | tf_op jit(solution)/shard_map/ppermute | solution.py:16
  32.1 6.8 %collective-permute-start.6 = (f32[4,256]{1,0:T(4,128)S(1)}, f32[4,256]{1,0:T(4,128)S(1)}, u32[]{:S(2)}, u32[]{:S(2)}) collective-permute-start(f32[4,256]{1,0:T(4,128)S(1)} %copy-done.10), channel_id=1, source_target_pairs={{1,0},{2,1},{3,2},{4,3},{5,4},{6,5},{7,6},{8,7},{9,8},{10,9},{11,1... | collective-permute-start | bytes 12296 | tf_op jit(solution)/shard_map/ppermute | solution.py:17
  34.0 4.9 %collective-permute-start.7 = (f32[4,256]{1,0:T(4,128)S(1)}, f32[4,256]{1,0:T(4,128)S(1)}, u32[]{:S(2)}, u32[]{:S(2)}) collective-permute-start(f32[4,256]{1,0:T(4,128)S(1)} %copy-done.10), channel_id=1, source_target_pairs={{2,0},{3,1},{4,2},{5,3},{6,4},{7,5},{8,6},{9,7},{10,8},{11,9},{12,... | collective-permute-start | bytes 12296 | tf_op jit(solution)/shard_map/ppermute | solution.py:17
  50.3 9.9 %collective-permute-start = (f32[8,4,256]{2,1,0:T(4,128)S(1)}, f32[8,4,256]{2,1,0:T(4,128)S(1)}, u32[]{:S(2)}, u32[]{:S(2)}) collective-permute-start(f32[8,4,256]{2,1,0:T(4,128)S(1)} %bitcast.133), channel_id=1, source_target_pairs={{0,2},{1,3},{2,4},{3,5},{4,6},{5,7},{6,8},{7,9},{8,10},{9,11},{10,... | collective-permute-start | bytes 98312 | tf_op jit(solution)/shard_map/ppermute | solution.py:16
  53.0 7.3 %collective-permute-start.1 = (f32[8,4,256]{2,1,0:T(4,128)S(1)}, f32[8,4,256]{2,1,0:T(4,128)S(1)}, u32[]{:S(2)}, u32[]{:S(2)}) collective-permute-start(f32[8,4,256]{2,1,0:T(4,128)S(1)} %bitcast.134), channel_id=1, source_target_pairs={{0,1},{1,2},{2,3},{3,4},{4,5},{5,6},{6,7},{7,8},{8,9},{9,10},{10,1... | collective-permute-start | bytes 98312 | tf_op jit(solution)/shard_map/ppermute | solution.py:16
  56.3 5.2 %collective-permute-start.2 = (f32[8,4,256]{2,1,0:T(4,128)S(1)}, f32[8,4,256]{2,1,0:T(4,128)S(1)}, u32[]{:S(2)}, u32[]{:S(2)}) collective-permute-start(f32[8,4,256]{2,1,0:T(4,128)S(1)} %bitcast.135), channel_id=1, source_target_pairs={{1,0},{2,1},{3,2},{4,3},{5,4},{6,5},{7,6},{8,7},{9,8},{10,9},{11,1... | collective-permute-start | bytes 98312 | tf_op jit(solution)/shard_map/ppermute | solution.py:17
  58.2 5.7 %collective-permute-start.3 = (f32[8,4,256]{2,1,0:T(4,128)S(1)}, f32[8,4,256]{2,1,0:T(4,128)S(1)}, u32[]{:S(2)}, u32[]{:S(2)}) collective-permute-start(f32[8,4,256]{2,1,0:T(4,128)S(1)} %bitcast.136), channel_id=1, source_target_pairs={{2,0},{3,1},{4,2},{5,3},{6,4},{7,5},{8,6},{9,7},{10,8},{11,9},{12,... | collective-permute-start | bytes 98312 | tf_op jit(solution)/shard_map/ppermute | solution.py:17
  64.8 45.1 %copy-start.2 = (f32[8,20,256]{2,1,0:T(8,128)}, f32[8,20,256]{2,1,0:T(8,128)S(1)}, u32[]{:S(2)}) copy-start(f32[8,20,256]{2,1,0:T(8,128)S(1)} %fusion.57) | copy-start | bytes 491524
  68.5 12.8 %all-to-all-start.1 = ((f32[4,4,64,128]{3,2,1,0:T(8,128)}), f32[4,4,64,128]{3,2,1,0:T(8,128)S(1)}, u32[]{:S(2)}, u32[]{:S(2)}) async-start(f32[4,4,64,128]{3,2,1,0:T(8,128)} %copy.33), calls=%async_computation.1 | async-start | bytes 1048576 | tf_op jit(solution)/shard_map/all_to_all | solution.py:157
  87.7 8.9 %all-to-all-start.2 = ((bf16[4,4,64,128]{3,2,1,0:T(8,128)(2,1)}), bf16[4,4,64,128]{3,2,1,0:T(8,128)(2,1)S(1)}, u32[]{:S(2)}, u32[]{:S(2)}) async-start(bf16[4,4,64,128]{3,2,1,0:T(8,128)(2,1)} %broadcast_in_dim.56), calls=%async_computation.2 | async-start | bytes 524288 | tf_op jit(solution)/shard_map/all_to_all | solution.py:170
  98.5 9.2 %collective-permute-start.8 = (f32[8,4,256]{2,1,0:T(4,128)S(1)}, f32[8,4,256]{2,1,0:T(4,128)S(1)}, u32[]{:S(2)}, u32[]{:S(2)}) collective-permute-start(f32[8,4,256]{2,1,0:T(4,128)S(1)} %bitcast.128), channel_id=1, source_target_pairs={{0,1},{1,2},{2,3},{3,4},{4,5},{5,6},{6,7},{7,8},{8,9},{9,10},{10,1... | collective-permute-start | bytes 98312 | tf_op jit(solution)/shard_map/ppermute | solution.py:16
  104.0 5.2 %collective-permute-start.9 = (f32[8,4,256]{2,1,0:T(4,128)S(1)}, f32[8,4,256]{2,1,0:T(4,128)S(1)}, u32[]{:S(2)}, u32[]{:S(2)}) collective-permute-start(f32[8,4,256]{2,1,0:T(4,128)S(1)} %bitcast.129), channel_id=1, source_target_pairs={{1,0},{2,1},{3,2},{4,3},{5,4},{6,5},{7,6},{8,7},{9,8},{10,9},{11,1... | collective-permute-start | bytes 98312 | tf_op jit(solution)/shard_map/ppermute | solution.py:17
  110.6 22.3 %copy-start.5 = (f32[8,4,256]{2,1,0:T(4,128)}, f32[8,4,256]{2,1,0:T(4,128)S(1)}, u32[]{:S(2)}) copy-start(f32[8,4,256]{2,1,0:T(4,128)S(1)} %get-tuple-element.11) | copy-start | bytes 98308
  110.6 19.5 %collective-permute-start.10 = (f32[8,4,256]{2,1,0:T(4,128)S(1)}, f32[8,4,256]{2,1,0:T(4,128)S(1)}, u32[]{:S(2)}, u32[]{:S(2)}) collective-permute-start(f32[8,4,256]{2,1,0:T(4,128)S(1)} %get-tuple-element.11), channel_id=1, source_target_pairs={{0,1},{1,2},{2,3},{3,4},{4,5},{5,6},{6,7},{7,8},{8,9},{9,10},{10,1... | collective-permute-start | bytes 98312 | tf_op jit(solution)/shard_map/ppermute | solution.py:16
  112.6 17.5 %collective-permute-start.11 = (f32[8,4,256]{2,1,0:T(4,128)S(1)}, f32[8,4,256]{2,1,0:T(4,128)S(1)}, u32[]{:S(2)}, u32[]{:S(2)}) collective-permute-start(f32[8,4,256]{2,1,0:T(4,128)S(1)} %get-tuple-element.11), channel_id=1, source_target_pairs={{1,0},{2,1},{3,2},{4,3},{5,4},{6,5},{7,6},{8,7},{9,8},{10,9},{11,1... | collective-permute-start | bytes 98312 | tf_op jit(solution)/shard_map/ppermute | solution.py:17
  119.5 23.5 %all-to-all-start.3 = ((f32[256,1,3]{2,1,0:T(1,128)}), f32[256,1,3]{2,1,0:T(1,128)S(1)}, u32[]{:S(2)}, u32[]{:S(2)}) async-start(f32[256,1,3]{2,1,0:T(1,128)} %broadcast_in_dim.57), calls=%async_computation.3 | async-start | bytes 262144 | tf_op jit(solution)/shard_map/all_to_all | solution.py:58
  143.7 17.8 %all-to-all-start.4 = ((f32[4,2,4,64,128]{4,3,2,1,0:T(8,128)}), f32[4,2,4,64,128]{4,3,2,1,0:T(8,128)S(1)}, u32[]{:S(2)}, u32[]{:S(2)}) async-start(f32[4,2,4,64,128]{4,3,2,1,0:T(8,128)} %copy.36), calls=%async_computation.4 | async-start | bytes 2097152 | tf_op jit(solution)/shard_map/all_to_all | solution.py:209
  162.3 25.1 %copy-start.6 = (f32[8,4,256]{2,1,0:T(4,128)S(1)}, f32[8,4,256]{2,1,0:T(4,128)}, u32[]{:S(2)}) copy-start(f32[8,4,256]{2,1,0:T(4,128)} %copy-done.5) | copy-start | bytes 98308
  162.3 26.6 %copy-start.9 = (f32[256,128]{1,0:T(8,128)S(1)}, f32[256,128]{1,0:T(8,128)}, u32[]{:S(2)}) copy-start(f32[256,128]{1,0:T(8,128)} %get-tuple-element.38) | copy-start | bytes 393220
  (6 other events, 47.9 us)

commit v7 on v5

--- a/solution.py
+++ b/solution.py
@@ -90,20 +90,14 @@
     ).astype(jnp.int32)
     slot_rank = jnp.sum((jnp.cumsum(onehot, axis=0) - onehot) * onehot, axis=1)
     slot_ids = jnp.where(is_live, owner_ids * capacity + slot_rank, total_slots)
-    source = (
-        jnp.full((total_slots,), obs_dev, jnp.int32)
-        .at[slot_ids]
-        .set(jnp.arange(obs_dev, dtype=jnp.int32), mode="drop")
-    )
-    filled = source < obs_dev
-    source = jnp.minimum(source, obs_dev - 1)
-    send_values = jnp.where(filled[:, None], innovations[source], 0.0)
-    send_cells = jnp.where(filled, obs_cell[source], 0).astype(jnp.float32)
-    send_marks = filled.astype(jnp.float32)
+    send_values = (
+        jnp.zeros((total_slots, channels), jnp.float32).at[slot_ids].set(innovations, mode="drop")
+    )
+    tags = jnp.stack([obs_cell.astype(jnp.float32), jnp.ones((obs_dev,), jnp.float32)], axis=1)
+    tags = jnp.zeros((total_slots, 2), jnp.float32).at[slot_ids].set(tags, mode="drop")
     side = jnp.concatenate(
         [
-            send_cells.reshape(blocks, capacity),
-            send_marks.reshape(blocks, capacity),
+            jnp.swapaxes(tags.reshape(blocks, capacity, 2), 1, 2).reshape(blocks, 2 * capacity),
             jnp.zeros((blocks, channels - 2 * capacity), jnp.float32),
         ],
         axis=1,
@@ -116,9 +110,13 @@
     obs_index = got_cells
     obs_gain = got_marks[:, None] * obs_weights[None, :]
 
+    placement = (
+        obs_index[None, :] == jnp.arange(rows_here * columns, dtype=jnp.int32)[:, None]
+    ).astype(jnp.float32)
+
     def spread_back(weighted):
         back = jnp.dot(weighted, obs_jacobian.T, precision=lax.Precision.HIGHEST)
-        grid = jnp.zeros((rows_here * columns, features), jnp.float32).at[obs_index].add(back)
+        grid = jnp.dot(placement, back, precision=lax.Precision.HIGHEST)
         return grid.reshape(rows_here, columns, features)
 
     def adjoint_parts(gradient):
@@ -151,6 +149,10 @@
     in_quarter = (cell_x >= offset) & (cell_x < offset + quarter)
     quarter_index = jnp.where(in_quarter, (obs_index // columns) * quarter + cell_x - offset, 0)
     quarter_gain = jnp.where(in_quarter[:, None], obs_gain, 0.0)
+    quarter_placement = (
+        (quarter_index[None, :] == jnp.arange(rows_here * quarter, dtype=jnp.int32)[:, None])
+        & in_quarter[None, :]
+    ).astype(jnp.float32)
 
     def observed(partial_sum):
         pieces = jnp.moveaxis(partial_sum.reshape(rows_here, parts, quarter, features), 1, 0)
@@ -161,7 +163,7 @@
 
     def observed_adjoint(model_obs):
         back = jnp.dot(quarter_gain * model_obs, obs_jacobian.T, precision=lax.Precision.HIGHEST)
-        own_gradient = jnp.zeros((rows_here * quarter, features), jnp.float32).at[quarter_index].add(back)
+        own_gradient = jnp.dot(quarter_placement, back, precision=lax.Precision.HIGHEST)
         static = jnp.dot(own_gradient, static_root.T, precision=lax.Precision.HIGHEST).reshape(
             rows_here, quarter, features
         )

time: 188 us -> 180 us (0.957)
  other arithmetic: 20 us -> 12.3 us
  local copies, waits for them, and re-layouts: 16.5 us -> 13.4 us
  matrix products: 11.3 us -> 14.3 us
    scatter-add x2 -> x0, other arithmetic: 7.49 us -> none  [the longest x1 4 us: observed_adjoint(): jnp.zeros((rows_here * quarter, features), jnp.float32).at[quarter_index]]
    gather x2 -> x0, local copies, waits for them, and re-layouts: 4.66 us -> none  [the longest x1 3.62 us: shards(): send_cells = jnp.where(filled, obs_cell[source], 0).astype(jnp.float32)]
    dot_general x0 -> x2, matrix products: none -> 2.1 us  [the longest x1 1.07 us: observed_adjoint(): jnp.dot(quarter_placement, back, precision=lax.Precision.HIGHEST)]
  transfers between devices with their start and end apart: 17 -> 17, of which waited for: 7 -> 7; matrix products, arithmetic and copies ran while one was open for 2% -> 3% of each run, Pallas kernels for 0% -> 0%
where the time goes in v7:
time: 180 us; the launch traced here: 179 us
  starting transfers between devices  71 us (39%)
  waiting for transfers between devices  35.8 us (20%)
  blocking collectives  19.5 us (11%)
  matrix products  14.3 us (8%)
  local copies, waits for them, and re-layouts  13.4 us (7%)
  between operations  12.6 us (7%)
  other arithmetic  12.3 us (7%)
    all_to_all x1, blocking collectives, global_sum(): return jnp.sum(lax.all_to_all(spread, axes, 0, 0, tiled=True), axis=0)  19.5 us
    ppermute x6, starting transfers between devices, neighbours(): below.insert(0, lax.ppermute(block, axis, forward))  19.4 us
    all_to_all x2, waiting for transfers between devices, observed(): own_image = jnp.sum(lax.all_to_all(pieces, 'mem', 0, 0, tiled=True), axis=0)  15.8 us
    ppermute x6, starting transfers between devices, neighbours(): above.append(lax.ppermute(block, axis, backward))  15.7 us
    all_to_all x1, starting transfers between devices, shards(): got = lax.all_to_all(packed, 'col', split_axis=0, concat_axis=0, tiled=True)  13.1 us
    all_to_all x1, starting transfers between devices, global_sum(): return jnp.sum(lax.all_to_all(spread, axes, 0, 0, tiled=True), axis=0)  11.7 us
    all_to_all x2, starting transfers between devices, observed(): own_image = jnp.sum(lax.all_to_all(pieces, 'mem', 0, 0, tiled=True), axis=0)  7.62 us
    all_to_all x1, waiting for transfers between devices, global_sum(): return jnp.sum(lax.all_to_all(spread, axes, 0, 0, tiled=True), axis=0)  6.87 us
  transfers between devices with their start and end apart: 17, of which 7 were waited for; matrix products, arithmetic and copies ran while one was open for 3% of the time, Pallas kernels for 0%

profile of v7, /device:TPU:1, one launch (start us, length us, event | category | flops | bytes accessed | tf_op | source)
XLA Modules:
  0.0 178.8 jit_solution(1564950445863113586)
XLA Ops:
  9.2 13.1 %all-to-all-start = ((f32[64,9,128]{2,1,0:T(8,128)}), f32[64,9,128]{2,1,0:T(8,128)S(1)}, u32[]{:S(2)}, u32[]{:S(2)}) async-start(f32[64,9,128]{2,1,0:T(8,128)} %pad_maximum_fusion), calls=%async_computation | async-start | bytes 1048576 | tf_op jit(solution)/shard_map/all_to_all | solution.py:106
  22.4 2.4 %collective-permute-start.6 = (f32[4,256]{1,0:T(4,128)S(1)}, f32[4,256]{1,0:T(4,128)S(1)}, u32[]{:S(2)}, u32[]{:S(2)}) collective-permute-start(f32[4,256]{1,0:T(4,128)S(1)} %copy-done.9), channel_id=1, source_target_pairs={{1,0},{2,1},{3,2},{4,3},{5,4},{6,5},{7,6},{8,7},{9,8},{10,9},{11,1... | collective-permute-start | bytes 12296 | tf_op jit(solution)/shard_map/ppermute | solution.py:17
  24.8 3.2 %collective-permute-start.5 = (f32[4,256]{1,0:T(4,128)S(1)}, f32[4,256]{1,0:T(4,128)S(1)}, u32[]{:S(2)}, u32[]{:S(2)}) collective-permute-start(f32[4,256]{1,0:T(4,128)S(1)} %copy-done.9), channel_id=1, source_target_pairs={{0,1},{1,2},{2,3},{3,4},{4,5},{5,6},{6,7},{7,8},{8,9},{9,10},{10,1... | collective-permute-start | bytes 12296 | tf_op jit(solution)/shard_map/ppermute | solution.py:16
  28.0 3.3 %collective-permute-start.4 = (f32[4,256]{1,0:T(4,128)S(1)}, f32[4,256]{1,0:T(4,128)S(1)}, u32[]{:S(2)}, u32[]{:S(2)}) collective-permute-start(f32[4,256]{1,0:T(4,128)S(1)} %copy-done.9), channel_id=1, source_target_pairs={{0,2},{1,3},{2,4},{3,5},{4,6},{5,7},{6,8},{7,9},{8,10},{9,11},{10,... | collective-permute-start | bytes 12296 | tf_op jit(solution)/shard_map/ppermute | solution.py:16
  32.5 3.6 %collective-permute-done.6 = f32[4,256]{1,0:T(4,128)S(1)} collective-permute-done((f32[4,256]{1,0:T(4,128)S(1)}, f32[4,256]{1,0:T(4,128)S(1)}, u32[]{:S(2)}, u32[]{:S(2)}) %collective-permute-start.6) | collective-permute-done | bytes 4128 | tf_op jit(solution)/shard_map/ppermute | solution.py:17
  36.4 3.6 %all-to-all-done = f32[64,9,128]{2,1,0:T(8,128)S(1)} async-done(((f32[64,9,128]{2,1,0:T(8,128)}), f32[64,9,128]{2,1,0:T(8,128)S(1)}, u32[]{:S(2)}, u32[]{:S(2)}) %all-to-all-start) | async-done | bytes 294944 | tf_op jit(solution)/shard_map/all_to_all | solution.py:106
  42.0 2.4 %fusion.7 = f32[4,256,1,8]{3,2,1,0:T(1,128)} fusion(bf16[8,4,256,128]{3,2,1,0:T(8,128)(2,1)S(1)} %copy-done, bf16[4,256,128,1]{2,1,0,3:T(8,128)(2,1)S(1)} %convert_bitcast_fusion), kind=kOutput, calls=%fused_computation.12 | convolution fusion | flops 2097152 | bytes 2392064 | tf_op jit(solution)/shard_map/kyxf,yxf->kyx/dot_general | solution.py:130
  46.8 2.3 %collective-permute-start.2 = (f32[8,4,256]{2,1,0:T(4,128)S(1)}, f32[8,4,256]{2,1,0:T(4,128)S(1)}, u32[]{:S(2)}, u32[]{:S(2)}) collective-permute-start(f32[8,4,256]{2,1,0:T(4,128)S(1)} %bitcast.131), channel_id=1, source_target_pairs={{1,0},{2,1},{3,2},{4,3},{5,4},{6,5},{7,6},{8,7},{9,8},{10,9},{11,1... | collective-permute-start | bytes 98312 | tf_op jit(solution)/shard_map/ppermute | solution.py:17
  49.1 4.2 %collective-permute-start.1 = (f32[8,4,256]{2,1,0:T(4,128)S(1)}, f32[8,4,256]{2,1,0:T(4,128)S(1)}, u32[]{:S(2)}, u32[]{:S(2)}) collective-permute-start(f32[8,4,256]{2,1,0:T(4,128)S(1)} %bitcast.132), channel_id=1, source_target_pairs={{0,1},{1,2},{2,3},{3,4},{4,5},{5,6},{6,7},{7,8},{8,9},{9,10},{10,1... | collective-permute-start | bytes 98312 | tf_op jit(solution)/shard_map/ppermute | solution.py:16
  53.3 3.1 %collective-permute-start = (f32[8,4,256]{2,1,0:T(4,128)S(1)}, f32[8,4,256]{2,1,0:T(4,128)S(1)}, u32[]{:S(2)}, u32[]{:S(2)}) collective-permute-start(f32[8,4,256]{2,1,0:T(4,128)S(1)} %bitcast.133), channel_id=1, source_target_pairs={{0,2},{1,3},{2,4},{3,5},{4,6},{5,7},{6,8},{7,9},{8,10},{9,11},{10,... | collective-permute-start | bytes 98312 | tf_op jit(solution)/shard_map/ppermute | solution.py:16
  62.2 4.0 %all-to-all-start.1 = ((f32[4,4,64,128]{3,2,1,0:T(8,128)}), f32[4,4,64,128]{3,2,1,0:T(8,128)S(1)}, u32[]{:S(2)}, u32[]{:S(2)}) async-start(f32[4,4,64,128]{3,2,1,0:T(8,128)} %copy.62), calls=%async_computation.1 | async-start | bytes 1048576 | tf_op jit(solution)/shard_map/all_to_all | solution.py:159
  66.3 9.0 %all-to-all-done.1 = f32[4,4,64,128]{3,2,1,0:T(8,128)S(1)} async-done(((f32[4,4,64,128]{3,2,1,0:T(8,128)}), f32[4,4,64,128]{3,2,1,0:T(8,128)S(1)}, u32[]{:S(2)}, u32[]{:S(2)}) %all-to-all-start.1) | async-done | bytes 524320 | tf_op jit(solution)/shard_map/all_to_all | solution.py:159
  78.9 3.4 %all-to-all-start.2 = ((bf16[4,4,64,128]{3,2,1,0:T(8,128)(2,1)}), bf16[4,4,64,128]{3,2,1,0:T(8,128)(2,1)S(1)}, u32[]{:S(2)}, u32[]{:S(2)}) async-start(bf16[4,4,64,128]{3,2,1,0:T(8,128)(2,1)} %broadcast_in_dim.33), calls=%async_computation.2 | async-start | bytes 524288 | tf_op jit(solution)/shard_map/all_to_all | solution.py:172
  82.4 5.4 %all-to-all-done.2 = bf16[4,4,64,128]{3,2,1,0:T(8,128)(2,1)S(1)} async-done(((bf16[4,4,64,128]{3,2,1,0:T(8,128)(2,1)}), bf16[4,4,64,128]{3,2,1,0:T(8,128)(2,1)S(1)}, u32[]{:S(2)}, u32[]{:S(2)}) %all-to-all-start.2) | async-done | bytes 262176 | tf_op jit(solution)/shard_map/all_to_all | solution.py:172
  89.7 4.4 %collective-permute-start.9 = (f32[8,4,256]{2,1,0:T(4,128)S(1)}, f32[8,4,256]{2,1,0:T(4,128)S(1)}, u32[]{:S(2)}, u32[]{:S(2)}) collective-permute-start(f32[8,4,256]{2,1,0:T(4,128)S(1)} %bitcast.126), channel_id=1, source_target_pairs={{1,0},{2,1},{3,2},{4,3},{5,4},{6,5},{7,6},{8,7},{9,8},{10,9},{11,1... | collective-permute-start | bytes 98312 | tf_op jit(solution)/shard_map/ppermute | solution.py:17
  94.1 3.8 %collective-permute-start.8 = (f32[8,4,256]{2,1,0:T(4,128)S(1)}, f32[8,4,256]{2,1,0:T(4,128)S(1)}, u32[]{:S(2)}, u32[]{:S(2)}) collective-permute-start(f32[8,4,256]{2,1,0:T(4,128)S(1)} %bitcast.127), channel_id=1, source_target_pairs={{0,1},{1,2},{2,3},{3,4},{4,5},{5,6},{6,7},{7,8},{8,9},{9,10},{10,1... | collective-permute-start | bytes 98312 | tf_op jit(solution)/shard_map/ppermute | solution.py:16
  97.9 1.9 %multiply_reduce_fusion.3 = (f32[]{:T(128)}, f32[]{:T(128)}, f32[]{:T(128)}, f32[256,128]{1,0:T(8,128)S(1)}, f32[256,128]{1,0:T(8,128)S(1)}) fusion(f32[256,128]{1,0:T(8,128)S(1)} %fusion.238, f32[256,128]{1,0:T(8,128)} %get-tuple-element.40, f32[128,128]{1,0:T(8,128)S(1)} %copy-done.1), kind=kOutput, calls=%fused_computation.265 | convolution fusion | flops 50561020 | bytes 589836 | tf_op jit(solution)/shard_map/dot_general | solution.py:167
  105.7 11.7 %all-to-all-start.3 = ((f32[256,1,3]{2,1,0:T(1,128)}), f32[256,1,3]{2,1,0:T(1,128)S(1)}, u32[]{:S(2)}, u32[]{:S(2)}) async-start(f32[256,1,3]{2,1,0:T(1,128)} %broadcast_in_dim.34), calls=%async_computation.3 | async-start | bytes 262144 | tf_op jit(solution)/shard_map/all_to_all | solution.py:58
  117.4 4.1 %collective-permute-start.11 = (f32[8,4,256]{2,1,0:T(4,128)S(1)}, f32[8,4,256]{2,1,0:T(4,128)S(1)}, u32[]{:S(2)}, u32[]{:S(2)}) collective-permute-start(f32[8,4,256]{2,1,0:T(4,128)S(1)} %get-tuple-element.11), channel_id=1, source_target_pairs={{1,0},{2,1},{3,2},{4,3},{5,4},{6,5},{7,6},{8,7},{9,8},{10,9},{11,1... | collective-permute-start | bytes 98312 | tf_op jit(solution)/shard_map/ppermute | solution.py:17
  121.5 1.9 %collective-permute-start.10 = (f32[8,4,256]{2,1,0:T(4,128)S(1)}, f32[8,4,256]{2,1,0:T(4,128)S(1)}, u32[]{:S(2)}, u32[]{:S(2)}) collective-permute-start(f32[8,4,256]{2,1,0:T(4,128)S(1)} %get-tuple-element.11), channel_id=1, source_target_pairs={{0,1},{1,2},{2,3},{3,4},{4,5},{5,6},{6,7},{7,8},{8,9},{9,10},{10,1... | collective-permute-start | bytes 98312 | tf_op jit(solution)/shard_map/ppermute | solution.py:16
  123.4 6.9 %all-to-all-done.3 = f32[256,1,3]{2,1,0:T(1,128)S(1)} async-done(((f32[256,1,3]{2,1,0:T(1,128)}), f32[256,1,3]{2,1,0:T(1,128)S(1)}, u32[]{:S(2)}, u32[]{:S(2)}) %all-to-all-start.3) | async-done | bytes 3104 | tf_op jit(solution)/shard_map/all_to_all | solution.py:58
  141.3 3.6 %all-to-all-start.4 = ((f32[4,4,64,128]{3,2,1,0:T(8,128)}), f32[4,4,64,128]{3,2,1,0:T(8,128)S(1)}, u32[]{:S(2)}, u32[]{:S(2)}) async-start(f32[4,4,64,128]{3,2,1,0:T(8,128)} %bitcast.103), calls=%async_computation.4 | async-start | bytes 1048576 | tf_op jit(solution)/shard_map/all_to_all | solution.py:159
  146.8 6.8 %all-to-all-done.4 = f32[4,4,64,128]{3,2,1,0:T(8,128)S(1)} async-done(((f32[4,4,64,128]{3,2,1,0:T(8,128)}), f32[4,4,64,128]{3,2,1,0:T(8,128)S(1)}, u32[]{:S(2)}, u32[]{:S(2)}) %all-to-all-start.4) | async-done | bytes 524320 | tf_op jit(solution)/shard_map/all_to_all | solution.py:159
  156.4 19.5 %all_to_all.32 = f32[256,1,1]{2,1,0:T(1,128)S(1)} all-to-all(f32[256,1,1]{2,1,0:T(1,128)S(1)} %broadcast_in_dim.35), channel_id=1, replica_groups=mesh['mem'=4,'col'=64] {'mem','col'}, dimensions={0} | all-to-all | bytes 2048 | tf_op jit(solution)/shard_map/all_to_all | solution.py:58
  (131 shorter events, 38.8 us)
Async XLA Ops:
  0.6 41.3 %copy-start = (bf16[8,4,256,128]{3,2,1,0:T(8,128)(2,1)S(1)}, bf16[8,4,256,128]{3,2,1,0:T(8,128)(2,1)}, u32[]{:S(2)}) copy-start(bf16[8,4,256,128]{3,2,1,0:T(8,128)(2,1)} %param.9) | copy-start | bytes 6291460
  0.6 21.7 %copy-start.9 = (f32[4,256]{1,0:T(4,128)S(1)}, f32[4,256]{1,0:T(4,128)}, u32[]{:S(2)}) copy-start(f32[4,256]{1,0:T(4,128)} %param.14) | copy-start | bytes 12292
  0.7 39.8 %copy-start.2 = (f32[128,128]{1,0:T(8,128)S(1)}, f32[128,128]{1,0:T(8,128)}, u32[]{:S(2)}) copy-start(f32[128,128]{1,0:T(8,128)} %param.11) | copy-start | bytes 196612
  0.7 39.8 %copy-start.10 = (f32[128]{0:T(128)S(1)}, f32[128]{0:T(128)}, u32[]{:S(2)}) copy-start(f32[128]{0:T(128)} %param.13) | copy-start | bytes 1540
  9.2 30.7 %all-to-all-start = ((f32[64,9,128]{2,1,0:T(8,128)}), f32[64,9,128]{2,1,0:T(8,128)S(1)}, u32[]{:S(2)}, u32[]{:S(2)}) async-start(f32[64,9,128]{2,1,0:T(8,128)} %pad_maximum_fusion), calls=%async_computation | async-start | bytes 1048576 | tf_op jit(solution)/shard_map/all_to_all | solution.py:106
  22.4 13.8 %collective-permute-start.6 = (f32[4,256]{1,0:T(4,128)S(1)}, f32[4,256]{1,0:T(4,128)S(1)}, u32[]{:S(2)}, u32[]{:S(2)}) collective-permute-start(f32[4,256]{1,0:T(4,128)S(1)} %copy-done.9), channel_id=1, source_target_pairs={{1,0},{2,1},{3,2},{4,3},{5,4},{6,5},{7,6},{8,7},{9,8},{10,9},{11,1... | collective-permute-start | bytes 12296 | tf_op jit(solution)/shard_map/ppermute | solution.py:17
  24.8 11.4 %collective-permute-start.5 = (f32[4,256]{1,0:T(4,128)S(1)}, f32[4,256]{1,0:T(4,128)S(1)}, u32[]{:S(2)}, u32[]{:S(2)}) collective-permute-start(f32[4,256]{1,0:T(4,128)S(1)} %copy-done.9), channel_id=1, source_target_pairs={{0,1},{1,2},{2,3},{3,4},{4,5},{5,6},{6,7},{7,8},{8,9},{9,10},{10,1... | collective-permute-start | bytes 12296 | tf_op jit(solution)/shard_map/ppermute | solution.py:16
  28.0 8.2 %collective-permute-start.4 = (f32[4,256]{1,0:T(4,128)S(1)}, f32[4,256]{1,0:T(4,128)S(1)}, u32[]{:S(2)}, u32[]{:S(2)}) collective-permute-start(f32[4,256]{1,0:T(4,128)S(1)} %copy-done.9), channel_id=1, source_target_pairs={{0,2},{1,3},{2,4},{3,5},{4,6},{5,7},{6,8},{7,9},{8,10},{9,11},{10,... | collective-permute-start | bytes 12296 | tf_op jit(solution)/shard_map/ppermute | solution.py:16
  31.2 4.9 %collective-permute-start.7 = (f32[4,256]{1,0:T(4,128)S(1)}, f32[4,256]{1,0:T(4,128)S(1)}, u32[]{:S(2)}, u32[]{:S(2)}) collective-permute-start(f32[4,256]{1,0:T(4,128)S(1)} %copy-done.9), channel_id=1, source_target_pairs={{2,0},{3,1},{4,2},{5,3},{6,4},{7,5},{8,6},{9,7},{10,8},{11,9},{12,... | collective-permute-start | bytes 12296 | tf_op jit(solution)/shard_map/ppermute | solution.py:17
  40.4 35.9 %copy-start.3 = (f32[512]{0:T(512)}, f32[512]{0:T(512)S(1)}, u32[]{:S(2)}) copy-start(f32[512]{0:T(512)S(1)} %mul.273) | copy-start | bytes 6148
  42.0 14.5 %copy-start.1 = (f32[128,128]{1,0:T(8,128)S(1)}, f32[128,128]{1,0:T(8,128)}, u32[]{:S(2)}) copy-start(f32[128,128]{1,0:T(8,128)} %param.10) | copy-start | bytes 196612
  45.5 11.6 %collective-permute-start.3 = (f32[8,4,256]{2,1,0:T(4,128)S(1)}, f32[8,4,256]{2,1,0:T(4,128)S(1)}, u32[]{:S(2)}, u32[]{:S(2)}) collective-permute-start(f32[8,4,256]{2,1,0:T(4,128)S(1)} %bitcast.130), channel_id=1, source_target_pairs={{2,0},{3,1},{4,2},{5,3},{6,4},{7,5},{8,6},{9,7},{10,8},{11,9},{12,... | collective-permute-start | bytes 98312 | tf_op jit(solution)/shard_map/ppermute | solution.py:17
  46.8 10.3 %collective-permute-start.2 = (f32[8,4,256]{2,1,0:T(4,128)S(1)}, f32[8,4,256]{2,1,0:T(4,128)S(1)}, u32[]{:S(2)}, u32[]{:S(2)}) collective-permute-start(f32[8,4,256]{2,1,0:T(4,128)S(1)} %bitcast.131), channel_id=1, source_target_pairs={{1,0},{2,1},{3,2},{4,3},{5,4},{6,5},{7,6},{8,7},{9,8},{10,9},{11,1... | collective-permute-start | bytes 98312 | tf_op jit(solution)/shard_map/ppermute | solution.py:17
  49.1 7.9 %collective-permute-start.1 = (f32[8,4,256]{2,1,0:T(4,128)S(1)}, f32[8,4,256]{2,1,0:T(4,128)S(1)}, u32[]{:S(2)}, u32[]{:S(2)}) collective-permute-start(f32[8,4,256]{2,1,0:T(4,128)S(1)} %bitcast.132), channel_id=1, source_target_pairs={{0,1},{1,2},{2,3},{3,4},{4,5},{5,6},{6,7},{7,8},{8,9},{9,10},{10,1... | collective-permute-start | bytes 98312 | tf_op jit(solution)/shard_map/ppermute | solution.py:16
  53.3 4.3 %collective-permute-start = (f32[8,4,256]{2,1,0:T(4,128)S(1)}, f32[8,4,256]{2,1,0:T(4,128)S(1)}, u32[]{:S(2)}, u32[]{:S(2)}) collective-permute-start(f32[8,4,256]{2,1,0:T(4,128)S(1)} %bitcast.133), channel_id=1, source_target_pairs={{0,2},{1,3},{2,4},{3,5},{4,6},{5,7},{6,8},{7,9},{8,10},{9,11},{10,... | collective-permute-start | bytes 98312 | tf_op jit(solution)/shard_map/ppermute | solution.py:16
  62.2 13.1 %all-to-all-start.1 = ((f32[4,4,64,128]{3,2,1,0:T(8,128)}), f32[4,4,64,128]{3,2,1,0:T(8,128)S(1)}, u32[]{:S(2)}, u32[]{:S(2)}) async-start(f32[4,4,64,128]{3,2,1,0:T(8,128)} %copy.62), calls=%async_computation.1 | async-start | bytes 1048576 | tf_op jit(solution)/shard_map/all_to_all | solution.py:159
  78.9 8.9 %all-to-all-start.2 = ((bf16[4,4,64,128]{3,2,1,0:T(8,128)(2,1)}), bf16[4,4,64,128]{3,2,1,0:T(8,128)(2,1)S(1)}, u32[]{:S(2)}, u32[]{:S(2)}) async-start(bf16[4,4,64,128]{3,2,1,0:T(8,128)(2,1)} %broadcast_in_dim.33), calls=%async_computation.2 | async-start | bytes 524288 | tf_op jit(solution)/shard_map/all_to_all | solution.py:172
  89.7 10.1 %collective-permute-start.9 = (f32[8,4,256]{2,1,0:T(4,128)S(1)}, f32[8,4,256]{2,1,0:T(4,128)S(1)}, u32[]{:S(2)}, u32[]{:S(2)}) collective-permute-start(f32[8,4,256]{2,1,0:T(4,128)S(1)} %bitcast.126), channel_id=1, source_target_pairs={{1,0},{2,1},{3,2},{4,3},{5,4},{6,5},{7,6},{8,7},{9,8},{10,9},{11,1... | collective-permute-start | bytes 98312 | tf_op jit(solution)/shard_map/ppermute | solution.py:17
  94.1 5.7 %collective-permute-start.8 = (f32[8,4,256]{2,1,0:T(4,128)S(1)}, f32[8,4,256]{2,1,0:T(4,128)S(1)}, u32[]{:S(2)}, u32[]{:S(2)}) collective-permute-start(f32[8,4,256]{2,1,0:T(4,128)S(1)} %bitcast.127), channel_id=1, source_target_pairs={{0,1},{1,2},{2,3},{3,4},{4,5},{5,6},{6,7},{7,8},{8,9},{9,10},{10,1... | collective-permute-start | bytes 98312 | tf_op jit(solution)/shard_map/ppermute | solution.py:16
  105.7 24.5 %all-to-all-start.3 = ((f32[256,1,3]{2,1,0:T(1,128)}), f32[256,1,3]{2,1,0:T(1,128)S(1)}, u32[]{:S(2)}, u32[]{:S(2)}) async-start(f32[256,1,3]{2,1,0:T(1,128)} %broadcast_in_dim.34), calls=%async_computation.3 | async-start | bytes 262144 | tf_op jit(solution)/shard_map/all_to_all | solution.py:58
  117.4 18.6 %collective-permute-start.11 = (f32[8,4,256]{2,1,0:T(4,128)S(1)}, f32[8,4,256]{2,1,0:T(4,128)S(1)}, u32[]{:S(2)}, u32[]{:S(2)}) collective-permute-start(f32[8,4,256]{2,1,0:T(4,128)S(1)} %get-tuple-element.11), channel_id=1, source_target_pairs={{1,0},{2,1},{3,2},{4,3},{5,4},{6,5},{7,6},{8,7},{9,8},{10,9},{11,1... | collective-permute-start | bytes 98312 | tf_op jit(solution)/shard_map/ppermute | solution.py:17
  121.5 14.5 %collective-permute-start.10 = (f32[8,4,256]{2,1,0:T(4,128)S(1)}, f32[8,4,256]{2,1,0:T(4,128)S(1)}, u32[]{:S(2)}, u32[]{:S(2)}) collective-permute-start(f32[8,4,256]{2,1,0:T(4,128)S(1)} %get-tuple-element.11), channel_id=1, source_target_pairs={{0,1},{1,2},{2,3},{3,4},{4,5},{5,6},{6,7},{7,8},{8,9},{9,10},{10,1... | collective-permute-start | bytes 98312 | tf_op jit(solution)/shard_map/ppermute | solution.py:16
  140.2 13.5 %copy-start.6 = (s32[1024]{0:T(1024)S(1)}, s32[1024]{0:T(1024)}, u32[]{:S(2)}) copy-start(s32[1024]{0:T(1024)} %copy-done.5) | copy-start | bytes 12292
  141.3 12.3 %all-to-all-start.4 = ((f32[4,4,64,128]{3,2,1,0:T(8,128)}), f32[4,4,64,128]{3,2,1,0:T(8,128)S(1)}, u32[]{:S(2)}, u32[]{:S(2)}) async-start(f32[4,4,64,128]{3,2,1,0:T(8,128)} %bitcast.103), calls=%async_computation.4 | async-start | bytes 1048576 | tf_op jit(solution)/shard_map/all_to_all | solution.py:159
  (5 other events, 62.0 us)

commit v8 on v7

--- a/solution.py
+++ b/solution.py
@@ -43,12 +43,6 @@
             + face_right * (padded[:, 1:-1, 2:] - centre)
         )
     return values
-
-
-def sweeps(values, coeffs):
-    rows = values.shape[1]
-    done = sweep_steps(neighbours(values, "col", 1, 1), coeffs, NSWEEP)
-    return done[:, rows : 2 * rows]
 
 
 def global_sum(values):
@@ -82,7 +76,6 @@
     capacity = max(2, 2 * obs_dev // blocks)
     total_slots = blocks * capacity
     coeffs_wide = face_coefficients(length_scale, 2)
-    coeffs = tuple(face[rows_here : 4 * rows_here] for face in coeffs_wide)
     is_live = jnp.arange(obs_dev, dtype=jnp.int32) < obs_count[0]
     owner_ids = obs_owner[:, 0]
     onehot = (
@@ -186,7 +179,11 @@
     partial0 = forward_partial(right_static, smoothed_right)
     own_image0, model_obs = observed(partial0)
     adj_static, adj_projected = observed_adjoint(model_obs)
-    image = (right_static + adj_static, right_ensemble + sweeps(adj_projected, coeffs))
+    wide = sweep_steps(neighbours(adj_projected, "col", 1, 2), coeffs_wide, NSWEEP)
+    smoothed_adjoint = wide[:, 2 * rows_here : 3 * rows_here]
+    wide = sweep_steps(wide, coeffs_wide, NSWEEP)
+    smoothed_image = smoothed_right + wide[:, 2 * rows_here : 3 * rows_here]
+    image = (right_static + adj_static, right_ensemble + smoothed_adjoint)
     sums = global_sum(
         jnp.stack(
             [
@@ -196,7 +193,6 @@
             ]
         )
     )
-    smoothed_image = sweeps(image[1], coeffs)
     norm_now, curve, image_norm = sums[0], sums[1], sums[2]
     step0 = norm_now / curve
     state = (step0 * direction[0], step0 * direction[1])

time: 180 us -> 184 us (1.022)
  blocking collectives: 19.5 us -> 27.4 us
  starting transfers between devices: 71 us -> 67.4 us
    all_to_all x0 -> x1, blocking collectives: none -> 7.92 us  [observed_adjoint(): quarters = lax.all_to_all(spread, 'mem', 0, 0, tiled=True)]
    all_to_all x1 -> x0, waiting for transfers between devices: 5.44 us -> none  [observed_adjoint(): quarters = lax.all_to_all(spread, 'mem', 0, 0, tiled=True)]
    all_to_all x1, waiting for transfers between devices: 6.87 us -> 11.9 us  [global_sum(): return jnp.sum(lax.all_to_all(spread, axes, 0, 0, tiled=True), axis=0)]
    all_to_all x1 -> x0, starting transfers between devices: 3.4 us -> none  [observed_adjoint(): quarters = lax.all_to_all(spread, 'mem', 0, 0, tiled=True)]
    ppermute x6, starting transfers between devices: 15.7 us -> 12.9 us  [neighbours(): above.append(lax.ppermute(block, axis, backward))]
    ppermute x6, starting transfers between devices: 19.4 us -> 21.8 us  [neighbours(): below.insert(0, lax.ppermute(block, axis, forward))]
  transfers between devices with their start and end apart: 17 -> 16, of which waited for: 7 -> 6; matrix products, arithmetic and copies ran while one was open for 3% -> 2% of each run, Pallas kernels for 0% -> 0%
where the time goes in v8:
time: 184 us; the launch traced here: 183 us
  starting transfers between devices  67.4 us (37%)
  waiting for transfers between devices  35.4 us (19%)
  blocking collectives  27.4 us (15%)
  matrix products  14.3 us (8%)
  other arithmetic  13.6 us (7%)
  local copies, waits for them, and re-layouts  12.6 us (7%)
  between operations  12.4 us (7%)
    ppermute x6, starting transfers between devices, neighbours(): below.insert(0, lax.ppermute(block, axis, forward))  21.8 us
    all_to_all x1, blocking collectives, global_sum(): return jnp.sum(lax.all_to_all(spread, axes, 0, 0, tiled=True), axis=0)  19.5 us
    all_to_all x2, waiting for transfers between devices, observed(): own_image = jnp.sum(lax.all_to_all(pieces, 'mem', 0, 0, tiled=True), axis=0)  15.8 us
    all_to_all x1, starting transfers between devices, shards(): got = lax.all_to_all(packed, 'col', split_axis=0, concat_axis=0, tiled=True)  13.1 us
    ppermute x6, starting transfers between devices, neighbours(): above.append(lax.ppermute(block, axis, backward))  12.9 us
    all_to_all x1, starting transfers between devices, global_sum(): return jnp.sum(lax.all_to_all(spread, axes, 0, 0, tiled=True), axis=0)  11.9 us
    all_to_all x1, waiting for transfers between devices, global_sum(): return jnp.sum(lax.all_to_all(spread, axes, 0, 0, tiled=True), axis=0)  11.9 us
    all_to_all x1, blocking collectives, observed_adjoint(): quarters = lax.all_to_all(spread, 'mem', 0, 0, tiled=True)  7.92 us
  transfers between devices with their start and end apart: 16, of which 6 were waited for; matrix products, arithmetic and copies ran while one was open for 2% of the time, Pallas kernels for 0%

profile of v8, /device:TPU:1, one launch (start us, length us, event | category | flops | bytes accessed | tf_op | source)
XLA Modules:
  0.0 183.0 jit_solution(1101547258520931112)
XLA Ops:
  9.2 13.1 %all-to-all-start = ((f32[64,9,128]{2,1,0:T(8,128)}), f32[64,9,128]{2,1,0:T(8,128)S(1)}, u32[]{:S(2)}, u32[]{:S(2)}) async-start(f32[64,9,128]{2,1,0:T(8,128)} %pad_maximum_fusion), calls=%async_computation | async-start | bytes 1048576 | tf_op jit(solution)/shard_map/all_to_all | solution.py:99
  22.4 2.4 %collective-permute-start.6 = (f32[4,256]{1,0:T(4,128)S(1)}, f32[4,256]{1,0:T(4,128)S(1)}, u32[]{:S(2)}, u32[]{:S(2)}) collective-permute-start(f32[4,256]{1,0:T(4,128)S(1)} %copy-done.9), channel_id=1, source_target_pairs={{1,0},{2,1},{3,2},{4,3},{5,4},{6,5},{7,6},{8,7},{9,8},{10,9},{11,1... | collective-permute-start | bytes 12296 | tf_op jit(solution)/shard_map/ppermute | solution.py:17
  24.8 3.2 %collective-permute-start.5 = (f32[4,256]{1,0:T(4,128)S(1)}, f32[4,256]{1,0:T(4,128)S(1)}, u32[]{:S(2)}, u32[]{:S(2)}) collective-permute-start(f32[4,256]{1,0:T(4,128)S(1)} %copy-done.9), channel_id=1, source_target_pairs={{0,1},{1,2},{2,3},{3,4},{4,5},{5,6},{6,7},{7,8},{8,9},{9,10},{10,1... | collective-permute-start | bytes 12296 | tf_op jit(solution)/shard_map/ppermute | solution.py:16
  28.0 3.3 %collective-permute-start.4 = (f32[4,256]{1,0:T(4,128)S(1)}, f32[4,256]{1,0:T(4,128)S(1)}, u32[]{:S(2)}, u32[]{:S(2)}) collective-permute-start(f32[4,256]{1,0:T(4,128)S(1)} %copy-done.9), channel_id=1, source_target_pairs={{0,2},{1,3},{2,4},{3,5},{4,6},{5,7},{6,8},{7,9},{8,10},{9,11},{10,... | collective-permute-start | bytes 12296 | tf_op jit(solution)/shard_map/ppermute | solution.py:16
  32.5 3.6 %collective-permute-done.6 = f32[4,256]{1,0:T(4,128)S(1)} collective-permute-done((f32[4,256]{1,0:T(4,128)S(1)}, f32[4,256]{1,0:T(4,128)S(1)}, u32[]{:S(2)}, u32[]{:S(2)}) %collective-permute-start.6) | collective-permute-done | bytes 4128 | tf_op jit(solution)/shard_map/ppermute | solution.py:17
  36.4 3.6 %all-to-all-done = f32[64,9,128]{2,1,0:T(8,128)S(1)} async-done(((f32[64,9,128]{2,1,0:T(8,128)}), f32[64,9,128]{2,1,0:T(8,128)S(1)}, u32[]{:S(2)}, u32[]{:S(2)}) %all-to-all-start) | async-done | bytes 294944 | tf_op jit(solution)/shard_map/all_to_all | solution.py:99
  42.0 2.4 %fusion.7 = f32[4,256,1,8]{3,2,1,0:T(1,128)} fusion(bf16[8,4,256,128]{3,2,1,0:T(8,128)(2,1)S(1)} %copy-done, bf16[4,256,128,1]{2,1,0,3:T(8,128)(2,1)S(1)} %convert_bitcast_fusion), kind=kOutput, calls=%fused_computation.12 | convolution fusion | flops 2097152 | bytes 2392064 | tf_op jit(solution)/shard_map/kyxf,yxf->kyx/dot_general | solution.py:123
  46.8 2.3 %collective-permute-start.2 = (f32[8,4,256]{2,1,0:T(4,128)S(1)}, f32[8,4,256]{2,1,0:T(4,128)S(1)}, u32[]{:S(2)}, u32[]{:S(2)}) collective-permute-start(f32[8,4,256]{2,1,0:T(4,128)S(1)} %bitcast.128), channel_id=1, source_target_pairs={{1,0},{2,1},{3,2},{4,3},{5,4},{6,5},{7,6},{8,7},{9,8},{10,9},{11,1... | collective-permute-start | bytes 98312 | tf_op jit(solution)/shard_map/ppermute | solution.py:17
  49.1 4.2 %collective-permute-start.1 = (f32[8,4,256]{2,1,0:T(4,128)S(1)}, f32[8,4,256]{2,1,0:T(4,128)S(1)}, u32[]{:S(2)}, u32[]{:S(2)}) collective-permute-start(f32[8,4,256]{2,1,0:T(4,128)S(1)} %bitcast.129), channel_id=1, source_target_pairs={{0,1},{1,2},{2,3},{3,4},{4,5},{5,6},{6,7},{7,8},{8,9},{9,10},{10,1... | collective-permute-start | bytes 98312 | tf_op jit(solution)/shard_map/ppermute | solution.py:16
  53.3 3.1 %collective-permute-start = (f32[8,4,256]{2,1,0:T(4,128)S(1)}, f32[8,4,256]{2,1,0:T(4,128)S(1)}, u32[]{:S(2)}, u32[]{:S(2)}) collective-permute-start(f32[8,4,256]{2,1,0:T(4,128)S(1)} %bitcast.130), channel_id=1, source_target_pairs={{0,2},{1,3},{2,4},{3,5},{4,6},{5,7},{6,8},{7,9},{8,10},{9,11},{10,... | collective-permute-start | bytes 98312 | tf_op jit(solution)/shard_map/ppermute | solution.py:16
  60.2 1.7 fusion.5
  62.8 4.0 %all-to-all-start.1 = ((f32[4,4,64,128]{3,2,1,0:T(8,128)}), f32[4,4,64,128]{3,2,1,0:T(8,128)S(1)}, u32[]{:S(2)}, u32[]{:S(2)}) async-start(f32[4,4,64,128]{3,2,1,0:T(8,128)} %copy.62), calls=%async_computation.1 | async-start | bytes 1048576 | tf_op jit(solution)/shard_map/all_to_all | solution.py:152
  66.9 9.0 %all-to-all-done.1 = f32[4,4,64,128]{3,2,1,0:T(8,128)S(1)} async-done(((f32[4,4,64,128]{3,2,1,0:T(8,128)}), f32[4,4,64,128]{3,2,1,0:T(8,128)S(1)}, u32[]{:S(2)}, u32[]{:S(2)}) %all-to-all-start.1) | async-done | bytes 524320 | tf_op jit(solution)/shard_map/all_to_all | solution.py:152
  78.9 7.9 %all_to_all.32 = bf16[4,4,64,128]{3,2,1,0:T(8,128)(2,1)S(1)} all-to-all(bf16[4,4,64,128]{3,2,1,0:T(8,128)(2,1)S(1)} %broadcast_in_dim.33), channel_id=1, replica_groups=mesh['mem'=4,'col'=64] {'mem'}, dimensions={0} | all-to-all | bytes 524288 | tf_op jit(solution)/shard_map/all_to_all | solution.py:165
  89.9 4.4 %collective-permute-start.10 = (f32[8,4,256]{2,1,0:T(4,128)S(1)}, f32[8,4,256]{2,1,0:T(4,128)S(1)}, u32[]{:S(2)}, u32[]{:S(2)}) collective-permute-start(f32[8,4,256]{2,1,0:T(4,128)S(1)} %bitcast.133), channel_id=1, source_target_pairs={{1,0},{2,1},{3,2},{4,3},{5,4},{6,5},{7,6},{8,7},{9,8},{10,9},{11,1... | collective-permute-start | bytes 98312 | tf_op jit(solution)/shard_map/ppermute | solution.py:17
  94.3 4.4 %collective-permute-start.9 = (f32[8,4,256]{2,1,0:T(4,128)S(1)}, f32[8,4,256]{2,1,0:T(4,128)S(1)}, u32[]{:S(2)}, u32[]{:S(2)}) collective-permute-start(f32[8,4,256]{2,1,0:T(4,128)S(1)} %bitcast.134), channel_id=1, source_target_pairs={{0,1},{1,2},{2,3},{3,4},{4,5},{5,6},{6,7},{7,8},{8,9},{9,10},{10,1... | collective-permute-start | bytes 98312 | tf_op jit(solution)/shard_map/ppermute | solution.py:16
  98.8 3.6 %collective-permute-start.8 = (f32[8,4,256]{2,1,0:T(4,128)S(1)}, f32[8,4,256]{2,1,0:T(4,128)S(1)}, u32[]{:S(2)}, u32[]{:S(2)}) collective-permute-start(f32[8,4,256]{2,1,0:T(4,128)S(1)} %bitcast.135), channel_id=1, source_target_pairs={{0,2},{1,3},{2,4},{3,5},{4,6},{5,7},{6,8},{7,9},{8,10},{9,11},{10,... | collective-permute-start | bytes 98312 | tf_op jit(solution)/shard_map/ppermute | solution.py:16
  102.4 1.9 %multiply_reduce_fusion.3 = (f32[]{:T(128)}, f32[]{:T(128)}, f32[]{:T(128)}, f32[256,128]{1,0:T(8,128)S(1)}, f32[256,128]{1,0:T(8,128)S(1)}) fusion(f32[256,128]{1,0:T(8,128)S(1)} %fusion.241, f32[256,128]{1,0:T(8,128)} %get-tuple-element.36, f32[128,128]{1,0:T(8,128)S(1)} %copy-done.1), kind=kOutput, calls=%fused_computation.275 | convolution fusion | flops 50561020 | bytes 589836 | tf_op jit(solution)/shard_map/dot_general | solution.py:160
  110.9 11.9 %all-to-all-start.3 = ((f32[256,1,3]{2,1,0:T(1,128)}), f32[256,1,3]{2,1,0:T(1,128)S(1)}, u32[]{:S(2)}, u32[]{:S(2)}) async-start(f32[256,1,3]{2,1,0:T(1,128)} %broadcast_in_dim.34), calls=%async_computation.3 | async-start | bytes 262144 | tf_op jit(solution)/shard_map/all_to_all | solution.py:52
  123.9 11.9 %all-to-all-done.3 = f32[256,1,3]{2,1,0:T(1,128)S(1)} async-done(((f32[256,1,3]{2,1,0:T(1,128)}), f32[256,1,3]{2,1,0:T(1,128)S(1)}, u32[]{:S(2)}, u32[]{:S(2)}) %all-to-all-start.3) | async-done | bytes 3104 | tf_op jit(solution)/shard_map/all_to_all | solution.py:52
  142.6 1.7 fusion.1
  145.4 3.6 %all-to-all-start.4 = ((f32[4,4,64,128]{3,2,1,0:T(8,128)}), f32[4,4,64,128]{3,2,1,0:T(8,128)S(1)}, u32[]{:S(2)}, u32[]{:S(2)}) async-start(f32[4,4,64,128]{3,2,1,0:T(8,128)} %bitcast.103), calls=%async_computation.4 | async-start | bytes 1048576 | tf_op jit(solution)/shard_map/all_to_all | solution.py:152
  151.0 6.8 %all-to-all-done.4 = f32[4,4,64,128]{3,2,1,0:T(8,128)S(1)} async-done(((f32[4,4,64,128]{3,2,1,0:T(8,128)}), f32[4,4,64,128]{3,2,1,0:T(8,128)S(1)}, u32[]{:S(2)}, u32[]{:S(2)}) %all-to-all-start.4) | async-done | bytes 524320 | tf_op jit(solution)/shard_map/all_to_all | solution.py:152
  160.6 19.5 %all_to_all.33 = f32[256,1,1]{2,1,0:T(1,128)S(1)} all-to-all(f32[256,1,1]{2,1,0:T(1,128)S(1)} %broadcast_in_dim.35), channel_id=1, replica_groups=mesh['mem'=4,'col'=64] {'mem','col'}, dimensions={0} | all-to-all | bytes 2048 | tf_op jit(solution)/shard_map/all_to_all | solution.py:52
  (125 shorter events, 37.2 us)
Async XLA Ops:
  0.6 41.3 %copy-start = (bf16[8,4,256,128]{3,2,1,0:T(8,128)(2,1)S(1)}, bf16[8,4,256,128]{3,2,1,0:T(8,128)(2,1)}, u32[]{:S(2)}) copy-start(bf16[8,4,256,128]{3,2,1,0:T(8,128)(2,1)} %param.9) | copy-start | bytes 6291460
  0.6 21.7 %copy-start.9 = (f32[4,256]{1,0:T(4,128)S(1)}, f32[4,256]{1,0:T(4,128)}, u32[]{:S(2)}) copy-start(f32[4,256]{1,0:T(4,128)} %param.14) | copy-start | bytes 12292
  0.7 39.8 %copy-start.2 = (f32[128,128]{1,0:T(8,128)S(1)}, f32[128,128]{1,0:T(8,128)}, u32[]{:S(2)}) copy-start(f32[128,128]{1,0:T(8,128)} %param.11) | copy-start | bytes 196612
  0.7 39.8 %copy-start.10 = (f32[128]{0:T(128)S(1)}, f32[128]{0:T(128)}, u32[]{:S(2)}) copy-start(f32[128]{0:T(128)} %param.13) | copy-start | bytes 1540
  9.2 30.7 %all-to-all-start = ((f32[64,9,128]{2,1,0:T(8,128)}), f32[64,9,128]{2,1,0:T(8,128)S(1)}, u32[]{:S(2)}, u32[]{:S(2)}) async-start(f32[64,9,128]{2,1,0:T(8,128)} %pad_maximum_fusion), calls=%async_computation | async-start | bytes 1048576 | tf_op jit(solution)/shard_map/all_to_all | solution.py:99
  22.4 13.8 %collective-permute-start.6 = (f32[4,256]{1,0:T(4,128)S(1)}, f32[4,256]{1,0:T(4,128)S(1)}, u32[]{:S(2)}, u32[]{:S(2)}) collective-permute-start(f32[4,256]{1,0:T(4,128)S(1)} %copy-done.9), channel_id=1, source_target_pairs={{1,0},{2,1},{3,2},{4,3},{5,4},{6,5},{7,6},{8,7},{9,8},{10,9},{11,1... | collective-permute-start | bytes 12296 | tf_op jit(solution)/shard_map/ppermute | solution.py:17
  24.8 11.4 %collective-permute-start.5 = (f32[4,256]{1,0:T(4,128)S(1)}, f32[4,256]{1,0:T(4,128)S(1)}, u32[]{:S(2)}, u32[]{:S(2)}) collective-permute-start(f32[4,256]{1,0:T(4,128)S(1)} %copy-done.9), channel_id=1, source_target_pairs={{0,1},{1,2},{2,3},{3,4},{4,5},{5,6},{6,7},{7,8},{8,9},{9,10},{10,1... | collective-permute-start | bytes 12296 | tf_op jit(solution)/shard_map/ppermute | solution.py:16
  28.0 8.2 %collective-permute-start.4 = (f32[4,256]{1,0:T(4,128)S(1)}, f32[4,256]{1,0:T(4,128)S(1)}, u32[]{:S(2)}, u32[]{:S(2)}) collective-permute-start(f32[4,256]{1,0:T(4,128)S(1)} %copy-done.9), channel_id=1, source_target_pairs={{0,2},{1,3},{2,4},{3,5},{4,6},{5,7},{6,8},{7,9},{8,10},{9,11},{10,... | collective-permute-start | bytes 12296 | tf_op jit(solution)/shard_map/ppermute | solution.py:16
  31.2 4.9 %collective-permute-start.7 = (f32[4,256]{1,0:T(4,128)S(1)}, f32[4,256]{1,0:T(4,128)S(1)}, u32[]{:S(2)}, u32[]{:S(2)}) collective-permute-start(f32[4,256]{1,0:T(4,128)S(1)} %copy-done.9), channel_id=1, source_target_pairs={{2,0},{3,1},{4,2},{5,3},{6,4},{7,5},{8,6},{9,7},{10,8},{11,9},{12,... | collective-permute-start | bytes 12296 | tf_op jit(solution)/shard_map/ppermute | solution.py:17
  40.4 36.5 %copy-start.3 = (f32[512]{0:T(512)}, f32[512]{0:T(512)S(1)}, u32[]{:S(2)}) copy-start(f32[512]{0:T(512)S(1)} %mul.265) | copy-start | bytes 6148
  42.0 14.5 %copy-start.1 = (f32[128,128]{1,0:T(8,128)S(1)}, f32[128,128]{1,0:T(8,128)}, u32[]{:S(2)}) copy-start(f32[128,128]{1,0:T(8,128)} %param.10) | copy-start | bytes 196612
  45.5 11.6 %collective-permute-start.3 = (f32[8,4,256]{2,1,0:T(4,128)S(1)}, f32[8,4,256]{2,1,0:T(4,128)S(1)}, u32[]{:S(2)}, u32[]{:S(2)}) collective-permute-start(f32[8,4,256]{2,1,0:T(4,128)S(1)} %bitcast.127), channel_id=1, source_target_pairs={{2,0},{3,1},{4,2},{5,3},{6,4},{7,5},{8,6},{9,7},{10,8},{11,9},{12,... | collective-permute-start | bytes 98312 | tf_op jit(solution)/shard_map/ppermute | solution.py:17
  46.8 10.3 %collective-permute-start.2 = (f32[8,4,256]{2,1,0:T(4,128)S(1)}, f32[8,4,256]{2,1,0:T(4,128)S(1)}, u32[]{:S(2)}, u32[]{:S(2)}) collective-permute-start(f32[8,4,256]{2,1,0:T(4,128)S(1)} %bitcast.128), channel_id=1, source_target_pairs={{1,0},{2,1},{3,2},{4,3},{5,4},{6,5},{7,6},{8,7},{9,8},{10,9},{11,1... | collective-permute-start | bytes 98312 | tf_op jit(solution)/shard_map/ppermute | solution.py:17
  49.1 7.9 %collective-permute-start.1 = (f32[8,4,256]{2,1,0:T(4,128)S(1)}, f32[8,4,256]{2,1,0:T(4,128)S(1)}, u32[]{:S(2)}, u32[]{:S(2)}) collective-permute-start(f32[8,4,256]{2,1,0:T(4,128)S(1)} %bitcast.129), channel_id=1, source_target_pairs={{0,1},{1,2},{2,3},{3,4},{4,5},{5,6},{6,7},{7,8},{8,9},{9,10},{10,1... | collective-permute-start | bytes 98312 | tf_op jit(solution)/shard_map/ppermute | solution.py:16
  53.3 4.3 %collective-permute-start = (f32[8,4,256]{2,1,0:T(4,128)S(1)}, f32[8,4,256]{2,1,0:T(4,128)S(1)}, u32[]{:S(2)}, u32[]{:S(2)}) collective-permute-start(f32[8,4,256]{2,1,0:T(4,128)S(1)} %bitcast.130), channel_id=1, source_target_pairs={{0,2},{1,3},{2,4},{3,5},{4,6},{5,7},{6,8},{7,9},{8,10},{9,11},{10,... | collective-permute-start | bytes 98312 | tf_op jit(solution)/shard_map/ppermute | solution.py:16
  62.8 13.1 %all-to-all-start.1 = ((f32[4,4,64,128]{3,2,1,0:T(8,128)}), f32[4,4,64,128]{3,2,1,0:T(8,128)S(1)}, u32[]{:S(2)}, u32[]{:S(2)}) async-start(f32[4,4,64,128]{3,2,1,0:T(8,128)} %copy.62), calls=%async_computation.1 | async-start | bytes 1048576 | tf_op jit(solution)/shard_map/all_to_all | solution.py:152
  88.6 15.7 %collective-permute-start.11 = (f32[8,4,256]{2,1,0:T(4,128)S(1)}, f32[8,4,256]{2,1,0:T(4,128)S(1)}, u32[]{:S(2)}, u32[]{:S(2)}) collective-permute-start(f32[8,4,256]{2,1,0:T(4,128)S(1)} %bitcast.132), channel_id=1, source_target_pairs={{2,0},{3,1},{4,2},{5,3},{6,4},{7,5},{8,6},{9,7},{10,8},{11,9},{12,... | collective-permute-start | bytes 98312 | tf_op jit(solution)/shard_map/ppermute | solution.py:17
  89.9 14.4 %collective-permute-start.10 = (f32[8,4,256]{2,1,0:T(4,128)S(1)}, f32[8,4,256]{2,1,0:T(4,128)S(1)}, u32[]{:S(2)}, u32[]{:S(2)}) collective-permute-start(f32[8,4,256]{2,1,0:T(4,128)S(1)} %bitcast.133), channel_id=1, source_target_pairs={{1,0},{2,1},{3,2},{4,3},{5,4},{6,5},{7,6},{8,7},{9,8},{10,9},{11,1... | collective-permute-start | bytes 98312 | tf_op jit(solution)/shard_map/ppermute | solution.py:17
  94.3 10.0 %collective-permute-start.9 = (f32[8,4,256]{2,1,0:T(4,128)S(1)}, f32[8,4,256]{2,1,0:T(4,128)S(1)}, u32[]{:S(2)}, u32[]{:S(2)}) collective-permute-start(f32[8,4,256]{2,1,0:T(4,128)S(1)} %bitcast.134), channel_id=1, source_target_pairs={{0,1},{1,2},{2,3},{3,4},{4,5},{5,6},{6,7},{7,8},{8,9},{9,10},{10,1... | collective-permute-start | bytes 98312 | tf_op jit(solution)/shard_map/ppermute | solution.py:16
  98.8 5.5 %collective-permute-start.8 = (f32[8,4,256]{2,1,0:T(4,128)S(1)}, f32[8,4,256]{2,1,0:T(4,128)S(1)}, u32[]{:S(2)}, u32[]{:S(2)}) collective-permute-start(f32[8,4,256]{2,1,0:T(4,128)S(1)} %bitcast.135), channel_id=1, source_target_pairs={{0,2},{1,3},{2,4},{3,5},{4,6},{5,7},{6,8},{7,9},{8,10},{9,11},{10,... | collective-permute-start | bytes 98312 | tf_op jit(solution)/shard_map/ppermute | solution.py:16
  110.9 24.8 %all-to-all-start.3 = ((f32[256,1,3]{2,1,0:T(1,128)}), f32[256,1,3]{2,1,0:T(1,128)S(1)}, u32[]{:S(2)}, u32[]{:S(2)}) async-start(f32[256,1,3]{2,1,0:T(1,128)} %broadcast_in_dim.34), calls=%async_computation.3 | async-start | bytes 262144 | tf_op jit(solution)/shard_map/all_to_all | solution.py:52
  144.3 13.5 %copy-start.6 = (s32[1024]{0:T(1024)S(1)}, s32[1024]{0:T(1024)}, u32[]{:S(2)}) copy-start(s32[1024]{0:T(1024)} %copy-done.5) | copy-start | bytes 12292
  145.4 13.4 %copy-start.11 = (f32[128]{0:T(128)S(1)}, f32[128]{0:T(128)}, u32[]{:S(2)}) copy-start(f32[128]{0:T(128)} %param.13) | copy-start | bytes 1540
  145.4 12.3 %all-to-all-start.4 = ((f32[4,4,64,128]{3,2,1,0:T(8,128)}), f32[4,4,64,128]{3,2,1,0:T(8,128)S(1)}, u32[]{:S(2)}, u32[]{:S(2)}) async-start(f32[4,4,64,128]{3,2,1,0:T(8,128)} %bitcast.103), calls=%async_computation.4 | async-start | bytes 1048576 | tf_op jit(solution)/shard_map/all_to_all | solution.py:152
  (4 other events, 48.6 us)

commit v9 on v7

--- a/solution.py
+++ b/solution.py
@@ -187,16 +187,16 @@
     own_image0, model_obs = observed(partial0)
     adj_static, adj_projected = observed_adjoint(model_obs)
     image = (right_static + adj_static, right_ensemble + sweeps(adj_projected, coeffs))
-    sums = global_sum(
-        jnp.stack(
-            [
-                local_inner(direction, direction),
-                local_inner(direction, image),
-                local_inner(image, image),
-            ]
-        )
-    )
-    smoothed_image = sweeps(image[1], coeffs)
+    local_sums = jnp.stack(
+        [
+            local_inner(direction, direction),
+            local_inner(direction, image),
+            local_inner(image, image),
+        ]
+    )
+    rimmed, local_sums = lax.optimization_barrier((neighbours(image[1], "col", 1, 1), local_sums))
+    sums = global_sum(local_sums)
+    smoothed_image = sweep_steps(rimmed, coeffs, NSWEEP)[:, rows_here : 2 * rows_here]
     norm_now, curve, image_norm = sums[0], sums[1], sums[2]
     step0 = norm_now / curve
     state = (step0 * direction[0], step0 * direction[1])

time: 180 us -> 187 us (1.039)
  waiting for transfers between devices: 35.8 us -> 40.5 us
    all_to_all x1, waiting for transfers between devices: 6.87 us -> 11.6 us  [global_sum(): return jnp.sum(lax.all_to_all(spread, axes, 0, 0, tiled=True), axis=0)]
    ppermute x6, starting transfers between devices: 15.7 us -> 13.6 us  [neighbours(): above.append(lax.ppermute(block, axis, backward))]
where the time goes in v9:
time: 187 us; the launch traced here: 186 us
  starting transfers between devices  71.6 us (38%)
  waiting for transfers between devices  40.5 us (22%)
  blocking collectives  19.5 us (10%)
  matrix products  14.3 us (8%)
  local copies, waits for them, and re-layouts  14.1 us (8%)
  other arithmetic  13.3 us (7%)
  between operations  12.5 us (7%)
    ppermute x6, starting transfers between devices, neighbours(): below.insert(0, lax.ppermute(block, axis, forward))  21.1 us
    all_to_all x1, blocking collectives, global_sum(): return jnp.sum(lax.all_to_all(spread, axes, 0, 0, tiled=True), axis=0)  19.5 us
    all_to_all x2, waiting for transfers between devices, observed(): own_image = jnp.sum(lax.all_to_all(pieces, 'mem', 0, 0, tiled=True), axis=0)  15.8 us
    ppermute x6, starting transfers between devices, neighbours(): above.append(lax.ppermute(block, axis, backward))  13.6 us
    all_to_all x1, starting transfers between devices, shards(): got = lax.all_to_all(packed, 'col', split_axis=0, concat_axis=0, tiled=True)  13.1 us
    all_to_all x1, starting transfers between devices, global_sum(): return jnp.sum(lax.all_to_all(spread, axes, 0, 0, tiled=True), axis=0)  12.8 us
    all_to_all x1, waiting for transfers between devices, global_sum(): return jnp.sum(lax.all_to_all(spread, axes, 0, 0, tiled=True), axis=0)  11.6 us
    all_to_all x2, starting transfers between devices, observed(): own_image = jnp.sum(lax.all_to_all(pieces, 'mem', 0, 0, tiled=True), axis=0)  7.62 us
  transfers between devices with their start and end apart: 17, of which 7 were waited for; matrix products, arithmetic and copies ran while one was open for 3% of the time, Pallas kernels for 0%

profile of v9, /device:TPU:1, one launch (start us, length us, event | category | flops | bytes accessed | tf_op | source)
XLA Modules:
  0.0 185.7 jit_solution(3826965153919068536)
XLA Ops:
  9.2 13.1 %all-to-all-start = ((f32[64,9,128]{2,1,0:T(8,128)}), f32[64,9,128]{2,1,0:T(8,128)S(1)}, u32[]{:S(2)}, u32[]{:S(2)}) async-start(f32[64,9,128]{2,1,0:T(8,128)} %pad_maximum_fusion), calls=%async_computation | async-start | bytes 1048576 | tf_op jit(solution)/shard_map/all_to_all | solution.py:106
  22.4 2.4 %collective-permute-start.6 = (f32[4,256]{1,0:T(4,128)S(1)}, f32[4,256]{1,0:T(4,128)S(1)}, u32[]{:S(2)}, u32[]{:S(2)}) collective-permute-start(f32[4,256]{1,0:T(4,128)S(1)} %copy-done.9), channel_id=1, source_target_pairs={{1,0},{2,1},{3,2},{4,3},{5,4},{6,5},{7,6},{8,7},{9,8},{10,9},{11,1... | collective-permute-start | bytes 12296 | tf_op jit(solution)/shard_map/ppermute | solution.py:17
  24.8 3.2 %collective-permute-start.5 = (f32[4,256]{1,0:T(4,128)S(1)}, f32[4,256]{1,0:T(4,128)S(1)}, u32[]{:S(2)}, u32[]{:S(2)}) collective-permute-start(f32[4,256]{1,0:T(4,128)S(1)} %copy-done.9), channel_id=1, source_target_pairs={{0,1},{1,2},{2,3},{3,4},{4,5},{5,6},{6,7},{7,8},{8,9},{9,10},{10,1... | collective-permute-start | bytes 12296 | tf_op jit(solution)/shard_map/ppermute | solution.py:16
  28.0 3.3 %collective-permute-start.4 = (f32[4,256]{1,0:T(4,128)S(1)}, f32[4,256]{1,0:T(4,128)S(1)}, u32[]{:S(2)}, u32[]{:S(2)}) collective-permute-start(f32[4,256]{1,0:T(4,128)S(1)} %copy-done.9), channel_id=1, source_target_pairs={{0,2},{1,3},{2,4},{3,5},{4,6},{5,7},{6,8},{7,9},{8,10},{9,11},{10,... | collective-permute-start | bytes 12296 | tf_op jit(solution)/shard_map/ppermute | solution.py:16
  32.5 3.6 %collective-permute-done.6 = f32[4,256]{1,0:T(4,128)S(1)} collective-permute-done((f32[4,256]{1,0:T(4,128)S(1)}, f32[4,256]{1,0:T(4,128)S(1)}, u32[]{:S(2)}, u32[]{:S(2)}) %collective-permute-start.6) | collective-permute-done | bytes 4128 | tf_op jit(solution)/shard_map/ppermute | solution.py:17
  36.4 3.6 %all-to-all-done = f32[64,9,128]{2,1,0:T(8,128)S(1)} async-done(((f32[64,9,128]{2,1,0:T(8,128)}), f32[64,9,128]{2,1,0:T(8,128)S(1)}, u32[]{:S(2)}, u32[]{:S(2)}) %all-to-all-start) | async-done | bytes 294944 | tf_op jit(solution)/shard_map/all_to_all | solution.py:106
  42.0 2.4 %fusion.7 = f32[4,256,1,8]{3,2,1,0:T(1,128)} fusion(bf16[8,4,256,128]{3,2,1,0:T(8,128)(2,1)S(1)} %copy-done, bf16[4,256,128,1]{2,1,0,3:T(8,128)(2,1)S(1)} %convert_bitcast_fusion), kind=kOutput, calls=%fused_computation.12 | convolution fusion | flops 2097152 | bytes 2392064 | tf_op jit(solution)/shard_map/kyxf,yxf->kyx/dot_general | solution.py:130
  46.8 2.3 %collective-permute-start.2 = (f32[8,4,256]{2,1,0:T(4,128)S(1)}, f32[8,4,256]{2,1,0:T(4,128)S(1)}, u32[]{:S(2)}, u32[]{:S(2)}) collective-permute-start(f32[8,4,256]{2,1,0:T(4,128)S(1)} %bitcast.131), channel_id=1, source_target_pairs={{1,0},{2,1},{3,2},{4,3},{5,4},{6,5},{7,6},{8,7},{9,8},{10,9},{11,1... | collective-permute-start | bytes 98312 | tf_op jit(solution)/shard_map/ppermute | solution.py:17
  49.1 4.2 %collective-permute-start.1 = (f32[8,4,256]{2,1,0:T(4,128)S(1)}, f32[8,4,256]{2,1,0:T(4,128)S(1)}, u32[]{:S(2)}, u32[]{:S(2)}) collective-permute-start(f32[8,4,256]{2,1,0:T(4,128)S(1)} %bitcast.132), channel_id=1, source_target_pairs={{0,1},{1,2},{2,3},{3,4},{4,5},{5,6},{6,7},{7,8},{8,9},{9,10},{10,1... | collective-permute-start | bytes 98312 | tf_op jit(solution)/shard_map/ppermute | solution.py:16
  53.3 3.1 %collective-permute-start = (f32[8,4,256]{2,1,0:T(4,128)S(1)}, f32[8,4,256]{2,1,0:T(4,128)S(1)}, u32[]{:S(2)}, u32[]{:S(2)}) collective-permute-start(f32[8,4,256]{2,1,0:T(4,128)S(1)} %bitcast.133), channel_id=1, source_target_pairs={{0,2},{1,3},{2,4},{3,5},{4,6},{5,7},{6,8},{7,9},{8,10},{9,11},{10,... | collective-permute-start | bytes 98312 | tf_op jit(solution)/shard_map/ppermute | solution.py:16
  62.2 4.0 %all-to-all-start.1 = ((f32[4,4,64,128]{3,2,1,0:T(8,128)}), f32[4,4,64,128]{3,2,1,0:T(8,128)S(1)}, u32[]{:S(2)}, u32[]{:S(2)}) async-start(f32[4,4,64,128]{3,2,1,0:T(8,128)} %copy.62), calls=%async_computation.1 | async-start | bytes 1048576 | tf_op jit(solution)/shard_map/all_to_all | solution.py:159
  66.3 9.0 %all-to-all-done.1 = f32[4,4,64,128]{3,2,1,0:T(8,128)S(1)} async-done(((f32[4,4,64,128]{3,2,1,0:T(8,128)}), f32[4,4,64,128]{3,2,1,0:T(8,128)S(1)}, u32[]{:S(2)}, u32[]{:S(2)}) %all-to-all-start.1) | async-done | bytes 524320 | tf_op jit(solution)/shard_map/all_to_all | solution.py:159
  78.9 3.4 %all-to-all-start.2 = ((bf16[4,4,64,128]{3,2,1,0:T(8,128)(2,1)}), bf16[4,4,64,128]{3,2,1,0:T(8,128)(2,1)S(1)}, u32[]{:S(2)}, u32[]{:S(2)}) async-start(bf16[4,4,64,128]{3,2,1,0:T(8,128)(2,1)} %broadcast_in_dim.33), calls=%async_computation.2 | async-start | bytes 524288 | tf_op jit(solution)/shard_map/all_to_all | solution.py:172
  82.4 5.4 %all-to-all-done.2 = bf16[4,4,64,128]{3,2,1,0:T(8,128)(2,1)S(1)} async-done(((bf16[4,4,64,128]{3,2,1,0:T(8,128)(2,1)}), bf16[4,4,64,128]{3,2,1,0:T(8,128)(2,1)S(1)}, u32[]{:S(2)}, u32[]{:S(2)}) %all-to-all-start.2) | async-done | bytes 262176 | tf_op jit(solution)/shard_map/all_to_all | solution.py:172
  89.7 4.4 %collective-permute-start.9 = (f32[8,4,256]{2,1,0:T(4,128)S(1)}, f32[8,4,256]{2,1,0:T(4,128)S(1)}, u32[]{:S(2)}, u32[]{:S(2)}) collective-permute-start(f32[8,4,256]{2,1,0:T(4,128)S(1)} %bitcast.126), channel_id=1, source_target_pairs={{1,0},{2,1},{3,2},{4,3},{5,4},{6,5},{7,6},{8,7},{9,8},{10,9},{11,1... | collective-permute-start | bytes 98312 | tf_op jit(solution)/shard_map/ppermute | solution.py:17
  94.1 3.8 %collective-permute-start.8 = (f32[8,4,256]{2,1,0:T(4,128)S(1)}, f32[8,4,256]{2,1,0:T(4,128)S(1)}, u32[]{:S(2)}, u32[]{:S(2)}) collective-permute-start(f32[8,4,256]{2,1,0:T(4,128)S(1)} %bitcast.127), channel_id=1, source_target_pairs={{0,1},{1,2},{2,3},{3,4},{4,5},{5,6},{6,7},{7,8},{8,9},{9,10},{10,1... | collective-permute-start | bytes 98312 | tf_op jit(solution)/shard_map/ppermute | solution.py:16
  97.9 1.9 %multiply_reduce_fusion.3 = (f32[]{:T(128)}, f32[]{:T(128)}, f32[]{:T(128)}, f32[256,128]{1,0:T(8,128)S(1)}, f32[256,128]{1,0:T(8,128)S(1)}) fusion(f32[256,128]{1,0:T(8,128)S(1)} %fusion.238, f32[256,128]{1,0:T(8,128)} %get-tuple-element.43, f32[128,128]{1,0:T(8,128)S(1)} %copy-done.1), kind=kOutput, calls=%fused_computation.264 | convolution fusion | flops 50561020 | bytes 589836 | tf_op jit(solution)/shard_map/dot_general | solution.py:167
  101.1 1.9 %collective-permute-start.11 = (f32[8,4,256]{2,1,0:T(4,128)S(1)}, f32[8,4,256]{2,1,0:T(4,128)S(1)}, u32[]{:S(2)}, u32[]{:S(2)}) collective-permute-start(f32[8,4,256]{2,1,0:T(4,128)S(1)} %get-tuple-element.15), channel_id=1, source_target_pairs={{1,0},{2,1},{3,2},{4,3},{5,4},{6,5},{7,6},{8,7},{9,8},{10,9},{11,1... | collective-permute-start | bytes 98312 | tf_op jit(solution)/shard_map/ppermute | solution.py:17
  103.1 3.6 %collective-permute-start.10 = (f32[8,4,256]{2,1,0:T(4,128)S(1)}, f32[8,4,256]{2,1,0:T(4,128)S(1)}, u32[]{:S(2)}, u32[]{:S(2)}) collective-permute-start(f32[8,4,256]{2,1,0:T(4,128)S(1)} %get-tuple-element.15), channel_id=1, source_target_pairs={{0,1},{1,2},{2,3},{3,4},{4,5},{5,6},{6,7},{7,8},{8,9},{9,10},{10,1... | collective-permute-start | bytes 98312 | tf_op jit(solution)/shard_map/ppermute | solution.py:16
  111.4 12.8 %all-to-all-start.3 = ((f32[256,1,3]{2,1,0:T(1,128)}), f32[256,1,3]{2,1,0:T(1,128)S(1)}, u32[]{:S(2)}, u32[]{:S(2)}) async-start(f32[256,1,3]{2,1,0:T(1,128)} %broadcast_in_dim.34), calls=%async_computation.3 | async-start | bytes 262144 | tf_op jit(solution)/shard_map/all_to_all | solution.py:58
  125.4 11.6 %all-to-all-done.3 = f32[256,1,3]{2,1,0:T(1,128)S(1)} async-done(((f32[256,1,3]{2,1,0:T(1,128)}), f32[256,1,3]{2,1,0:T(1,128)S(1)}, u32[]{:S(2)}, u32[]{:S(2)}) %all-to-all-start.3) | async-done | bytes 3104 | tf_op jit(solution)/shard_map/all_to_all | solution.py:58
  148.1 3.6 %all-to-all-start.4 = ((f32[4,4,64,128]{3,2,1,0:T(8,128)}), f32[4,4,64,128]{3,2,1,0:T(8,128)S(1)}, u32[]{:S(2)}, u32[]{:S(2)}) async-start(f32[4,4,64,128]{3,2,1,0:T(8,128)} %bitcast.103), calls=%async_computation.4 | async-start | bytes 1048576 | tf_op jit(solution)/shard_map/all_to_all | solution.py:159
  153.7 6.8 %all-to-all-done.4 = f32[4,4,64,128]{3,2,1,0:T(8,128)S(1)} async-done(((f32[4,4,64,128]{3,2,1,0:T(8,128)}), f32[4,4,64,128]{3,2,1,0:T(8,128)S(1)}, u32[]{:S(2)}, u32[]{:S(2)}) %all-to-all-start.4) | async-done | bytes 524320 | tf_op jit(solution)/shard_map/all_to_all | solution.py:159
  163.3 19.5 %all_to_all.32 = f32[256,1,1]{2,1,0:T(1,128)S(1)} all-to-all(f32[256,1,1]{2,1,0:T(1,128)S(1)} %broadcast_in_dim.35), channel_id=1, replica_groups=mesh['mem'=4,'col'=64] {'mem','col'}, dimensions={0} | all-to-all | bytes 2048 | tf_op jit(solution)/shard_map/all_to_all | solution.py:58
  (131 shorter events, 40.4 us)
Async XLA Ops:
  0.6 41.3 %copy-start = (bf16[8,4,256,128]{3,2,1,0:T(8,128)(2,1)S(1)}, bf16[8,4,256,128]{3,2,1,0:T(8,128)(2,1)}, u32[]{:S(2)}) copy-start(bf16[8,4,256,128]{3,2,1,0:T(8,128)(2,1)} %param.9) | copy-start | bytes 6291460
  0.6 21.7 %copy-start.9 = (f32[4,256]{1,0:T(4,128)S(1)}, f32[4,256]{1,0:T(4,128)}, u32[]{:S(2)}) copy-start(f32[4,256]{1,0:T(4,128)} %param.14) | copy-start | bytes 12292
  0.7 39.8 %copy-start.2 = (f32[128,128]{1,0:T(8,128)S(1)}, f32[128,128]{1,0:T(8,128)}, u32[]{:S(2)}) copy-start(f32[128,128]{1,0:T(8,128)} %param.11) | copy-start | bytes 196612
  0.7 39.8 %copy-start.10 = (f32[128]{0:T(128)S(1)}, f32[128]{0:T(128)}, u32[]{:S(2)}) copy-start(f32[128]{0:T(128)} %param.13) | copy-start | bytes 1540
  9.2 30.7 %all-to-all-start = ((f32[64,9,128]{2,1,0:T(8,128)}), f32[64,9,128]{2,1,0:T(8,128)S(1)}, u32[]{:S(2)}, u32[]{:S(2)}) async-start(f32[64,9,128]{2,1,0:T(8,128)} %pad_maximum_fusion), calls=%async_computation | async-start | bytes 1048576 | tf_op jit(solution)/shard_map/all_to_all | solution.py:106
  22.4 13.8 %collective-permute-start.6 = (f32[4,256]{1,0:T(4,128)S(1)}, f32[4,256]{1,0:T(4,128)S(1)}, u32[]{:S(2)}, u32[]{:S(2)}) collective-permute-start(f32[4,256]{1,0:T(4,128)S(1)} %copy-done.9), channel_id=1, source_target_pairs={{1,0},{2,1},{3,2},{4,3},{5,4},{6,5},{7,6},{8,7},{9,8},{10,9},{11,1... | collective-permute-start | bytes 12296 | tf_op jit(solution)/shard_map/ppermute | solution.py:17
  24.8 11.4 %collective-permute-start.5 = (f32[4,256]{1,0:T(4,128)S(1)}, f32[4,256]{1,0:T(4,128)S(1)}, u32[]{:S(2)}, u32[]{:S(2)}) collective-permute-start(f32[4,256]{1,0:T(4,128)S(1)} %copy-done.9), channel_id=1, source_target_pairs={{0,1},{1,2},{2,3},{3,4},{4,5},{5,6},{6,7},{7,8},{8,9},{9,10},{10,1... | collective-permute-start | bytes 12296 | tf_op jit(solution)/shard_map/ppermute | solution.py:16
  28.0 8.2 %collective-permute-start.4 = (f32[4,256]{1,0:T(4,128)S(1)}, f32[4,256]{1,0:T(4,128)S(1)}, u32[]{:S(2)}, u32[]{:S(2)}) collective-permute-start(f32[4,256]{1,0:T(4,128)S(1)} %copy-done.9), channel_id=1, source_target_pairs={{0,2},{1,3},{2,4},{3,5},{4,6},{5,7},{6,8},{7,9},{8,10},{9,11},{10,... | collective-permute-start | bytes 12296 | tf_op jit(solution)/shard_map/ppermute | solution.py:16
  31.2 4.9 %collective-permute-start.7 = (f32[4,256]{1,0:T(4,128)S(1)}, f32[4,256]{1,0:T(4,128)S(1)}, u32[]{:S(2)}, u32[]{:S(2)}) collective-permute-start(f32[4,256]{1,0:T(4,128)S(1)} %copy-done.9), channel_id=1, source_target_pairs={{2,0},{3,1},{4,2},{5,3},{6,4},{7,5},{8,6},{9,7},{10,8},{11,9},{12,... | collective-permute-start | bytes 12296 | tf_op jit(solution)/shard_map/ppermute | solution.py:17
  40.4 35.9 %copy-start.3 = (f32[512]{0:T(512)}, f32[512]{0:T(512)S(1)}, u32[]{:S(2)}) copy-start(f32[512]{0:T(512)S(1)} %mul.273) | copy-start | bytes 6148
  42.0 14.5 %copy-start.1 = (f32[128,128]{1,0:T(8,128)S(1)}, f32[128,128]{1,0:T(8,128)}, u32[]{:S(2)}) copy-start(f32[128,128]{1,0:T(8,128)} %param.10) | copy-start | bytes 196612
  45.5 11.6 %collective-permute-start.3 = (f32[8,4,256]{2,1,0:T(4,128)S(1)}, f32[8,4,256]{2,1,0:T(4,128)S(1)}, u32[]{:S(2)}, u32[]{:S(2)}) collective-permute-start(f32[8,4,256]{2,1,0:T(4,128)S(1)} %bitcast.130), channel_id=1, source_target_pairs={{2,0},{3,1},{4,2},{5,3},{6,4},{7,5},{8,6},{9,7},{10,8},{11,9},{12,... | collective-permute-start | bytes 98312 | tf_op jit(solution)/shard_map/ppermute | solution.py:17
  46.8 10.3 %collective-permute-start.2 = (f32[8,4,256]{2,1,0:T(4,128)S(1)}, f32[8,4,256]{2,1,0:T(4,128)S(1)}, u32[]{:S(2)}, u32[]{:S(2)}) collective-permute-start(f32[8,4,256]{2,1,0:T(4,128)S(1)} %bitcast.131), channel_id=1, source_target_pairs={{1,0},{2,1},{3,2},{4,3},{5,4},{6,5},{7,6},{8,7},{9,8},{10,9},{11,1... | collective-permute-start | bytes 98312 | tf_op jit(solution)/shard_map/ppermute | solution.py:17
  49.1 7.9 %collective-permute-start.1 = (f32[8,4,256]{2,1,0:T(4,128)S(1)}, f32[8,4,256]{2,1,0:T(4,128)S(1)}, u32[]{:S(2)}, u32[]{:S(2)}) collective-permute-start(f32[8,4,256]{2,1,0:T(4,128)S(1)} %bitcast.132), channel_id=1, source_target_pairs={{0,1},{1,2},{2,3},{3,4},{4,5},{5,6},{6,7},{7,8},{8,9},{9,10},{10,1... | collective-permute-start | bytes 98312 | tf_op jit(solution)/shard_map/ppermute | solution.py:16
  53.3 4.3 %collective-permute-start = (f32[8,4,256]{2,1,0:T(4,128)S(1)}, f32[8,4,256]{2,1,0:T(4,128)S(1)}, u32[]{:S(2)}, u32[]{:S(2)}) collective-permute-start(f32[8,4,256]{2,1,0:T(4,128)S(1)} %bitcast.133), channel_id=1, source_target_pairs={{0,2},{1,3},{2,4},{3,5},{4,6},{5,7},{6,8},{7,9},{8,10},{9,11},{10,... | collective-permute-start | bytes 98312 | tf_op jit(solution)/shard_map/ppermute | solution.py:16
  62.2 13.1 %all-to-all-start.1 = ((f32[4,4,64,128]{3,2,1,0:T(8,128)}), f32[4,4,64,128]{3,2,1,0:T(8,128)S(1)}, u32[]{:S(2)}, u32[]{:S(2)}) async-start(f32[4,4,64,128]{3,2,1,0:T(8,128)} %copy.62), calls=%async_computation.1 | async-start | bytes 1048576 | tf_op jit(solution)/shard_map/all_to_all | solution.py:159
  78.9 8.9 %all-to-all-start.2 = ((bf16[4,4,64,128]{3,2,1,0:T(8,128)(2,1)}), bf16[4,4,64,128]{3,2,1,0:T(8,128)(2,1)S(1)}, u32[]{:S(2)}, u32[]{:S(2)}) async-start(bf16[4,4,64,128]{3,2,1,0:T(8,128)(2,1)} %broadcast_in_dim.33), calls=%async_computation.2 | async-start | bytes 524288 | tf_op jit(solution)/shard_map/all_to_all | solution.py:172
  89.7 10.1 %collective-permute-start.9 = (f32[8,4,256]{2,1,0:T(4,128)S(1)}, f32[8,4,256]{2,1,0:T(4,128)S(1)}, u32[]{:S(2)}, u32[]{:S(2)}) collective-permute-start(f32[8,4,256]{2,1,0:T(4,128)S(1)} %bitcast.126), channel_id=1, source_target_pairs={{1,0},{2,1},{3,2},{4,3},{5,4},{6,5},{7,6},{8,7},{9,8},{10,9},{11,1... | collective-permute-start | bytes 98312 | tf_op jit(solution)/shard_map/ppermute | solution.py:17
  94.1 5.7 %collective-permute-start.8 = (f32[8,4,256]{2,1,0:T(4,128)S(1)}, f32[8,4,256]{2,1,0:T(4,128)S(1)}, u32[]{:S(2)}, u32[]{:S(2)}) collective-permute-start(f32[8,4,256]{2,1,0:T(4,128)S(1)} %bitcast.127), channel_id=1, source_target_pairs={{0,1},{1,2},{2,3},{3,4},{4,5},{5,6},{6,7},{7,8},{8,9},{9,10},{10,1... | collective-permute-start | bytes 98312 | tf_op jit(solution)/shard_map/ppermute | solution.py:16
  101.1 9.5 %collective-permute-start.11 = (f32[8,4,256]{2,1,0:T(4,128)S(1)}, f32[8,4,256]{2,1,0:T(4,128)S(1)}, u32[]{:S(2)}, u32[]{:S(2)}) collective-permute-start(f32[8,4,256]{2,1,0:T(4,128)S(1)} %get-tuple-element.15), channel_id=1, source_target_pairs={{1,0},{2,1},{3,2},{4,3},{5,4},{6,5},{7,6},{8,7},{9,8},{10,9},{11,1... | collective-permute-start | bytes 98312 | tf_op jit(solution)/shard_map/ppermute | solution.py:17
  103.1 7.6 %collective-permute-start.10 = (f32[8,4,256]{2,1,0:T(4,128)S(1)}, f32[8,4,256]{2,1,0:T(4,128)S(1)}, u32[]{:S(2)}, u32[]{:S(2)}) collective-permute-start(f32[8,4,256]{2,1,0:T(4,128)S(1)} %get-tuple-element.15), channel_id=1, source_target_pairs={{0,1},{1,2},{2,3},{3,4},{4,5},{5,6},{6,7},{7,8},{8,9},{9,10},{10,1... | collective-permute-start | bytes 98312 | tf_op jit(solution)/shard_map/ppermute | solution.py:16
  111.4 25.6 %all-to-all-start.3 = ((f32[256,1,3]{2,1,0:T(1,128)}), f32[256,1,3]{2,1,0:T(1,128)S(1)}, u32[]{:S(2)}, u32[]{:S(2)}) async-start(f32[256,1,3]{2,1,0:T(1,128)} %broadcast_in_dim.34), calls=%async_computation.3 | async-start | bytes 262144 | tf_op jit(solution)/shard_map/all_to_all | solution.py:58
  147.0 13.5 %copy-start.6 = (s32[1024]{0:T(1024)S(1)}, s32[1024]{0:T(1024)}, u32[]{:S(2)}) copy-start(s32[1024]{0:T(1024)} %copy-done.5) | copy-start | bytes 12292
  148.1 12.3 %all-to-all-start.4 = ((f32[4,4,64,128]{3,2,1,0:T(8,128)}), f32[4,4,64,128]{3,2,1,0:T(8,128)S(1)}, u32[]{:S(2)}, u32[]{:S(2)}) async-start(f32[4,4,64,128]{3,2,1,0:T(8,128)} %bitcast.103), calls=%async_computation.4 | async-start | bytes 1048576 | tf_op jit(solution)/shard_map/all_to_all | solution.py:159
  (5 other events, 62.0 us)

commit v10 on v7

--- a/solution.py
+++ b/solution.py
@@ -132,18 +132,21 @@
         )
         return static, projected
 
+    split_perturbations = perturbations.reshape(members, rows_here, parts, quarter, features)
+    mem_index = lax.axis_index("mem")
+
     def forward_partial(static_part, smoothed_field):
-        smoothed = smoothed_field.astype(jnp.bfloat16)
+        smoothed = smoothed_field.astype(jnp.bfloat16).reshape(members, rows_here, parts, quarter)
         partial_sum = jnp.einsum(
-            "kyxf,kyx->yxf", perturbations, smoothed, preferred_element_type=jnp.float32
+            "kyqxf,kyqx->qyxf", split_perturbations, smoothed, preferred_element_type=jnp.float32
         )
         forward_static = jnp.dot(
             static_part.reshape(rows_here * quarter, features),
             static_root,
             precision=lax.Precision.HIGHEST,
         ).reshape(rows_here, quarter, features)
-        own_slice = lax.dynamic_slice_in_dim(partial_sum, offset, quarter, 1) + forward_static
-        return lax.dynamic_update_slice_in_dim(partial_sum, own_slice, offset, 1)
+        own_slice = lax.dynamic_index_in_dim(partial_sum, mem_index, 0, keepdims=False) + forward_static
+        return lax.dynamic_update_index_in_dim(partial_sum, own_slice, mem_index, 0)
 
     cell_x = obs_index % columns
     in_quarter = (cell_x >= offset) & (cell_x < offset + quarter)
@@ -155,8 +158,7 @@
     ).astype(jnp.float32)
 
     def observed(partial_sum):
-        pieces = jnp.moveaxis(partial_sum.reshape(rows_here, parts, quarter, features), 1, 0)
-        own_image = jnp.sum(lax.all_to_all(pieces, "mem", 0, 0, tiled=True), axis=0)
+        own_image = jnp.sum(lax.all_to_all(partial_sum, "mem", 0, 0, tiled=True), axis=0)
         gathered = own_image.reshape(rows_here * quarter, features)[quarter_index]
         model_obs = jnp.dot(gathered, obs_jacobian, precision=lax.Precision.HIGHEST)
         return own_image, model_obs
@@ -170,10 +172,9 @@
         rounded = own_gradient.reshape(rows_here, quarter, features).astype(jnp.bfloat16)
         spread = jnp.broadcast_to(rounded[None], (parts,) + rounded.shape)
         quarters = lax.all_to_all(spread, "mem", 0, 0, tiled=True)
-        rounded = jnp.moveaxis(quarters, 0, 1).reshape(rows_here, columns, features)
         projected = jnp.einsum(
-            "kyxf,yxf->kyx", perturbations, rounded, preferred_element_type=jnp.float32
-        )
+            "kyqxf,qyxf->kyqx", split_perturbations, quarters, preferred_element_type=jnp.float32
+        ).reshape(members, rows_here, columns)
         return static, projected
 
     right_static, right_projected = adjoint_parts(spread_back(obs_gain * got_values))

time: 180 us -> 185 us (1.028)
  matrix products: 14.3 us -> 17.5 us
    dot_general x3, matrix products: 4.99 us -> 7.56 us  [the longest x2 5.03 us: forward_partial(): jnp.einsum('kyqxf,kyqx->qyxf', split_perturbations, smoothed, preferred_e...]
where the time goes in v10:
time: 185 us; the launch traced here: 184 us
  starting transfers between devices  71.6 us (39%)
  waiting for transfers between devices  35.9 us (19%)
  blocking collectives  19.5 us (11%)
  matrix products  17.5 us (9%)
  other arithmetic  13.9 us (8%)
  local copies, waits for them, and re-layouts  12.8 us (7%)
  between operations  12.6 us (7%)
    all_to_all x1, blocking collectives, global_sum(): return jnp.sum(lax.all_to_all(spread, axes, 0, 0, tiled=True), axis=0)  19.5 us
    ppermute x6, starting transfers between devices, neighbours(): below.insert(0, lax.ppermute(block, axis, forward))  19.4 us
    all_to_all x2, waiting for transfers between devices, observed(): lax.all_to_all(partial_sum, 'mem', 0, 0, tiled=True)  15.8 us
    ppermute x6, starting transfers between devices, neighbours(): above.append(lax.ppermute(block, axis, backward))  15.7 us
    all_to_all x1, starting transfers between devices, shards(): got = lax.all_to_all(packed, 'col', split_axis=0, concat_axis=0, tiled=True)  13.1 us
    all_to_all x1, starting transfers between devices, global_sum(): return jnp.sum(lax.all_to_all(spread, axes, 0, 0, tiled=True), axis=0)  11.7 us
    all_to_all x2, starting transfers between devices, observed(): lax.all_to_all(partial_sum, 'mem', 0, 0, tiled=True)  7.64 us
    all_to_all x1, waiting for transfers between devices, global_sum(): return jnp.sum(lax.all_to_all(spread, axes, 0, 0, tiled=True), axis=0)  6.87 us
  transfers between devices with their start and end apart: 17, of which 7 were waited for; matrix products, arithmetic and copies ran while one was open for 3% of the time, Pallas kernels for 0%

profile of v10, /device:TPU:1, one launch (start us, length us, event | category | flops | bytes accessed | tf_op | source)
XLA Modules:
  0.0 183.8 jit_solution(11006595770049395999)
XLA Ops:
  9.2 13.1 %all-to-all-start = ((f32[64,9,128]{2,1,0:T(8,128)}), f32[64,9,128]{2,1,0:T(8,128)S(1)}, u32[]{:S(2)}, u32[]{:S(2)}) async-start(f32[64,9,128]{2,1,0:T(8,128)} %pad_maximum_fusion), calls=%async_computation | async-start | bytes 1048576 | tf_op jit(solution)/shard_map/all_to_all | solution.py:106
  22.4 2.4 %collective-permute-start.6 = (f32[4,256]{1,0:T(4,128)S(1)}, f32[4,256]{1,0:T(4,128)S(1)}, u32[]{:S(2)}, u32[]{:S(2)}) collective-permute-start(f32[4,256]{1,0:T(4,128)S(1)} %copy-done.9), channel_id=1, source_target_pairs={{1,0},{2,1},{3,2},{4,3},{5,4},{6,5},{7,6},{8,7},{9,8},{10,9},{11,1... | collective-permute-start | bytes 12296 | tf_op jit(solution)/shard_map/ppermute | solution.py:17
  24.8 3.2 %collective-permute-start.5 = (f32[4,256]{1,0:T(4,128)S(1)}, f32[4,256]{1,0:T(4,128)S(1)}, u32[]{:S(2)}, u32[]{:S(2)}) collective-permute-start(f32[4,256]{1,0:T(4,128)S(1)} %copy-done.9), channel_id=1, source_target_pairs={{0,1},{1,2},{2,3},{3,4},{4,5},{5,6},{6,7},{7,8},{8,9},{9,10},{10,1... | collective-permute-start | bytes 12296 | tf_op jit(solution)/shard_map/ppermute | solution.py:16
  28.0 3.3 %collective-permute-start.4 = (f32[4,256]{1,0:T(4,128)S(1)}, f32[4,256]{1,0:T(4,128)S(1)}, u32[]{:S(2)}, u32[]{:S(2)}) collective-permute-start(f32[4,256]{1,0:T(4,128)S(1)} %copy-done.9), channel_id=1, source_target_pairs={{0,2},{1,3},{2,4},{3,5},{4,6},{5,7},{6,8},{7,9},{8,10},{9,11},{10,... | collective-permute-start | bytes 12296 | tf_op jit(solution)/shard_map/ppermute | solution.py:16
  32.5 3.6 %collective-permute-done.6 = f32[4,256]{1,0:T(4,128)S(1)} collective-permute-done((f32[4,256]{1,0:T(4,128)S(1)}, f32[4,256]{1,0:T(4,128)S(1)}, u32[]{:S(2)}, u32[]{:S(2)}) %collective-permute-start.6) | collective-permute-done | bytes 4128 | tf_op jit(solution)/shard_map/ppermute | solution.py:17
  36.4 3.6 %all-to-all-done = f32[64,9,128]{2,1,0:T(8,128)S(1)} async-done(((f32[64,9,128]{2,1,0:T(8,128)}), f32[64,9,128]{2,1,0:T(8,128)S(1)}, u32[]{:S(2)}, u32[]{:S(2)}) %all-to-all-start) | async-done | bytes 294944 | tf_op jit(solution)/shard_map/all_to_all | solution.py:106
  42.0 2.4 %fusion.2 = f32[4,256,1,8]{3,2,1,0:T(1,128)} fusion(bf16[8,4,256,128]{3,2,1,0:T(8,128)(2,1)S(1)} %copy-done, bf16[4,256,128,1]{2,1,0,3:T(8,128)(2,1)S(1)} %convert_bitcast_fusion), kind=kOutput, calls=%fused_computation.7 | convolution fusion | flops 2097152 | bytes 2392064 | tf_op jit(solution)/shard_map/kyxf,yxf->kyx/dot_general | solution.py:130
  49.1 4.2 %collective-permute-start.1 = (f32[8,4,256]{2,1,0:T(4,128)S(1)}, f32[8,4,256]{2,1,0:T(4,128)S(1)}, u32[]{:S(2)}, u32[]{:S(2)}) collective-permute-start(f32[8,4,256]{2,1,0:T(4,128)S(1)} %bitcast.120), channel_id=1, source_target_pairs={{0,1},{1,2},{2,3},{3,4},{4,5},{5,6},{6,7},{7,8},{8,9},{9,10},{10,1... | collective-permute-start | bytes 98312 | tf_op jit(solution)/shard_map/ppermute | solution.py:16
  53.3 3.1 %collective-permute-start = (f32[8,4,256]{2,1,0:T(4,128)S(1)}, f32[8,4,256]{2,1,0:T(4,128)S(1)}, u32[]{:S(2)}, u32[]{:S(2)}) collective-permute-start(f32[8,4,256]{2,1,0:T(4,128)S(1)} %bitcast.121), channel_id=1, source_target_pairs={{0,2},{1,3},{2,4},{3,5},{4,6},{5,7},{6,8},{7,9},{8,10},{9,11},{10,... | collective-permute-start | bytes 98312 | tf_op jit(solution)/shard_map/ppermute | solution.py:16
  59.7 2.5 %fusion.7 = f32[4,4,64,1,128]{4,3,2,1,0:T(1,128)} fusion(bf16[8,4,4,64,1]{0,4,3,1,2:T(2,128)(2,1)S(1)} %copy.51, bf16[8,4,4,64,128]{4,3,2,1,0:T(8,128)(2,1)S(1)} %bitcast.101), kind=kOutput, calls=%fused_computation.12 | convolution fusion | flops 2097152 | bytes 2637824 | tf_op jit(solution)/shard_map/kyqxf,kyqx->qyxf/dot_general | solution.py:140
  63.8 4.0 %all-to-all-start.1 = ((f32[4,4,64,128]{3,2,1,0:T(8,128)}), f32[4,4,64,128]{3,2,1,0:T(8,128)S(1)}, u32[]{:S(2)}, u32[]{:S(2)}) async-start(f32[4,4,64,128]{3,2,1,0:T(8,128)} %add_dynamic-update-slice_fusion), calls=%async_computation.1 | async-start | bytes 1048576 | tf_op jit(solution)/shard_map/all_to_all | solution.py:161
  67.9 9.0 %all-to-all-done.1 = f32[4,4,64,128]{3,2,1,0:T(8,128)S(1)} async-done(((f32[4,4,64,128]{3,2,1,0:T(8,128)}), f32[4,4,64,128]{3,2,1,0:T(8,128)S(1)}, u32[]{:S(2)}, u32[]{:S(2)}) %all-to-all-start.1) | async-done | bytes 524320 | tf_op jit(solution)/shard_map/all_to_all | solution.py:161
  80.6 4.0 %all-to-all-start.2 = ((bf16[4,4,64,128]{3,2,1,0:T(8,128)(2,1)}), bf16[4,4,64,128]{3,2,1,0:T(8,128)(2,1)}, u32[]{:S(2)}, u32[]{:S(2)}) async-start(bf16[4,4,64,128]{3,2,1,0:T(8,128)(2,1)} %broadcast_in_dim.37), calls=%async_computation.2 | async-start | bytes 524288 | tf_op jit(solution)/shard_map/all_to_all | solution.py:174
  84.7 5.5 %all-to-all-done.2 = bf16[4,4,64,128]{3,2,1,0:T(8,128)(2,1)} async-done(((bf16[4,4,64,128]{3,2,1,0:T(8,128)(2,1)}), bf16[4,4,64,128]{3,2,1,0:T(8,128)(2,1)}, u32[]{:S(2)}, u32[]{:S(2)}) %all-to-all-start.2) | async-done | bytes 262176 | tf_op jit(solution)/shard_map/all_to_all | solution.py:174
  90.2 2.5 %fusion = f32[4,4,64,1,8]{4,3,2,1,0:T(1,128)S(1)} fusion(bf16[8,4,4,64,128]{4,3,2,1,0:T(8,128)(2,1)S(1)} %bitcast.102, bf16[4,4,64,128,1]{3,2,1,0,4:T(8,128)(2,1)} %bitcast.28), kind=kOutput, calls=%fused_computation.5 | convolution fusion | flops 2097152 | bytes 2392064 | tf_op jit(solution)/shard_map/kyqxf,qyxf->kyqx/dot_general | solution.py:175
  93.2 4.4 %collective-permute-start.9 = (f32[8,4,256]{2,1,0:T(4,128)S(1)}, f32[8,4,256]{2,1,0:T(4,128)S(1)}, u32[]{:S(2)}, u32[]{:S(2)}) collective-permute-start(f32[8,4,256]{2,1,0:T(4,128)S(1)} %reshape.277), channel_id=1, source_target_pairs={{1,0},{2,1},{3,2},{4,3},{5,4},{6,5},{7,6},{8,7},{9,8},{10,9},{11,1... | collective-permute-start | bytes 98312 | tf_op jit(solution)/shard_map/ppermute | solution.py:17
  97.6 3.8 %collective-permute-start.8 = (f32[8,4,256]{2,1,0:T(4,128)S(1)}, f32[8,4,256]{2,1,0:T(4,128)S(1)}, u32[]{:S(2)}, u32[]{:S(2)}) collective-permute-start(f32[8,4,256]{2,1,0:T(4,128)S(1)} %reshape.277), channel_id=1, source_target_pairs={{0,1},{1,2},{2,3},{3,4},{4,5},{5,6},{6,7},{7,8},{8,9},{9,10},{10,1... | collective-permute-start | bytes 98312 | tf_op jit(solution)/shard_map/ppermute | solution.py:16
  109.1 11.7 %all-to-all-start.3 = ((f32[256,1,3]{2,1,0:T(1,128)}), f32[256,1,3]{2,1,0:T(1,128)S(1)}, u32[]{:S(2)}, u32[]{:S(2)}) async-start(f32[256,1,3]{2,1,0:T(1,128)} %broadcast_in_dim.38), calls=%async_computation.3 | async-start | bytes 262144 | tf_op jit(solution)/shard_map/all_to_all | solution.py:58
  120.8 4.1 %collective-permute-start.11 = (f32[8,4,256]{2,1,0:T(4,128)S(1)}, f32[8,4,256]{2,1,0:T(4,128)S(1)}, u32[]{:S(2)}, u32[]{:S(2)}) collective-permute-start(f32[8,4,256]{2,1,0:T(4,128)S(1)} %get-tuple-element.11), channel_id=1, source_target_pairs={{1,0},{2,1},{3,2},{4,3},{5,4},{6,5},{7,6},{8,7},{9,8},{10,9},{11,1... | collective-permute-start | bytes 98312 | tf_op jit(solution)/shard_map/ppermute | solution.py:17
  126.8 6.9 %all-to-all-done.3 = f32[256,1,3]{2,1,0:T(1,128)S(1)} async-done(((f32[256,1,3]{2,1,0:T(1,128)}), f32[256,1,3]{2,1,0:T(1,128)S(1)}, u32[]{:S(2)}, u32[]{:S(2)}) %all-to-all-start.3) | async-done | bytes 3104 | tf_op jit(solution)/shard_map/all_to_all | solution.py:58
  141.9 2.5 %fusion.5 = f32[4,4,64,1,128]{4,3,2,1,0:T(1,128)} fusion(bf16[8,4,4,64,1]{0,4,3,1,2:T(2,128)(2,1)S(1)} %copy.57, bf16[8,4,4,64,128]{4,3,2,1,0:T(8,128)(2,1)S(1)} %bitcast.103), kind=kOutput, calls=%fused_computation.10 | convolution fusion | flops 2097152 | bytes 2637824 | tf_op jit(solution)/shard_map/kyqxf,kyqx->qyxf/dot_general | solution.py:140
  146.2 3.6 %all-to-all-start.4 = ((f32[4,4,64,128]{3,2,1,0:T(8,128)}), f32[4,4,64,128]{3,2,1,0:T(8,128)S(1)}, u32[]{:S(2)}, u32[]{:S(2)}) async-start(f32[4,4,64,128]{3,2,1,0:T(8,128)} %fusion.10), calls=%async_computation.4 | async-start | bytes 1048576 | tf_op jit(solution)/shard_map/all_to_all | solution.py:161
  151.8 6.8 %all-to-all-done.4 = f32[4,4,64,128]{3,2,1,0:T(8,128)S(1)} async-done(((f32[4,4,64,128]{3,2,1,0:T(8,128)}), f32[4,4,64,128]{3,2,1,0:T(8,128)S(1)}, u32[]{:S(2)}, u32[]{:S(2)}) %all-to-all-start.4) | async-done | bytes 524320 | tf_op jit(solution)/shard_map/all_to_all | solution.py:161
  161.4 19.5 %all_to_all.32 = f32[256,1,1]{2,1,0:T(1,128)S(1)} all-to-all(f32[256,1,1]{2,1,0:T(1,128)S(1)} %broadcast_in_dim.40), channel_id=1, replica_groups=mesh['mem'=4,'col'=64] {'mem','col'}, dimensions={0} | all-to-all | bytes 2048 | tf_op jit(solution)/shard_map/all_to_all | solution.py:58
  (132 shorter events, 41.6 us)
Async XLA Ops:
  0.6 41.3 %copy-start = (bf16[8,4,256,128]{3,2,1,0:T(8,128)(2,1)S(1)}, bf16[8,4,256,128]{3,2,1,0:T(8,128)(2,1)}, u32[]{:S(2)}) copy-start(bf16[8,4,256,128]{3,2,1,0:T(8,128)(2,1)} %param.9) | copy-start | bytes 6291460
  0.6 21.7 %copy-start.9 = (f32[4,256]{1,0:T(4,128)S(1)}, f32[4,256]{1,0:T(4,128)}, u32[]{:S(2)}) copy-start(f32[4,256]{1,0:T(4,128)} %param.14) | copy-start | bytes 12292
  0.7 39.8 %copy-start.2 = (f32[128,128]{1,0:T(8,128)S(1)}, f32[128,128]{1,0:T(8,128)}, u32[]{:S(2)}) copy-start(f32[128,128]{1,0:T(8,128)} %param.11) | copy-start | bytes 196612
  0.7 39.8 %copy-start.10 = (f32[128]{0:T(128)S(1)}, f32[128]{0:T(128)}, u32[]{:S(2)}) copy-start(f32[128]{0:T(128)} %param.13) | copy-start | bytes 1540
  9.2 30.7 %all-to-all-start = ((f32[64,9,128]{2,1,0:T(8,128)}), f32[64,9,128]{2,1,0:T(8,128)S(1)}, u32[]{:S(2)}, u32[]{:S(2)}) async-start(f32[64,9,128]{2,1,0:T(8,128)} %pad_maximum_fusion), calls=%async_computation | async-start | bytes 1048576 | tf_op jit(solution)/shard_map/all_to_all | solution.py:106
  22.4 13.8 %collective-permute-start.6 = (f32[4,256]{1,0:T(4,128)S(1)}, f32[4,256]{1,0:T(4,128)S(1)}, u32[]{:S(2)}, u32[]{:S(2)}) collective-permute-start(f32[4,256]{1,0:T(4,128)S(1)} %copy-done.9), channel_id=1, source_target_pairs={{1,0},{2,1},{3,2},{4,3},{5,4},{6,5},{7,6},{8,7},{9,8},{10,9},{11,1... | collective-permute-start | bytes 12296 | tf_op jit(solution)/shard_map/ppermute | solution.py:17
  24.8 11.4 %collective-permute-start.5 = (f32[4,256]{1,0:T(4,128)S(1)}, f32[4,256]{1,0:T(4,128)S(1)}, u32[]{:S(2)}, u32[]{:S(2)}) collective-permute-start(f32[4,256]{1,0:T(4,128)S(1)} %copy-done.9), channel_id=1, source_target_pairs={{0,1},{1,2},{2,3},{3,4},{4,5},{5,6},{6,7},{7,8},{8,9},{9,10},{10,1... | collective-permute-start | bytes 12296 | tf_op jit(solution)/shard_map/ppermute | solution.py:16
  28.0 8.2 %collective-permute-start.4 = (f32[4,256]{1,0:T(4,128)S(1)}, f32[4,256]{1,0:T(4,128)S(1)}, u32[]{:S(2)}, u32[]{:S(2)}) collective-permute-start(f32[4,256]{1,0:T(4,128)S(1)} %copy-done.9), channel_id=1, source_target_pairs={{0,2},{1,3},{2,4},{3,5},{4,6},{5,7},{6,8},{7,9},{8,10},{9,11},{10,... | collective-permute-start | bytes 12296 | tf_op jit(solution)/shard_map/ppermute | solution.py:16
  31.2 4.9 %collective-permute-start.7 = (f32[4,256]{1,0:T(4,128)S(1)}, f32[4,256]{1,0:T(4,128)S(1)}, u32[]{:S(2)}, u32[]{:S(2)}) collective-permute-start(f32[4,256]{1,0:T(4,128)S(1)} %copy-done.9), channel_id=1, source_target_pairs={{2,0},{3,1},{4,2},{5,3},{6,4},{7,5},{8,6},{9,7},{10,8},{11,9},{12,... | collective-permute-start | bytes 12296 | tf_op jit(solution)/shard_map/ppermute | solution.py:17
  40.4 37.5 %copy-start.3 = (f32[512]{0:T(512)}, f32[512]{0:T(512)S(1)}, u32[]{:S(2)}) copy-start(f32[512]{0:T(512)S(1)} %mul.273) | copy-start | bytes 6148
  42.0 14.5 %copy-start.1 = (f32[128,128]{1,0:T(8,128)S(1)}, f32[128,128]{1,0:T(8,128)}, u32[]{:S(2)}) copy-start(f32[128,128]{1,0:T(8,128)} %param.10) | copy-start | bytes 196612
  45.5 11.6 %collective-permute-start.3 = (f32[8,4,256]{2,1,0:T(4,128)S(1)}, f32[8,4,256]{2,1,0:T(4,128)S(1)}, u32[]{:S(2)}, u32[]{:S(2)}) collective-permute-start(f32[8,4,256]{2,1,0:T(4,128)S(1)} %bitcast.118), channel_id=1, source_target_pairs={{2,0},{3,1},{4,2},{5,3},{6,4},{7,5},{8,6},{9,7},{10,8},{11,9},{12,... | collective-permute-start | bytes 98312 | tf_op jit(solution)/shard_map/ppermute | solution.py:17
  46.8 10.3 %collective-permute-start.2 = (f32[8,4,256]{2,1,0:T(4,128)S(1)}, f32[8,4,256]{2,1,0:T(4,128)S(1)}, u32[]{:S(2)}, u32[]{:S(2)}) collective-permute-start(f32[8,4,256]{2,1,0:T(4,128)S(1)} %bitcast.119), channel_id=1, source_target_pairs={{1,0},{2,1},{3,2},{4,3},{5,4},{6,5},{7,6},{8,7},{9,8},{10,9},{11,1... | collective-permute-start | bytes 98312 | tf_op jit(solution)/shard_map/ppermute | solution.py:17
  49.1 7.9 %collective-permute-start.1 = (f32[8,4,256]{2,1,0:T(4,128)S(1)}, f32[8,4,256]{2,1,0:T(4,128)S(1)}, u32[]{:S(2)}, u32[]{:S(2)}) collective-permute-start(f32[8,4,256]{2,1,0:T(4,128)S(1)} %bitcast.120), channel_id=1, source_target_pairs={{0,1},{1,2},{2,3},{3,4},{4,5},{5,6},{6,7},{7,8},{8,9},{9,10},{10,1... | collective-permute-start | bytes 98312 | tf_op jit(solution)/shard_map/ppermute | solution.py:16
  53.3 4.3 %collective-permute-start = (f32[8,4,256]{2,1,0:T(4,128)S(1)}, f32[8,4,256]{2,1,0:T(4,128)S(1)}, u32[]{:S(2)}, u32[]{:S(2)}) collective-permute-start(f32[8,4,256]{2,1,0:T(4,128)S(1)} %bitcast.121), channel_id=1, source_target_pairs={{0,2},{1,3},{2,4},{3,5},{4,6},{5,7},{6,8},{7,9},{8,10},{9,11},{10,... | collective-permute-start | bytes 98312 | tf_op jit(solution)/shard_map/ppermute | solution.py:16
  63.8 13.1 %all-to-all-start.1 = ((f32[4,4,64,128]{3,2,1,0:T(8,128)}), f32[4,4,64,128]{3,2,1,0:T(8,128)S(1)}, u32[]{:S(2)}, u32[]{:S(2)}) async-start(f32[4,4,64,128]{3,2,1,0:T(8,128)} %add_dynamic-update-slice_fusion), calls=%async_computation.1 | async-start | bytes 1048576 | tf_op jit(solution)/shard_map/all_to_all | solution.py:161
  80.6 9.6 %all-to-all-start.2 = ((bf16[4,4,64,128]{3,2,1,0:T(8,128)(2,1)}), bf16[4,4,64,128]{3,2,1,0:T(8,128)(2,1)}, u32[]{:S(2)}, u32[]{:S(2)}) async-start(bf16[4,4,64,128]{3,2,1,0:T(8,128)(2,1)} %broadcast_in_dim.37), calls=%async_computation.2 | async-start | bytes 524288 | tf_op jit(solution)/shard_map/all_to_all | solution.py:174
  93.2 10.1 %collective-permute-start.9 = (f32[8,4,256]{2,1,0:T(4,128)S(1)}, f32[8,4,256]{2,1,0:T(4,128)S(1)}, u32[]{:S(2)}, u32[]{:S(2)}) collective-permute-start(f32[8,4,256]{2,1,0:T(4,128)S(1)} %reshape.277), channel_id=1, source_target_pairs={{1,0},{2,1},{3,2},{4,3},{5,4},{6,5},{7,6},{8,7},{9,8},{10,9},{11,1... | collective-permute-start | bytes 98312 | tf_op jit(solution)/shard_map/ppermute | solution.py:17
  97.6 5.7 %collective-permute-start.8 = (f32[8,4,256]{2,1,0:T(4,128)S(1)}, f32[8,4,256]{2,1,0:T(4,128)S(1)}, u32[]{:S(2)}, u32[]{:S(2)}) collective-permute-start(f32[8,4,256]{2,1,0:T(4,128)S(1)} %reshape.277), channel_id=1, source_target_pairs={{0,1},{1,2},{2,3},{3,4},{4,5},{5,6},{6,7},{7,8},{8,9},{9,10},{10,1... | collective-permute-start | bytes 98312 | tf_op jit(solution)/shard_map/ppermute | solution.py:16
  109.1 24.5 %all-to-all-start.3 = ((f32[256,1,3]{2,1,0:T(1,128)}), f32[256,1,3]{2,1,0:T(1,128)S(1)}, u32[]{:S(2)}, u32[]{:S(2)}) async-start(f32[256,1,3]{2,1,0:T(1,128)} %broadcast_in_dim.38), calls=%async_computation.3 | async-start | bytes 262144 | tf_op jit(solution)/shard_map/all_to_all | solution.py:58
  120.8 18.6 %collective-permute-start.11 = (f32[8,4,256]{2,1,0:T(4,128)S(1)}, f32[8,4,256]{2,1,0:T(4,128)S(1)}, u32[]{:S(2)}, u32[]{:S(2)}) collective-permute-start(f32[8,4,256]{2,1,0:T(4,128)S(1)} %get-tuple-element.11), channel_id=1, source_target_pairs={{1,0},{2,1},{3,2},{4,3},{5,4},{6,5},{7,6},{8,7},{9,8},{10,9},{11,1... | collective-permute-start | bytes 98312 | tf_op jit(solution)/shard_map/ppermute | solution.py:17
  124.9 14.5 %collective-permute-start.10 = (f32[8,4,256]{2,1,0:T(4,128)S(1)}, f32[8,4,256]{2,1,0:T(4,128)S(1)}, u32[]{:S(2)}, u32[]{:S(2)}) collective-permute-start(f32[8,4,256]{2,1,0:T(4,128)S(1)} %get-tuple-element.11), channel_id=1, source_target_pairs={{0,1},{1,2},{2,3},{3,4},{4,5},{5,6},{6,7},{7,8},{8,9},{9,10},{10,1... | collective-permute-start | bytes 98312 | tf_op jit(solution)/shard_map/ppermute | solution.py:16
  144.4 14.2 %copy-start.6 = (s32[1024]{0:T(1024)S(1)}, s32[1024]{0:T(1024)}, u32[]{:S(2)}) copy-start(s32[1024]{0:T(1024)} %copy-done.5) | copy-start | bytes 12292
  146.2 12.3 %all-to-all-start.4 = ((f32[4,4,64,128]{3,2,1,0:T(8,128)}), f32[4,4,64,128]{3,2,1,0:T(8,128)S(1)}, u32[]{:S(2)}, u32[]{:S(2)}) async-start(f32[4,4,64,128]{3,2,1,0:T(8,128)} %fusion.10), calls=%async_computation.4 | async-start | bytes 1048576 | tf_op jit(solution)/shard_map/all_to_all | solution.py:161
  (5 other events, 62.1 us)

commit v11 on v7

--- a/solution.py
+++ b/solution.py
@@ -177,10 +177,8 @@
         return static, projected
 
     right_static, right_projected = adjoint_parts(spread_back(obs_gain * got_values))
-    wide = sweep_steps(neighbours(right_projected, "col", 1, 2), coeffs_wide, NSWEEP)
-    right_ensemble = wide[:, 2 * rows_here : 3 * rows_here]
-    wide = sweep_steps(wide, coeffs_wide, NSWEEP)
-    smoothed_right = wide[:, 2 * rows_here : 3 * rows_here]
+    right_ensemble = sweeps(right_projected, coeffs)
+    smoothed_right = sweeps(right_ensemble, coeffs)
     direction = (right_static, right_ensemble)
 
     partial0 = forward_partial(right_static, smoothed_right)

time: 180 us -> 176 us (0.978)
  blocking collectives: 19.5 us -> 28.9 us
  waiting for transfers between devices: 35.8 us -> 30.7 us
  starting transfers between devices: 71 us -> 68.4 us
  matrix products: 14.3 us -> 11.8 us
  local copies, waits for them, and re-layouts: 13.4 us -> 10.9 us
    all_to_all x0 -> x1, blocking collectives: none -> 9.43 us  [observed_adjoint(): quarters = lax.all_to_all(spread, 'mem', 0, 0, tiled=True)]
    all_to_all x1 -> x0, waiting for transfers between devices: 5.44 us -> none  [observed_adjoint(): quarters = lax.all_to_all(spread, 'mem', 0, 0, tiled=True)]
    all_to_all x1 -> x0, starting transfers between devices: 3.4 us -> none  [observed_adjoint(): quarters = lax.all_to_all(spread, 'mem', 0, 0, tiled=True)]
    all_to_all x1, starting transfers between devices: 11.7 us -> 14 us  [global_sum(): return jnp.sum(lax.all_to_all(spread, axes, 0, 0, tiled=True), axis=0)]
  transfers between devices with their start and end apart: 17 -> 16, of which waited for: 7 -> 8; matrix products, arithmetic and copies ran while one was open for 3% -> 2% of each run, Pallas kernels for 0% -> 0%
where the time goes in v11:
time: 176 us; the launch traced here: 175 us
  starting transfers between devices  68.4 us (39%)
  waiting for transfers between devices  30.7 us (17%)
  blocking collectives  28.9 us (16%)
  between operations  12.5 us (7%)
  matrix products  11.8 us (7%)
  other arithmetic  11.3 us (6%)
  local copies, waits for them, and re-layouts  10.9 us (6%)
    ppermute x6, starting transfers between devices, neighbours(): below.insert(0, lax.ppermute(block, axis, forward))  19.5 us
    all_to_all x1, blocking collectives, global_sum(): return jnp.sum(lax.all_to_all(spread, axes, 0, 0, tiled=True), axis=0)  19.5 us
    all_to_all x2, waiting for transfers between devices, observed(): own_image = jnp.sum(lax.all_to_all(pieces, 'mem', 0, 0, tiled=True), axis=0)  15.2 us
    ppermute x6, starting transfers between devices, neighbours(): above.append(lax.ppermute(block, axis, backward))  14.2 us
    all_to_all x1, starting transfers between devices, global_sum(): return jnp.sum(lax.all_to_all(spread, axes, 0, 0, tiled=True), axis=0)  14 us
    all_to_all x1, starting transfers between devices, shards(): got = lax.all_to_all(packed, 'col', split_axis=0, concat_axis=0, tiled=True)  13.1 us
    all_to_all x1, blocking collectives, observed_adjoint(): quarters = lax.all_to_all(spread, 'mem', 0, 0, tiled=True)  9.43 us
    all_to_all x2, starting transfers between devices, observed(): own_image = jnp.sum(lax.all_to_all(pieces, 'mem', 0, 0, tiled=True), axis=0)  7.6 us
  transfers between devices with their start and end apart: 16, of which 8 were waited for; matrix products, arithmetic and copies ran while one was open for 2% of the time, Pallas kernels for 0%

profile of v11, /device:TPU:1, one launch (start us, length us, event | category | flops | bytes accessed | tf_op | source)
XLA Modules:
  0.0 174.7 jit_solution(18042660981809561875)
XLA Ops:
  9.2 13.1 %all-to-all-start = ((f32[64,9,128]{2,1,0:T(8,128)}), f32[64,9,128]{2,1,0:T(8,128)S(1)}, u32[]{:S(2)}, u32[]{:S(2)}) async-start(f32[64,9,128]{2,1,0:T(8,128)} %pad_maximum_fusion), calls=%async_computation | async-start | bytes 1048576 | tf_op jit(solution)/shard_map/all_to_all | solution.py:106
  22.4 2.4 %collective-permute-start.4 = (f32[4,256]{1,0:T(4,128)S(1)}, f32[4,256]{1,0:T(4,128)S(1)}, u32[]{:S(2)}, u32[]{:S(2)}) collective-permute-start(f32[4,256]{1,0:T(4,128)S(1)} %copy-done.7), channel_id=1, source_target_pairs={{1,0},{2,1},{3,2},{4,3},{5,4},{6,5},{7,6},{8,7},{9,8},{10,9},{11,1... | collective-permute-start | bytes 12296 | tf_op jit(solution)/shard_map/ppermute | solution.py:17
  24.8 3.2 %collective-permute-start.3 = (f32[4,256]{1,0:T(4,128)S(1)}, f32[4,256]{1,0:T(4,128)S(1)}, u32[]{:S(2)}, u32[]{:S(2)}) collective-permute-start(f32[4,256]{1,0:T(4,128)S(1)} %copy-done.7), channel_id=1, source_target_pairs={{0,1},{1,2},{2,3},{3,4},{4,5},{5,6},{6,7},{7,8},{8,9},{9,10},{10,1... | collective-permute-start | bytes 12296 | tf_op jit(solution)/shard_map/ppermute | solution.py:16
  28.0 3.3 %collective-permute-start.2 = (f32[4,256]{1,0:T(4,128)S(1)}, f32[4,256]{1,0:T(4,128)S(1)}, u32[]{:S(2)}, u32[]{:S(2)}) collective-permute-start(f32[4,256]{1,0:T(4,128)S(1)} %copy-done.7), channel_id=1, source_target_pairs={{0,2},{1,3},{2,4},{3,5},{4,6},{5,7},{6,8},{7,9},{8,10},{9,11},{10,... | collective-permute-start | bytes 12296 | tf_op jit(solution)/shard_map/ppermute | solution.py:16
  32.5 3.6 %collective-permute-done.4 = f32[4,256]{1,0:T(4,128)S(1)} collective-permute-done((f32[4,256]{1,0:T(4,128)S(1)}, f32[4,256]{1,0:T(4,128)S(1)}, u32[]{:S(2)}, u32[]{:S(2)}) %collective-permute-start.4) | collective-permute-done | bytes 4128 | tf_op jit(solution)/shard_map/ppermute | solution.py:17
  36.4 3.6 %all-to-all-done = f32[64,9,128]{2,1,0:T(8,128)S(1)} async-done(((f32[64,9,128]{2,1,0:T(8,128)}), f32[64,9,128]{2,1,0:T(8,128)S(1)}, u32[]{:S(2)}, u32[]{:S(2)}) %all-to-all-start) | async-done | bytes 294944 | tf_op jit(solution)/shard_map/all_to_all | solution.py:106
  43.9 2.3 %collective-permute-start.1 = (f32[8,4,256]{2,1,0:T(4,128)S(1)}, f32[8,4,256]{2,1,0:T(4,128)S(1)}, u32[]{:S(2)}, u32[]{:S(2)}) collective-permute-start(f32[8,4,256]{2,1,0:T(4,128)S(1)} %bitcast.134), channel_id=1, source_target_pairs={{1,0},{2,1},{3,2},{4,3},{5,4},{6,5},{7,6},{8,7},{9,8},{10,9},{11,1... | collective-permute-start | bytes 98312 | tf_op jit(solution)/shard_map/ppermute | solution.py:17
  46.2 3.3 %collective-permute-start = (f32[8,4,256]{2,1,0:T(4,128)S(1)}, f32[8,4,256]{2,1,0:T(4,128)S(1)}, u32[]{:S(2)}, u32[]{:S(2)}) collective-permute-start(f32[8,4,256]{2,1,0:T(4,128)S(1)} %bitcast.135), channel_id=1, source_target_pairs={{0,1},{1,2},{2,3},{3,4},{4,5},{5,6},{6,7},{7,8},{8,9},{9,10},{10,1... | collective-permute-start | bytes 98312 | tf_op jit(solution)/shard_map/ppermute | solution.py:16
  51.1 1.9 %collective-permute-start.7 = (f32[8,4,256]{2,1,0:T(4,128)S(1)}, f32[8,4,256]{2,1,0:T(4,128)S(1)}, u32[]{:S(2)}, u32[]{:S(2)}) collective-permute-start(f32[8,4,256]{2,1,0:T(4,128)S(1)} %fusion.207), channel_id=1, source_target_pairs={{1,0},{2,1},{3,2},{4,3},{5,4},{6,5},{7,6},{8,7},{9,8},{10,9},{11,1... | collective-permute-start | bytes 98312 | tf_op jit(solution)/shard_map/ppermute | solution.py:17
  53.0 4.2 %collective-permute-start.6 = (f32[8,4,256]{2,1,0:T(4,128)S(1)}, f32[8,4,256]{2,1,0:T(4,128)S(1)}, u32[]{:S(2)}, u32[]{:S(2)}) collective-permute-start(f32[8,4,256]{2,1,0:T(4,128)S(1)} %fusion.207), channel_id=1, source_target_pairs={{0,1},{1,2},{2,3},{3,4},{4,5},{5,6},{6,7},{7,8},{8,9},{9,10},{10,1... | collective-permute-start | bytes 98312 | tf_op jit(solution)/shard_map/ppermute | solution.py:16
  59.3 1.7 fusion.5
  61.9 4.1 %all-to-all-start.1 = ((f32[4,4,64,128]{3,2,1,0:T(8,128)}), f32[4,4,64,128]{3,2,1,0:T(8,128)S(1)}, u32[]{:S(2)}, u32[]{:S(2)}) async-start(f32[4,4,64,128]{3,2,1,0:T(8,128)} %copy.62), calls=%async_computation.1 | async-start | bytes 1048576 | tf_op jit(solution)/shard_map/all_to_all | solution.py:159
  66.1 8.4 %all-to-all-done.1 = f32[4,4,64,128]{3,2,1,0:T(8,128)S(1)} async-done(((f32[4,4,64,128]{3,2,1,0:T(8,128)}), f32[4,4,64,128]{3,2,1,0:T(8,128)S(1)}, u32[]{:S(2)}, u32[]{:S(2)}) %all-to-all-start.1) | async-done | bytes 524320 | tf_op jit(solution)/shard_map/all_to_all | solution.py:159
  76.9 9.4 %all_to_all.32 = bf16[4,4,64,128]{3,2,1,0:T(8,128)(2,1)S(1)} all-to-all(bf16[4,4,64,128]{3,2,1,0:T(8,128)(2,1)S(1)} %broadcast_in_dim.33), channel_id=1, replica_groups=mesh['mem'=4,'col'=64] {'mem'}, dimensions={0} | all-to-all | bytes 524288 | tf_op jit(solution)/shard_map/all_to_all | solution.py:172
  88.2 2.3 %collective-permute-start.9 = (f32[8,4,256]{2,1,0:T(4,128)S(1)}, f32[8,4,256]{2,1,0:T(4,128)S(1)}, u32[]{:S(2)}, u32[]{:S(2)}) collective-permute-start(f32[8,4,256]{2,1,0:T(4,128)S(1)} %bitcast.131), channel_id=1, source_target_pairs={{1,0},{2,1},{3,2},{4,3},{5,4},{6,5},{7,6},{8,7},{9,8},{10,9},{11,1... | collective-permute-start | bytes 98312 | tf_op jit(solution)/shard_map/ppermute | solution.py:17
  90.5 3.6 %collective-permute-start.8 = (f32[8,4,256]{2,1,0:T(4,128)S(1)}, f32[8,4,256]{2,1,0:T(4,128)S(1)}, u32[]{:S(2)}, u32[]{:S(2)}) collective-permute-start(f32[8,4,256]{2,1,0:T(4,128)S(1)} %bitcast.132), channel_id=1, source_target_pairs={{0,1},{1,2},{2,3},{3,4},{4,5},{5,6},{6,7},{7,8},{8,9},{9,10},{10,1... | collective-permute-start | bytes 98312 | tf_op jit(solution)/shard_map/ppermute | solution.py:16
  101.1 14.0 %all-to-all-start.3 = ((f32[256,1,3]{2,1,0:T(1,128)}), f32[256,1,3]{2,1,0:T(1,128)S(1)}, u32[]{:S(2)}, u32[]{:S(2)}) async-start(f32[256,1,3]{2,1,0:T(1,128)} %broadcast_in_dim.34), calls=%async_computation.3 | async-start | bytes 262144 | tf_op jit(solution)/shard_map/all_to_all | solution.py:58
  115.0 4.1 %collective-permute-start.11 = (f32[8,4,256]{2,1,0:T(4,128)S(1)}, f32[8,4,256]{2,1,0:T(4,128)S(1)}, u32[]{:S(2)}, u32[]{:S(2)}) collective-permute-start(f32[8,4,256]{2,1,0:T(4,128)S(1)} %get-tuple-element.11), channel_id=1, source_target_pairs={{1,0},{2,1},{3,2},{4,3},{5,4},{6,5},{7,6},{8,7},{9,8},{10,9},{11,1... | collective-permute-start | bytes 98312 | tf_op jit(solution)/shard_map/ppermute | solution.py:17
  119.1 1.9 %collective-permute-start.10 = (f32[8,4,256]{2,1,0:T(4,128)S(1)}, f32[8,4,256]{2,1,0:T(4,128)S(1)}, u32[]{:S(2)}, u32[]{:S(2)}) collective-permute-start(f32[8,4,256]{2,1,0:T(4,128)S(1)} %get-tuple-element.11), channel_id=1, source_target_pairs={{0,1},{1,2},{2,3},{3,4},{4,5},{5,6},{6,7},{7,8},{8,9},{9,10},{10,1... | collective-permute-start | bytes 98312 | tf_op jit(solution)/shard_map/ppermute | solution.py:16
  121.0 6.9 %all-to-all-done.3 = f32[256,1,3]{2,1,0:T(1,128)S(1)} async-done(((f32[256,1,3]{2,1,0:T(1,128)}), f32[256,1,3]{2,1,0:T(1,128)S(1)}, u32[]{:S(2)}, u32[]{:S(2)}) %all-to-all-start.3) | async-done | bytes 3104 | tf_op jit(solution)/shard_map/all_to_all | solution.py:58
  134.5 1.7 fusion.1
  137.3 3.5 %all-to-all-start.4 = ((f32[4,4,64,128]{3,2,1,0:T(8,128)}), f32[4,4,64,128]{3,2,1,0:T(8,128)S(1)}, u32[]{:S(2)}, u32[]{:S(2)}) async-start(f32[4,4,64,128]{3,2,1,0:T(8,128)} %bitcast.103), calls=%async_computation.4 | async-start | bytes 1048576 | tf_op jit(solution)/shard_map/all_to_all | solution.py:159
  142.7 6.8 %all-to-all-done.4 = f32[4,4,64,128]{3,2,1,0:T(8,128)S(1)} async-done(((f32[4,4,64,128]{3,2,1,0:T(8,128)}), f32[4,4,64,128]{3,2,1,0:T(8,128)S(1)}, u32[]{:S(2)}, u32[]{:S(2)}) %all-to-all-start.4) | async-done | bytes 524320 | tf_op jit(solution)/shard_map/all_to_all | solution.py:159
  152.3 19.5 %all_to_all.33 = f32[256,1,1]{2,1,0:T(1,128)S(1)} all-to-all(f32[256,1,1]{2,1,0:T(1,128)S(1)} %broadcast_in_dim.35), channel_id=1, replica_groups=mesh['mem'=4,'col'=64] {'mem','col'}, dimensions={0} | all-to-all | bytes 2048 | tf_op jit(solution)/shard_map/all_to_all | solution.py:58
  (125 shorter events, 33.4 us)
Async XLA Ops:
  0.6 41.3 %copy-start = (bf16[8,4,256,128]{3,2,1,0:T(8,128)(2,1)S(1)}, bf16[8,4,256,128]{3,2,1,0:T(8,128)(2,1)}, u32[]{:S(2)}) copy-start(bf16[8,4,256,128]{3,2,1,0:T(8,128)(2,1)} %param.9) | copy-start | bytes 6291460
  0.6 21.7 %copy-start.7 = (f32[4,256]{1,0:T(4,128)S(1)}, f32[4,256]{1,0:T(4,128)}, u32[]{:S(2)}) copy-start(f32[4,256]{1,0:T(4,128)} %param.14) | copy-start | bytes 12292
  0.7 39.8 %copy-start.2 = (f32[128,128]{1,0:T(8,128)S(1)}, f32[128,128]{1,0:T(8,128)}, u32[]{:S(2)}) copy-start(f32[128,128]{1,0:T(8,128)} %param.11) | copy-start | bytes 196612
  0.7 39.8 %copy-start.8 = (f32[128]{0:T(128)S(1)}, f32[128]{0:T(128)}, u32[]{:S(2)}) copy-start(f32[128]{0:T(128)} %param.13) | copy-start | bytes 1540
  9.2 30.7 %all-to-all-start = ((f32[64,9,128]{2,1,0:T(8,128)}), f32[64,9,128]{2,1,0:T(8,128)S(1)}, u32[]{:S(2)}, u32[]{:S(2)}) async-start(f32[64,9,128]{2,1,0:T(8,128)} %pad_maximum_fusion), calls=%async_computation | async-start | bytes 1048576 | tf_op jit(solution)/shard_map/all_to_all | solution.py:106
  22.4 13.8 %collective-permute-start.4 = (f32[4,256]{1,0:T(4,128)S(1)}, f32[4,256]{1,0:T(4,128)S(1)}, u32[]{:S(2)}, u32[]{:S(2)}) collective-permute-start(f32[4,256]{1,0:T(4,128)S(1)} %copy-done.7), channel_id=1, source_target_pairs={{1,0},{2,1},{3,2},{4,3},{5,4},{6,5},{7,6},{8,7},{9,8},{10,9},{11,1... | collective-permute-start | bytes 12296 | tf_op jit(solution)/shard_map/ppermute | solution.py:17
  24.8 11.4 %collective-permute-start.3 = (f32[4,256]{1,0:T(4,128)S(1)}, f32[4,256]{1,0:T(4,128)S(1)}, u32[]{:S(2)}, u32[]{:S(2)}) collective-permute-start(f32[4,256]{1,0:T(4,128)S(1)} %copy-done.7), channel_id=1, source_target_pairs={{0,1},{1,2},{2,3},{3,4},{4,5},{5,6},{6,7},{7,8},{8,9},{9,10},{10,1... | collective-permute-start | bytes 12296 | tf_op jit(solution)/shard_map/ppermute | solution.py:16
  28.0 8.2 %collective-permute-start.2 = (f32[4,256]{1,0:T(4,128)S(1)}, f32[4,256]{1,0:T(4,128)S(1)}, u32[]{:S(2)}, u32[]{:S(2)}) collective-permute-start(f32[4,256]{1,0:T(4,128)S(1)} %copy-done.7), channel_id=1, source_target_pairs={{0,2},{1,3},{2,4},{3,5},{4,6},{5,7},{6,8},{7,9},{8,10},{9,11},{10,... | collective-permute-start | bytes 12296 | tf_op jit(solution)/shard_map/ppermute | solution.py:16
  31.2 4.9 %collective-permute-start.5 = (f32[4,256]{1,0:T(4,128)S(1)}, f32[4,256]{1,0:T(4,128)S(1)}, u32[]{:S(2)}, u32[]{:S(2)}) collective-permute-start(f32[4,256]{1,0:T(4,128)S(1)} %copy-done.7), channel_id=1, source_target_pairs={{2,0},{3,1},{4,2},{5,3},{6,4},{7,5},{8,6},{9,7},{10,8},{11,9},{12,... | collective-permute-start | bytes 12296 | tf_op jit(solution)/shard_map/ppermute | solution.py:17
  42.0 7.5 %copy-start.1 = (f32[128,128]{1,0:T(8,128)S(1)}, f32[128,128]{1,0:T(8,128)}, u32[]{:S(2)}) copy-start(f32[128,128]{1,0:T(8,128)} %param.10) | copy-start | bytes 196612
  43.9 5.9 %collective-permute-start.1 = (f32[8,4,256]{2,1,0:T(4,128)S(1)}, f32[8,4,256]{2,1,0:T(4,128)S(1)}, u32[]{:S(2)}, u32[]{:S(2)}) collective-permute-start(f32[8,4,256]{2,1,0:T(4,128)S(1)} %bitcast.134), channel_id=1, source_target_pairs={{1,0},{2,1},{3,2},{4,3},{5,4},{6,5},{7,6},{8,7},{9,8},{10,9},{11,1... | collective-permute-start | bytes 98312 | tf_op jit(solution)/shard_map/ppermute | solution.py:17
  46.2 4.3 %collective-permute-start = (f32[8,4,256]{2,1,0:T(4,128)S(1)}, f32[8,4,256]{2,1,0:T(4,128)S(1)}, u32[]{:S(2)}, u32[]{:S(2)}) collective-permute-start(f32[8,4,256]{2,1,0:T(4,128)S(1)} %bitcast.135), channel_id=1, source_target_pairs={{0,1},{1,2},{2,3},{3,4},{4,5},{5,6},{6,7},{7,8},{8,9},{9,10},{10,1... | collective-permute-start | bytes 98312 | tf_op jit(solution)/shard_map/ppermute | solution.py:16
  51.1 6.5 %collective-permute-start.7 = (f32[8,4,256]{2,1,0:T(4,128)S(1)}, f32[8,4,256]{2,1,0:T(4,128)S(1)}, u32[]{:S(2)}, u32[]{:S(2)}) collective-permute-start(f32[8,4,256]{2,1,0:T(4,128)S(1)} %fusion.207), channel_id=1, source_target_pairs={{1,0},{2,1},{3,2},{4,3},{5,4},{6,5},{7,6},{8,7},{9,8},{10,9},{11,1... | collective-permute-start | bytes 98312 | tf_op jit(solution)/shard_map/ppermute | solution.py:17
  53.0 5.2 %collective-permute-start.6 = (f32[8,4,256]{2,1,0:T(4,128)S(1)}, f32[8,4,256]{2,1,0:T(4,128)S(1)}, u32[]{:S(2)}, u32[]{:S(2)}) collective-permute-start(f32[8,4,256]{2,1,0:T(4,128)S(1)} %fusion.207), channel_id=1, source_target_pairs={{0,1},{1,2},{2,3},{3,4},{4,5},{5,6},{6,7},{7,8},{8,9},{9,10},{10,1... | collective-permute-start | bytes 98312 | tf_op jit(solution)/shard_map/ppermute | solution.py:16
  61.0 5.1 %copy-start.6 = (s32[512]{0:T(512)S(1)}, s32[512]{0:T(512)}, u32[]{:S(2)}) copy-start(s32[512]{0:T(512)} %copy-done.5) | copy-start | bytes 6148
  61.9 13.7 %copy-start.4 = (f32[512]{0:T(512)S(1)}, f32[512]{0:T(512)}, u32[]{:S(2)}) copy-start(f32[512]{0:T(512)} %copy-done.3) | copy-start | bytes 6148
  61.9 13.7 %copy-start.9 = (f32[128]{0:T(128)S(1)}, f32[128]{0:T(128)}, u32[]{:S(2)}) copy-start(f32[128]{0:T(128)} %param.13) | copy-start | bytes 1540
  61.9 12.6 %all-to-all-start.1 = ((f32[4,4,64,128]{3,2,1,0:T(8,128)}), f32[4,4,64,128]{3,2,1,0:T(8,128)S(1)}, u32[]{:S(2)}, u32[]{:S(2)}) async-start(f32[4,4,64,128]{3,2,1,0:T(8,128)} %copy.62), calls=%async_computation.1 | async-start | bytes 1048576 | tf_op jit(solution)/shard_map/all_to_all | solution.py:159
  88.2 6.8 %collective-permute-start.9 = (f32[8,4,256]{2,1,0:T(4,128)S(1)}, f32[8,4,256]{2,1,0:T(4,128)S(1)}, u32[]{:S(2)}, u32[]{:S(2)}) collective-permute-start(f32[8,4,256]{2,1,0:T(4,128)S(1)} %bitcast.131), channel_id=1, source_target_pairs={{1,0},{2,1},{3,2},{4,3},{5,4},{6,5},{7,6},{8,7},{9,8},{10,9},{11,1... | collective-permute-start | bytes 98312 | tf_op jit(solution)/shard_map/ppermute | solution.py:17
  90.5 4.6 %collective-permute-start.8 = (f32[8,4,256]{2,1,0:T(4,128)S(1)}, f32[8,4,256]{2,1,0:T(4,128)S(1)}, u32[]{:S(2)}, u32[]{:S(2)}) collective-permute-start(f32[8,4,256]{2,1,0:T(4,128)S(1)} %bitcast.132), channel_id=1, source_target_pairs={{0,1},{1,2},{2,3},{3,4},{4,5},{5,6},{6,7},{7,8},{8,9},{9,10},{10,1... | collective-permute-start | bytes 98312 | tf_op jit(solution)/shard_map/ppermute | solution.py:16
  101.1 26.8 %all-to-all-start.3 = ((f32[256,1,3]{2,1,0:T(1,128)}), f32[256,1,3]{2,1,0:T(1,128)S(1)}, u32[]{:S(2)}, u32[]{:S(2)}) async-start(f32[256,1,3]{2,1,0:T(1,128)} %broadcast_in_dim.34), calls=%async_computation.3 | async-start | bytes 262144 | tf_op jit(solution)/shard_map/all_to_all | solution.py:58
  115.0 18.3 %collective-permute-start.11 = (f32[8,4,256]{2,1,0:T(4,128)S(1)}, f32[8,4,256]{2,1,0:T(4,128)S(1)}, u32[]{:S(2)}, u32[]{:S(2)}) collective-permute-start(f32[8,4,256]{2,1,0:T(4,128)S(1)} %get-tuple-element.11), channel_id=1, source_target_pairs={{1,0},{2,1},{3,2},{4,3},{5,4},{6,5},{7,6},{8,7},{9,8},{10,9},{11,1... | collective-permute-start | bytes 98312 | tf_op jit(solution)/shard_map/ppermute | solution.py:17
  119.1 14.3 %collective-permute-start.10 = (f32[8,4,256]{2,1,0:T(4,128)S(1)}, f32[8,4,256]{2,1,0:T(4,128)S(1)}, u32[]{:S(2)}, u32[]{:S(2)}) collective-permute-start(f32[8,4,256]{2,1,0:T(4,128)S(1)} %get-tuple-element.11), channel_id=1, source_target_pairs={{0,1},{1,2},{2,3},{3,4},{4,5},{5,6},{6,7},{7,8},{8,9},{9,10},{10,1... | collective-permute-start | bytes 98312 | tf_op jit(solution)/shard_map/ppermute | solution.py:16
  137.3 12.2 %all-to-all-start.4 = ((f32[4,4,64,128]{3,2,1,0:T(8,128)}), f32[4,4,64,128]{3,2,1,0:T(8,128)S(1)}, u32[]{:S(2)}, u32[]{:S(2)}) async-start(f32[4,4,64,128]{3,2,1,0:T(8,128)} %bitcast.103), calls=%async_computation.4 | async-start | bytes 1048576 | tf_op jit(solution)/shard_map/all_to_all | solution.py:159
  (2 other events, 6.6 us)

commit v12 on v11

--- a/solution.py
+++ b/solution.py
@@ -81,8 +81,7 @@
     obs_dev, channels = innovations.shape
     capacity = max(2, 2 * obs_dev // blocks)
     total_slots = blocks * capacity
-    coeffs_wide = face_coefficients(length_scale, 2)
-    coeffs = tuple(face[rows_here : 4 * rows_here] for face in coeffs_wide)
+    coeffs = face_coefficients(length_scale, 1)
     is_live = jnp.arange(obs_dev, dtype=jnp.int32) < obs_count[0]
     owner_ids = obs_owner[:, 0]
     onehot = (

time: 176 us -> 175 us (level)
  starting transfers between devices: 68.4 us -> 63.1 us
  waiting for transfers between devices: 30.7 us -> 35.4 us
    ppermute x6 -> x5, waiting for transfers between devices: 1.43 us -> 4.4 us  [neighbours(): below.insert(0, lax.ppermute(block, axis, forward))]
    ppermute x6 -> x5, starting transfers between devices: 19.5 us -> 16.6 us  [neighbours(): below.insert(0, lax.ppermute(block, axis, forward))]
    ppermute x6 -> x5, starting transfers between devices: 14.2 us -> 12.5 us  [neighbours(): above.append(lax.ppermute(block, axis, backward))]
    ppermute x6 -> x5, waiting for transfers between devices: 3.62 us -> 5.25 us  [neighbours(): above.append(lax.ppermute(block, axis, backward))]
  transfers between devices with their start and end apart: 16 -> 14, of which waited for: 8 -> 9; matrix products, arithmetic and copies ran while one was open for 2% -> 2% of each run, Pallas kernels for 0% -> 0%
where the time goes in v12:
time: 175 us; the launch traced here: 174 us
  starting transfers between devices  63.1 us (36%)
  waiting for transfers between devices  35.4 us (20%)
  blocking collectives  28.9 us (17%)
  between operations  12.5 us (7%)
  matrix products  11.8 us (7%)
  other arithmetic  11.4 us (7%)
  local copies, waits for them, and re-layouts  10.8 us (6%)
    all_to_all x1, blocking collectives, global_sum(): return jnp.sum(lax.all_to_all(spread, axes, 0, 0, tiled=True), axis=0)  19.5 us
    ppermute x5, starting transfers between devices, neighbours(): below.insert(0, lax.ppermute(block, axis, forward))  16.6 us
    all_to_all x2, waiting for transfers between devices, observed(): own_image = jnp.sum(lax.all_to_all(pieces, 'mem', 0, 0, tiled=True), axis=0)  15.2 us
    all_to_all x1, starting transfers between devices, global_sum(): return jnp.sum(lax.all_to_all(spread, axes, 0, 0, tiled=True), axis=0)  13.3 us
    all_to_all x1, starting transfers between devices, shards(): got = lax.all_to_all(packed, 'col', split_axis=0, concat_axis=0, tiled=True)  13.1 us
    ppermute x5, starting transfers between devices, neighbours(): above.append(lax.ppermute(block, axis, backward))  12.5 us
    all_to_all x1, blocking collectives, observed_adjoint(): quarters = lax.all_to_all(spread, 'mem', 0, 0, tiled=True)  9.45 us
    all_to_all x2, starting transfers between devices, observed(): own_image = jnp.sum(lax.all_to_all(pieces, 'mem', 0, 0, tiled=True), axis=0)  7.61 us
  transfers between devices with their start and end apart: 14, of which 9 were waited for; matrix products, arithmetic and copies ran while one was open for 2% of the time, Pallas kernels for 0%

profile of v12, /device:TPU:1, one launch (start us, length us, event | category | flops | bytes accessed | tf_op | source)
XLA Modules:
  0.0 174.0 jit_solution(940205024541825148)
XLA Ops:
  9.2 13.1 %all-to-all-start = ((f32[64,9,128]{2,1,0:T(8,128)}), f32[64,9,128]{2,1,0:T(8,128)S(1)}, u32[]{:S(2)}, u32[]{:S(2)}) async-start(f32[64,9,128]{2,1,0:T(8,128)} %pad_maximum_fusion), calls=%async_computation | async-start | bytes 1048576 | tf_op jit(solution)/shard_map/all_to_all | solution.py:105
  22.4 3.5 %collective-permute-start.2 = (f32[4,256]{1,0:T(4,128)S(1)}, f32[4,256]{1,0:T(4,128)S(1)}, u32[]{:S(2)}, u32[]{:S(2)}) collective-permute-start(f32[4,256]{1,0:T(4,128)S(1)} %copy-done.7), channel_id=1, source_target_pairs={{0,1},{1,2},{2,3},{3,4},{4,5},{5,6},{6,7},{7,8},{8,9},{9,10},{10,1... | collective-permute-start | bytes 12296 | tf_op jit(solution)/shard_map/ppermute | solution.py:16
  25.9 1.9 %collective-permute-start.3 = (f32[4,256]{1,0:T(4,128)S(1)}, f32[4,256]{1,0:T(4,128)S(1)}, u32[]{:S(2)}, u32[]{:S(2)}) collective-permute-start(f32[4,256]{1,0:T(4,128)S(1)} %copy-done.7), channel_id=1, source_target_pairs={{1,0},{2,1},{3,2},{4,3},{5,4},{6,5},{7,6},{8,7},{9,8},{10,9},{11,1... | collective-permute-start | bytes 12296 | tf_op jit(solution)/shard_map/ppermute | solution.py:17
  27.9 3.0 %collective-permute-done.2 = f32[4,256]{1,0:T(4,128)S(1)} collective-permute-done((f32[4,256]{1,0:T(4,128)S(1)}, f32[4,256]{1,0:T(4,128)S(1)}, u32[]{:S(2)}, u32[]{:S(2)}) %collective-permute-start.2) | collective-permute-done | bytes 4128 | tf_op jit(solution)/shard_map/ppermute | solution.py:16
  30.9 5.2 %collective-permute-done.3 = f32[4,256]{1,0:T(4,128)S(1)} collective-permute-done((f32[4,256]{1,0:T(4,128)S(1)}, f32[4,256]{1,0:T(4,128)S(1)}, u32[]{:S(2)}, u32[]{:S(2)}) %collective-permute-start.3) | collective-permute-done | bytes 4128 | tf_op jit(solution)/shard_map/ppermute | solution.py:17
  36.3 3.6 %all-to-all-done = f32[64,9,128]{2,1,0:T(8,128)S(1)} async-done(((f32[64,9,128]{2,1,0:T(8,128)}), f32[64,9,128]{2,1,0:T(8,128)S(1)}, u32[]{:S(2)}, u32[]{:S(2)}) %all-to-all-start) | async-done | bytes 294944 | tf_op jit(solution)/shard_map/all_to_all | solution.py:105
  43.8 2.3 %collective-permute-start.1 = (f32[8,4,256]{2,1,0:T(4,128)S(1)}, f32[8,4,256]{2,1,0:T(4,128)S(1)}, u32[]{:S(2)}, u32[]{:S(2)}) collective-permute-start(f32[8,4,256]{2,1,0:T(4,128)S(1)} %bitcast.134), channel_id=1, source_target_pairs={{1,0},{2,1},{3,2},{4,3},{5,4},{6,5},{7,6},{8,7},{9,8},{10,9},{11,1... | collective-permute-start | bytes 98312 | tf_op jit(solution)/shard_map/ppermute | solution.py:17
  46.1 3.3 %collective-permute-start = (f32[8,4,256]{2,1,0:T(4,128)S(1)}, f32[8,4,256]{2,1,0:T(4,128)S(1)}, u32[]{:S(2)}, u32[]{:S(2)}) collective-permute-start(f32[8,4,256]{2,1,0:T(4,128)S(1)} %bitcast.135), channel_id=1, source_target_pairs={{0,1},{1,2},{2,3},{3,4},{4,5},{5,6},{6,7},{7,8},{8,9},{9,10},{10,1... | collective-permute-start | bytes 98312 | tf_op jit(solution)/shard_map/ppermute | solution.py:16
  51.0 1.9 %collective-permute-start.5 = (f32[8,4,256]{2,1,0:T(4,128)S(1)}, f32[8,4,256]{2,1,0:T(4,128)S(1)}, u32[]{:S(2)}, u32[]{:S(2)}) collective-permute-start(f32[8,4,256]{2,1,0:T(4,128)S(1)} %fusion.207), channel_id=1, source_target_pairs={{1,0},{2,1},{3,2},{4,3},{5,4},{6,5},{7,6},{8,7},{9,8},{10,9},{11,1... | collective-permute-start | bytes 98312 | tf_op jit(solution)/shard_map/ppermute | solution.py:17
  53.0 4.2 %collective-permute-start.4 = (f32[8,4,256]{2,1,0:T(4,128)S(1)}, f32[8,4,256]{2,1,0:T(4,128)S(1)}, u32[]{:S(2)}, u32[]{:S(2)}) collective-permute-start(f32[8,4,256]{2,1,0:T(4,128)S(1)} %fusion.207), channel_id=1, source_target_pairs={{0,1},{1,2},{2,3},{3,4},{4,5},{5,6},{6,7},{7,8},{8,9},{9,10},{10,1... | collective-permute-start | bytes 98312 | tf_op jit(solution)/shard_map/ppermute | solution.py:16
  59.3 1.7 fusion.5
  61.8 4.1 %all-to-all-start.1 = ((f32[4,4,64,128]{3,2,1,0:T(8,128)}), f32[4,4,64,128]{3,2,1,0:T(8,128)S(1)}, u32[]{:S(2)}, u32[]{:S(2)}) async-start(f32[4,4,64,128]{3,2,1,0:T(8,128)} %copy.62), calls=%async_computation.1 | async-start | bytes 1048576 | tf_op jit(solution)/shard_map/all_to_all | solution.py:158
  66.1 8.4 %all-to-all-done.1 = f32[4,4,64,128]{3,2,1,0:T(8,128)S(1)} async-done(((f32[4,4,64,128]{3,2,1,0:T(8,128)}), f32[4,4,64,128]{3,2,1,0:T(8,128)S(1)}, u32[]{:S(2)}, u32[]{:S(2)}) %all-to-all-start.1) | async-done | bytes 524320 | tf_op jit(solution)/shard_map/all_to_all | solution.py:158
  76.8 9.5 %all_to_all.32 = bf16[4,4,64,128]{3,2,1,0:T(8,128)(2,1)S(1)} all-to-all(bf16[4,4,64,128]{3,2,1,0:T(8,128)(2,1)S(1)} %broadcast_in_dim.33), channel_id=1, replica_groups=mesh['mem'=4,'col'=64] {'mem'}, dimensions={0} | all-to-all | bytes 524288 | tf_op jit(solution)/shard_map/all_to_all | solution.py:171
  88.2 2.3 %collective-permute-start.7 = (f32[8,4,256]{2,1,0:T(4,128)S(1)}, f32[8,4,256]{2,1,0:T(4,128)S(1)}, u32[]{:S(2)}, u32[]{:S(2)}) collective-permute-start(f32[8,4,256]{2,1,0:T(4,128)S(1)} %bitcast.131), channel_id=1, source_target_pairs={{1,0},{2,1},{3,2},{4,3},{5,4},{6,5},{7,6},{8,7},{9,8},{10,9},{11,1... | collective-permute-start | bytes 98312 | tf_op jit(solution)/shard_map/ppermute | solution.py:17
  90.5 3.7 %collective-permute-start.6 = (f32[8,4,256]{2,1,0:T(4,128)S(1)}, f32[8,4,256]{2,1,0:T(4,128)S(1)}, u32[]{:S(2)}, u32[]{:S(2)}) collective-permute-start(f32[8,4,256]{2,1,0:T(4,128)S(1)} %bitcast.132), channel_id=1, source_target_pairs={{0,1},{1,2},{2,3},{3,4},{4,5},{5,6},{6,7},{7,8},{8,9},{9,10},{10,1... | collective-permute-start | bytes 98312 | tf_op jit(solution)/shard_map/ppermute | solution.py:16
  101.1 13.3 %all-to-all-start.3 = ((f32[256,1,3]{2,1,0:T(1,128)}), f32[256,1,3]{2,1,0:T(1,128)S(1)}, u32[]{:S(2)}, u32[]{:S(2)}) async-start(f32[256,1,3]{2,1,0:T(1,128)} %broadcast_in_dim.34), calls=%async_computation.3 | async-start | bytes 262144 | tf_op jit(solution)/shard_map/all_to_all | solution.py:58
  114.3 4.1 %collective-permute-start.9 = (f32[8,4,256]{2,1,0:T(4,128)S(1)}, f32[8,4,256]{2,1,0:T(4,128)S(1)}, u32[]{:S(2)}, u32[]{:S(2)}) collective-permute-start(f32[8,4,256]{2,1,0:T(4,128)S(1)} %get-tuple-element.11), channel_id=1, source_target_pairs={{1,0},{2,1},{3,2},{4,3},{5,4},{6,5},{7,6},{8,7},{9,8},{10,9},{11,1... | collective-permute-start | bytes 98312 | tf_op jit(solution)/shard_map/ppermute | solution.py:17
  118.4 1.9 %collective-permute-start.8 = (f32[8,4,256]{2,1,0:T(4,128)S(1)}, f32[8,4,256]{2,1,0:T(4,128)S(1)}, u32[]{:S(2)}, u32[]{:S(2)}) collective-permute-start(f32[8,4,256]{2,1,0:T(4,128)S(1)} %get-tuple-element.11), channel_id=1, source_target_pairs={{0,1},{1,2},{2,3},{3,4},{4,5},{5,6},{6,7},{7,8},{8,9},{9,10},{10,1... | collective-permute-start | bytes 98312 | tf_op jit(solution)/shard_map/ppermute | solution.py:16
  120.3 6.9 %all-to-all-done.3 = f32[256,1,3]{2,1,0:T(1,128)S(1)} async-done(((f32[256,1,3]{2,1,0:T(1,128)}), f32[256,1,3]{2,1,0:T(1,128)S(1)}, u32[]{:S(2)}, u32[]{:S(2)}) %all-to-all-start.3) | async-done | bytes 3104 | tf_op jit(solution)/shard_map/all_to_all | solution.py:58
  133.8 1.7 fusion.1
  136.6 3.5 %all-to-all-start.4 = ((f32[4,4,64,128]{3,2,1,0:T(8,128)}), f32[4,4,64,128]{3,2,1,0:T(8,128)S(1)}, u32[]{:S(2)}, u32[]{:S(2)}) async-start(f32[4,4,64,128]{3,2,1,0:T(8,128)} %bitcast.103), calls=%async_computation.4 | async-start | bytes 1048576 | tf_op jit(solution)/shard_map/all_to_all | solution.py:158
  142.0 6.8 %all-to-all-done.4 = f32[4,4,64,128]{3,2,1,0:T(8,128)S(1)} async-done(((f32[4,4,64,128]{3,2,1,0:T(8,128)}), f32[4,4,64,128]{3,2,1,0:T(8,128)S(1)}, u32[]{:S(2)}, u32[]{:S(2)}) %all-to-all-start.4) | async-done | bytes 524320 | tf_op jit(solution)/shard_map/all_to_all | solution.py:158
  151.5 19.5 %all_to_all.33 = f32[256,1,1]{2,1,0:T(1,128)S(1)} all-to-all(f32[256,1,1]{2,1,0:T(1,128)S(1)} %broadcast_in_dim.35), channel_id=1, replica_groups=mesh['mem'=4,'col'=64] {'mem','col'}, dimensions={0} | all-to-all | bytes 2048 | tf_op jit(solution)/shard_map/all_to_all | solution.py:58
  (120 shorter events, 32.1 us)
Async XLA Ops:
  0.6 41.3 %copy-start = (bf16[8,4,256,128]{3,2,1,0:T(8,128)(2,1)S(1)}, bf16[8,4,256,128]{3,2,1,0:T(8,128)(2,1)}, u32[]{:S(2)}) copy-start(bf16[8,4,256,128]{3,2,1,0:T(8,128)(2,1)} %param.9) | copy-start | bytes 6291460
  0.6 21.7 %copy-start.7 = (f32[4,256]{1,0:T(4,128)S(1)}, f32[4,256]{1,0:T(4,128)}, u32[]{:S(2)}) copy-start(f32[4,256]{1,0:T(4,128)} %param.14) | copy-start | bytes 12292
  0.7 39.7 %copy-start.2 = (f32[128,128]{1,0:T(8,128)S(1)}, f32[128,128]{1,0:T(8,128)}, u32[]{:S(2)}) copy-start(f32[128,128]{1,0:T(8,128)} %param.11) | copy-start | bytes 196612
  0.7 39.7 %copy-start.8 = (f32[128]{0:T(128)S(1)}, f32[128]{0:T(128)}, u32[]{:S(2)}) copy-start(f32[128]{0:T(128)} %param.13) | copy-start | bytes 1540
  9.2 30.6 %all-to-all-start = ((f32[64,9,128]{2,1,0:T(8,128)}), f32[64,9,128]{2,1,0:T(8,128)S(1)}, u32[]{:S(2)}, u32[]{:S(2)}) async-start(f32[64,9,128]{2,1,0:T(8,128)} %pad_maximum_fusion), calls=%async_computation | async-start | bytes 1048576 | tf_op jit(solution)/shard_map/all_to_all | solution.py:105
  22.4 8.5 %collective-permute-start.2 = (f32[4,256]{1,0:T(4,128)S(1)}, f32[4,256]{1,0:T(4,128)S(1)}, u32[]{:S(2)}, u32[]{:S(2)}) collective-permute-start(f32[4,256]{1,0:T(4,128)S(1)} %copy-done.7), channel_id=1, source_target_pairs={{0,1},{1,2},{2,3},{3,4},{4,5},{5,6},{6,7},{7,8},{8,9},{9,10},{10,1... | collective-permute-start | bytes 12296 | tf_op jit(solution)/shard_map/ppermute | solution.py:16
  25.9 10.2 %collective-permute-start.3 = (f32[4,256]{1,0:T(4,128)S(1)}, f32[4,256]{1,0:T(4,128)S(1)}, u32[]{:S(2)}, u32[]{:S(2)}) collective-permute-start(f32[4,256]{1,0:T(4,128)S(1)} %copy-done.7), channel_id=1, source_target_pairs={{1,0},{2,1},{3,2},{4,3},{5,4},{6,5},{7,6},{8,7},{9,8},{10,9},{11,1... | collective-permute-start | bytes 12296 | tf_op jit(solution)/shard_map/ppermute | solution.py:17
  40.1 1.8 %copy-start.5 = (s32[512]{0:T(512)}, s32[512]{0:T(512)S(1)}, u32[]{:S(2)}) copy-start(s32[512]{0:T(512)S(1)} %convert_element_type.83) | copy-start | bytes 6148
  40.4 1.5 copy-start.3
  41.9 7.5 %copy-start.1 = (f32[128,128]{1,0:T(8,128)S(1)}, f32[128,128]{1,0:T(8,128)}, u32[]{:S(2)}) copy-start(f32[128,128]{1,0:T(8,128)} %param.10) | copy-start | bytes 196612
  43.8 5.9 %collective-permute-start.1 = (f32[8,4,256]{2,1,0:T(4,128)S(1)}, f32[8,4,256]{2,1,0:T(4,128)S(1)}, u32[]{:S(2)}, u32[]{:S(2)}) collective-permute-start(f32[8,4,256]{2,1,0:T(4,128)S(1)} %bitcast.134), channel_id=1, source_target_pairs={{1,0},{2,1},{3,2},{4,3},{5,4},{6,5},{7,6},{8,7},{9,8},{10,9},{11,1... | collective-permute-start | bytes 98312 | tf_op jit(solution)/shard_map/ppermute | solution.py:17
  46.1 4.3 %collective-permute-start = (f32[8,4,256]{2,1,0:T(4,128)S(1)}, f32[8,4,256]{2,1,0:T(4,128)S(1)}, u32[]{:S(2)}, u32[]{:S(2)}) collective-permute-start(f32[8,4,256]{2,1,0:T(4,128)S(1)} %bitcast.135), channel_id=1, source_target_pairs={{0,1},{1,2},{2,3},{3,4},{4,5},{5,6},{6,7},{7,8},{8,9},{9,10},{10,1... | collective-permute-start | bytes 98312 | tf_op jit(solution)/shard_map/ppermute | solution.py:16
  51.0 6.5 %collective-permute-start.5 = (f32[8,4,256]{2,1,0:T(4,128)S(1)}, f32[8,4,256]{2,1,0:T(4,128)S(1)}, u32[]{:S(2)}, u32[]{:S(2)}) collective-permute-start(f32[8,4,256]{2,1,0:T(4,128)S(1)} %fusion.207), channel_id=1, source_target_pairs={{1,0},{2,1},{3,2},{4,3},{5,4},{6,5},{7,6},{8,7},{9,8},{10,9},{11,1... | collective-permute-start | bytes 98312 | tf_op jit(solution)/shard_map/ppermute | solution.py:17
  53.0 5.2 %collective-permute-start.4 = (f32[8,4,256]{2,1,0:T(4,128)S(1)}, f32[8,4,256]{2,1,0:T(4,128)S(1)}, u32[]{:S(2)}, u32[]{:S(2)}) collective-permute-start(f32[8,4,256]{2,1,0:T(4,128)S(1)} %fusion.207), channel_id=1, source_target_pairs={{0,1},{1,2},{2,3},{3,4},{4,5},{5,6},{6,7},{7,8},{8,9},{9,10},{10,1... | collective-permute-start | bytes 98312 | tf_op jit(solution)/shard_map/ppermute | solution.py:16
  61.0 5.1 %copy-start.6 = (s32[512]{0:T(512)S(1)}, s32[512]{0:T(512)}, u32[]{:S(2)}) copy-start(s32[512]{0:T(512)} %copy-done.5) | copy-start | bytes 6148
  61.8 13.7 %copy-start.4 = (f32[512]{0:T(512)S(1)}, f32[512]{0:T(512)}, u32[]{:S(2)}) copy-start(f32[512]{0:T(512)} %copy-done.3) | copy-start | bytes 6148
  61.8 13.8 %copy-start.9 = (f32[128]{0:T(128)S(1)}, f32[128]{0:T(128)}, u32[]{:S(2)}) copy-start(f32[128]{0:T(128)} %param.13) | copy-start | bytes 1540
  61.8 12.7 %all-to-all-start.1 = ((f32[4,4,64,128]{3,2,1,0:T(8,128)}), f32[4,4,64,128]{3,2,1,0:T(8,128)S(1)}, u32[]{:S(2)}, u32[]{:S(2)}) async-start(f32[4,4,64,128]{3,2,1,0:T(8,128)} %copy.62), calls=%async_computation.1 | async-start | bytes 1048576 | tf_op jit(solution)/shard_map/all_to_all | solution.py:158
  88.2 6.9 %collective-permute-start.7 = (f32[8,4,256]{2,1,0:T(4,128)S(1)}, f32[8,4,256]{2,1,0:T(4,128)S(1)}, u32[]{:S(2)}, u32[]{:S(2)}) collective-permute-start(f32[8,4,256]{2,1,0:T(4,128)S(1)} %bitcast.131), channel_id=1, source_target_pairs={{1,0},{2,1},{3,2},{4,3},{5,4},{6,5},{7,6},{8,7},{9,8},{10,9},{11,1... | collective-permute-start | bytes 98312 | tf_op jit(solution)/shard_map/ppermute | solution.py:17
  90.5 4.7 %collective-permute-start.6 = (f32[8,4,256]{2,1,0:T(4,128)S(1)}, f32[8,4,256]{2,1,0:T(4,128)S(1)}, u32[]{:S(2)}, u32[]{:S(2)}) collective-permute-start(f32[8,4,256]{2,1,0:T(4,128)S(1)} %bitcast.132), channel_id=1, source_target_pairs={{0,1},{1,2},{2,3},{3,4},{4,5},{5,6},{6,7},{7,8},{8,9},{9,10},{10,1... | collective-permute-start | bytes 98312 | tf_op jit(solution)/shard_map/ppermute | solution.py:16
  101.1 26.1 %all-to-all-start.3 = ((f32[256,1,3]{2,1,0:T(1,128)}), f32[256,1,3]{2,1,0:T(1,128)S(1)}, u32[]{:S(2)}, u32[]{:S(2)}) async-start(f32[256,1,3]{2,1,0:T(1,128)} %broadcast_in_dim.34), calls=%async_computation.3 | async-start | bytes 262144 | tf_op jit(solution)/shard_map/all_to_all | solution.py:58
  114.3 18.3 %collective-permute-start.9 = (f32[8,4,256]{2,1,0:T(4,128)S(1)}, f32[8,4,256]{2,1,0:T(4,128)S(1)}, u32[]{:S(2)}, u32[]{:S(2)}) collective-permute-start(f32[8,4,256]{2,1,0:T(4,128)S(1)} %get-tuple-element.11), channel_id=1, source_target_pairs={{1,0},{2,1},{3,2},{4,3},{5,4},{6,5},{7,6},{8,7},{9,8},{10,9},{11,1... | collective-permute-start | bytes 98312 | tf_op jit(solution)/shard_map/ppermute | solution.py:17
  118.4 14.3 %collective-permute-start.8 = (f32[8,4,256]{2,1,0:T(4,128)S(1)}, f32[8,4,256]{2,1,0:T(4,128)S(1)}, u32[]{:S(2)}, u32[]{:S(2)}) collective-permute-start(f32[8,4,256]{2,1,0:T(4,128)S(1)} %get-tuple-element.11), channel_id=1, source_target_pairs={{0,1},{1,2},{2,3},{3,4},{4,5},{5,6},{6,7},{7,8},{8,9},{9,10},{10,1... | collective-permute-start | bytes 98312 | tf_op jit(solution)/shard_map/ppermute | solution.py:16
  136.6 12.2 %all-to-all-start.4 = ((f32[4,4,64,128]{3,2,1,0:T(8,128)}), f32[4,4,64,128]{3,2,1,0:T(8,128)S(1)}, u32[]{:S(2)}, u32[]{:S(2)}) async-start(f32[4,4,64,128]{3,2,1,0:T(8,128)} %bitcast.103), calls=%async_computation.4 | async-start | bytes 1048576 | tf_op jit(solution)/shard_map/all_to_all | solution.py:158

commit v13 on v12

--- a/solution.py
+++ b/solution.py
@@ -156,7 +156,11 @@
     def observed(partial_sum):
         pieces = jnp.moveaxis(partial_sum.reshape(rows_here, parts, quarter, features), 1, 0)
         own_image = jnp.sum(lax.all_to_all(pieces, "mem", 0, 0, tiled=True), axis=0)
-        gathered = own_image.reshape(rows_here * quarter, features)[quarter_index]
+        gathered = jnp.dot(
+            quarter_placement.T,
+            own_image.reshape(rows_here * quarter, features),
+            precision=lax.Precision.HIGHEST,
+        )
         model_obs = jnp.dot(gathered, obs_jacobian, precision=lax.Precision.HIGHEST)
         return own_image, model_obs
 

time: 175 us -> 174 us (level)
  local copies, waits for them, and re-layouts: 10.8 us -> 8.77 us
    gather x2 -> x0, local copies, waits for them, and re-layouts: 2.07 us -> none  [observed(): gathered = own_image.reshape(rows_here * quarter, features)[quarter_index]]
where the time goes in v13:
time: 174 us; the launch traced here: 173 us
  starting transfers between devices  63 us (36%)
  waiting for transfers between devices  35.5 us (20%)
  blocking collectives  28.9 us (17%)
  matrix products  13.1 us (8%)
  between operations  12.4 us (7%)
  other arithmetic  11.2 us (6%)
  local copies, waits for them, and re-layouts  8.77 us (5%)
    all_to_all x1, blocking collectives, global_sum(): return jnp.sum(lax.all_to_all(spread, axes, 0, 0, tiled=True), axis=0)  19.5 us
    ppermute x5, starting transfers between devices, neighbours(): below.insert(0, lax.ppermute(block, axis, forward))  16.6 us
    all_to_all x2, waiting for transfers between devices, observed(): own_image = jnp.sum(lax.all_to_all(pieces, 'mem', 0, 0, tiled=True), axis=0)  15.3 us
    all_to_all x1, starting transfers between devices, global_sum(): return jnp.sum(lax.all_to_all(spread, axes, 0, 0, tiled=True), axis=0)  13.3 us
    all_to_all x1, starting transfers between devices, shards(): got = lax.all_to_all(packed, 'col', split_axis=0, concat_axis=0, tiled=True)  13.1 us
    ppermute x5, starting transfers between devices, neighbours(): above.append(lax.ppermute(block, axis, backward))  12.5 us
    all_to_all x1, blocking collectives, observed_adjoint(): quarters = lax.all_to_all(spread, 'mem', 0, 0, tiled=True)  9.44 us
    all_to_all x2, starting transfers between devices, observed(): own_image = jnp.sum(lax.all_to_all(pieces, 'mem', 0, 0, tiled=True), axis=0)  7.47 us
  transfers between devices with their start and end apart: 14, of which 9 were waited for; matrix products, arithmetic and copies ran while one was open for 2% of the time, Pallas kernels for 0%

profile of v13, /device:TPU:1, one launch (start us, length us, event | category | flops | bytes accessed | tf_op | source)
XLA Modules:
  0.0 172.9 jit_solution(8858537026923247751)
XLA Ops:
  9.2 13.1 %all-to-all-start = ((f32[64,9,128]{2,1,0:T(8,128)}), f32[64,9,128]{2,1,0:T(8,128)S(1)}, u32[]{:S(2)}, u32[]{:S(2)}) async-start(f32[64,9,128]{2,1,0:T(8,128)} %pad_maximum_fusion), calls=%async_computation | async-start | bytes 1048576 | tf_op jit(solution)/shard_map/all_to_all | solution.py:105
  22.4 3.5 %collective-permute-start.2 = (f32[4,256]{1,0:T(4,128)S(1)}, f32[4,256]{1,0:T(4,128)S(1)}, u32[]{:S(2)}, u32[]{:S(2)}) collective-permute-start(f32[4,256]{1,0:T(4,128)S(1)} %copy-done.3), channel_id=1, source_target_pairs={{0,1},{1,2},{2,3},{3,4},{4,5},{5,6},{6,7},{7,8},{8,9},{9,10},{10,1... | collective-permute-start | bytes 12296 | tf_op jit(solution)/shard_map/ppermute | solution.py:16
  25.9 1.9 %collective-permute-start.3 = (f32[4,256]{1,0:T(4,128)S(1)}, f32[4,256]{1,0:T(4,128)S(1)}, u32[]{:S(2)}, u32[]{:S(2)}) collective-permute-start(f32[4,256]{1,0:T(4,128)S(1)} %copy-done.3), channel_id=1, source_target_pairs={{1,0},{2,1},{3,2},{4,3},{5,4},{6,5},{7,6},{8,7},{9,8},{10,9},{11,1... | collective-permute-start | bytes 12296 | tf_op jit(solution)/shard_map/ppermute | solution.py:17
  27.9 3.0 %collective-permute-done.2 = f32[4,256]{1,0:T(4,128)S(1)} collective-permute-done((f32[4,256]{1,0:T(4,128)S(1)}, f32[4,256]{1,0:T(4,128)S(1)}, u32[]{:S(2)}, u32[]{:S(2)}) %collective-permute-start.2) | collective-permute-done | bytes 4128 | tf_op jit(solution)/shard_map/ppermute | solution.py:16
  30.9 5.2 %collective-permute-done.3 = f32[4,256]{1,0:T(4,128)S(1)} collective-permute-done((f32[4,256]{1,0:T(4,128)S(1)}, f32[4,256]{1,0:T(4,128)S(1)}, u32[]{:S(2)}, u32[]{:S(2)}) %collective-permute-start.3) | collective-permute-done | bytes 4128 | tf_op jit(solution)/shard_map/ppermute | solution.py:17
  36.3 3.6 %all-to-all-done = f32[64,9,128]{2,1,0:T(8,128)S(1)} async-done(((f32[64,9,128]{2,1,0:T(8,128)}), f32[64,9,128]{2,1,0:T(8,128)S(1)}, u32[]{:S(2)}, u32[]{:S(2)}) %all-to-all-start) | async-done | bytes 294944 | tf_op jit(solution)/shard_map/all_to_all | solution.py:105
  43.7 2.3 %collective-permute-start.1 = (f32[8,4,256]{2,1,0:T(4,128)S(1)}, f32[8,4,256]{2,1,0:T(4,128)S(1)}, u32[]{:S(2)}, u32[]{:S(2)}) collective-permute-start(f32[8,4,256]{2,1,0:T(4,128)S(1)} %bitcast.134), channel_id=1, source_target_pairs={{1,0},{2,1},{3,2},{4,3},{5,4},{6,5},{7,6},{8,7},{9,8},{10,9},{11,1... | collective-permute-start | bytes 98312 | tf_op jit(solution)/shard_map/ppermute | solution.py:17
  46.0 3.3 %collective-permute-start = (f32[8,4,256]{2,1,0:T(4,128)S(1)}, f32[8,4,256]{2,1,0:T(4,128)S(1)}, u32[]{:S(2)}, u32[]{:S(2)}) collective-permute-start(f32[8,4,256]{2,1,0:T(4,128)S(1)} %bitcast.135), channel_id=1, source_target_pairs={{0,1},{1,2},{2,3},{3,4},{4,5},{5,6},{6,7},{7,8},{8,9},{9,10},{10,1... | collective-permute-start | bytes 98312 | tf_op jit(solution)/shard_map/ppermute | solution.py:16
  51.0 1.9 %collective-permute-start.5 = (f32[8,4,256]{2,1,0:T(4,128)S(1)}, f32[8,4,256]{2,1,0:T(4,128)S(1)}, u32[]{:S(2)}, u32[]{:S(2)}) collective-permute-start(f32[8,4,256]{2,1,0:T(4,128)S(1)} %fusion.215), channel_id=1, source_target_pairs={{1,0},{2,1},{3,2},{4,3},{5,4},{6,5},{7,6},{8,7},{9,8},{10,9},{11,1... | collective-permute-start | bytes 98312 | tf_op jit(solution)/shard_map/ppermute | solution.py:17
  52.9 4.2 %collective-permute-start.4 = (f32[8,4,256]{2,1,0:T(4,128)S(1)}, f32[8,4,256]{2,1,0:T(4,128)S(1)}, u32[]{:S(2)}, u32[]{:S(2)}) collective-permute-start(f32[8,4,256]{2,1,0:T(4,128)S(1)} %fusion.215), channel_id=1, source_target_pairs={{0,1},{1,2},{2,3},{3,4},{4,5},{5,6},{6,7},{7,8},{8,9},{9,10},{10,1... | collective-permute-start | bytes 98312 | tf_op jit(solution)/shard_map/ppermute | solution.py:16
  59.2 1.7 fusion.5
  61.8 4.0 %all-to-all-start.1 = ((f32[4,4,64,128]{3,2,1,0:T(8,128)}), f32[4,4,64,128]{3,2,1,0:T(8,128)S(1)}, u32[]{:S(2)}, u32[]{:S(2)}) async-start(f32[4,4,64,128]{3,2,1,0:T(8,128)} %copy.62), calls=%async_computation.1 | async-start | bytes 1048576 | tf_op jit(solution)/shard_map/all_to_all | solution.py:158
  65.8 8.5 %all-to-all-done.1 = f32[4,4,64,128]{3,2,1,0:T(8,128)S(1)} async-done(((f32[4,4,64,128]{3,2,1,0:T(8,128)}), f32[4,4,64,128]{3,2,1,0:T(8,128)S(1)}, u32[]{:S(2)}, u32[]{:S(2)}) %all-to-all-start.1) | async-done | bytes 524320 | tf_op jit(solution)/shard_map/all_to_all | solution.py:158
  76.2 9.4 %all_to_all.32 = bf16[4,4,64,128]{3,2,1,0:T(8,128)(2,1)S(1)} all-to-all(bf16[4,4,64,128]{3,2,1,0:T(8,128)(2,1)S(1)} %broadcast_in_dim.33), channel_id=1, replica_groups=mesh['mem'=4,'col'=64] {'mem'}, dimensions={0} | all-to-all | bytes 524288 | tf_op jit(solution)/shard_map/all_to_all | solution.py:175
  87.5 2.3 %collective-permute-start.7 = (f32[8,4,256]{2,1,0:T(4,128)S(1)}, f32[8,4,256]{2,1,0:T(4,128)S(1)}, u32[]{:S(2)}, u32[]{:S(2)}) collective-permute-start(f32[8,4,256]{2,1,0:T(4,128)S(1)} %bitcast.131), channel_id=1, source_target_pairs={{1,0},{2,1},{3,2},{4,3},{5,4},{6,5},{7,6},{8,7},{9,8},{10,9},{11,1... | collective-permute-start | bytes 98312 | tf_op jit(solution)/shard_map/ppermute | solution.py:17
  89.8 3.7 %collective-permute-start.6 = (f32[8,4,256]{2,1,0:T(4,128)S(1)}, f32[8,4,256]{2,1,0:T(4,128)S(1)}, u32[]{:S(2)}, u32[]{:S(2)}) collective-permute-start(f32[8,4,256]{2,1,0:T(4,128)S(1)} %bitcast.132), channel_id=1, source_target_pairs={{0,1},{1,2},{2,3},{3,4},{4,5},{5,6},{6,7},{7,8},{8,9},{9,10},{10,1... | collective-permute-start | bytes 98312 | tf_op jit(solution)/shard_map/ppermute | solution.py:16
  100.4 13.3 %all-to-all-start.3 = ((f32[256,1,3]{2,1,0:T(1,128)}), f32[256,1,3]{2,1,0:T(1,128)S(1)}, u32[]{:S(2)}, u32[]{:S(2)}) async-start(f32[256,1,3]{2,1,0:T(1,128)} %broadcast_in_dim.34), calls=%async_computation.3 | async-start | bytes 262144 | tf_op jit(solution)/shard_map/all_to_all | solution.py:58
  113.7 4.1 %collective-permute-start.9 = (f32[8,4,256]{2,1,0:T(4,128)S(1)}, f32[8,4,256]{2,1,0:T(4,128)S(1)}, u32[]{:S(2)}, u32[]{:S(2)}) collective-permute-start(f32[8,4,256]{2,1,0:T(4,128)S(1)} %get-tuple-element.11), channel_id=1, source_target_pairs={{1,0},{2,1},{3,2},{4,3},{5,4},{6,5},{7,6},{8,7},{9,8},{10,9},{11,1... | collective-permute-start | bytes 98312 | tf_op jit(solution)/shard_map/ppermute | solution.py:17
  117.8 1.9 %collective-permute-start.8 = (f32[8,4,256]{2,1,0:T(4,128)S(1)}, f32[8,4,256]{2,1,0:T(4,128)S(1)}, u32[]{:S(2)}, u32[]{:S(2)}) collective-permute-start(f32[8,4,256]{2,1,0:T(4,128)S(1)} %get-tuple-element.11), channel_id=1, source_target_pairs={{0,1},{1,2},{2,3},{3,4},{4,5},{5,6},{6,7},{7,8},{8,9},{9,10},{10,1... | collective-permute-start | bytes 98312 | tf_op jit(solution)/shard_map/ppermute | solution.py:16
  119.7 6.9 %all-to-all-done.3 = f32[256,1,3]{2,1,0:T(1,128)S(1)} async-done(((f32[256,1,3]{2,1,0:T(1,128)}), f32[256,1,3]{2,1,0:T(1,128)S(1)}, u32[]{:S(2)}, u32[]{:S(2)}) %all-to-all-start.3) | async-done | bytes 3104 | tf_op jit(solution)/shard_map/all_to_all | solution.py:58
  133.2 1.7 fusion.1
  136.0 3.5 %all-to-all-start.4 = ((f32[4,4,64,128]{3,2,1,0:T(8,128)}), f32[4,4,64,128]{3,2,1,0:T(8,128)S(1)}, u32[]{:S(2)}, u32[]{:S(2)}) async-start(f32[4,4,64,128]{3,2,1,0:T(8,128)} %bitcast.103), calls=%async_computation.4 | async-start | bytes 1048576 | tf_op jit(solution)/shard_map/all_to_all | solution.py:158
  141.4 6.8 %all-to-all-done.4 = f32[4,4,64,128]{3,2,1,0:T(8,128)S(1)} async-done(((f32[4,4,64,128]{3,2,1,0:T(8,128)}), f32[4,4,64,128]{3,2,1,0:T(8,128)S(1)}, u32[]{:S(2)}, u32[]{:S(2)}) %all-to-all-start.4) | async-done | bytes 524320 | tf_op jit(solution)/shard_map/all_to_all | solution.py:158
  150.5 19.5 %all_to_all.33 = f32[256,1,1]{2,1,0:T(1,128)S(1)} all-to-all(f32[256,1,1]{2,1,0:T(1,128)S(1)} %broadcast_in_dim.35), channel_id=1, replica_groups=mesh['mem'=4,'col'=64] {'mem','col'}, dimensions={0} | all-to-all | bytes 2048 | tf_op jit(solution)/shard_map/all_to_all | solution.py:58
  (107 shorter events, 31.1 us)
Async XLA Ops:
  0.6 41.2 %copy-start = (bf16[8,4,256,128]{3,2,1,0:T(8,128)(2,1)S(1)}, bf16[8,4,256,128]{3,2,1,0:T(8,128)(2,1)}, u32[]{:S(2)}) copy-start(bf16[8,4,256,128]{3,2,1,0:T(8,128)(2,1)} %param.9) | copy-start | bytes 6291460
  0.6 21.7 %copy-start.3 = (f32[4,256]{1,0:T(4,128)S(1)}, f32[4,256]{1,0:T(4,128)}, u32[]{:S(2)}) copy-start(f32[4,256]{1,0:T(4,128)} %param.14) | copy-start | bytes 12292
  0.7 39.7 %copy-start.2 = (f32[128,128]{1,0:T(8,128)S(1)}, f32[128,128]{1,0:T(8,128)}, u32[]{:S(2)}) copy-start(f32[128,128]{1,0:T(8,128)} %param.11) | copy-start | bytes 196612
  0.7 39.7 %copy-start.4 = (f32[128]{0:T(128)S(1)}, f32[128]{0:T(128)}, u32[]{:S(2)}) copy-start(f32[128]{0:T(128)} %param.13) | copy-start | bytes 1540
  9.2 30.6 %all-to-all-start = ((f32[64,9,128]{2,1,0:T(8,128)}), f32[64,9,128]{2,1,0:T(8,128)S(1)}, u32[]{:S(2)}, u32[]{:S(2)}) async-start(f32[64,9,128]{2,1,0:T(8,128)} %pad_maximum_fusion), calls=%async_computation | async-start | bytes 1048576 | tf_op jit(solution)/shard_map/all_to_all | solution.py:105
  22.4 8.5 %collective-permute-start.2 = (f32[4,256]{1,0:T(4,128)S(1)}, f32[4,256]{1,0:T(4,128)S(1)}, u32[]{:S(2)}, u32[]{:S(2)}) collective-permute-start(f32[4,256]{1,0:T(4,128)S(1)} %copy-done.3), channel_id=1, source_target_pairs={{0,1},{1,2},{2,3},{3,4},{4,5},{5,6},{6,7},{7,8},{8,9},{9,10},{10,1... | collective-permute-start | bytes 12296 | tf_op jit(solution)/shard_map/ppermute | solution.py:16
  25.9 10.2 %collective-permute-start.3 = (f32[4,256]{1,0:T(4,128)S(1)}, f32[4,256]{1,0:T(4,128)S(1)}, u32[]{:S(2)}, u32[]{:S(2)}) collective-permute-start(f32[4,256]{1,0:T(4,128)S(1)} %copy-done.3), channel_id=1, source_target_pairs={{1,0},{2,1},{3,2},{4,3},{5,4},{6,5},{7,6},{8,7},{9,8},{10,9},{11,1... | collective-permute-start | bytes 12296 | tf_op jit(solution)/shard_map/ppermute | solution.py:17
  41.9 7.5 %copy-start.1 = (f32[128,128]{1,0:T(8,128)S(1)}, f32[128,128]{1,0:T(8,128)}, u32[]{:S(2)}) copy-start(f32[128,128]{1,0:T(8,128)} %param.10) | copy-start | bytes 196612
  43.7 5.9 %collective-permute-start.1 = (f32[8,4,256]{2,1,0:T(4,128)S(1)}, f32[8,4,256]{2,1,0:T(4,128)S(1)}, u32[]{:S(2)}, u32[]{:S(2)}) collective-permute-start(f32[8,4,256]{2,1,0:T(4,128)S(1)} %bitcast.134), channel_id=1, source_target_pairs={{1,0},{2,1},{3,2},{4,3},{5,4},{6,5},{7,6},{8,7},{9,8},{10,9},{11,1... | collective-permute-start | bytes 98312 | tf_op jit(solution)/shard_map/ppermute | solution.py:17
  46.0 4.3 %collective-permute-start = (f32[8,4,256]{2,1,0:T(4,128)S(1)}, f32[8,4,256]{2,1,0:T(4,128)S(1)}, u32[]{:S(2)}, u32[]{:S(2)}) collective-permute-start(f32[8,4,256]{2,1,0:T(4,128)S(1)} %bitcast.135), channel_id=1, source_target_pairs={{0,1},{1,2},{2,3},{3,4},{4,5},{5,6},{6,7},{7,8},{8,9},{9,10},{10,1... | collective-permute-start | bytes 98312 | tf_op jit(solution)/shard_map/ppermute | solution.py:16
  51.0 6.4 %collective-permute-start.5 = (f32[8,4,256]{2,1,0:T(4,128)S(1)}, f32[8,4,256]{2,1,0:T(4,128)S(1)}, u32[]{:S(2)}, u32[]{:S(2)}) collective-permute-start(f32[8,4,256]{2,1,0:T(4,128)S(1)} %fusion.215), channel_id=1, source_target_pairs={{1,0},{2,1},{3,2},{4,3},{5,4},{6,5},{7,6},{8,7},{9,8},{10,9},{11,1... | collective-permute-start | bytes 98312 | tf_op jit(solution)/shard_map/ppermute | solution.py:17
  52.9 5.2 %collective-permute-start.4 = (f32[8,4,256]{2,1,0:T(4,128)S(1)}, f32[8,4,256]{2,1,0:T(4,128)S(1)}, u32[]{:S(2)}, u32[]{:S(2)}) collective-permute-start(f32[8,4,256]{2,1,0:T(4,128)S(1)} %fusion.215), channel_id=1, source_target_pairs={{0,1},{1,2},{2,3},{3,4},{4,5},{5,6},{6,7},{7,8},{8,9},{9,10},{10,1... | collective-permute-start | bytes 98312 | tf_op jit(solution)/shard_map/ppermute | solution.py:16
  61.8 12.5 %all-to-all-start.1 = ((f32[4,4,64,128]{3,2,1,0:T(8,128)}), f32[4,4,64,128]{3,2,1,0:T(8,128)S(1)}, u32[]{:S(2)}, u32[]{:S(2)}) async-start(f32[4,4,64,128]{3,2,1,0:T(8,128)} %copy.62), calls=%async_computation.1 | async-start | bytes 1048576 | tf_op jit(solution)/shard_map/all_to_all | solution.py:158
  87.5 6.9 %collective-permute-start.7 = (f32[8,4,256]{2,1,0:T(4,128)S(1)}, f32[8,4,256]{2,1,0:T(4,128)S(1)}, u32[]{:S(2)}, u32[]{:S(2)}) collective-permute-start(f32[8,4,256]{2,1,0:T(4,128)S(1)} %bitcast.131), channel_id=1, source_target_pairs={{1,0},{2,1},{3,2},{4,3},{5,4},{6,5},{7,6},{8,7},{9,8},{10,9},{11,1... | collective-permute-start | bytes 98312 | tf_op jit(solution)/shard_map/ppermute | solution.py:17
  89.8 4.7 %collective-permute-start.6 = (f32[8,4,256]{2,1,0:T(4,128)S(1)}, f32[8,4,256]{2,1,0:T(4,128)S(1)}, u32[]{:S(2)}, u32[]{:S(2)}) collective-permute-start(f32[8,4,256]{2,1,0:T(4,128)S(1)} %bitcast.132), channel_id=1, source_target_pairs={{0,1},{1,2},{2,3},{3,4},{4,5},{5,6},{6,7},{7,8},{8,9},{9,10},{10,1... | collective-permute-start | bytes 98312 | tf_op jit(solution)/shard_map/ppermute | solution.py:16
  100.4 26.2 %all-to-all-start.3 = ((f32[256,1,3]{2,1,0:T(1,128)}), f32[256,1,3]{2,1,0:T(1,128)S(1)}, u32[]{:S(2)}, u32[]{:S(2)}) async-start(f32[256,1,3]{2,1,0:T(1,128)} %broadcast_in_dim.34), calls=%async_computation.3 | async-start | bytes 262144 | tf_op jit(solution)/shard_map/all_to_all | solution.py:58
  113.7 18.3 %collective-permute-start.9 = (f32[8,4,256]{2,1,0:T(4,128)S(1)}, f32[8,4,256]{2,1,0:T(4,128)S(1)}, u32[]{:S(2)}, u32[]{:S(2)}) collective-permute-start(f32[8,4,256]{2,1,0:T(4,128)S(1)} %get-tuple-element.11), channel_id=1, source_target_pairs={{1,0},{2,1},{3,2},{4,3},{5,4},{6,5},{7,6},{8,7},{9,8},{10,9},{11,1... | collective-permute-start | bytes 98312 | tf_op jit(solution)/shard_map/ppermute | solution.py:17
  117.8 14.3 %collective-permute-start.8 = (f32[8,4,256]{2,1,0:T(4,128)S(1)}, f32[8,4,256]{2,1,0:T(4,128)S(1)}, u32[]{:S(2)}, u32[]{:S(2)}) collective-permute-start(f32[8,4,256]{2,1,0:T(4,128)S(1)} %get-tuple-element.11), channel_id=1, source_target_pairs={{0,1},{1,2},{2,3},{3,4},{4,5},{5,6},{6,7},{7,8},{8,9},{9,10},{10,1... | collective-permute-start | bytes 98312 | tf_op jit(solution)/shard_map/ppermute | solution.py:16
  136.0 12.2 %all-to-all-start.4 = ((f32[4,4,64,128]{3,2,1,0:T(8,128)}), f32[4,4,64,128]{3,2,1,0:T(8,128)S(1)}, u32[]{:S(2)}, u32[]{:S(2)}) async-start(f32[4,4,64,128]{3,2,1,0:T(8,128)} %bitcast.103), calls=%async_computation.4 | async-start | bytes 1048576 | tf_op jit(solution)/shard_map/all_to_all | solution.py:158

commit v14 on v13

--- a/solution.py
+++ b/solution.py
@@ -141,8 +141,7 @@
             static_root,
             precision=lax.Precision.HIGHEST,
         ).reshape(rows_here, quarter, features)
-        own_slice = lax.dynamic_slice_in_dim(partial_sum, offset, quarter, 1) + forward_static
-        return lax.dynamic_update_slice_in_dim(partial_sum, own_slice, offset, 1)
+        return partial_sum, forward_static
 
     cell_x = obs_index % columns
     in_quarter = (cell_x >= offset) & (cell_x < offset + quarter)
@@ -153,9 +152,10 @@
         & in_quarter[None, :]
     ).astype(jnp.float32)
 
-    def observed(partial_sum):
+    def observed(parts_of_image):
+        partial_sum, forward_static = parts_of_image
         pieces = jnp.moveaxis(partial_sum.reshape(rows_here, parts, quarter, features), 1, 0)
-        own_image = jnp.sum(lax.all_to_all(pieces, "mem", 0, 0, tiled=True), axis=0)
+        own_image = jnp.sum(lax.all_to_all(pieces, "mem", 0, 0, tiled=True), axis=0) + forward_static
         gathered = jnp.dot(
             quarter_placement.T,
             own_image.reshape(rows_here * quarter, features),

time: 174 us -> 179 us (1.029)
  waiting for transfers between devices: 35.5 us -> 41 us
  starting transfers between devices: 63 us -> 57.7 us
  matrix products: 13.1 us -> 16.2 us
  other arithmetic: 11.2 us -> 13.3 us
    ppermute x5, waiting for transfers between devices: 5.25 us -> 12.9 us  [neighbours(): above.append(lax.ppermute(block, axis, backward))]
    all_to_all x1, starting transfers between devices: 13.3 us -> 10.9 us  [global_sum(): return jnp.sum(lax.all_to_all(spread, axes, 0, 0, tiled=True), axis=0)]
    ppermute x5, starting transfers between devices: 12.5 us -> 10.1 us  [neighbours(): above.append(lax.ppermute(block, axis, backward))]
  transfers between devices with their start and end apart: 14 -> 14, of which waited for: 9 -> 9; matrix products, arithmetic and copies ran while one was open for 2% -> 3% of each run, Pallas kernels for 0% -> 0%
where the time goes in v14:
time: 179 us; the launch traced here: 178 us
  starting transfers between devices  57.7 us (32%)
  waiting for transfers between devices  41 us (23%)
  blocking collectives  28.8 us (16%)
  matrix products  16.2 us (9%)
  other arithmetic  13.3 us (7%)
  between operations  12.4 us (7%)
  local copies, waits for them, and re-layouts  8.87 us (5%)
    all_to_all x1, blocking collectives, global_sum(): return jnp.sum(lax.all_to_all(spread, axes, 0, 0, tiled=True), axis=0)  19.5 us
    ppermute x5, starting transfers between devices, neighbours(): below.insert(0, lax.ppermute(block, axis, forward))  16.1 us
    all_to_all x2, waiting for transfers between devices, observed(): lax.all_to_all(pieces, 'mem', 0, 0, tiled=True)  14.1 us
    all_to_all x1, starting transfers between devices, shards(): got = lax.all_to_all(packed, 'col', split_axis=0, concat_axis=0, tiled=True)  13.1 us
    ppermute x5, waiting for transfers between devices, neighbours(): above.append(lax.ppermute(block, axis, backward))  12.9 us
    all_to_all x1, starting transfers between devices, global_sum(): return jnp.sum(lax.all_to_all(spread, axes, 0, 0, tiled=True), axis=0)  10.9 us
    ppermute x5, starting transfers between devices, neighbours(): above.append(lax.ppermute(block, axis, backward))  10.1 us
    all_to_all x1, blocking collectives, observed_adjoint(): quarters = lax.all_to_all(spread, 'mem', 0, 0, tiled=True)  9.36 us
  transfers between devices with their start and end apart: 14, of which 9 were waited for; matrix products, arithmetic and copies ran while one was open for 3% of the time, Pallas kernels for 0%

profile of v14, /device:TPU:1, one launch (start us, length us, event | category | flops | bytes accessed | tf_op | source)
XLA Modules:
  0.0 178.1 jit_solution(2169177047017050347)
XLA Ops:
  9.2 13.1 %all-to-all-start = ((f32[64,9,128]{2,1,0:T(8,128)}), f32[64,9,128]{2,1,0:T(8,128)S(1)}, u32[]{:S(2)}, u32[]{:S(2)}) async-start(f32[64,9,128]{2,1,0:T(8,128)} %pad_maximum_fusion), calls=%async_computation | async-start | bytes 1048576 | tf_op jit(solution)/shard_map/all_to_all | solution.py:105
  22.4 3.5 %collective-permute-start.2 = (f32[4,256]{1,0:T(4,128)S(1)}, f32[4,256]{1,0:T(4,128)S(1)}, u32[]{:S(2)}, u32[]{:S(2)}) collective-permute-start(f32[4,256]{1,0:T(4,128)S(1)} %copy-done.15), channel_id=1, source_target_pairs={{0,1},{1,2},{2,3},{3,4},{4,5},{5,6},{6,7},{7,8},{8,9},{9,10},{10,1... | collective-permute-start | bytes 12296 | tf_op jit(solution)/shard_map/ppermute | solution.py:16
  25.9 1.9 %collective-permute-start.3 = (f32[4,256]{1,0:T(4,128)S(1)}, f32[4,256]{1,0:T(4,128)S(1)}, u32[]{:S(2)}, u32[]{:S(2)}) collective-permute-start(f32[4,256]{1,0:T(4,128)S(1)} %copy-done.15), channel_id=1, source_target_pairs={{1,0},{2,1},{3,2},{4,3},{5,4},{6,5},{7,6},{8,7},{9,8},{10,9},{11,1... | collective-permute-start | bytes 12296 | tf_op jit(solution)/shard_map/ppermute | solution.py:17
  27.9 3.0 %collective-permute-done.2 = f32[4,256]{1,0:T(4,128)S(1)} collective-permute-done((f32[4,256]{1,0:T(4,128)S(1)}, f32[4,256]{1,0:T(4,128)S(1)}, u32[]{:S(2)}, u32[]{:S(2)}) %collective-permute-start.2) | collective-permute-done | bytes 4128 | tf_op jit(solution)/shard_map/ppermute | solution.py:16
  30.9 5.2 %collective-permute-done.3 = f32[4,256]{1,0:T(4,128)S(1)} collective-permute-done((f32[4,256]{1,0:T(4,128)S(1)}, f32[4,256]{1,0:T(4,128)S(1)}, u32[]{:S(2)}, u32[]{:S(2)}) %collective-permute-start.3) | collective-permute-done | bytes 4128 | tf_op jit(solution)/shard_map/ppermute | solution.py:17
  36.1 3.8 %all-to-all-done = f32[64,9,128]{2,1,0:T(8,128)S(1)} async-done(((f32[64,9,128]{2,1,0:T(8,128)}), f32[64,9,128]{2,1,0:T(8,128)S(1)}, u32[]{:S(2)}, u32[]{:S(2)}) %all-to-all-start) | async-done | bytes 294944 | tf_op jit(solution)/shard_map/all_to_all | solution.py:105
  43.7 3.1 %collective-permute-start = (f32[8,4,256]{2,1,0:T(4,128)S(1)}, f32[8,4,256]{2,1,0:T(4,128)S(1)}, u32[]{:S(2)}, u32[]{:S(2)}) collective-permute-start(f32[8,4,256]{2,1,0:T(4,128)S(1)} %bitcast.128), channel_id=1, source_target_pairs={{0,1},{1,2},{2,3},{3,4},{4,5},{5,6},{6,7},{7,8},{8,9},{9,10},{10,1... | collective-permute-start | bytes 98312 | tf_op jit(solution)/shard_map/ppermute | solution.py:16
  46.9 1.9 %collective-permute-start.1 = (f32[8,4,256]{2,1,0:T(4,128)S(1)}, f32[8,4,256]{2,1,0:T(4,128)S(1)}, u32[]{:S(2)}, u32[]{:S(2)}) collective-permute-start(f32[8,4,256]{2,1,0:T(4,128)S(1)} %bitcast.129), channel_id=1, source_target_pairs={{1,0},{2,1},{3,2},{4,3},{5,4},{6,5},{7,6},{8,7},{9,8},{10,9},{11,1... | collective-permute-start | bytes 98312 | tf_op jit(solution)/shard_map/ppermute | solution.py:17
  49.0 3.2 %collective-permute-done.1 = f32[8,4,256]{2,1,0:T(4,128)S(1)} collective-permute-done((f32[8,4,256]{2,1,0:T(4,128)S(1)}, f32[8,4,256]{2,1,0:T(4,128)S(1)}, u32[]{:S(2)}, u32[]{:S(2)}) %collective-permute-start.1) | collective-permute-done | bytes 32800 | tf_op jit(solution)/shard_map/ppermute | solution.py:17
  52.8 1.9 %collective-permute-start.4 = (f32[8,4,256]{2,1,0:T(4,128)S(1)}, f32[8,4,256]{2,1,0:T(4,128)S(1)}, u32[]{:S(2)}, u32[]{:S(2)}) collective-permute-start(f32[8,4,256]{2,1,0:T(4,128)S(1)} %fusion.214), channel_id=1, source_target_pairs={{0,1},{1,2},{2,3},{3,4},{4,5},{5,6},{6,7},{7,8},{8,9},{9,10},{10,1... | collective-permute-start | bytes 98312 | tf_op jit(solution)/shard_map/ppermute | solution.py:16
  54.7 2.4 %collective-permute-start.5 = (f32[8,4,256]{2,1,0:T(4,128)S(1)}, f32[8,4,256]{2,1,0:T(4,128)S(1)}, u32[]{:S(2)}, u32[]{:S(2)}) collective-permute-start(f32[8,4,256]{2,1,0:T(4,128)S(1)} %fusion.214), channel_id=1, source_target_pairs={{1,0},{2,1},{3,2},{4,3},{5,4},{6,5},{7,6},{8,7},{9,8},{10,9},{11,1... | collective-permute-start | bytes 98312 | tf_op jit(solution)/shard_map/ppermute | solution.py:17
  57.1 2.8 %collective-permute-done.5 = f32[8,4,256]{2,1,0:T(4,128)S(1)} collective-permute-done((f32[8,4,256]{2,1,0:T(4,128)S(1)}, f32[8,4,256]{2,1,0:T(4,128)S(1)}, u32[]{:S(2)}, u32[]{:S(2)}) %collective-permute-start.5) | collective-permute-done | bytes 32800 | tf_op jit(solution)/shard_map/ppermute | solution.py:17
  64.2 4.0 %all-to-all-start.1 = ((f32[4,4,64,128]{3,2,1,0:T(8,128)}), f32[4,4,64,128]{3,2,1,0:T(8,128)S(1)}, u32[]{:S(2)}, u32[]{:S(2)}) async-start(f32[4,4,64,128]{3,2,1,0:T(8,128)} %copy.61), calls=%async_computation.1 | async-start | bytes 1048576 | tf_op jit(solution)/shard_map/all_to_all | solution.py:158
  69.1 7.9 %all-to-all-done.1 = f32[4,4,64,128]{3,2,1,0:T(8,128)S(1)} async-done(((f32[4,4,64,128]{3,2,1,0:T(8,128)}), f32[4,4,64,128]{3,2,1,0:T(8,128)S(1)}, u32[]{:S(2)}, u32[]{:S(2)}) %all-to-all-start.1) | async-done | bytes 524320 | tf_op jit(solution)/shard_map/all_to_all | solution.py:158
  81.6 9.4 %all_to_all.32 = bf16[4,4,64,128]{3,2,1,0:T(8,128)(2,1)S(1)} all-to-all(bf16[4,4,64,128]{3,2,1,0:T(8,128)(2,1)S(1)} %broadcast_in_dim.33), channel_id=1, replica_groups=mesh['mem'=4,'col'=64] {'mem'}, dimensions={0} | all-to-all | bytes 524288 | tf_op jit(solution)/shard_map/all_to_all | solution.py:175
  92.8 3.8 %collective-permute-start.6 = (f32[8,4,256]{2,1,0:T(4,128)S(1)}, f32[8,4,256]{2,1,0:T(4,128)S(1)}, u32[]{:S(2)}, u32[]{:S(2)}) collective-permute-start(f32[8,4,256]{2,1,0:T(4,128)S(1)} %bitcast.131), channel_id=1, source_target_pairs={{0,1},{1,2},{2,3},{3,4},{4,5},{5,6},{6,7},{7,8},{8,9},{9,10},{10,1... | collective-permute-start | bytes 98312 | tf_op jit(solution)/shard_map/ppermute | solution.py:16
  96.7 1.9 %collective-permute-start.7 = (f32[8,4,256]{2,1,0:T(4,128)S(1)}, f32[8,4,256]{2,1,0:T(4,128)S(1)}, u32[]{:S(2)}, u32[]{:S(2)}) collective-permute-start(f32[8,4,256]{2,1,0:T(4,128)S(1)} %bitcast.132), channel_id=1, source_target_pairs={{1,0},{2,1},{3,2},{4,3},{5,4},{6,5},{7,6},{8,7},{9,8},{10,9},{11,1... | collective-permute-start | bytes 98312 | tf_op jit(solution)/shard_map/ppermute | solution.py:17
  107.8 10.9 %all-to-all-start.3 = ((f32[256,1,3]{2,1,0:T(1,128)}), f32[256,1,3]{2,1,0:T(1,128)S(1)}, u32[]{:S(2)}, u32[]{:S(2)}) async-start(f32[256,1,3]{2,1,0:T(1,128)} %broadcast_in_dim.34), calls=%async_computation.3 | async-start | bytes 262144 | tf_op jit(solution)/shard_map/all_to_all | solution.py:58
  118.7 3.7 %collective-permute-start.8 = (f32[8,4,256]{2,1,0:T(4,128)S(1)}, f32[8,4,256]{2,1,0:T(4,128)S(1)}, u32[]{:S(2)}, u32[]{:S(2)}) collective-permute-start(f32[8,4,256]{2,1,0:T(4,128)S(1)} %get-tuple-element.11), channel_id=1, source_target_pairs={{0,1},{1,2},{2,3},{3,4},{4,5},{5,6},{6,7},{7,8},{8,9},{9,10},{10,1... | collective-permute-start | bytes 98312 | tf_op jit(solution)/shard_map/ppermute | solution.py:16
  122.3 1.9 %collective-permute-start.9 = (f32[8,4,256]{2,1,0:T(4,128)S(1)}, f32[8,4,256]{2,1,0:T(4,128)S(1)}, u32[]{:S(2)}, u32[]{:S(2)}) collective-permute-start(f32[8,4,256]{2,1,0:T(4,128)S(1)} %get-tuple-element.11), channel_id=1, source_target_pairs={{1,0},{2,1},{3,2},{4,3},{5,4},{6,5},{7,6},{8,7},{9,8},{10,9},{11,1... | collective-permute-start | bytes 98312 | tf_op jit(solution)/shard_map/ppermute | solution.py:17
  124.3 7.3 %all-to-all-done.3 = f32[256,1,3]{2,1,0:T(1,128)S(1)} async-done(((f32[256,1,3]{2,1,0:T(1,128)}), f32[256,1,3]{2,1,0:T(1,128)S(1)}, u32[]{:S(2)}, u32[]{:S(2)}) %all-to-all-start.3) | async-done | bytes 3104 | tf_op jit(solution)/shard_map/all_to_all | solution.py:58
  140.0 3.5 %all-to-all-start.4 = ((f32[4,4,64,128]{3,2,1,0:T(8,128)}), f32[4,4,64,128]{3,2,1,0:T(8,128)S(1)}, u32[]{:S(2)}, u32[]{:S(2)}) async-start(f32[4,4,64,128]{3,2,1,0:T(8,128)} %copy.64), calls=%async_computation.4 | async-start | bytes 1048576 | tf_op jit(solution)/shard_map/all_to_all | solution.py:158
  146.0 6.2 %all-to-all-done.4 = f32[4,4,64,128]{3,2,1,0:T(8,128)S(1)} async-done(((f32[4,4,64,128]{3,2,1,0:T(8,128)}), f32[4,4,64,128]{3,2,1,0:T(8,128)S(1)}, u32[]{:S(2)}, u32[]{:S(2)}) %all-to-all-start.4) | async-done | bytes 524320 | tf_op jit(solution)/shard_map/all_to_all | solution.py:158
  154.8 19.5 %all_to_all.33 = f32[256,1,1]{2,1,0:T(1,128)S(1)} all-to-all(f32[256,1,1]{2,1,0:T(1,128)S(1)} %broadcast_in_dim.35), channel_id=1, replica_groups=mesh['mem'=4,'col'=64] {'mem','col'}, dimensions={0} | all-to-all | bytes 2048 | tf_op jit(solution)/shard_map/all_to_all | solution.py:58
  (132 shorter events, 40.0 us)
Async XLA Ops:
  0.6 41.2 %copy-start = (bf16[8,4,256,128]{3,2,1,0:T(8,128)(2,1)S(1)}, bf16[8,4,256,128]{3,2,1,0:T(8,128)(2,1)}, u32[]{:S(2)}) copy-start(bf16[8,4,256,128]{3,2,1,0:T(8,128)(2,1)} %param.9) | copy-start | bytes 6291460
  0.6 21.7 %copy-start.15 = (f32[4,256]{1,0:T(4,128)S(1)}, f32[4,256]{1,0:T(4,128)}, u32[]{:S(2)}) copy-start(f32[4,256]{1,0:T(4,128)} %param.14) | copy-start | bytes 12292
  0.7 39.7 %copy-start.4 = (f32[128,128]{1,0:T(8,128)S(1)}, f32[128,128]{1,0:T(8,128)}, u32[]{:S(2)}) copy-start(f32[128,128]{1,0:T(8,128)} %param.11) | copy-start | bytes 196612
  0.7 39.7 %copy-start.16 = (f32[128]{0:T(128)S(1)}, f32[128]{0:T(128)}, u32[]{:S(2)}) copy-start(f32[128]{0:T(128)} %param.13) | copy-start | bytes 1540
  9.2 30.6 %all-to-all-start = ((f32[64,9,128]{2,1,0:T(8,128)}), f32[64,9,128]{2,1,0:T(8,128)S(1)}, u32[]{:S(2)}, u32[]{:S(2)}) async-start(f32[64,9,128]{2,1,0:T(8,128)} %pad_maximum_fusion), calls=%async_computation | async-start | bytes 1048576 | tf_op jit(solution)/shard_map/all_to_all | solution.py:105
  22.4 8.5 %collective-permute-start.2 = (f32[4,256]{1,0:T(4,128)S(1)}, f32[4,256]{1,0:T(4,128)S(1)}, u32[]{:S(2)}, u32[]{:S(2)}) collective-permute-start(f32[4,256]{1,0:T(4,128)S(1)} %copy-done.15), channel_id=1, source_target_pairs={{0,1},{1,2},{2,3},{3,4},{4,5},{5,6},{6,7},{7,8},{8,9},{9,10},{10,1... | collective-permute-start | bytes 12296 | tf_op jit(solution)/shard_map/ppermute | solution.py:16
  25.9 10.2 %collective-permute-start.3 = (f32[4,256]{1,0:T(4,128)S(1)}, f32[4,256]{1,0:T(4,128)S(1)}, u32[]{:S(2)}, u32[]{:S(2)}) collective-permute-start(f32[4,256]{1,0:T(4,128)S(1)} %copy-done.15), channel_id=1, source_target_pairs={{1,0},{2,1},{3,2},{4,3},{5,4},{6,5},{7,6},{8,7},{9,8},{10,9},{11,1... | collective-permute-start | bytes 12296 | tf_op jit(solution)/shard_map/ppermute | solution.py:17
  43.7 5.2 %collective-permute-start = (f32[8,4,256]{2,1,0:T(4,128)S(1)}, f32[8,4,256]{2,1,0:T(4,128)S(1)}, u32[]{:S(2)}, u32[]{:S(2)}) collective-permute-start(f32[8,4,256]{2,1,0:T(4,128)S(1)} %bitcast.128), channel_id=1, source_target_pairs={{0,1},{1,2},{2,3},{3,4},{4,5},{5,6},{6,7},{7,8},{8,9},{9,10},{10,1... | collective-permute-start | bytes 98312 | tf_op jit(solution)/shard_map/ppermute | solution.py:16
  46.9 5.2 %collective-permute-start.1 = (f32[8,4,256]{2,1,0:T(4,128)S(1)}, f32[8,4,256]{2,1,0:T(4,128)S(1)}, u32[]{:S(2)}, u32[]{:S(2)}) collective-permute-start(f32[8,4,256]{2,1,0:T(4,128)S(1)} %bitcast.129), channel_id=1, source_target_pairs={{1,0},{2,1},{3,2},{4,3},{5,4},{6,5},{7,6},{8,7},{9,8},{10,9},{11,1... | collective-permute-start | bytes 98312 | tf_op jit(solution)/shard_map/ppermute | solution.py:17
  52.8 4.3 %collective-permute-start.4 = (f32[8,4,256]{2,1,0:T(4,128)S(1)}, f32[8,4,256]{2,1,0:T(4,128)S(1)}, u32[]{:S(2)}, u32[]{:S(2)}) collective-permute-start(f32[8,4,256]{2,1,0:T(4,128)S(1)} %fusion.214), channel_id=1, source_target_pairs={{0,1},{1,2},{2,3},{3,4},{4,5},{5,6},{6,7},{7,8},{8,9},{9,10},{10,1... | collective-permute-start | bytes 98312 | tf_op jit(solution)/shard_map/ppermute | solution.py:16
  54.7 5.2 %collective-permute-start.5 = (f32[8,4,256]{2,1,0:T(4,128)S(1)}, f32[8,4,256]{2,1,0:T(4,128)S(1)}, u32[]{:S(2)}, u32[]{:S(2)}) collective-permute-start(f32[8,4,256]{2,1,0:T(4,128)S(1)} %fusion.214), channel_id=1, source_target_pairs={{1,0},{2,1},{3,2},{4,3},{5,4},{6,5},{7,6},{8,7},{9,8},{10,9},{11,1... | collective-permute-start | bytes 98312 | tf_op jit(solution)/shard_map/ppermute | solution.py:17
  64.2 12.9 %all-to-all-start.1 = ((f32[4,4,64,128]{3,2,1,0:T(8,128)}), f32[4,4,64,128]{3,2,1,0:T(8,128)S(1)}, u32[]{:S(2)}, u32[]{:S(2)}) async-start(f32[4,4,64,128]{3,2,1,0:T(8,128)} %copy.61), calls=%async_computation.1 | async-start | bytes 1048576 | tf_op jit(solution)/shard_map/all_to_all | solution.py:158
  92.8 7.4 %collective-permute-start.6 = (f32[8,4,256]{2,1,0:T(4,128)S(1)}, f32[8,4,256]{2,1,0:T(4,128)S(1)}, u32[]{:S(2)}, u32[]{:S(2)}) collective-permute-start(f32[8,4,256]{2,1,0:T(4,128)S(1)} %bitcast.131), channel_id=1, source_target_pairs={{0,1},{1,2},{2,3},{3,4},{4,5},{5,6},{6,7},{7,8},{8,9},{9,10},{10,1... | collective-permute-start | bytes 98312 | tf_op jit(solution)/shard_map/ppermute | solution.py:16
  96.7 5.2 %collective-permute-start.7 = (f32[8,4,256]{2,1,0:T(4,128)S(1)}, f32[8,4,256]{2,1,0:T(4,128)S(1)}, u32[]{:S(2)}, u32[]{:S(2)}) collective-permute-start(f32[8,4,256]{2,1,0:T(4,128)S(1)} %bitcast.132), channel_id=1, source_target_pairs={{1,0},{2,1},{3,2},{4,3},{5,4},{6,5},{7,6},{8,7},{9,8},{10,9},{11,1... | collective-permute-start | bytes 98312 | tf_op jit(solution)/shard_map/ppermute | solution.py:17
  101.9 35.0 %copy-start.6 = (f32[8,4,256]{2,1,0:T(4,128)S(1)}, f32[8,4,256]{2,1,0:T(4,128)}, u32[]{:S(2)}) copy-start(f32[8,4,256]{2,1,0:T(4,128)} %get-tuple-element.16) | copy-start | bytes 98308
  107.8 23.7 %all-to-all-start.3 = ((f32[256,1,3]{2,1,0:T(1,128)}), f32[256,1,3]{2,1,0:T(1,128)S(1)}, u32[]{:S(2)}, u32[]{:S(2)}) async-start(f32[256,1,3]{2,1,0:T(1,128)} %broadcast_in_dim.34), calls=%async_computation.3 | async-start | bytes 262144 | tf_op jit(solution)/shard_map/all_to_all | solution.py:58
  118.7 17.6 %collective-permute-start.8 = (f32[8,4,256]{2,1,0:T(4,128)S(1)}, f32[8,4,256]{2,1,0:T(4,128)S(1)}, u32[]{:S(2)}, u32[]{:S(2)}) collective-permute-start(f32[8,4,256]{2,1,0:T(4,128)S(1)} %get-tuple-element.11), channel_id=1, source_target_pairs={{0,1},{1,2},{2,3},{3,4},{4,5},{5,6},{6,7},{7,8},{8,9},{9,10},{10,1... | collective-permute-start | bytes 98312 | tf_op jit(solution)/shard_map/ppermute | solution.py:16
  122.3 13.9 %collective-permute-start.9 = (f32[8,4,256]{2,1,0:T(4,128)S(1)}, f32[8,4,256]{2,1,0:T(4,128)S(1)}, u32[]{:S(2)}, u32[]{:S(2)}) collective-permute-start(f32[8,4,256]{2,1,0:T(4,128)S(1)} %get-tuple-element.11), channel_id=1, source_target_pairs={{1,0},{2,1},{3,2},{4,3},{5,4},{6,5},{7,6},{8,7},{9,8},{10,9},{11,1... | collective-permute-start | bytes 98312 | tf_op jit(solution)/shard_map/ppermute | solution.py:17
  139.1 13.4 %copy-start.8 = (s32[512]{0:T(512)S(1)}, s32[512]{0:T(512)}, u32[]{:S(2)}) copy-start(s32[512]{0:T(512)} %get-tuple-element.13) | copy-start | bytes 6148
  139.1 13.4 %copy-start.12 = (pred[512]{0:T(512)(128)(4,1)S(1)}, pred[512]{0:T(512)(128)(4,1)}, u32[]{:S(2)}) copy-start(pred[512]{0:T(512)(128)(4,1)} %get-tuple-element.14) | copy-start | bytes 1540
  139.1 14.0 %copy-start.5 = (f32[128,128]{1,0:T(8,128)S(1)}, f32[128,128]{1,0:T(8,128)}, u32[]{:S(2)}) copy-start(f32[128,128]{1,0:T(8,128)} %param.11) | copy-start | bytes 196612
  139.1 14.0 %copy-start.10 = (f32[512]{0:T(512)S(1)}, f32[512]{0:T(512)}, u32[]{:S(2)}) copy-start(f32[512]{0:T(512)} %copy-done.9) | copy-start | bytes 6148
  139.1 14.0 %copy-start.17 = (f32[128]{0:T(128)S(1)}, f32[128]{0:T(128)}, u32[]{:S(2)}) copy-start(f32[128]{0:T(128)} %param.13) | copy-start | bytes 1540
  140.0 12.2 %all-to-all-start.4 = ((f32[4,4,64,128]{3,2,1,0:T(8,128)}), f32[4,4,64,128]{3,2,1,0:T(8,128)S(1)}, u32[]{:S(2)}, u32[]{:S(2)}) async-start(f32[4,4,64,128]{3,2,1,0:T(8,128)} %copy.64), calls=%async_computation.4 | async-start | bytes 1048576 | tf_op jit(solution)/shard_map/all_to_all | solution.py:158
  (8 other events, 67.0 us)
